TPU v7x, 128 devices: a whole 4x4x4 slice. The times are simulated.
128 devices in a mesh: frow: 16 (over y, z), fcol: 8 (over x, core).
Axes of the slice: x: 4, y: 4, z: 4, core: 2. Of those that a mesh axis runs over, the one named last changes fastest.
Arguments:
- front_orig: float32 [16, 1024, 8, 2048], P('frow', None, 'fcol'), may hold values from -0.1 to 45, as said below
- child_tiles: bfloat16 [8192, 128, 128], P(('frow', 'fcol')), may hold values from -0.25 to 0.25
- tile_target: int32 [8192, 2], P(('frow', 'fcol')), may hold values from 0 to 127, as said below
- tile_rows: int32 [8192, 128], P(('frow', 'fcol')), may hold values from 0 to 127, each once within a row
- tile_cols: int32 [8192, 128], P(('frow', 'fcol')), may hold values from 0 to 127, each once within a row
Outputs:
- front_out: float32 [16, 1024, 8, 2048], P('frow', None, 'fcol')
Inputs may be any that keep to these rules, and one draw needn't show every extreme that they name: `front_orig`: Symmetric; the lower triangle of the front after every tile is added defines a positive definite matrix. `tile_target`: rows come 64 to a device in device order. Column 0 is the owner, frow index times 8 plus fcol index; column 1 the local block on that owner, local block row times 16 plus local block column; the block lies on or below the front's block diagonal. At most 2 tiles of one device go to one owner, and one owner receives exactly 2 from every device.
All inputs are finite; a program needn't handle non-finite values.
Results may differ from a plain program's by a relative error of at most 0.0003.
Values may be sent and summed in bfloat16 or wider, within the bound.
No kernel may reach another device: no remote copies, remote signals or barrier semaphores. Data moves between devices by JAX's collectives and lax.ppermute only.
A program may use at most 128 MiB of HBM per device.

v0:
```python
import jax
import jax.numpy as jnp
from jax import lax
from jax.sharding import PartitionSpec as P

PW = 512
NPANEL = 2
CAP = 2


def as_sent(x):
    return jax.tree.map(lambda a: a.astype(jnp.bfloat16) if a.dtype == jnp.float32 else a, x)


def broadcast(block, axis, source):
    block = jnp.where(lax.axis_index(axis) == source, block, jnp.zeros_like(block))
    return lax.psum(block, axis)


def place_tiles(received):
    tile_block, perm_block, target_block = received
    width = tile_block.shape[-1]
    positions = jnp.arange(width, dtype=jnp.int32)
    row_onehot = (perm_block[:, :, 0, None, :] == positions[:, None]).astype(jnp.bfloat16)
    col_onehot = (perm_block[:, :, 1, None, :] == positions[:, None]).astype(jnp.bfloat16)
    moved = jnp.einsum(
        "abxi,abij->abxj", row_onehot, tile_block, preferred_element_type=jnp.float32
    ).astype(jnp.bfloat16)
    placed = jnp.einsum(
        "abxj,abyj->abxy", moved, col_onehot, preferred_element_type=jnp.float32
    ).astype(jnp.bfloat16)
    return (placed, target_block)


def subtract_product(matrix, row_factor, col_factor):
    product = jnp.dot(
        row_factor,
        col_factor.T,
        precision=lax.Precision.HIGHEST,
        preferred_element_type=jnp.float32,
    )
    return matrix - product


def shards(front_orig, child_tiles, tile_target, tile_rows, tile_cols):
    row_devs = lax.axis_size("frow")
    col_devs = lax.axis_size("fcol")
    owners = row_devs * col_devs
    row_here = lax.axis_index("frow")
    col_here = lax.axis_index("fcol")
    width = child_tiles.shape[1]
    held = child_tiles.shape[0]
    slot_count = owners * CAP
    owner_of = tile_target[:, 0]
    block_of = tile_target[:, 1]
    tile_order = jnp.arange(held, dtype=jnp.int32)
    same_owner = owner_of[:, None] == owner_of[None, :]
    earlier = tile_order[None, :] < tile_order[:, None]
    rank_of = jnp.sum(jnp.where(same_owner & earlier, 1, 0), axis=1).astype(jnp.int32)
    slot_of = owner_of * CAP + rank_of
    slot_match = slot_of[None, :] == jnp.arange(slot_count, dtype=jnp.int32)[:, None]
    source_tile = jnp.sum(jnp.where(slot_match, tile_order[None, :], 0), axis=1)
    filled = jnp.any(slot_match, axis=1)
    send_tiles = jnp.where(
        filled[:, None, None],
        jnp.take(child_tiles, source_tile, axis=0),
        jnp.zeros((), jnp.bfloat16),
    )
    send_perms = jnp.stack(
        [jnp.take(tile_rows, source_tile, axis=0), jnp.take(tile_cols, source_tile, axis=0)], axis=1
    )
    send_blocks = jnp.take(block_of, source_tile, axis=0)
    placed, blocks_in = place_tiles(
        (
            lax.all_to_all(
                send_tiles.reshape(owners, CAP, width, width),
                ("frow", "fcol"),
                split_axis=0,
                concat_axis=0,
                tiled=True,
            ),
            lax.all_to_all(
                send_perms.reshape(owners, CAP, 2, width),
                ("frow", "fcol"),
                split_axis=0,
                concat_axis=0,
                tiled=True,
            ),
            lax.all_to_all(
                send_blocks.reshape(owners, CAP),
                ("frow", "fcol"),
                split_axis=0,
                concat_axis=0,
                tiled=True,
            ),
        )
    )
    local = front_orig[0, :, 0, :]
    row_blocks = local.shape[0] // width
    col_blocks = local.shape[1] // width
    block_ids = jnp.arange(row_blocks * col_blocks, dtype=jnp.int32)
    block_onehot = (blocks_in.reshape(1, slot_count) == block_ids[:, None]).astype(jnp.bfloat16)
    summed = jnp.dot(
        block_onehot, placed.reshape(slot_count, width * width), preferred_element_type=jnp.float32
    )
    added = (
        summed.reshape(row_blocks, col_blocks, width, width)
        .transpose(0, 2, 1, 3)
        .reshape(local.shape)
    )
    matrix = local + added
    local_rows = jnp.arange(local.shape[0], dtype=jnp.int32)
    local_cols = jnp.arange(local.shape[1], dtype=jnp.int32)
    global_rows = (local_rows // width * row_devs + row_here) * width + local_rows % width
    global_cols = (local_cols // width * col_devs + col_here) * width + local_cols % width
    panel_blocks = PW // width
    ratio = row_devs // col_devs
    for panel_idx in range(NPANEL):
        start = panel_idx * PW
        stop = start + PW
        first_block = panel_idx * panel_blocks
        col_slot = first_block // col_devs
        col_first = first_block % col_devs
        row_slot = first_block // row_devs
        row_first = first_block % row_devs
        own_column = matrix[:, col_slot * width : (col_slot + 1) * width]
        wide_panel = lax.all_gather(
            own_column.astype(jnp.bfloat16), "fcol", axis=1, tiled=True
        ).astype(own_column.dtype)
        panel = wide_panel[:, col_first * width : col_first * width + PW]
        diag_rows = lax.all_gather(
            panel[row_slot * width : (row_slot + 1) * width].astype(jnp.bfloat16),
            "frow",
            axis=0,
            tiled=True,
        ).astype(jnp.float32)
        diag_block = diag_rows[row_first * width : row_first * width + PW]
        symmetric = jnp.tril(diag_block) + jnp.tril(diag_block, -1).T
        factor = jnp.linalg.cholesky(symmetric)
        solved = lax.linalg.triangular_solve(
            factor, panel, left_side=False, lower=True, transpose_a=True
        )
        below = (global_rows >= stop)[:, None]
        inside = (global_rows >= start)[:, None]
        factor_rows = jnp.take(factor, jnp.clip(global_rows - start, 0, PW - 1), axis=0)
        new_panel = jnp.where(below, solved, jnp.where(inside, factor_rows, 0.0))
        row_factor = jnp.where(below, solved, 0.0)
        stacked = row_factor.reshape(row_blocks, width, PW)
        pieces = []
        for offset in range(ratio):
            pieces.append(
                broadcast(as_sent(stacked), "frow", col_here + col_devs * offset).astype(
                    stacked.dtype
                )
            )
        col_factor = jnp.stack(pieces, axis=1).reshape(local.shape[1], PW)
        matrix = subtract_product(matrix, row_factor, col_factor)
        in_panel = (col_here >= col_first) & (col_here < col_first + panel_blocks)
        shift_cols = jnp.clip(col_here - col_first, 0, panel_blocks - 1) * width
        own_part = lax.dynamic_slice_in_dim(new_panel, shift_cols, width, axis=1)
        current = matrix[:, col_slot * width : (col_slot + 1) * width]
        matrix = matrix.at[:, col_slot * width : (col_slot + 1) * width].set(
            jnp.where(in_panel, own_part, current)
        )
    lower_part = global_rows[:, None] >= global_cols[None, :]
    result = jnp.where(lower_part, matrix, 0.0)
    return result[None, :, None, :]


def solution(mesh):
    return jax.shard_map(
        shards,
        mesh=mesh,
        in_specs=(
            P("frow", None, "fcol", None),
            P(("frow", "fcol"), None, None),
            P(("frow", "fcol"), None),
            P(("frow", "fcol"), None),
            P(("frow", "fcol"), None),
        ),
        out_specs=P("frow", None, "fcol", None),
        check_vma=False,
    )
```

profile of v0, /device:TPU:6, one launch (start us, length us, event | category | flops | bytes accessed | tf_op | source)
XLA Modules:
  0.0 935.0 jit_solution(13525251485987118323)
XLA Ops:
  8.5 1.9 gather_fusion
  11.2 10.5 %all-to-all-start = ((s32[128,1,2]{2,1,0:T(1,128)}), s32[128,1,2]{2,1,0:T(1,128)S(1)}, u32[]{:S(2)}, u32[]{:S(2)}) async-start(s32[128,1,2]{2,1,0:T(1,128)} %bitcast.4), calls=%async_computation | async-start | bytes 131072 | tf_op jit(solution)/shard_map/all_to_all | solution.py:89
  24.3 8.6 gather_fusion.1
  33.1 9.8 %all-to-all-start.1 = ((s32[128,2,2,128]{3,1,2,0:T(2,128)}), s32[128,2,2,128]{3,1,2,0:T(2,128)S(1)}, u32[]{:S(2)}, u32[]{:S(2)}) async-start(s32[128,2,2,128]{3,1,2,0:T(2,128)} %pad_add_fusion), calls=%async_computation.1 | async-start | bytes 524288 | tf_op jit(solution)/shard_map/all_to_all | solution.py:82
  42.8 7.4 select_select_fusion
  50.3 2.2 all-to-all-done.1
  52.5 8.0 all-to-all-start.2
  62.0 98.2 %all-to-all-done.2 = bf16[128,2,128,128]{3,2,1,0:T(8,128)(2,1)} async-done(((bf16[128,2,128,128]{3,2,1,0:T(8,128)(2,1)}), bf16[128,2,128,128]{3,2,1,0:T(8,128)(2,1)}, u32[]{:S(2)}, u32[]{:S(2)}) %all-to-all-start.2) | async-done | bytes 8388640 | tf_op jit(solution)/shard_map/all_to_all | solution.py:75
  160.2 13.3 %fusion.6 = bf16[128,2,128,128]{3,2,1,0:T(8,128)(2,1)} fusion(s32[128,2,128]{2,1,0:T(2,128)S(1)} %get-tuple-element.84, bf16[128,2,128,128]{3,2,1,0:T(8,128)(2,1)} %all-to-all-done.2, s32[128,2,128]{2,1,0:T(2,128)S(1)} %get-tuple-element.83), kind=kOutput, calls=%fused_computation.21 | convolution fusion | flops 2164260864 | bytes 17039360 | tf_op jit(solution)/shard_map/abxj,abyj->abxy/dot_general | solution.py:29
  173.5 34.5 %copy.135 = bf16[32,8,128,128]{3,1,2,0:T(8,128)(2,1)} copy(bf16[32,8,128,128]{3,2,1,0:T(8,128)(2,1)} %bitcast.182) | data formatting | bytes 16777216
  207.9 11.9 %copy.86 = bf16[16384,256]{1,0:T(8,128)(2,1)} copy(bf16[16384,256]{0,1:T(8,128)(2,1)} %bitcast.168) | data formatting | bytes 16777216 | tf_op jit(solution)/shard_map/dot_general | solution.py:103
  219.8 9.4 %fusion.69 = f32[8,16,128,128]{3,1,2,0:T(8,128)} fusion(bf16[128,128,256,1]{2,1,0,3:T(8,128)(2,1)} %bitcast.183, s32[8,16]{1,0:T(8,128)S(1)} %multiply_add_fusion, s32[256]{0:T(256)S(1)} %eq.100), kind=kOutput, calls=%fused_computation.128 | convolution fusion | flops 1073774592 | bytes 16778752 | tf_op jit(solution)/shard_map/dot_general | solution.py:103
  229.3 17.6 %bitcast_add_fusion = f32[1024,2048]{1,0:T(8,128)} fusion(f32[128,8,16,128]{3,2,1,0:T(8,128)} %bitcast.179, f32[1,1024,1,2048]{3,2,1,0:T(1,128)} %param.16), kind=kLoop, calls=%fused_computation.14 | loop fusion | flops 2097152 | bytes 25165824 | tf_op jit(solution)/shard_map/add | solution.py:111
  246.8 1.8 slice.359
  248.7 32.0 %all-gather.5.cloned.1.call-done = bf16[1024,1024]{1,0:T(8,128)(2,1)} async-done(((bf16[1024,128]{1,0:T(8,128)(2,1)}), bf16[1024,1024]{1,0:T(8,128)(2,1)}) %all-gather.5.cloned.1.call-update) | async-done | bytes 2097168 | tf_op jit(solution)/shard_map/all_gather | solution.py:127
  280.7 1.6 slice.263
  282.8 2.9 slice_convert_fusion.1
  285.6 44.1 %all-gather.7.cloned.1.call-done = bf16[2048,512]{1,0:T(8,128)(2,1)} async-done(((bf16[128,512]{1,0:T(8,128)(2,1)}), bf16[2048,512]{1,0:T(8,128)(2,1)}) %all-gather.7.cloned.1.call-update) | async-done | bytes 2097168 | tf_op jit(solution)/shard_map/all_gather | solution.py:131
  333.2 11.7 %cholesky.286 = f32[128,128]{1,0:T(8,128)S(1)} custom-call(f32[128,128]{1,0:T(8,128)S(1)} %cholesky.426), custom_call_target="Cholesky" | custom-call | tf_op jit(solution)/shard_map/jit(cholesky)/cholesky | solution.py:139
  345.0 9.8 %custom-call.27 = f32[1,128,128]{1,2,0:T(8,128)S(1)} custom-call(f32[1,128,128]{2,1,0:T(8,128)S(1)} %get-tuple-element.104), custom_call_target="InvertDiagBlocksLowerTriangular" | custom-call | tf_op jit(solution)/shard_map/jit(cholesky)/cholesky | solution.py:139
  355.5 11.7 %cholesky.305 = f32[128,128]{1,0:T(8,128)S(1)} custom-call(f32[128,128]{1,0:T(8,128)S(1)} %cholesky.430), custom_call_target="Cholesky" | custom-call | tf_op jit(solution)/shard_map/jit(cholesky)/cholesky | solution.py:139
  367.3 10.0 %custom-call.28 = f32[1,128,128]{1,2,0:T(8,128)S(1)} custom-call(f32[1,128,128]{2,1,0:T(8,128)S(1)} %get-tuple-element.101), custom_call_target="InvertDiagBlocksLowerTriangular" | custom-call | tf_op jit(solution)/shard_map/jit(cholesky)/cholesky | solution.py:139
  377.9 11.7 %cholesky.326 = f32[128,128]{1,0:T(8,128)S(1)} custom-call(f32[128,128]{1,0:T(8,128)S(1)} %cholesky.435), custom_call_target="Cholesky" | custom-call | tf_op jit(solution)/shard_map/jit(cholesky)/cholesky | solution.py:139
  389.7 9.8 %custom-call.29 = f32[1,128,128]{1,2,0:T(8,128)S(1)} custom-call(f32[1,128,128]{2,1,0:T(8,128)S(1)} %get-tuple-element.98), custom_call_target="InvertDiagBlocksLowerTriangular" | custom-call | tf_op jit(solution)/shard_map/jit(cholesky)/cholesky | solution.py:139
  400.1 12.1 %cholesky.343 = f32[128,128]{1,0:T(8,128)S(1)} custom-call(f32[128,128]{1,0:T(8,128)S(1)} %convolution_subtract_fusion.11), custom_call_target="Cholesky" | custom-call | tf_op jit(solution)/shard_map/jit(cholesky)/cholesky | solution.py:139
  416.8 7.8 while.6
  424.7 39.3 %custom-call.30 = f32[4,128,128]{1,2,0:T(8,128)S(1)} custom-call(f32[4,128,128]{2,1,0:T(8,128)S(1)} %get-tuple-element.47), custom_call_target="InvertDiagBlocksLowerTriangular" | custom-call | tf_op jit(solution)/shard_map/triangular_solve/custom-call.3 | solution.py:140
  464.0 1.7 fusion.51
  465.7 2.8 convolution_subtract_fusion.5
  468.7 1.6 fusion.80
  470.4 2.0 convolution_subtract_fusion.3
  473.0 2.6 fusion.26
  476.1 1.7 broadcast_select_fusion.3
  478.6 4.9 gather_fusion.4
  485.0 82.8 %all-reduce.8.cloned.1.call-done = (bf16[8,1,128,512]{3,2,1,0:T(8,128)(2,1)}, bf16[8,1,128,512]{3,2,1,0:T(8,128)(2,1)}) async-done(((bf16[8,1,128,512]{3,2,1,0:T(8,128)(2,1)}, bf16[8,1,128,512]{3,2,1,0:T(8,128)(2,1)}), (bf16[8,1,128,512]{3,2,1,0:T(8,128)(2,1)}, bf16[8,1,128,512]{3,2,1,0:T(8,128)(2,1)})) %all-reduce.8.cloned.1.call-update) | async-done | bytes 2097168 | tf_op jit(solution)/shard_map/psum | solution.py:17
  567.8 1.7 pad_maximum_fusion.1
  569.5 9.9 %convolution_subtract_fusion.1 = f32[1024,2048]{1,0:T(8,128)S(1)} fusion(f32[1024,2048]{1,0:T(8,128)} %bitcast_add_fusion, bf16[2048,512]{1,0:T(8,128)(2,1)S(1)} %bitcast.180, pred[1024]{0:T(1024)(128)(4,1)S(1)} %get-tuple-element.118, f32[1024,128]{1,0:T(8,128)S(1)} %fusion.78, f32[1024,128]{1,0:T(8,128)S(1)} %fusion.79, f32[1024,128]{1,0:T(8,128)S(1)} %fusion.80, ...), kind=kOutput, calls=%fused_computation.23 | convolution fusion | flops 12889096192 | bytes 20972544 | tf_op jit(solution)/shard_map/dot_general | solution.py:36
  579.5 3.4 copy-done.2
  582.8 3.3 fusion.124
  586.2 26.1 %all-gather.9.cloned.1.call-done = bf16[1024,1024]{1,0:T(8,128)(2,1)} async-done(((bf16[1024,128]{1,0:T(8,128)(2,1)}), bf16[1024,1024]{1,0:T(8,128)(2,1)}) %all-gather.9.cloned.1.call-update) | async-done | bytes 2097168 | tf_op jit(solution)/shard_map/all_gather | solution.py:127
  614.7 2.9 slice_convert_fusion
  617.5 44.0 %all-gather.11.cloned.1.call-done = bf16[2048,512]{1,0:T(8,128)(2,1)} async-done(((bf16[128,512]{1,0:T(8,128)(2,1)}), bf16[2048,512]{1,0:T(8,128)(2,1)}) %all-gather.11.cloned.1.call-update) | async-done | bytes 2097168 | tf_op jit(solution)/shard_map/all_gather | solution.py:131
  665.0 11.7 %cholesky.358 = f32[128,128]{1,0:T(8,128)S(1)} custom-call(f32[128,128]{1,0:T(8,128)S(1)} %cholesky.439), custom_call_target="Cholesky" | custom-call | tf_op jit(solution)/shard_map/jit(cholesky)/cholesky | solution.py:139
  676.8 9.8 %custom-call.31 = f32[1,128,128]{1,2,0:T(8,128)S(1)} custom-call(f32[1,128,128]{2,1,0:T(8,128)S(1)} %get-tuple-element.94), custom_call_target="InvertDiagBlocksLowerTriangular" | custom-call | tf_op jit(solution)/shard_map/jit(cholesky)/cholesky | solution.py:139
  687.3 11.9 %cholesky.377 = f32[128,128]{1,0:T(8,128)S(1)} custom-call(f32[128,128]{1,0:T(8,128)S(1)} %cholesky.443), custom_call_target="Cholesky" | custom-call | tf_op jit(solution)/shard_map/jit(cholesky)/cholesky | solution.py:139
  699.2 9.8 %custom-call.32 = f32[1,128,128]{1,2,0:T(8,128)S(1)} custom-call(f32[1,128,128]{2,1,0:T(8,128)S(1)} %get-tuple-element.91), custom_call_target="InvertDiagBlocksLowerTriangular" | custom-call | tf_op jit(solution)/shard_map/jit(cholesky)/cholesky | solution.py:139
  709.7 11.7 %cholesky.398 = f32[128,128]{1,0:T(8,128)S(1)} custom-call(f32[128,128]{1,0:T(8,128)S(1)} %cholesky.448), custom_call_target="Cholesky" | custom-call | tf_op jit(solution)/shard_map/jit(cholesky)/cholesky | solution.py:139
  721.5 9.8 %custom-call.33 = f32[1,128,128]{1,2,0:T(8,128)S(1)} custom-call(f32[1,128,128]{2,1,0:T(8,128)S(1)} %get-tuple-element.88), custom_call_target="InvertDiagBlocksLowerTriangular" | custom-call | tf_op jit(solution)/shard_map/jit(cholesky)/cholesky | solution.py:139
  731.9 12.1 %cholesky.415 = f32[128,128]{1,0:T(8,128)S(1)} custom-call(f32[128,128]{1,0:T(8,128)S(1)} %convolution_subtract_fusion.10), custom_call_target="Cholesky" | custom-call | tf_op jit(solution)/shard_map/jit(cholesky)/cholesky | solution.py:139
  749.5 7.9 while.7
  757.4 39.3 %custom-call.34 = f32[4,128,128]{1,2,0:T(8,128)S(1)} custom-call(f32[4,128,128]{2,1,0:T(8,128)S(1)} %get-tuple-element.48), custom_call_target="InvertDiagBlocksLowerTriangular" | custom-call | tf_op jit(solution)/shard_map/triangular_solve/custom-call.3 | solution.py:140
  796.8 1.7 fusion.48
  798.4 2.8 convolution_subtract_fusion.4
  801.5 1.6 fusion.74
  803.1 2.0 convolution_subtract_fusion.2
  805.7 2.6 fusion.23
  808.9 1.7 broadcast_select_fusion.2
  810.6 1.9 constant_dynamic-update-slice_fusion.2
  812.5 4.9 gather_fusion.5
  818.9 81.6 %all-reduce.6.cloned.1.call-done = (bf16[8,1,128,512]{3,2,1,0:T(8,128)(2,1)}, bf16[8,1,128,512]{3,2,1,0:T(8,128)(2,1)}) async-done(((bf16[8,1,128,512]{3,2,1,0:T(8,128)(2,1)}, bf16[8,1,128,512]{3,2,1,0:T(8,128)(2,1)}), (bf16[8,1,128,512]{3,2,1,0:T(8,128)(2,1)}, bf16[8,1,128,512]{3,2,1,0:T(8,128)(2,1)})) %all-reduce.6.cloned.1.call-update) | async-done | bytes 2097168 | tf_op jit(solution)/shard_map/psum | solution.py:17
  900.5 1.7 pad_maximum_fusion.3
  902.2 10.0 %convolution_subtract_fusion = f32[1024,2048]{1,0:T(8,128)S(1)} fusion(f32[1024,2048]{1,0:T(8,128)} %constant_dynamic-update-slice_fusion.2, bf16[2048,512]{1,0:T(8,128)(2,1)S(1)} %bitcast.181, pred[1024]{0:T(1024)(128)(4,1)S(1)} %get-tuple-element.117, f32[1024,128]{1,0:T(8,128)S(1)} %fusion.72, f32[1024,128]{1,0:T(8,128)S(1)} %fusion.73, ...), kind=kOutput, calls=%fused_computation.22 | convolution fusion | flops 12889096192 | bytes 20972544 | tf_op jit(solution)/shard_map/dot_general | solution.py:36
  912.2 2.6 fusion.46
  915.5 12.5 %copy.111 = f32[1,1024,1,2048]{3,2,1,0:T(1,128)} copy(f32[1,1024,1,2048]{3,1,2,0:T(8,128)S(1)} %select_bitcast_fusion) | data formatting | bytes 16777216 | tf_op jit(solution)/shard_map/broadcast_in_dim | solution.py:167
  (146 shorter events, 48.6 us)
Async XLA Ops:
  6.5 17.8 %copy-start = (bf16[64,128,128]{2,1,0:T(8,128)(2,1)S(1)}, bf16[64,128,128]{2,1,0:T(8,128)(2,1)}, u32[]{:S(2)}) copy-start(bf16[64,128,128]{2,1,0:T(8,128)(2,1)} %param.17) | copy-start | bytes 6291460
  6.5 15.3 %copy-start.3 = (s32[64,128]{1,0:T(8,128)S(1)}, s32[64,128]{1,0:T(8,128)}, u32[]{:S(2)}) copy-start(s32[64,128]{1,0:T(8,128)} %param.19) | copy-start | bytes 98308
  6.5 16.0 %copy-start.4 = (s32[64,128]{1,0:T(8,128)S(1)}, s32[64,128]{1,0:T(8,128)}, u32[]{:S(2)}) copy-start(s32[64,128]{1,0:T(8,128)} %param.20) | copy-start | bytes 98308
  11.2 21.9 %all-to-all-start = ((s32[128,1,2]{2,1,0:T(1,128)}), s32[128,1,2]{2,1,0:T(1,128)S(1)}, u32[]{:S(2)}, u32[]{:S(2)}) async-start(s32[128,1,2]{2,1,0:T(1,128)} %bitcast.4), calls=%async_computation | async-start | bytes 131072 | tf_op jit(solution)/shard_map/all_to_all | solution.py:89
  33.1 19.4 %all-to-all-start.1 = ((s32[128,2,2,128]{3,1,2,0:T(2,128)}), s32[128,2,2,128]{3,1,2,0:T(2,128)S(1)}, u32[]{:S(2)}, u32[]{:S(2)}) async-start(s32[128,2,2,128]{3,1,2,0:T(2,128)} %pad_add_fusion), calls=%async_computation.1 | async-start | bytes 524288 | tf_op jit(solution)/shard_map/all_to_all | solution.py:82
  52.5 107.7 %all-to-all-start.2 = ((bf16[128,2,128,128]{3,2,1,0:T(8,128)(2,1)}), bf16[128,2,128,128]{3,2,1,0:T(8,128)(2,1)}, u32[]{:S(2)}, u32[]{:S(2)}) async-start(bf16[128,2,128,128]{3,2,1,0:T(8,128)(2,1)} %select_select_fusion), calls=%async_computation.2 | async-start | bytes 16777216 | tf_op jit(solution)/shard_map/all_to_all | solution.py:75
  60.5 220.2 %all-gather.5.cloned.1.call-start = ((), (), s32[]{:S(2)}) async-start(), calls=%async_computation.3 | async-start | bytes 2359296 | tf_op jit(solution)/shard_map/all_gather | solution.py:127
  248.6 81.2 %all-gather.7.cloned.1.call-start = ((), (), s32[]{:S(2)}) async-start(), calls=%async_computation.4 | async-start | bytes 2228224 | tf_op jit(solution)/shard_map/all_gather | solution.py:131
  282.3 285.5 %all-reduce.8.cloned.1.call-start = ((), (), s32[]{:S(2)}) async-start(), calls=%async_computation.8 | async-start | bytes 4194304 | tf_op jit(solution)/shard_map/psum | solution.py:17
  424.7 45.7 %copy-start.6 = (f32[512,512]{1,0:T(8,128)}, f32[512,512]{1,0:T(8,128)S(1)}, u32[]{:S(2)}) copy-start(f32[512,512]{1,0:T(8,128)S(1)} %get-tuple-element.230) | copy-start | bytes 3145732
  477.9 134.5 %all-gather.9.cloned.1.call-start = ((), (), s32[]{:S(2)}) async-start(), calls=%async_computation.5 | async-start | bytes 2359296 | tf_op jit(solution)/shard_map/all_gather | solution.py:127
  579.4 3.4 copy-start.2
  586.2 75.4 %all-gather.11.cloned.1.call-start = ((), (), s32[]{:S(2)}) async-start(), calls=%async_computation.6 | async-start | bytes 2228224 | tf_op jit(solution)/shard_map/all_gather | solution.py:131
  613.9 286.5 %all-reduce.6.cloned.1.call-start = ((), (), s32[]{:S(2)}) async-start(), calls=%async_computation.7 | async-start | bytes 4194304 | tf_op jit(solution)/shard_map/psum | solution.py:17
  757.4 45.7 %copy-start.5 = (f32[512,512]{1,0:T(8,128)}, f32[512,512]{1,0:T(8,128)S(1)}, u32[]{:S(2)}) copy-start(f32[512,512]{1,0:T(8,128)S(1)} %get-tuple-element.229) | copy-start | bytes 3145732
  915.5 12.5 %copy-start.1 = (bf16[64,128,128]{2,1,0:T(8,128)(2,1)S(1)}, bf16[64,128,128]{2,1,0:T(8,128)(2,1)}, u32[]{:S(2)}) copy-start(bf16[64,128,128]{2,1,0:T(8,128)(2,1)} %param.17) | copy-start | bytes 6291460
Sparse Core Ops, SparseCore 0:
  248.7 31.8 all-gather.4
  282.8 46.9 all-gather.6
  478.0 89.7 all-reduce.7
  586.3 26.0 all-gather.8
  614.6 46.9 all-gather.10
  810.7 89.7 all-reduce.5
where the time goes:
time: 944 us; the launch traced here: 935 us
  waiting for transfers between devices  411 us (44%)
  other arithmetic  294 us (31%)
  local copies, waits for them, and re-layouts  111 us (12%)
  matrix products  70 us (7%)
  starting transfers between devices  29.1 us (3%)
  between operations  19.4 us (2%)
    psum x2, waiting for transfers between devices, broadcast(): return lax.psum(block, axis)  164 us
    another operation x29, other arithmetic, shards(): factor = jnp.linalg.cholesky(symmetric)  159 us
    all_to_all x1, waiting for transfers between devices, shards(): lax.all_to_all(send_tiles.reshape(owners, CAP, width, width), ('frow', 'f...  98.2 us
    all_gather x2, waiting for transfers between devices, shards(): lax.all_gather(panel[row_slot * width:(row_slot + 1) * width].astype(jnp....  88.1 us
    another operation x7, other arithmetic, shards(): lax.linalg.triangular_solve(factor, panel, left_side=False, lower=True, t...  82.1 us
    all_gather x2, waiting for transfers between devices, shards(): lax.all_gather(own_column.astype(jnp.bfloat16), 'fcol', axis=1, tiled=True)  58.1 us
    unnamed x15, local copies, waits for them, and re-layouts  37.9 us
    another operation x14, matrix products, shards(): lax.linalg.triangular_solve(factor, panel, left_side=False, lower=True, t...  23.7 us
  transfers between devices with their start and end apart: 9, of which 8 were waited for; matrix products, arithmetic and copies ran while one was open for 4% of the time, Pallas kernels for 0%

commit v1 on v0

--- a/solution.py
+++ b/solution.py
@@ -113,55 +113,75 @@
     local_cols = jnp.arange(local.shape[1], dtype=jnp.int32)
     global_rows = (local_rows // width * row_devs + row_here) * width + local_rows % width
     global_cols = (local_cols // width * col_devs + col_here) * width + local_cols % width
-    panel_blocks = PW // width
-    ratio = row_devs // col_devs
+    total = NPANEL * PW
+    hi = lax.Precision.HIGHEST
+    row_panel = lax.all_gather(
+        matrix[:, :width].astype(jnp.bfloat16), "fcol", axis=1, tiled=True
+    )[:, :total]
+    half = row_devs // col_devs
+    perms = []
+    for shift in range(half):
+        pairs = []
+        for src_row in range(row_devs):
+            for src_col in range(col_devs):
+                part = src_row // col_devs
+                dst_row = ((part + shift) % half) * col_devs + src_col
+                dst_col = src_row % col_devs
+                pairs.append((src_row * col_devs + src_col, dst_row * col_devs + dst_col))
+        perms.append(pairs)
+    got = [lax.ppermute(row_panel, ("frow", "fcol"), perm) for perm in perms]
+    my_part = row_here // col_devs
+    ordered = []
+    for part in range(half):
+        pick = got[0]
+        for shift in range(1, half):
+            pick = jnp.where((my_part - shift) % half == part, got[shift], pick)
+        if half == 1:
+            pick = got[0]
+        ordered.append(pick.reshape(row_blocks, width, total))
+    col_panel = jnp.stack(ordered, axis=1).reshape(local.shape[1], total)
+    corner_blocks = total // width
+    first = matrix[:width, :width].astype(jnp.bfloat16)
+    every = lax.all_gather(first, ("frow", "fcol"), axis=0, tiled=False)
+    every = every.reshape(row_devs, col_devs, width, width)[:corner_blocks, :corner_blocks]
+    corner = every.transpose(0, 2, 1, 3).reshape(total, total).astype(jnp.float32)
+    rows_all = jnp.concatenate([row_panel, col_panel], axis=0).astype(jnp.float32)
+    n_own = local.shape[0]
+    factor_full = jnp.zeros((total, total), jnp.float32)
+    pieces = []
+    eye = jnp.eye(PW, dtype=jnp.float32)
     for panel_idx in range(NPANEL):
         start = panel_idx * PW
         stop = start + PW
-        first_block = panel_idx * panel_blocks
-        col_slot = first_block // col_devs
-        col_first = first_block % col_devs
-        row_slot = first_block // row_devs
-        row_first = first_block % row_devs
-        own_column = matrix[:, col_slot * width : (col_slot + 1) * width]
-        wide_panel = lax.all_gather(
-            own_column.astype(jnp.bfloat16), "fcol", axis=1, tiled=True
-        ).astype(own_column.dtype)
-        panel = wide_panel[:, col_first * width : col_first * width + PW]
-        diag_rows = lax.all_gather(
-            panel[row_slot * width : (row_slot + 1) * width].astype(jnp.bfloat16),
-            "frow",
-            axis=0,
-            tiled=True,
-        ).astype(jnp.float32)
-        diag_block = diag_rows[row_first * width : row_first * width + PW]
+        diag_block = corner[start:stop, start:stop]
         symmetric = jnp.tril(diag_block) + jnp.tril(diag_block, -1).T
         factor = jnp.linalg.cholesky(symmetric)
-        solved = lax.linalg.triangular_solve(
-            factor, panel, left_side=False, lower=True, transpose_a=True
+        inverse = lax.linalg.triangular_solve(factor, eye, left_side=True, lower=True)
+        factor_full = factor_full.at[start:stop, start:stop].set(factor)
+        solved_rows = jnp.dot(
+            rows_all[:, start:stop], inverse.T, precision=hi, preferred_element_type=jnp.float32
         )
-        below = (global_rows >= stop)[:, None]
-        inside = (global_rows >= start)[:, None]
-        factor_rows = jnp.take(factor, jnp.clip(global_rows - start, 0, PW - 1), axis=0)
-        new_panel = jnp.where(below, solved, jnp.where(inside, factor_rows, 0.0))
-        row_factor = jnp.where(below, solved, 0.0)
-        stacked = row_factor.reshape(row_blocks, width, PW)
-        pieces = []
-        for offset in range(ratio):
-            pieces.append(
-                broadcast(as_sent(stacked), "frow", col_here + col_devs * offset).astype(
-                    stacked.dtype
-                )
+        pieces.append(solved_rows)
+        if stop < total:
+            below = jnp.dot(
+                corner[stop:, start:stop], inverse.T, precision=hi, preferred_element_type=jnp.float32
             )
-        col_factor = jnp.stack(pieces, axis=1).reshape(local.shape[1], PW)
-        matrix = subtract_product(matrix, row_factor, col_factor)
-        in_panel = (col_here >= col_first) & (col_here < col_first + panel_blocks)
-        shift_cols = jnp.clip(col_here - col_first, 0, panel_blocks - 1) * width
-        own_part = lax.dynamic_slice_in_dim(new_panel, shift_cols, width, axis=1)
-        current = matrix[:, col_slot * width : (col_slot + 1) * width]
-        matrix = matrix.at[:, col_slot * width : (col_slot + 1) * width].set(
-            jnp.where(in_panel, own_part, current)
-        )
+            factor_full = factor_full.at[stop:, start:stop].set(below)
+            corner = corner.at[stop:, stop:].add(
+                -jnp.dot(below, below.T, precision=hi, preferred_element_type=jnp.float32)
+            )
+            rows_all = rows_all.at[:, stop:].add(
+                -jnp.dot(solved_rows, below.T, precision=hi, preferred_element_type=jnp.float32)
+            )
+    solved = jnp.concatenate(pieces, axis=1)
+    row_factor = solved[:n_own]
+    col_factor = solved[n_own:]
+    matrix = subtract_product(matrix, row_factor, col_factor)
+    in_corner = (global_rows < total)[:, None]
+    corner_rows = jnp.take(factor_full, jnp.clip(global_rows, 0, total - 1), axis=0)
+    panel_vals = jnp.where(in_corner, corner_rows, row_factor)
+    own_part = lax.dynamic_slice_in_dim(panel_vals, col_here * width, width, axis=1)
+    matrix = matrix.at[:, :width].set(own_part)
     lower_part = global_rows[:, None] >= global_cols[None, :]
     result = jnp.where(lower_part, matrix, 0.0)
     return result[None, :, None, :]

time: 944 us -> 987 us (1.046)
  waiting for transfers between devices: 411 us -> 308 us
  local copies, waits for them, and re-layouts: 111 us -> 194 us
  matrix products: 70 us -> 125 us
    ppermute x0 -> x2, waiting for transfers between devices: none -> 175 us  [shards(): got = [lax.ppermute(row_panel, ('frow', 'fcol'), perm) for perm in perms]]
    psum x2 -> x0, waiting for transfers between devices: 164 us -> none  [broadcast(): return lax.psum(block, axis)]
    all_gather x4 -> x2, waiting for transfers between devices: 146 us -> 54.1 us  [the longest x1 28.2 us: shards(): lax.all_gather(matrix[:, :width].astype(jnp.bfloat16), 'fcol', axis=1, ti...]
    dot_general x0 -> x5, matrix products: none -> 48.2 us  [the longest x1 21.5 us: shards(): jnp.dot(solved_rows, below.T, precision=hi, preferred_element_type=jnp.fl...]
    unnamed x15 -> x56, local copies, waits for them, and re-layouts: 37.9 us -> 77 us
    all_to_all x1, waiting for transfers between devices: 98.2 us -> 77.4 us  [shards(): lax.all_to_all(send_tiles.reshape(owners, CAP, width, width), ('frow', 'f...]
    add x1 -> x0, other arithmetic: 17.6 us -> none  [shards(): matrix = local + added]
    another operation x29, local copies, waits for them, and re-layouts: 16 us -> 31.2 us  [the longest x27 23.2 us: shards(): lax.linalg.triangular_solve(factor, eye, left_side=True, lower=True)]
  transfers between devices with their start and end apart: 9 -> 7, of which waited for: 8 -> 6; matrix products, arithmetic and copies ran while one was open for 4% -> 7% of each run, Pallas kernels for 0% -> 0%
where the time goes in v1:
time: 987 us; the launch traced here: 973 us
  waiting for transfers between devices  308 us (31%)
  other arithmetic  287 us (29%)
  local copies, waits for them, and re-layouts  194 us (20%)
  matrix products  125 us (13%)
  starting transfers between devices  38.4 us (4%)
  between operations  19.6 us (2%)
    ppermute x2, waiting for transfers between devices, shards(): got = [lax.ppermute(row_panel, ('frow', 'fcol'), perm) for perm in perms]  175 us
    another operation x29, other arithmetic, shards(): factor = jnp.linalg.cholesky(symmetric)  158 us
    another operation x4, other arithmetic, shards(): lax.linalg.triangular_solve(factor, eye, left_side=True, lower=True)  80.3 us
    all_to_all x1, waiting for transfers between devices, shards(): lax.all_to_all(send_tiles.reshape(owners, CAP, width, width), ('frow', 'f...  77.4 us
    unnamed x56, local copies, waits for them, and re-layouts  77 us
    dot_general x1, matrix products, subtract_product(): jnp.dot(row_factor, col_factor.T, precision=lax.Precision.HIGHEST, prefer...  30.5 us
    all_gather x1, waiting for transfers between devices, shards(): lax.all_gather(matrix[:, :width].astype(jnp.bfloat16), 'fcol', axis=1, ti...  28.2 us
    all_gather x1, waiting for transfers between devices, shards(): every = lax.all_gather(first, ('frow', 'fcol'), axis=0, tiled=False)  25.8 us
  transfers between devices with their start and end apart: 7, of which 6 were waited for; matrix products, arithmetic and copies ran while one was open for 7% of the time, Pallas kernels for 0%

profile of v1, /device:TPU:6, one launch (start us, length us, event | category | flops | bytes accessed | tf_op | source)
XLA Modules:
  0.0 972.8 jit_solution(10013576491422661252)
XLA Ops:
  11.2 10.5 %all-to-all-start = ((s32[128,1,2]{2,1,0:T(1,128)}), s32[128,1,2]{2,1,0:T(1,128)S(1)}, u32[]{:S(2)}, u32[]{:S(2)}) async-start(s32[128,1,2]{2,1,0:T(1,128)} %bitcast.5), calls=%async_computation | async-start | bytes 131072 | tf_op jit(solution)/shard_map/all_to_all | solution.py:89
  26.0 8.6 gather_fusion.1
  34.5 9.8 %all-to-all-start.1 = ((s32[128,2,2,128]{3,1,2,0:T(2,128)}), s32[128,2,2,128]{3,1,2,0:T(2,128)S(1)}, u32[]{:S(2)}, u32[]{:S(2)}) async-start(s32[128,2,2,128]{3,1,2,0:T(2,128)} %pad_add_fusion), calls=%async_computation.1 | async-start | bytes 524288 | tf_op jit(solution)/shard_map/all_to_all | solution.py:82
  44.3 7.4 select_select_fusion
  51.8 2.2 all-to-all-done.1
  54.0 8.0 all-to-all-start.2
  62.0 20.7 %copy.55 = f32[1,1024,1,2048]{1,3,2,0:T(8,128)} copy(f32[1,1024,1,2048]{3,2,1,0:T(1,128)} %param.22) | data formatting | bytes 16777216 | tf_op args[0]
  84.3 77.4 %all-to-all-done.2 = bf16[128,2,128,128]{3,2,1,0:T(8,128)(2,1)} async-done(((bf16[128,2,128,128]{3,2,1,0:T(8,128)(2,1)}), bf16[128,2,128,128]{3,2,1,0:T(8,128)(2,1)}, u32[]{:S(2)}, u32[]{:S(2)}) %all-to-all-start.2) | async-done | bytes 8388640 | tf_op jit(solution)/shard_map/all_to_all | solution.py:75
  161.7 13.1 %fusion.8 = bf16[128,2,128,128]{3,2,1,0:T(8,128)(2,1)} fusion(s32[128,2,128]{2,1,0:T(2,128)S(1)} %get-tuple-element.125, bf16[128,2,128,128]{3,2,1,0:T(8,128)(2,1)} %all-to-all-done.2, s32[128,2,128]{2,1,0:T(2,128)S(1)} %get-tuple-element.124), kind=kOutput, calls=%fused_computation.24 | convolution fusion | flops 2164260864 | bytes 17039360 | tf_op jit(solution)/shard_map/abxj,abyj->abxy/dot_general | solution.py:29
  174.8 35.1 %copy.100 = bf16[32,8,128,128]{3,1,2,0:T(8,128)(2,1)} copy(bf16[32,8,128,128]{3,2,1,0:T(8,128)(2,1)} %bitcast.180) | data formatting | bytes 16777216
  209.9 11.9 %copy.59 = bf16[16384,256]{1,0:T(8,128)(2,1)} copy(bf16[16384,256]{0,1:T(8,128)(2,1)} %bitcast.176) | data formatting | bytes 16777216 | tf_op jit(solution)/shard_map/dot_general | solution.py:103
  221.8 6.2 fusion.83
  228.1 7.5 copy.99
  235.6 9.2 copy.60
  244.8 7.3 fusion.17
  256.3 28.2 %all-gather.4.cloned.1.call-done = bf16[1024,1024]{0,1:T(8,128)(2,1)} async-done(((bf16[1024,128]{0,1:T(8,128)(2,1)}), bf16[1024,1024]{0,1:T(8,128)(2,1)}) %all-gather.4.cloned.1.call-update) | async-done | bytes 2097168 | tf_op jit(solution)/shard_map/all_gather | solution.py:118
  284.5 6.9 collective-permute-start.1
  291.4 3.2 collective-permute-start
  297.8 3.9 copy.63
  301.7 128.4 %collective-permute-done.1 = bf16[1024,1024]{0,1:T(8,128)(2,1)} collective-permute-done((bf16[1024,1024]{0,1:T(8,128)(2,1)}, bf16[1024,1024]{0,1:T(8,128)(2,1)}, u32[]{:S(2)}, u32[]{:S(2)}) %collective-permute-start.1) | collective-permute-done | bytes 2097184 | tf_op jit(solution)/shard_map/ppermute | solution.py:132
  430.1 46.3 %collective-permute-done = bf16[1024,1024]{0,1:T(8,128)(2,1)} collective-permute-done((bf16[1024,1024]{0,1:T(8,128)(2,1)}, bf16[1024,1024]{0,1:T(8,128)(2,1)}, u32[]{:S(2)}, u32[]{:S(2)}) %collective-permute-start) | collective-permute-done | bytes 2097184 | tf_op jit(solution)/shard_map/ppermute | solution.py:132
  476.5 4.5 broadcast_select_fusion.1
  481.0 3.9 copy.76
  484.9 4.0 copy.77
  488.9 4.6 pad_maximum_fusion.2
  493.5 25.8 %all-gather.6.cloned.1.call-done = bf16[16384,128]{0,1:T(8,128)(2,1)} async-done(((bf16[128,128]{0,1:T(8,128)(2,1)}), bf16[16384,128]{0,1:T(8,128)(2,1)}) %all-gather.6.cloned.1.call-update) | async-done | bytes 4194320 | tf_op jit(solution)/shard_map/all_gather | solution.py:145
  523.0 4.9 copy.64
  528.0 3.7 copy_bitcast_fusion.1
  537.0 11.7 %cholesky.286 = f32[128,128]{1,0:T(8,128)S(1)} custom-call(f32[128,128]{1,0:T(8,128)S(1)} %cholesky.426), custom_call_target="Cholesky" | custom-call | tf_op jit(solution)/shard_map/jit(cholesky)/cholesky | solution.py:158
  548.8 9.8 %custom-call.27 = f32[1,128,128]{1,2,0:T(8,128)S(1)} custom-call(f32[1,128,128]{2,1,0:T(8,128)S(1)} %get-tuple-element.145), custom_call_target="InvertDiagBlocksLowerTriangular" | custom-call | tf_op jit(solution)/shard_map/jit(cholesky)/cholesky | solution.py:158
  561.3 11.7 %cholesky.305 = f32[128,128]{1,0:T(8,128)S(1)} custom-call(f32[128,128]{1,0:T(8,128)S(1)} %cholesky.430), custom_call_target="Cholesky" | custom-call | tf_op jit(solution)/shard_map/jit(cholesky)/cholesky | solution.py:158
  573.0 10.0 %custom-call.28 = f32[1,128,128]{1,2,0:T(8,128)S(1)} custom-call(f32[1,128,128]{2,1,0:T(8,128)S(1)} %get-tuple-element.142), custom_call_target="InvertDiagBlocksLowerTriangular" | custom-call | tf_op jit(solution)/shard_map/jit(cholesky)/cholesky | solution.py:158
  584.6 11.7 %cholesky.326 = f32[128,128]{1,0:T(8,128)S(1)} custom-call(f32[128,128]{1,0:T(8,128)S(1)} %cholesky.435), custom_call_target="Cholesky" | custom-call | tf_op jit(solution)/shard_map/jit(cholesky)/cholesky | solution.py:158
  597.0 9.8 %custom-call.29 = f32[1,128,128]{1,2,0:T(8,128)S(1)} custom-call(f32[1,128,128]{2,1,0:T(8,128)S(1)} %get-tuple-element.139), custom_call_target="InvertDiagBlocksLowerTriangular" | custom-call | tf_op jit(solution)/shard_map/jit(cholesky)/cholesky | solution.py:158
  608.2 12.1 %cholesky.343 = f32[128,128]{1,0:T(8,128)S(1)} custom-call(f32[128,128]{1,0:T(8,128)S(1)} %convolution_subtract_fusion.11), custom_call_target="Cholesky" | custom-call | tf_op jit(solution)/shard_map/jit(cholesky)/cholesky | solution.py:158
  625.2 11.6 %while.10 = (s32[]{:T(128)}, f32[512,512]{1,0:T(8,128)}, s32[4,2]{0,1:T(2,128)S(1)}, f32[4,128,128]{2,1,0:T(8,128)S(1)}, s32[]{:T(128)}) while((s32[]{:T(128)}, f32[512,512]{1,0:T(8,128)}, s32[4,2]{0,1:T(2,128)S(1)}, f32[4,128,128]{2,1,0:T(8,128)S(1)}, s32[]{:T(128)}) %tuple.86), condition=%wide.while_cond.6, body=%wide.while_body.6.sunk | while | flops 2 | bytes 131189 | solution.py:159
  625.9 2.2 bitcast_dynamic-update-slice_fusion.4
  628.8 2.2 bitcast_dynamic-update-slice_fusion.4
  631.7 2.2 bitcast_dynamic-update-slice_fusion.4
  636.8 39.3 %custom-call.30 = f32[4,128,128]{1,2,0:T(8,128)S(1)} custom-call(f32[4,128,128]{2,1,0:T(8,128)S(1)} %get-tuple-element.94), custom_call_target="InvertDiagBlocksLowerTriangular" | custom-call | tf_op jit(solution)/shard_map/triangular_solve/custom-call.3 | solution.py:159
  682.2 2.5 scatter.14
  684.7 3.1 constant_dynamic-update-slice_fusion.4
  687.8 4.1 broadcast_select_fusion.2
  698.8 11.7 %cholesky.358 = f32[128,128]{1,0:T(8,128)S(1)} custom-call(f32[128,128]{1,0:T(8,128)S(1)} %cholesky.439), custom_call_target="Cholesky" | custom-call | tf_op jit(solution)/shard_map/jit(cholesky)/cholesky | solution.py:158
  711.2 10.0 %custom-call.31 = f32[1,128,128]{1,2,0:T(8,128)S(1)} custom-call(f32[1,128,128]{2,1,0:T(8,128)S(1)} %get-tuple-element.135), custom_call_target="InvertDiagBlocksLowerTriangular" | custom-call | tf_op jit(solution)/shard_map/jit(cholesky)/cholesky | solution.py:158
  724.5 11.7 %cholesky.377 = f32[128,128]{1,0:T(8,128)S(1)} custom-call(f32[128,128]{1,0:T(8,128)S(1)} %cholesky.443), custom_call_target="Cholesky" | custom-call | tf_op jit(solution)/shard_map/jit(cholesky)/cholesky | solution.py:158
  736.9 9.8 %custom-call.32 = f32[1,128,128]{1,2,0:T(8,128)S(1)} custom-call(f32[1,128,128]{2,1,0:T(8,128)S(1)} %get-tuple-element.132), custom_call_target="InvertDiagBlocksLowerTriangular" | custom-call | tf_op jit(solution)/shard_map/jit(cholesky)/cholesky | solution.py:158
  749.9 11.7 %cholesky.398 = f32[128,128]{1,0:T(8,128)S(1)} custom-call(f32[128,128]{1,0:T(8,128)S(1)} %cholesky.448), custom_call_target="Cholesky" | custom-call | tf_op jit(solution)/shard_map/jit(cholesky)/cholesky | solution.py:158
  762.3 10.0 %custom-call.33 = f32[1,128,128]{1,2,0:T(8,128)S(1)} custom-call(f32[1,128,128]{2,1,0:T(8,128)S(1)} %get-tuple-element.129), custom_call_target="InvertDiagBlocksLowerTriangular" | custom-call | tf_op jit(solution)/shard_map/jit(cholesky)/cholesky | solution.py:158
  774.5 11.7 %cholesky.415 = f32[128,128]{1,0:T(8,128)S(1)} custom-call(f32[128,128]{1,0:T(8,128)S(1)} %convolution_subtract_fusion.10), custom_call_target="Cholesky" | custom-call | tf_op jit(solution)/shard_map/jit(cholesky)/cholesky | solution.py:158
  791.1 8.8 gather_fusion.2
  803.8 11.8 %while.11 = (s32[]{:T(128)}, f32[512,512]{1,0:T(8,128)}, s32[4,2]{0,1:T(2,128)S(1)}, f32[4,128,128]{2,1,0:T(8,128)S(1)}, s32[]{:T(128)}) while((s32[]{:T(128)}, f32[512,512]{1,0:T(8,128)}, s32[4,2]{0,1:T(2,128)S(1)}, f32[4,128,128]{2,1,0:T(8,128)S(1)}, s32[]{:T(128)}) %tuple.96), condition=%wide.while_cond.6.clone, body=%wide.while_body.6.clone.sunk | while | flops 2 | bytes 131189 | solution.py:159
  804.5 2.3 bitcast_dynamic-update-slice_fusion.5
  807.5 2.3 bitcast_dynamic-update-slice_fusion.5
  810.4 2.3 bitcast_dynamic-update-slice_fusion.5
  813.4 2.2 bitcast_dynamic-update-slice_fusion.5
  815.7 39.7 %custom-call.34 = f32[4,128,128]{1,2,0:T(8,128)S(1)} custom-call(f32[4,128,128]{2,1,0:T(8,128)S(1)} %get-tuple-element.95), custom_call_target="InvertDiagBlocksLowerTriangular" | custom-call | tf_op jit(solution)/shard_map/triangular_solve/custom-call.3 | solution.py:159
  864.7 7.0 fusion.21
  871.7 21.5 %fusion.149 = f32[3072,512]{1,0:T(8,128)S(1)} fusion(f32[3072,512]{0,1:T(8,128)S(1)} %fusion.21, f32[512,512]{1,0:T(8,128)S(1)} %get-tuple-element.153), kind=kOutput, calls=%fused_computation.282 | convolution fusion | flops 9663676416 | bytes 13631488 | tf_op jit(solution)/shard_map/dot_general | solution.py:174
  893.3 12.4 %fusion.11 = f32[3072,512]{0,1:T(8,128)S(1)} fusion(f32[3072,512]{1,0:T(8,128)S(1)} %fusion.149, bf16[2048,1024]{1,0:T(8,128)(2,1)} %bitcast.179, bf16[1024,1024]{1,0:T(8,128)(2,1)S(1)} %copy-done.3, f32[128,512]{1,0:T(8,128)S(1)} %fusion.86, f32[128,512]{1,0:T(8,128)S(1)} %copy-done.12, f32[128,512]{1,0:T(8,128)S(1)} %copy-done.6, f32[128,512]{1,0:T(8,128)S(1)} %fusion.65), kind=kOutput, calls=%fused_computation.27 | convolution fusion | flops 9673900032 | bytes 19922944 | tf_op jit(solution)/shard_map/dot_general | solution.py:161
  905.7 30.5 %fusion.16 = f32[1024,2048]{0,1:T(8,128)} fusion(f32[1024,2048]{0,1:T(8,128)} %copy.60, f32[1,1024,1,2048]{1,3,2,0:T(8,128)S(1)} %bitcast.174, f32[3072,512]{0,1:T(8,128)S(1)} %fusion.11, f32[3072,512]{0,1:T(8,128)S(1)} %fusion.21), kind=kOutput, calls=%fused_computation.33 | convolution fusion | flops 25777143808 | bytes 37748736 | tf_op jit(solution)/shard_map/dot_general | solution.py:36
  936.3 2.8 fusion.55
  939.1 5.9 select_bitcast_fusion
  945.0 20.5 %copy.73 = f32[1,1024,1,2048]{3,2,1,0:T(1,128)} copy(f32[1,1024,1,2048]{1,3,2,0:T(8,128)} %select_bitcast_fusion) | data formatting | bytes 16777216 | tf_op jit(solution)/shard_map/broadcast_in_dim | solution.py:187
  (179 shorter events, 82.2 us)
Async XLA Ops:
  6.5 19.4 %copy-start = (bf16[64,128,128]{2,1,0:T(8,128)(2,1)S(1)}, bf16[64,128,128]{2,1,0:T(8,128)(2,1)}, u32[]{:S(2)}) copy-start(bf16[64,128,128]{2,1,0:T(8,128)(2,1)} %param.23) | copy-start | bytes 6291460
  11.2 23.4 %all-to-all-start = ((s32[128,1,2]{2,1,0:T(1,128)}), s32[128,1,2]{2,1,0:T(1,128)S(1)}, u32[]{:S(2)}, u32[]{:S(2)}) async-start(s32[128,1,2]{2,1,0:T(1,128)} %bitcast.5), calls=%async_computation | async-start | bytes 131072 | tf_op jit(solution)/shard_map/all_to_all | solution.py:89
  34.5 19.4 %all-to-all-start.1 = ((s32[128,2,2,128]{3,1,2,0:T(2,128)}), s32[128,2,2,128]{3,1,2,0:T(2,128)S(1)}, u32[]{:S(2)}, u32[]{:S(2)}) async-start(s32[128,2,2,128]{3,1,2,0:T(2,128)} %pad_add_fusion), calls=%async_computation.1 | async-start | bytes 524288 | tf_op jit(solution)/shard_map/all_to_all | solution.py:82
  54.0 107.7 %all-to-all-start.2 = ((bf16[128,2,128,128]{3,2,1,0:T(8,128)(2,1)}), bf16[128,2,128,128]{3,2,1,0:T(8,128)(2,1)}, u32[]{:S(2)}, u32[]{:S(2)}) async-start(bf16[128,2,128,128]{3,2,1,0:T(8,128)(2,1)} %select_select_fusion), calls=%async_computation.2 | async-start | bytes 16777216 | tf_op jit(solution)/shard_map/all_to_all | solution.py:75
  62.0 222.5 %all-gather.4.cloned.1.call-start = ((), (), s32[]{:S(2)}) async-start(), calls=%async_computation.3 | async-start | bytes 2359296 | tf_op jit(solution)/shard_map/all_gather | solution.py:118
  252.1 2.0 copy-start.4
  254.9 264.5 %all-gather.6.cloned.1.call-start = ((), (), s32[]{:S(2)}) async-start(), calls=%async_computation.4 | async-start | bytes 4227072 | tf_op jit(solution)/shard_map/all_gather | solution.py:145
  284.5 145.6 %collective-permute-start.1 = (bf16[1024,1024]{0,1:T(8,128)(2,1)}, bf16[1024,1024]{0,1:T(8,128)(2,1)}, u32[]{:S(2)}, u32[]{:S(2)}) collective-permute-start(bf16[1024,1024]{0,1:T(8,128)(2,1)} %all-gather.4.cloned.1.call-done), channel_id=1, source_target_pairs={{0,0},{1,8},{2,16},{3,24},{4,32},{5,40},{6,48},{7,56},{8,1},{9,9},... | collective-permute-start | bytes 6291464 | tf_op jit(solution)/shard_map/ppermute | solution.py:132
  291.4 185.1 %collective-permute-start = (bf16[1024,1024]{0,1:T(8,128)(2,1)}, bf16[1024,1024]{0,1:T(8,128)(2,1)}, u32[]{:S(2)}, u32[]{:S(2)}) collective-permute-start(bf16[1024,1024]{0,1:T(8,128)(2,1)} %all-gather.4.cloned.1.call-done), channel_id=1, source_target_pairs={{0,64},{1,72},{2,80},{3,88},{4,96},{5,104},{6,112},{7,120},{8,65},... | collective-permute-start | bytes 6291464 | tf_op jit(solution)/shard_map/ppermute | solution.py:132
  531.7 1.9 copy-start.2
  536.1 1.0 copy-start.10
  678.2 9.6 copy-start.7
  678.2 9.6 copy-start.17
  680.1 11.9 %copy-start.13 = (f32[128,512]{1,0:T(8,128)}, f32[128,512]{1,0:T(8,128)S(1)}, u32[]{:S(2)}) copy-start(f32[128,512]{1,0:T(8,128)S(1)} %fusion.93) | copy-start | bytes 786436
  682.2 9.8 %copy-start.16 = (f32[128,512]{1,0:T(8,128)}, f32[128,512]{1,0:T(8,128)S(1)}, u32[]{:S(2)}) copy-start(f32[128,512]{1,0:T(8,128)S(1)} %fusion.92) | copy-start | bytes 786436
  697.8 1.0 copy-start.9
  723.8 0.7 copy-start.18
  749.2 0.7 copy-start.19
  799.9 64.8 %copy-start.8 = (f32[128,512]{1,0:T(8,128)S(1)}, f32[128,512]{1,0:T(8,128)}, u32[]{:S(2)}) copy-start(f32[128,512]{1,0:T(8,128)} %copy-done.7) | copy-start | bytes 786436
  799.9 64.8 %copy-start.14 = (f32[128,512]{1,0:T(8,128)S(1)}, f32[128,512]{1,0:T(8,128)}, u32[]{:S(2)}) copy-start(f32[128,512]{1,0:T(8,128)} %copy-done.13) | copy-start | bytes 786436
  855.4 0.7 copy-start.20
  859.0 5.6 copy-start.5
  861.7 2.9 copy-start.11
  871.7 21.5 %copy-start.3 = (bf16[1024,1024]{1,0:T(8,128)(2,1)S(1)}, bf16[1024,1024]{1,0:T(8,128)(2,1)}, u32[]{:S(2)}) copy-start(bf16[1024,1024]{1,0:T(8,128)(2,1)} %copy.63) | copy-start | bytes 6291460
  871.7 21.5 %copy-start.6 = (f32[128,512]{1,0:T(8,128)S(1)}, f32[128,512]{1,0:T(8,128)}, u32[]{:S(2)}) copy-start(f32[128,512]{1,0:T(8,128)} %copy-done.5) | copy-start | bytes 786436
  871.7 21.5 %copy-start.12 = (f32[128,512]{1,0:T(8,128)S(1)}, f32[128,512]{1,0:T(8,128)}, u32[]{:S(2)}) copy-start(f32[128,512]{1,0:T(8,128)} %copy-done.11) | copy-start | bytes 786436
  871.7 34.0 %slice-start = ((s8[8388608]{0:T(1024)(128)(4,1)}), s8[4194304]{0:T(1024)(128)(4,1)S(1)}, s32[]{:S(2)}) async-start(s8[8388608]{0:T(1024)(128)(4,1)} %bitcast.173), calls=%async_computation.5 | async-start | bytes 8388608
  893.2 12.4 %slice-start.1 = ((s8[8388608]{0:T(1024)(128)(4,1)}), s8[4194304]{0:T(1024)(128)(4,1)S(1)}, s32[]{:S(2)}) async-start(s8[8388608]{0:T(1024)(128)(4,1)} %bitcast.173), calls=%async_computation.6 | async-start | bytes 8388608
  905.7 30.6 %copy-start.15 = (f32[1024,128]{0,1:T(8,128)S(1)}, f32[1024,128]{0,1:T(8,128)}, u32[]{:S(2)}) copy-start(f32[1024,128]{0,1:T(8,128)} %copy.89) | copy-start | bytes 1572868
  905.7 30.5 %copy-start.21 = (pred[1024]{0:T(1024)(128)(4,1)S(1)}, pred[1024]{0:T(1024)(128)(4,1)}, u32[]{:S(2)}) copy-start(pred[1024]{0:T(1024)(128)(4,1)} %get-tuple-element.158) | copy-start | bytes 3076
  905.7 30.5 %copy-start.22 = (pred[1024]{0:T(1024)(128)(4,1)S(1)}, pred[1024]{0:T(1024)(128)(4,1)}, u32[]{:S(2)}) copy-start(pred[1024]{0:T(1024)(128)(4,1)} %get-tuple-element.159) | copy-start | bytes 3076
  939.1 26.4 %copy-start.1 = (bf16[64,128,128]{2,1,0:T(8,128)(2,1)S(1)}, bf16[64,128,128]{2,1,0:T(8,128)(2,1)}, u32[]{:S(2)}) copy-start(bf16[64,128,128]{2,1,0:T(8,128)(2,1)} %param.23) | copy-start | bytes 6291460
Sparse Core Ops, SparseCore 0:
  255.0 29.4 all-gather.3
  287.3 231.9 all-gather.5

commit v2 on v1

--- a/solution.py
+++ b/solution.py
@@ -119,27 +119,20 @@
         matrix[:, :width].astype(jnp.bfloat16), "fcol", axis=1, tiled=True
     )[:, :total]
     half = row_devs // col_devs
-    perms = []
-    for shift in range(half):
-        pairs = []
-        for src_row in range(row_devs):
-            for src_col in range(col_devs):
-                part = src_row // col_devs
-                dst_row = ((part + shift) % half) * col_devs + src_col
-                dst_col = src_row % col_devs
-                pairs.append((src_row * col_devs + src_col, dst_row * col_devs + dst_col))
-        perms.append(pairs)
-    got = [lax.ppermute(row_panel, ("frow", "fcol"), perm) for perm in perms]
-    my_part = row_here // col_devs
-    ordered = []
-    for part in range(half):
-        pick = got[0]
-        for shift in range(1, half):
-            pick = jnp.where((my_part - shift) % half == part, got[shift], pick)
-        if half == 1:
-            pick = got[0]
-        ordered.append(pick.reshape(row_blocks, width, total))
-    col_panel = jnp.stack(ordered, axis=1).reshape(local.shape[1], total)
+    pairs = []
+    for src_row in range(row_devs):
+        for src_col in range(col_devs):
+            dst_row = (src_row // col_devs) * col_devs + src_col
+            dst_col = src_row % col_devs
+            pairs.append((src_row * col_devs + src_col, dst_row * col_devs + dst_col))
+    piece = lax.dynamic_slice_in_dim(row_panel, col_here * width, width, axis=0)
+    piece = lax.ppermute(piece, ("frow", "fcol"), pairs)
+    col_all = lax.all_gather(piece, "frow", axis=0, tiled=False)
+    col_panel = (
+        col_all.reshape(half, row_blocks, width, total)
+        .transpose(1, 0, 2, 3)
+        .reshape(local.shape[1], total)
+    )
     corner_blocks = total // width
     first = matrix[:width, :width].astype(jnp.bfloat16)
     every = lax.all_gather(first, ("frow", "fcol"), axis=0, tiled=False)

time: 987 us -> 823 us (0.83)
  waiting for transfers between devices: 308 us -> 164 us
    ppermute x2 -> x1, waiting for transfers between devices: 175 us -> 7.97 us  [shards(): piece = lax.ppermute(piece, ('frow', 'fcol'), pairs)]
    all_gather x1, waiting for transfers between devices: 25.8 us -> 49.6 us  [shards(): every = lax.all_gather(first, ('frow', 'fcol'), axis=0, tiled=False)]
    unnamed x56 -> x59, local copies, waits for them, and re-layouts: 77 us -> 69.7 us
  transfers between devices with their start and end apart: 7 -> 7, of which waited for: 6 -> 5; matrix products, arithmetic and copies ran while one was open for 7% -> 48% of each run, Pallas kernels for 0% -> 0%
where the time goes in v2:
time: 823 us; the launch traced here: 810 us
  other arithmetic  281 us (34%)
  local copies, waits for them, and re-layouts  186 us (23%)
  waiting for transfers between devices  164 us (20%)
  matrix products  123 us (15%)
  starting transfers between devices  35.3 us (4%)
  between operations  19.4 us (2%)
    another operation x29, other arithmetic, shards(): factor = jnp.linalg.cholesky(symmetric)  162 us
    another operation x4, other arithmetic, shards(): lax.linalg.triangular_solve(factor, eye, left_side=True, lower=True)  79.9 us
    all_to_all x1, waiting for transfers between devices, shards(): lax.all_to_all(send_tiles.reshape(owners, CAP, width, width), ('frow', 'f...  77.3 us
    unnamed x59, local copies, waits for them, and re-layouts  69.7 us
    all_gather x1, waiting for transfers between devices, shards(): every = lax.all_gather(first, ('frow', 'fcol'), axis=0, tiled=False)  49.6 us
    dot_general x1, matrix products, subtract_product(): jnp.dot(row_factor, col_factor.T, precision=lax.Precision.HIGHEST, prefer...  30.6 us
    all_gather x1, waiting for transfers between devices, shards(): lax.all_gather(matrix[:, :width].astype(jnp.bfloat16), 'fcol', axis=1, ti...  27.3 us
    another operation x27, local copies, waits for them, and re-layouts, shards(): lax.linalg.triangular_solve(factor, eye, left_side=True, lower=True)  23.5 us
  transfers between devices with their start and end apart: 7, of which 5 were waited for; matrix products, arithmetic and copies ran while one was open for 48% of the time, Pallas kernels for 0%

profile of v2, /device:TPU:6, one launch (start us, length us, event | category | flops | bytes accessed | tf_op | source)
XLA Modules:
  0.0 809.8 jit_solution(5765808666919731463)
XLA Ops:
  11.2 10.5 %all-to-all-start = ((s32[128,1,2]{2,1,0:T(1,128)}), s32[128,1,2]{2,1,0:T(1,128)S(1)}, u32[]{:S(2)}, u32[]{:S(2)}) async-start(s32[128,1,2]{2,1,0:T(1,128)} %bitcast.5), calls=%async_computation | async-start | bytes 131072 | tf_op jit(solution)/shard_map/all_to_all | solution.py:89
  26.0 8.5 %gather_fusion.1 = bf16[256,128,128]{2,1,0:T(8,128)(2,1)} fusion(bf16[64,128,128]{2,1,0:T(8,128)(2,1)S(1)} %copy-done, s32[1024]{0:T(1024)S(1)} %pad_clamp_fusion.1), kind=kCustom, calls=%fused_computation.3 | custom fusion | bytes 16778240 | tf_op jit(solution)/shard_map/jit(_take)/gather | solution.py:66
  34.5 9.8 %all-to-all-start.1 = ((s32[128,2,2,128]{3,1,2,0:T(2,128)}), s32[128,2,2,128]{3,1,2,0:T(2,128)S(1)}, u32[]{:S(2)}, u32[]{:S(2)}) async-start(s32[128,2,2,128]{3,1,2,0:T(2,128)} %pad_add_fusion), calls=%async_computation.1 | async-start | bytes 524288 | tf_op jit(solution)/shard_map/all_to_all | solution.py:82
  44.3 7.4 select_select_fusion
  51.8 2.2 all-to-all-done.1
  54.0 8.0 all-to-all-start.2
  62.0 20.7 %copy.53 = f32[1,1024,1,2048]{1,3,2,0:T(8,128)} copy(f32[1,1024,1,2048]{3,2,1,0:T(1,128)} %param.22) | data formatting | bytes 16777216 | tf_op args[0]
  84.4 77.3 %all-to-all-done.2 = bf16[128,2,128,128]{3,2,1,0:T(8,128)(2,1)} async-done(((bf16[128,2,128,128]{3,2,1,0:T(8,128)(2,1)}), bf16[128,2,128,128]{3,2,1,0:T(8,128)(2,1)}, u32[]{:S(2)}, u32[]{:S(2)}) %all-to-all-start.2) | async-done | bytes 8388640 | tf_op jit(solution)/shard_map/all_to_all | solution.py:75
  161.7 13.3 %fusion.8 = bf16[128,2,128,128]{3,2,1,0:T(8,128)(2,1)} fusion(s32[128,2,128]{2,1,0:T(2,128)S(1)} %get-tuple-element.123, bf16[128,2,128,128]{3,2,1,0:T(8,128)(2,1)} %all-to-all-done.2, s32[128,2,128]{2,1,0:T(2,128)S(1)} %get-tuple-element.122), kind=kOutput, calls=%fused_computation.24 | convolution fusion | flops 2164260864 | bytes 17039360 | tf_op jit(solution)/shard_map/abxj,abyj->abxy/dot_general | solution.py:29
  175.0 23.1 %copy.96 = bf16[32,8,128,128]{3,1,2,0:T(8,128)(2,1)} copy(bf16[32,8,128,128]{3,2,1,0:T(8,128)(2,1)} %bitcast.186) | data formatting | bytes 16777216
  198.2 11.9 %copy.57 = bf16[16384,256]{1,0:T(8,128)(2,1)} copy(bf16[16384,256]{0,1:T(8,128)(2,1)} %bitcast.181) | data formatting | bytes 16777216 | tf_op jit(solution)/shard_map/dot_general | solution.py:103
  210.1 6.2 fusion.83
  216.3 7.5 copy.95
  223.8 9.3 %copy.58 = f32[1024,2048]{0,1:T(8,128)} copy(f32[1024,2048]{1,0:T(8,128)} %bitcast.182) | data formatting | bytes 16777216 | tf_op jit(solution)/shard_map/reshape | solution.py:109
  233.0 7.3 fusion.17
  240.3 2.0 copy-done.4
  245.4 27.3 %all-gather.6.cloned.1.call-done = bf16[1024,1024]{0,1:T(8,128)(2,1)} async-done(((bf16[1024,128]{0,1:T(8,128)(2,1)}), bf16[1024,1024]{0,1:T(8,128)(2,1)}) %all-gather.6.cloned.1.call-update) | async-done | bytes 2097168 | tf_op jit(solution)/shard_map/all_gather | solution.py:118
  273.7 6.9 collective-permute-start
  282.9 3.9 copy.60
  286.8 8.0 collective-permute-done
  295.5 49.6 %all-gather.10.cloned.1.call-done = bf16[16384,128]{0,1:T(8,128)(2,1)} async-done(((bf16[128,128]{0,1:T(8,128)(2,1)}), bf16[16384,128]{0,1:T(8,128)(2,1)}) %all-gather.10.cloned.1.call-update) | async-done | bytes 4194320 | tf_op jit(solution)/shard_map/all_gather | solution.py:138
  346.9 1.9 copy.87
  348.8 4.9 copy.61
  353.7 3.7 copy_bitcast_fusion.1
  357.5 2.0 copy-done.2
  362.9 11.7 %cholesky.286 = f32[128,128]{1,0:T(8,128)S(1)} custom-call(f32[128,128]{1,0:T(8,128)S(1)} %cholesky.426), custom_call_target="Cholesky" | custom-call | tf_op jit(solution)/shard_map/jit(cholesky)/cholesky | solution.py:151
  374.6 9.8 %custom-call.27 = f32[1,128,128]{1,2,0:T(8,128)S(1)} custom-call(f32[1,128,128]{2,1,0:T(8,128)S(1)} %get-tuple-element.143), custom_call_target="InvertDiagBlocksLowerTriangular" | custom-call | tf_op jit(solution)/shard_map/jit(cholesky)/cholesky | solution.py:151
  387.1 11.7 %cholesky.305 = f32[128,128]{1,0:T(8,128)S(1)} custom-call(f32[128,128]{1,0:T(8,128)S(1)} %cholesky.430), custom_call_target="Cholesky" | custom-call | tf_op jit(solution)/shard_map/jit(cholesky)/cholesky | solution.py:151
  398.9 10.0 %custom-call.28 = f32[1,128,128]{1,2,0:T(8,128)S(1)} custom-call(f32[1,128,128]{2,1,0:T(8,128)S(1)} %get-tuple-element.140), custom_call_target="InvertDiagBlocksLowerTriangular" | custom-call | tf_op jit(solution)/shard_map/jit(cholesky)/cholesky | solution.py:151
  410.4 11.7 %cholesky.326 = f32[128,128]{1,0:T(8,128)S(1)} custom-call(f32[128,128]{1,0:T(8,128)S(1)} %cholesky.435), custom_call_target="Cholesky" | custom-call | tf_op jit(solution)/shard_map/jit(cholesky)/cholesky | solution.py:151
  422.9 9.8 %custom-call.29 = f32[1,128,128]{1,2,0:T(8,128)S(1)} custom-call(f32[1,128,128]{2,1,0:T(8,128)S(1)} %get-tuple-element.137), custom_call_target="InvertDiagBlocksLowerTriangular" | custom-call | tf_op jit(solution)/shard_map/jit(cholesky)/cholesky | solution.py:151
  434.1 12.1 %cholesky.343 = f32[128,128]{1,0:T(8,128)S(1)} custom-call(f32[128,128]{1,0:T(8,128)S(1)} %convolution_subtract_fusion.11), custom_call_target="Cholesky" | custom-call | tf_op jit(solution)/shard_map/jit(cholesky)/cholesky | solution.py:151
  451.4 11.6 %while.10 = (s32[]{:T(128)}, f32[512,512]{1,0:T(8,128)}, s32[4,2]{0,1:T(2,128)S(1)}, f32[4,128,128]{2,1,0:T(8,128)S(1)}, s32[]{:T(128)}) while((s32[]{:T(128)}, f32[512,512]{1,0:T(8,128)}, s32[4,2]{0,1:T(2,128)S(1)}, f32[4,128,128]{2,1,0:T(8,128)S(1)}, s32[]{:T(128)}) %tuple.85), condition=%wide.while_cond.6, body=%wide.while_body.6.sunk | while | flops 2 | bytes 131189 | solution.py:152
  452.0 2.2 bitcast_dynamic-update-slice_fusion.4
  454.9 2.2 bitcast_dynamic-update-slice_fusion.4
  457.9 2.2 bitcast_dynamic-update-slice_fusion.4
  460.8 2.2 bitcast_dynamic-update-slice_fusion.4
  463.0 39.3 %custom-call.30 = f32[4,128,128]{1,2,0:T(8,128)S(1)} custom-call(f32[4,128,128]{2,1,0:T(8,128)S(1)} %get-tuple-element.94), custom_call_target="InvertDiagBlocksLowerTriangular" | custom-call | tf_op jit(solution)/shard_map/triangular_solve/custom-call.3 | solution.py:152
  506.2 2.5 scatter.14
  510.8 3.2 constant_dynamic-update-slice_fusion.2
  514.0 4.1 broadcast_select_fusion
  524.9 11.7 %cholesky.358 = f32[128,128]{1,0:T(8,128)S(1)} custom-call(f32[128,128]{1,0:T(8,128)S(1)} %cholesky.439), custom_call_target="Cholesky" | custom-call | tf_op jit(solution)/shard_map/jit(cholesky)/cholesky | solution.py:151
  537.2 10.0 %custom-call.31 = f32[1,128,128]{1,2,0:T(8,128)S(1)} custom-call(f32[1,128,128]{2,1,0:T(8,128)S(1)} %get-tuple-element.133), custom_call_target="InvertDiagBlocksLowerTriangular" | custom-call | tf_op jit(solution)/shard_map/jit(cholesky)/cholesky | solution.py:151
  550.5 11.7 %cholesky.377 = f32[128,128]{1,0:T(8,128)S(1)} custom-call(f32[128,128]{1,0:T(8,128)S(1)} %cholesky.443), custom_call_target="Cholesky" | custom-call | tf_op jit(solution)/shard_map/jit(cholesky)/cholesky | solution.py:151
  562.9 9.8 %custom-call.32 = f32[1,128,128]{1,2,0:T(8,128)S(1)} custom-call(f32[1,128,128]{2,1,0:T(8,128)S(1)} %get-tuple-element.130), custom_call_target="InvertDiagBlocksLowerTriangular" | custom-call | tf_op jit(solution)/shard_map/jit(cholesky)/cholesky | solution.py:151
  575.8 11.7 %cholesky.398 = f32[128,128]{1,0:T(8,128)S(1)} custom-call(f32[128,128]{1,0:T(8,128)S(1)} %cholesky.448), custom_call_target="Cholesky" | custom-call | tf_op jit(solution)/shard_map/jit(cholesky)/cholesky | solution.py:151
  588.1 10.2 %custom-call.33 = f32[1,128,128]{1,2,0:T(8,128)S(1)} custom-call(f32[1,128,128]{2,1,0:T(8,128)S(1)} %get-tuple-element.127), custom_call_target="InvertDiagBlocksLowerTriangular" | custom-call | tf_op jit(solution)/shard_map/jit(cholesky)/cholesky | solution.py:151
  600.6 11.7 %cholesky.415 = f32[128,128]{1,0:T(8,128)S(1)} custom-call(f32[128,128]{1,0:T(8,128)S(1)} %convolution_subtract_fusion.10), custom_call_target="Cholesky" | custom-call | tf_op jit(solution)/shard_map/jit(cholesky)/cholesky | solution.py:151
  621.2 8.8 %gather_fusion.2 = f32[1024,1024]{1,0:T(8,128)} fusion(f32[1024,1024]{1,0:T(8,128)} %get-tuple-element.120, s32[1024]{0:T(1024)} %broadcast_clamp_fusion), kind=kCustom, calls=%fused_computation.4 | custom fusion | bytes 8392704 | tf_op jit(solution)/shard_map/jit(_take)/gather | solution.py:174
  632.1 12.0 %while.11 = (s32[]{:T(128)}, f32[512,512]{1,0:T(8,128)}, s32[4,2]{0,1:T(2,128)S(1)}, f32[4,128,128]{2,1,0:T(8,128)S(1)}, s32[]{:T(128)}) while((s32[]{:T(128)}, f32[512,512]{1,0:T(8,128)}, s32[4,2]{0,1:T(2,128)S(1)}, f32[4,128,128]{2,1,0:T(8,128)S(1)}, s32[]{:T(128)}) %tuple.97), condition=%wide.while_cond.6.clone, body=%wide.while_body.6.clone.sunk | while | flops 2 | bytes 131189 | solution.py:152
  632.8 2.3 bitcast_dynamic-update-slice_fusion.5
  635.8 2.3 bitcast_dynamic-update-slice_fusion.5
  638.8 2.3 bitcast_dynamic-update-slice_fusion.5
  641.9 2.3 bitcast_dynamic-update-slice_fusion.5
  644.1 39.3 %custom-call.34 = f32[4,128,128]{1,2,0:T(8,128)S(1)} custom-call(f32[4,128,128]{2,1,0:T(8,128)S(1)} %get-tuple-element.95), custom_call_target="InvertDiagBlocksLowerTriangular" | custom-call | tf_op jit(solution)/shard_map/triangular_solve/custom-call.3 | solution.py:152
  689.6 5.6 copy.89
  695.2 7.0 copy.59
  702.2 7.0 fusion.21
  709.2 21.7 %fusion.149 = f32[3072,512]{1,0:T(8,128)S(1)} fusion(f32[3072,512]{0,1:T(8,128)S(1)} %fusion.21, f32[512,512]{1,0:T(8,128)S(1)} %get-tuple-element.151), kind=kOutput, calls=%fused_computation.280 | convolution fusion | flops 9663676416 | bytes 13631488 | tf_op jit(solution)/shard_map/dot_general | solution.py:167
  731.0 12.1 %fusion.11 = f32[3072,512]{0,1:T(8,128)S(1)} fusion(f32[3072,512]{1,0:T(8,128)S(1)} %fusion.149, bf16[2048,1024]{1,0:T(8,128)(2,1)} %bitcast.184, bf16[1024,1024]{1,0:T(8,128)(2,1)S(1)} %copy-done.3, f32[128,512]{1,0:T(8,128)S(1)} %fusion.86, f32[128,512]{1,0:T(8,128)S(1)} %copy-done.12, f32[128,512]{1,0:T(8,128)S(1)} %copy-done.6, f32[128,512]{1,0:T(8,128)S(1)} %fusion.65), kind=kOutput, calls=%fused_computation.27 | convolution fusion | flops 9673900032 | bytes 19922944 | tf_op jit(solution)/shard_map/dot_general | solution.py:154
  743.2 30.6 %fusion.16 = f32[1024,2048]{0,1:T(8,128)} fusion(f32[1024,2048]{0,1:T(8,128)} %copy.58, f32[1,1024,1,2048]{1,3,2,0:T(8,128)S(1)} %bitcast.179, f32[3072,512]{0,1:T(8,128)S(1)} %fusion.11, f32[3072,512]{0,1:T(8,128)S(1)} %fusion.21), kind=kOutput, calls=%fused_computation.32 | convolution fusion | flops 25777143808 | bytes 37748736 | tf_op jit(solution)/shard_map/dot_general | solution.py:36
  773.9 2.8 fusion.55
  776.6 5.9 select_bitcast_fusion
  782.6 20.5 %copy.70 = f32[1,1024,1,2048]{3,2,1,0:T(1,128)} copy(f32[1,1024,1,2048]{1,3,2,0:T(8,128)} %select_bitcast_fusion) | data formatting | bytes 16777216 | tf_op jit(solution)/shard_map/broadcast_in_dim | solution.py:180
  (181 shorter events, 74.7 us)
Async XLA Ops:
  6.5 19.4 %copy-start = (bf16[64,128,128]{2,1,0:T(8,128)(2,1)S(1)}, bf16[64,128,128]{2,1,0:T(8,128)(2,1)}, u32[]{:S(2)}) copy-start(bf16[64,128,128]{2,1,0:T(8,128)(2,1)} %param.23) | copy-start | bytes 6291460
  11.2 23.4 %all-to-all-start = ((s32[128,1,2]{2,1,0:T(1,128)}), s32[128,1,2]{2,1,0:T(1,128)S(1)}, u32[]{:S(2)}, u32[]{:S(2)}) async-start(s32[128,1,2]{2,1,0:T(1,128)} %bitcast.5), calls=%async_computation | async-start | bytes 131072 | tf_op jit(solution)/shard_map/all_to_all | solution.py:89
  34.5 19.4 %all-to-all-start.1 = ((s32[128,2,2,128]{3,1,2,0:T(2,128)}), s32[128,2,2,128]{3,1,2,0:T(2,128)S(1)}, u32[]{:S(2)}, u32[]{:S(2)}) async-start(s32[128,2,2,128]{3,1,2,0:T(2,128)} %pad_add_fusion), calls=%async_computation.1 | async-start | bytes 524288 | tf_op jit(solution)/shard_map/all_to_all | solution.py:82
  54.0 107.7 %all-to-all-start.2 = ((bf16[128,2,128,128]{3,2,1,0:T(8,128)(2,1)}), bf16[128,2,128,128]{3,2,1,0:T(8,128)(2,1)}, u32[]{:S(2)}, u32[]{:S(2)}) async-start(bf16[128,2,128,128]{3,2,1,0:T(8,128)(2,1)} %select_select_fusion), calls=%async_computation.2 | async-start | bytes 16777216 | tf_op jit(solution)/shard_map/all_to_all | solution.py:75
  62.0 210.7 %all-gather.6.cloned.1.call-start = ((), (), s32[]{:S(2)}) async-start(), calls=%async_computation.3 | async-start | bytes 2359296 | tf_op jit(solution)/shard_map/all_gather | solution.py:118
  240.3 2.0 copy-start.4
  243.1 102.0 %all-gather.10.cloned.1.call-start = ((), (), s32[]{:S(2)}) async-start(), calls=%async_computation.5 | async-start | bytes 4227072 | tf_op jit(solution)/shard_map/all_gather | solution.py:138
  244.5 445.0 %all-gather.8.cloned.1.call-start = ((), (), s32[]{:S(2)}) async-start(), calls=%async_computation.4 | async-start | bytes 4456448 | tf_op jit(solution)/shard_map/all_gather | solution.py:130
  273.7 21.1 %collective-permute-start = (bf16[128,1024]{0,1:T(8,128)(2,1)S(1)}, bf16[128,1024]{0,1:T(8,128)(2,1)S(1)}, u32[]{:S(2)}, u32[]{:S(2)}) collective-permute-start(bf16[128,1024]{0,1:T(8,128)(2,1)S(1)} %constant_dynamic-slice_fusion.2), channel_id=1, source_target_pairs={{0,0},{1,8},{2,16},{3,24},{4,32},{5,40},{6,48},{7,56},{8,1},{9,9},... | collective-permute-start | bytes 786440 | tf_op jit(solution)/shard_map/ppermute | solution.py:129
  294.8 0.7 copy-start.21
  357.5 2.0 copy-start.2
  361.9 1.0 copy-start.9
  504.3 9.6 %copy-start.7 = (f32[128,512]{1,0:T(8,128)}, f32[128,512]{1,0:T(8,128)S(1)}, u32[]{:S(2)}) copy-start(f32[128,512]{1,0:T(8,128)S(1)} %fusion.95) | copy-start | bytes 786436
  504.4 9.6 %copy-start.18 = (pred[512,512]{1,0:T(32,128)(4,1)S(1)}, pred[512,512]{1,0:T(32,128)(4,1)}, u32[]{:S(2)}) copy-start(pred[512,512]{1,0:T(32,128)(4,1)} %copy.65) | copy-start | bytes 786436
  506.2 11.9 %copy-start.13 = (f32[128,512]{1,0:T(8,128)}, f32[128,512]{1,0:T(8,128)S(1)}, u32[]{:S(2)}) copy-start(f32[128,512]{1,0:T(8,128)S(1)} %fusion.93) | copy-start | bytes 786436
  510.8 3.2 copy-start.16
  523.9 1.0 copy-start.10
  549.8 0.7 copy-start.19
  575.1 0.7 copy-start.20
  685.5 3.5 copy-start.5
  687.4 1.7 copy-start.11
  695.2 7.0 copy-start.8
  695.2 7.0 copy-start.14
  695.2 7.0 copy-start.17
  709.2 21.8 %copy-start.3 = (bf16[1024,1024]{1,0:T(8,128)(2,1)S(1)}, bf16[1024,1024]{1,0:T(8,128)(2,1)}, u32[]{:S(2)}) copy-start(bf16[1024,1024]{1,0:T(8,128)(2,1)} %copy.60) | copy-start | bytes 6291460
  709.2 21.8 %copy-start.6 = (f32[128,512]{1,0:T(8,128)S(1)}, f32[128,512]{1,0:T(8,128)}, u32[]{:S(2)}) copy-start(f32[128,512]{1,0:T(8,128)} %copy-done.5) | copy-start | bytes 786436
  709.2 21.8 %copy-start.12 = (f32[128,512]{1,0:T(8,128)S(1)}, f32[128,512]{1,0:T(8,128)}, u32[]{:S(2)}) copy-start(f32[128,512]{1,0:T(8,128)} %copy-done.11) | copy-start | bytes 786436
  709.2 33.9 %slice-start = ((s8[8388608]{0:T(1024)(128)(4,1)}), s8[4194304]{0:T(1024)(128)(4,1)S(1)}, s32[]{:S(2)}) async-start(s8[8388608]{0:T(1024)(128)(4,1)} %bitcast.178), calls=%async_computation.6 | async-start | bytes 8388608
  731.0 12.2 %slice-start.1 = ((s8[8388608]{0:T(1024)(128)(4,1)}), s8[4194304]{0:T(1024)(128)(4,1)S(1)}, s32[]{:S(2)}) async-start(s8[8388608]{0:T(1024)(128)(4,1)} %bitcast.178), calls=%async_computation.7 | async-start | bytes 8388608
  743.2 30.7 %copy-start.15 = (f32[1024,128]{0,1:T(8,128)S(1)}, f32[1024,128]{0,1:T(8,128)}, u32[]{:S(2)}) copy-start(f32[1024,128]{0,1:T(8,128)} %copy.84) | copy-start | bytes 1572868
  743.2 30.7 %copy-start.22 = (pred[1024]{0:T(1024)(128)(4,1)S(1)}, pred[1024]{0:T(1024)(128)(4,1)}, u32[]{:S(2)}) copy-start(pred[1024]{0:T(1024)(128)(4,1)} %get-tuple-element.158) | copy-start | bytes 3076
  743.2 30.7 %copy-start.23 = (pred[1024]{0:T(1024)(128)(4,1)S(1)}, pred[1024]{0:T(1024)(128)(4,1)}, u32[]{:S(2)}) copy-start(pred[1024]{0:T(1024)(128)(4,1)} %get-tuple-element.159) | copy-start | bytes 3076
  776.6 26.4 %copy-start.1 = (bf16[64,128,128]{2,1,0:T(8,128)(2,1)S(1)}, bf16[64,128,128]{2,1,0:T(8,128)(2,1)}, u32[]{:S(2)}) copy-start(bf16[64,128,128]{2,1,0:T(8,128)(2,1)} %param.23) | copy-start | bytes 6291460
Sparse Core Ops, SparseCore 0:
  243.2 29.4 all-gather.5
  275.5 69.5 all-gather.9
  347.2 57.9 all-gather.7

commit v3 on v2

--- a/solution.py
+++ b/solution.py
@@ -61,39 +61,28 @@
     slot_match = slot_of[None, :] == jnp.arange(slot_count, dtype=jnp.int32)[:, None]
     source_tile = jnp.sum(jnp.where(slot_match, tile_order[None, :], 0), axis=1)
     filled = jnp.any(slot_match, axis=1)
+    own_perms = jnp.stack([tile_rows, tile_cols], axis=1)
+    placed_here, _ = place_tiles((child_tiles[None], own_perms[None], block_of[None]))
+    placed_here = placed_here[0]
     send_tiles = jnp.where(
         filled[:, None, None],
-        jnp.take(child_tiles, source_tile, axis=0),
+        jnp.take(placed_here, source_tile, axis=0),
         jnp.zeros((), jnp.bfloat16),
     )
-    send_perms = jnp.stack(
-        [jnp.take(tile_rows, source_tile, axis=0), jnp.take(tile_cols, source_tile, axis=0)], axis=1
+    send_blocks = jnp.where(filled, jnp.take(block_of, source_tile, axis=0), -1)
+    placed = lax.all_to_all(
+        send_tiles.reshape(owners, CAP, width, width),
+        ("frow", "fcol"),
+        split_axis=0,
+        concat_axis=0,
+        tiled=True,
     )
-    send_blocks = jnp.take(block_of, source_tile, axis=0)
-    placed, blocks_in = place_tiles(
-        (
-            lax.all_to_all(
-                send_tiles.reshape(owners, CAP, width, width),
-                ("frow", "fcol"),
-                split_axis=0,
-                concat_axis=0,
-                tiled=True,
-            ),
-            lax.all_to_all(
-                send_perms.reshape(owners, CAP, 2, width),
-                ("frow", "fcol"),
-                split_axis=0,
-                concat_axis=0,
-                tiled=True,
-            ),
-            lax.all_to_all(
-                send_blocks.reshape(owners, CAP),
-                ("frow", "fcol"),
-                split_axis=0,
-                concat_axis=0,
-                tiled=True,
-            ),
-        )
+    blocks_in = lax.all_to_all(
+        send_blocks.reshape(owners, CAP),
+        ("frow", "fcol"),
+        split_axis=0,
+        concat_axis=0,
+        tiled=True,
     )
     local = front_orig[0, :, 0, :]
     row_blocks = local.shape[0] // width

time: 823 us -> 800 us (0.972)
  matrix products: 123 us -> 113 us
    reshape x0 -> x1, local copies, waits for them, and re-layouts: none -> 11.9 us  [shards(): placed.reshape(slot_count, width * width)]
    dot_general x1 -> x0, local copies, waits for them, and re-layouts: 11.9 us -> none  [shards(): jnp.dot(block_onehot, placed.reshape(slot_count, width * width), preferre...]
    all_to_all x1 -> x0, starting transfers between devices: 9.77 us -> none  [shards(): lax.all_to_all(send_perms.reshape(owners, CAP, 2, width), ('frow', 'fcol'...]
    dot_general x1, matrix products: 13.3 us -> 3.62 us  [place_tiles(): jnp.einsum('abxj,abyj->abxy', moved, col_onehot, preferred_element_type=j...]
  transfers between devices with their start and end apart: 7 -> 6, of which waited for: 5 -> 4; matrix products, arithmetic and copies ran while one was open for 48% -> 49% of each run, Pallas kernels for 0% -> 0%
where the time goes in v3:
time: 800 us; the launch traced here: 789 us
  other arithmetic  281 us (35%)
  local copies, waits for them, and re-layouts  185 us (23%)
  waiting for transfers between devices  162 us (20%)
  matrix products  113 us (14%)
  starting transfers between devices  27.7 us (3%)
  between operations  19.5 us (2%)
    another operation x29, other arithmetic, shards(): factor = jnp.linalg.cholesky(symmetric)  162 us
    another operation x4, other arithmetic, shards(): lax.linalg.triangular_solve(factor, eye, left_side=True, lower=True)  79.9 us
    all_to_all x1, waiting for transfers between devices, shards(): lax.all_to_all(send_tiles.reshape(owners, CAP, width, width), ('frow', 'f...  77.2 us
    unnamed x59, local copies, waits for them, and re-layouts  70.3 us
    all_gather x1, waiting for transfers between devices, shards(): every = lax.all_gather(first, ('frow', 'fcol'), axis=0, tiled=False)  49.6 us
    dot_general x1, matrix products, subtract_product(): jnp.dot(row_factor, col_factor.T, precision=lax.Precision.HIGHEST, prefer...  30.7 us
    all_gather x1, waiting for transfers between devices, shards(): lax.all_gather(matrix[:, :width].astype(jnp.bfloat16), 'fcol', axis=1, ti...  27.3 us
    another operation x27, local copies, waits for them, and re-layouts, shards(): lax.linalg.triangular_solve(factor, eye, left_side=True, lower=True)  23.1 us
  transfers between devices with their start and end apart: 6, of which 4 were waited for; matrix products, arithmetic and copies ran while one was open for 49% of the time, Pallas kernels for 0%

profile of v3, /device:TPU:6, one launch (start us, length us, event | category | flops | bytes accessed | tf_op | source)
XLA Modules:
  0.0 789.3 jit_solution(6141938255219168206)
XLA Ops:
  8.8 1.9 gather_fusion
  11.4 10.5 %all-to-all-start = ((s32[128,1,2]{2,1,0:T(1,128)}), s32[128,1,2]{2,1,0:T(1,128)S(1)}, u32[]{:S(2)}, u32[]{:S(2)}) async-start(s32[128,1,2]{2,1,0:T(1,128)} %bitcast.5), calls=%async_computation | async-start | bytes 131072 | tf_op jit(solution)/shard_map/all_to_all | solution.py:80
  23.1 3.6 fusion.23
  26.7 10.2 %gather_fusion.1 = bf16[256,128,128]{2,1,0:T(8,128)(2,1)} fusion(bf16[64,128,128]{2,1,0:T(8,128)(2,1)} %fusion.23, s32[1024]{0:T(1024)S(1)} %pad_clamp_fusion), kind=kCustom, calls=%fused_computation.1 | custom fusion | bytes 16778240 | tf_op jit(solution)/shard_map/jit(_take)/gather | solution.py:69
  36.8 7.4 select_select_fusion
  44.3 10.2 %all-to-all-start.1 = ((bf16[128,2,128,128]{3,2,1,0:T(8,128)(2,1)}), bf16[128,2,128,128]{3,2,1,0:T(8,128)(2,1)}, u32[]{:S(2)}, u32[]{:S(2)}) async-start(bf16[128,2,128,128]{3,2,1,0:T(8,128)(2,1)} %select_select_fusion), calls=%async_computation.1 | async-start | bytes 16777216 | tf_op jit(solution)/shard_map/all_to_all | solution.py:73
  54.5 20.9 %copy.51 = f32[1,1024,1,2048]{1,3,2,0:T(8,128)} copy(f32[1,1024,1,2048]{3,2,1,0:T(1,128)} %param.20) | data formatting | bytes 16777216 | tf_op args[0]
  76.9 77.2 %all-to-all-done.1 = bf16[128,2,128,128]{3,2,1,0:T(8,128)(2,1)} async-done(((bf16[128,2,128,128]{3,2,1,0:T(8,128)(2,1)}), bf16[128,2,128,128]{3,2,1,0:T(8,128)(2,1)}, u32[]{:S(2)}, u32[]{:S(2)}) %all-to-all-start.1) | async-done | bytes 8388640 | tf_op jit(solution)/shard_map/all_to_all | solution.py:73
  154.2 23.6 %copy.92 = bf16[32,8,128,128]{3,1,2,0:T(8,128)(2,1)} copy(bf16[32,8,128,128]{3,2,1,0:T(8,128)(2,1)} %bitcast.58) | data formatting | bytes 16777216
  177.8 11.9 %copy.53 = bf16[256,16384]{0,1:T(8,128)(2,1)} copy(bf16[256,16384]{1,0:T(8,128)(2,1)} %bitcast.178) | data formatting | bytes 16777216 | tf_op jit(solution)/shard_map/reshape | solution.py:93
  189.7 6.2 fusion.83
  195.9 7.5 copy.91
  203.4 9.3 %copy.54 = f32[1024,2048]{0,1:T(8,128)} copy(f32[1024,2048]{1,0:T(8,128)} %bitcast.179) | data formatting | bytes 16777216 | tf_op jit(solution)/shard_map/reshape | solution.py:98
  212.7 7.3 fusion.10
  220.0 2.0 copy-done.4
  225.1 27.3 %all-gather.6.cloned.1.call-done = bf16[1024,1024]{0,1:T(8,128)(2,1)} async-done(((bf16[1024,128]{0,1:T(8,128)(2,1)}), bf16[1024,1024]{0,1:T(8,128)(2,1)}) %all-gather.6.cloned.1.call-update) | async-done | bytes 2097168 | tf_op jit(solution)/shard_map/all_gather | solution.py:107
  253.4 6.9 collective-permute-start
  262.6 3.9 copy.56
  266.5 7.9 %collective-permute-done = bf16[128,1024]{0,1:T(8,128)(2,1)S(1)} collective-permute-done((bf16[128,1024]{0,1:T(8,128)(2,1)S(1)}, bf16[128,1024]{0,1:T(8,128)(2,1)S(1)}, u32[]{:S(2)}, u32[]{:S(2)}) %collective-permute-start) | collective-permute-done | bytes 262176 | tf_op jit(solution)/shard_map/ppermute | solution.py:118
  275.2 49.6 %all-gather.10.cloned.1.call-done = bf16[16384,128]{0,1:T(8,128)(2,1)} async-done(((bf16[128,128]{0,1:T(8,128)(2,1)}), bf16[16384,128]{0,1:T(8,128)(2,1)}) %all-gather.10.cloned.1.call-update) | async-done | bytes 4194320 | tf_op jit(solution)/shard_map/all_gather | solution.py:127
  324.8 1.7 slice_bitcast_fusion
  326.5 1.9 copy.83
  328.4 4.7 copy.57
  333.2 3.7 copy_bitcast_fusion.2
  336.9 2.0 copy-done.2
  342.3 11.7 %cholesky.286 = f32[128,128]{1,0:T(8,128)S(1)} custom-call(f32[128,128]{1,0:T(8,128)S(1)} %cholesky.426), custom_call_target="Cholesky" | custom-call | tf_op jit(solution)/shard_map/jit(cholesky)/cholesky | solution.py:140
  354.1 9.8 %custom-call.27 = f32[1,128,128]{1,2,0:T(8,128)S(1)} custom-call(f32[1,128,128]{2,1,0:T(8,128)S(1)} %get-tuple-element.140), custom_call_target="InvertDiagBlocksLowerTriangular" | custom-call | tf_op jit(solution)/shard_map/jit(cholesky)/cholesky | solution.py:140
  366.5 11.7 %cholesky.305 = f32[128,128]{1,0:T(8,128)S(1)} custom-call(f32[128,128]{1,0:T(8,128)S(1)} %cholesky.430), custom_call_target="Cholesky" | custom-call | tf_op jit(solution)/shard_map/jit(cholesky)/cholesky | solution.py:140
  378.3 10.2 %custom-call.28 = f32[1,128,128]{1,2,0:T(8,128)S(1)} custom-call(f32[1,128,128]{2,1,0:T(8,128)S(1)} %get-tuple-element.137), custom_call_target="InvertDiagBlocksLowerTriangular" | custom-call | tf_op jit(solution)/shard_map/jit(cholesky)/cholesky | solution.py:140
  390.1 11.7 %cholesky.326 = f32[128,128]{1,0:T(8,128)S(1)} custom-call(f32[128,128]{1,0:T(8,128)S(1)} %cholesky.435), custom_call_target="Cholesky" | custom-call | tf_op jit(solution)/shard_map/jit(cholesky)/cholesky | solution.py:140
  402.5 9.8 %custom-call.29 = f32[1,128,128]{1,2,0:T(8,128)S(1)} custom-call(f32[1,128,128]{2,1,0:T(8,128)S(1)} %get-tuple-element.134), custom_call_target="InvertDiagBlocksLowerTriangular" | custom-call | tf_op jit(solution)/shard_map/jit(cholesky)/cholesky | solution.py:140
  413.8 11.9 %cholesky.343 = f32[128,128]{1,0:T(8,128)S(1)} custom-call(f32[128,128]{1,0:T(8,128)S(1)} %convolution_subtract_fusion.11), custom_call_target="Cholesky" | custom-call | tf_op jit(solution)/shard_map/jit(cholesky)/cholesky | solution.py:140
  430.9 11.6 %while.10 = (s32[]{:T(128)}, f32[512,512]{1,0:T(8,128)}, s32[4,2]{0,1:T(2,128)S(1)}, f32[4,128,128]{2,1,0:T(8,128)S(1)}, s32[]{:T(128)}) while((s32[]{:T(128)}, f32[512,512]{1,0:T(8,128)}, s32[4,2]{0,1:T(2,128)S(1)}, f32[4,128,128]{2,1,0:T(8,128)S(1)}, s32[]{:T(128)}) %tuple.83), condition=%wide.while_cond.6, body=%wide.while_body.6.sunk | while | flops 2 | bytes 131189 | solution.py:141
  431.5 2.2 bitcast_dynamic-update-slice_fusion.4
  434.4 2.2 bitcast_dynamic-update-slice_fusion.4
  437.4 2.2 bitcast_dynamic-update-slice_fusion.4
  440.3 2.2 bitcast_dynamic-update-slice_fusion.4
  442.5 39.3 %custom-call.30 = f32[4,128,128]{1,2,0:T(8,128)S(1)} custom-call(f32[4,128,128]{2,1,0:T(8,128)S(1)} %get-tuple-element.93), custom_call_target="InvertDiagBlocksLowerTriangular" | custom-call | tf_op jit(solution)/shard_map/triangular_solve/custom-call.3 | solution.py:141
  485.7 2.5 scatter.14
  490.3 3.2 constant_dynamic-update-slice_fusion.2
  493.5 4.1 broadcast_select_fusion
  504.4 11.7 %cholesky.358 = f32[128,128]{1,0:T(8,128)S(1)} custom-call(f32[128,128]{1,0:T(8,128)S(1)} %cholesky.439), custom_call_target="Cholesky" | custom-call | tf_op jit(solution)/shard_map/jit(cholesky)/cholesky | solution.py:140
  516.7 10.2 %custom-call.31 = f32[1,128,128]{1,2,0:T(8,128)S(1)} custom-call(f32[1,128,128]{2,1,0:T(8,128)S(1)} %get-tuple-element.130), custom_call_target="InvertDiagBlocksLowerTriangular" | custom-call | tf_op jit(solution)/shard_map/jit(cholesky)/cholesky | solution.py:140
  530.2 11.7 %cholesky.377 = f32[128,128]{1,0:T(8,128)S(1)} custom-call(f32[128,128]{1,0:T(8,128)S(1)} %cholesky.443), custom_call_target="Cholesky" | custom-call | tf_op jit(solution)/shard_map/jit(cholesky)/cholesky | solution.py:140
  542.6 9.8 %custom-call.32 = f32[1,128,128]{1,2,0:T(8,128)S(1)} custom-call(f32[1,128,128]{2,1,0:T(8,128)S(1)} %get-tuple-element.127), custom_call_target="InvertDiagBlocksLowerTriangular" | custom-call | tf_op jit(solution)/shard_map/jit(cholesky)/cholesky | solution.py:140
  555.5 11.7 %cholesky.398 = f32[128,128]{1,0:T(8,128)S(1)} custom-call(f32[128,128]{1,0:T(8,128)S(1)} %cholesky.448), custom_call_target="Cholesky" | custom-call | tf_op jit(solution)/shard_map/jit(cholesky)/cholesky | solution.py:140
  567.8 9.9 %custom-call.33 = f32[1,128,128]{1,2,0:T(8,128)S(1)} custom-call(f32[1,128,128]{2,1,0:T(8,128)S(1)} %get-tuple-element.124), custom_call_target="InvertDiagBlocksLowerTriangular" | custom-call | tf_op jit(solution)/shard_map/jit(cholesky)/cholesky | solution.py:140
  580.0 11.7 %cholesky.415 = f32[128,128]{1,0:T(8,128)S(1)} custom-call(f32[128,128]{1,0:T(8,128)S(1)} %convolution_subtract_fusion.10), custom_call_target="Cholesky" | custom-call | tf_op jit(solution)/shard_map/jit(cholesky)/cholesky | solution.py:140
  600.7 8.8 %gather_fusion.2 = f32[1024,1024]{1,0:T(8,128)} fusion(f32[1024,1024]{1,0:T(8,128)} %get-tuple-element.119, s32[1024]{0:T(1024)} %broadcast_clamp_fusion), kind=kCustom, calls=%fused_computation.2 | custom fusion | bytes 8392704 | tf_op jit(solution)/shard_map/jit(_take)/gather | solution.py:163
  611.5 11.7 %while.11 = (s32[]{:T(128)}, f32[512,512]{1,0:T(8,128)}, s32[4,2]{0,1:T(2,128)S(1)}, f32[4,128,128]{2,1,0:T(8,128)S(1)}, s32[]{:T(128)}) while((s32[]{:T(128)}, f32[512,512]{1,0:T(8,128)}, s32[4,2]{0,1:T(2,128)S(1)}, f32[4,128,128]{2,1,0:T(8,128)S(1)}, s32[]{:T(128)}) %tuple.95), condition=%wide.while_cond.6.clone, body=%wide.while_body.6.clone.sunk | while | flops 2 | bytes 131189 | solution.py:141
  612.2 2.3 bitcast_dynamic-update-slice_fusion.5
  615.1 2.3 bitcast_dynamic-update-slice_fusion.5
  618.1 2.3 bitcast_dynamic-update-slice_fusion.5
  621.0 2.2 bitcast_dynamic-update-slice_fusion.5
  623.2 39.3 %custom-call.34 = f32[4,128,128]{1,2,0:T(8,128)S(1)} custom-call(f32[4,128,128]{2,1,0:T(8,128)S(1)} %get-tuple-element.94), custom_call_target="InvertDiagBlocksLowerTriangular" | custom-call | tf_op jit(solution)/shard_map/triangular_solve/custom-call.3 | solution.py:141
  668.6 5.6 copy.85
  674.3 7.3 copy.55
  681.6 7.0 fusion.14
  688.6 21.5 %fusion.149 = f32[3072,512]{1,0:T(8,128)S(1)} fusion(f32[3072,512]{0,1:T(8,128)S(1)} %fusion.14, f32[512,512]{1,0:T(8,128)S(1)} %get-tuple-element.148), kind=kOutput, calls=%fused_computation.273 | convolution fusion | flops 9663676416 | bytes 13631488 | tf_op jit(solution)/shard_map/dot_general | solution.py:156
  710.1 12.1 %fusion.2 = f32[3072,512]{0,1:T(8,128)S(1)} fusion(f32[3072,512]{1,0:T(8,128)S(1)} %fusion.149, bf16[2048,1024]{1,0:T(8,128)(2,1)} %bitcast.181, bf16[1024,1024]{1,0:T(8,128)(2,1)S(1)} %copy-done.3, f32[128,512]{1,0:T(8,128)S(1)} %fusion.86, f32[128,512]{1,0:T(8,128)S(1)} %copy-done.12, f32[128,512]{1,0:T(8,128)S(1)} %copy-done.6, f32[128,512]{1,0:T(8,128)S(1)} %fusion.65), kind=kOutput, calls=%fused_computation.17 | convolution fusion | flops 9673900032 | bytes 19922944 | tf_op jit(solution)/shard_map/dot_general | solution.py:143
  722.4 30.7 %fusion.9 = f32[1024,2048]{0,1:T(8,128)} fusion(f32[1024,2048]{0,1:T(8,128)} %copy.54, f32[1,1024,1,2048]{1,3,2,0:T(8,128)S(1)} %bitcast.176, f32[3072,512]{0,1:T(8,128)S(1)} %fusion.2, f32[3072,512]{0,1:T(8,128)S(1)} %fusion.14), kind=kOutput, calls=%fused_computation.26 | convolution fusion | flops 25777143808 | bytes 37748736 | tf_op jit(solution)/shard_map/dot_general | solution.py:36
  753.1 2.8 fusion.55
  755.9 5.9 select_bitcast_fusion
  761.8 20.5 %copy.66 = f32[1,1024,1,2048]{3,2,1,0:T(1,128)} copy(f32[1,1024,1,2048]{1,3,2,0:T(8,128)} %select_bitcast_fusion) | data formatting | bytes 16777216 | tf_op jit(solution)/shard_map/broadcast_in_dim | solution.py:169
  (174 shorter events, 68.0 us)
Async XLA Ops:
  6.5 16.5 %copy-start = (bf16[64,128,128]{2,1,0:T(8,128)(2,1)S(1)}, bf16[64,128,128]{2,1,0:T(8,128)(2,1)}, u32[]{:S(2)}) copy-start(bf16[64,128,128]{2,1,0:T(8,128)(2,1)} %param.21) | copy-start | bytes 6291460
  11.4 32.8 %all-to-all-start = ((s32[128,1,2]{2,1,0:T(1,128)}), s32[128,1,2]{2,1,0:T(1,128)S(1)}, u32[]{:S(2)}, u32[]{:S(2)}) async-start(s32[128,1,2]{2,1,0:T(1,128)} %bitcast.5), calls=%async_computation | async-start | bytes 131072 | tf_op jit(solution)/shard_map/all_to_all | solution.py:80
  44.3 109.9 %all-to-all-start.1 = ((bf16[128,2,128,128]{3,2,1,0:T(8,128)(2,1)}), bf16[128,2,128,128]{3,2,1,0:T(8,128)(2,1)}, u32[]{:S(2)}, u32[]{:S(2)}) async-start(bf16[128,2,128,128]{3,2,1,0:T(8,128)(2,1)} %select_select_fusion), calls=%async_computation.1 | async-start | bytes 16777216 | tf_op jit(solution)/shard_map/all_to_all | solution.py:73
  54.5 197.9 %all-gather.6.cloned.1.call-start = ((), (), s32[]{:S(2)}) async-start(), calls=%async_computation.2 | async-start | bytes 2359296 | tf_op jit(solution)/shard_map/all_gather | solution.py:107
  220.0 2.0 copy-start.4
  222.7 102.0 %all-gather.10.cloned.1.call-start = ((), (), s32[]{:S(2)}) async-start(), calls=%async_computation.4 | async-start | bytes 4227072 | tf_op jit(solution)/shard_map/all_gather | solution.py:127
  224.2 444.4 %all-gather.8.cloned.1.call-start = ((), (), s32[]{:S(2)}) async-start(), calls=%async_computation.3 | async-start | bytes 4456448 | tf_op jit(solution)/shard_map/all_gather | solution.py:119
  253.4 21.1 %collective-permute-start = (bf16[128,1024]{0,1:T(8,128)(2,1)S(1)}, bf16[128,1024]{0,1:T(8,128)(2,1)S(1)}, u32[]{:S(2)}, u32[]{:S(2)}) collective-permute-start(bf16[128,1024]{0,1:T(8,128)(2,1)S(1)} %constant_dynamic-slice_fusion.2), channel_id=1, source_target_pairs={{0,0},{1,8},{2,16},{3,24},{4,32},{5,40},{6,48},{7,56},{8,1},{9,9},... | collective-permute-start | bytes 786440 | tf_op jit(solution)/shard_map/ppermute | solution.py:118
  274.5 0.7 copy-start.21
  336.9 2.0 copy-start.2
  341.3 1.0 copy-start.9
  483.8 9.6 %copy-start.7 = (f32[128,512]{1,0:T(8,128)}, f32[128,512]{1,0:T(8,128)S(1)}, u32[]{:S(2)}) copy-start(f32[128,512]{1,0:T(8,128)S(1)} %fusion.95) | copy-start | bytes 786436
  483.9 9.6 %copy-start.18 = (pred[512,512]{1,0:T(32,128)(4,1)S(1)}, pred[512,512]{1,0:T(32,128)(4,1)}, u32[]{:S(2)}) copy-start(pred[512,512]{1,0:T(32,128)(4,1)} %copy.61) | copy-start | bytes 786436
  485.7 11.9 %copy-start.13 = (f32[128,512]{1,0:T(8,128)}, f32[128,512]{1,0:T(8,128)S(1)}, u32[]{:S(2)}) copy-start(f32[128,512]{1,0:T(8,128)S(1)} %fusion.93) | copy-start | bytes 786436
  490.2 3.2 copy-start.16
  503.4 1.0 copy-start.10
  529.5 0.7 copy-start.19
  554.8 0.7 copy-start.20
  664.6 3.5 copy-start.5
  666.5 1.7 copy-start.11
  674.2 7.3 copy-start.8
  674.2 7.3 copy-start.14
  674.2 7.3 copy-start.17
  688.6 21.5 %copy-start.3 = (bf16[1024,1024]{1,0:T(8,128)(2,1)S(1)}, bf16[1024,1024]{1,0:T(8,128)(2,1)}, u32[]{:S(2)}) copy-start(bf16[1024,1024]{1,0:T(8,128)(2,1)} %copy.56) | copy-start | bytes 6291460
  688.6 21.5 %copy-start.6 = (f32[128,512]{1,0:T(8,128)S(1)}, f32[128,512]{1,0:T(8,128)}, u32[]{:S(2)}) copy-start(f32[128,512]{1,0:T(8,128)} %copy-done.5) | copy-start | bytes 786436
  688.6 21.5 %copy-start.12 = (f32[128,512]{1,0:T(8,128)S(1)}, f32[128,512]{1,0:T(8,128)}, u32[]{:S(2)}) copy-start(f32[128,512]{1,0:T(8,128)} %copy-done.11) | copy-start | bytes 786436
  688.6 33.7 %slice-start = ((s8[8388608]{0:T(1024)(128)(4,1)}), s8[4194304]{0:T(1024)(128)(4,1)S(1)}, s32[]{:S(2)}) async-start(s8[8388608]{0:T(1024)(128)(4,1)} %bitcast.175), calls=%async_computation.5 | async-start | bytes 8388608
  710.1 12.2 %slice-start.1 = ((s8[8388608]{0:T(1024)(128)(4,1)}), s8[4194304]{0:T(1024)(128)(4,1)S(1)}, s32[]{:S(2)}) async-start(s8[8388608]{0:T(1024)(128)(4,1)} %bitcast.175), calls=%async_computation.6 | async-start | bytes 8388608
  722.3 30.8 %copy-start.15 = (f32[1024,128]{0,1:T(8,128)S(1)}, f32[1024,128]{0,1:T(8,128)}, u32[]{:S(2)}) copy-start(f32[1024,128]{0,1:T(8,128)} %copy.80) | copy-start | bytes 1572868
  722.3 30.7 %copy-start.22 = (pred[1024]{0:T(1024)(128)(4,1)S(1)}, pred[1024]{0:T(1024)(128)(4,1)}, u32[]{:S(2)}) copy-start(pred[1024]{0:T(1024)(128)(4,1)} %get-tuple-element.155) | copy-start | bytes 3076
  722.3 30.7 %copy-start.23 = (pred[1024]{0:T(1024)(128)(4,1)S(1)}, pred[1024]{0:T(1024)(128)(4,1)}, u32[]{:S(2)}) copy-start(pred[1024]{0:T(1024)(128)(4,1)} %get-tuple-element.156) | copy-start | bytes 3076
  755.9 26.4 %copy-start.1 = (bf16[64,128,128]{2,1,0:T(8,128)(2,1)S(1)}, bf16[64,128,128]{2,1,0:T(8,128)(2,1)}, u32[]{:S(2)}) copy-start(bf16[64,128,128]{2,1,0:T(8,128)(2,1)} %param.21) | copy-start | bytes 6291460
Sparse Core Ops, SparseCore 0:
  222.9 29.4 all-gather.5
  255.2 69.5 all-gather.9
  326.9 57.9 all-gather.7

commit v4 on v3

--- a/solution.py
+++ b/solution.py
@@ -36,7 +36,7 @@
     product = jnp.dot(
         row_factor,
         col_factor.T,
-        precision=lax.Precision.HIGHEST,
+        precision=lax.Precision.HIGH,
         preferred_element_type=jnp.float32,
     )
     return matrix - product
@@ -103,9 +103,16 @@
     global_rows = (local_rows // width * row_devs + row_here) * width + local_rows % width
     global_cols = (local_cols // width * col_devs + col_here) * width + local_cols % width
     total = NPANEL * PW
-    hi = lax.Precision.HIGHEST
+    hi = lax.Precision.HIGH
+
+    corner_blocks = total // width
+    first = matrix[:width, :width].astype(jnp.bfloat16)
+    every = lax.all_gather(first, ("frow", "fcol"), axis=0, tiled=False)
+    every, own_column = lax.optimization_barrier((every, matrix[:, :width]))
+    every = every.reshape(row_devs, col_devs, width, width)[:corner_blocks, :corner_blocks]
+    corner = every.transpose(0, 2, 1, 3).reshape(total, total).astype(jnp.float32)
     row_panel = lax.all_gather(
-        matrix[:, :width].astype(jnp.bfloat16), "fcol", axis=1, tiled=True
+        own_column.astype(jnp.bfloat16), "fcol", axis=1, tiled=True
     )[:, :total]
     half = row_devs // col_devs
     pairs = []
@@ -122,11 +129,6 @@
         .transpose(1, 0, 2, 3)
         .reshape(local.shape[1], total)
     )
-    corner_blocks = total // width
-    first = matrix[:width, :width].astype(jnp.bfloat16)
-    every = lax.all_gather(first, ("frow", "fcol"), axis=0, tiled=False)
-    every = every.reshape(row_devs, col_devs, width, width)[:corner_blocks, :corner_blocks]
-    corner = every.transpose(0, 2, 1, 3).reshape(total, total).astype(jnp.float32)
     rows_all = jnp.concatenate([row_panel, col_panel], axis=0).astype(jnp.float32)
     n_own = local.shape[0]
     factor_full = jnp.zeros((total, total), jnp.float32)

time: 800 us -> 771 us (0.964)
  matrix products: 113 us -> 81.1 us
    all_gather x1, waiting for transfers between devices: 27.3 us -> 0.02 us  [shards(): lax.all_gather(own_column.astype(jnp.bfloat16), 'fcol', axis=1, tiled=True)]
    all_gather x1, waiting for transfers between devices: 49.6 us -> 68.7 us  [shards(): every = lax.all_gather(first, ('frow', 'fcol'), axis=0, tiled=False)]
    dot_general x1, matrix products: 30.7 us -> 18 us  [subtract_product(): jnp.dot(row_factor, col_factor.T, precision=lax.Precision.HIGH, preferred...]
    add x0 -> x1, other arithmetic: none -> 12.1 us  [shards(): matrix = local + added]
    dot_general x1, matrix products: 21.5 us -> 11 us  [shards(): jnp.dot(solved_rows, below.T, precision=hi, preferred_element_type=jnp.fl...]
    dot_general x2, matrix products: 19.1 us -> 10.8 us  [shards(): jnp.dot(rows_all[:, start:stop], inverse.T, precision=hi, preferred_eleme...]
    unnamed x59 -> x48, local copies, waits for them, and re-layouts: 70.3 us -> 72 us
  transfers between devices with their start and end apart: 6 -> 6, of which waited for: 4 -> 3; matrix products, arithmetic and copies ran while one was open for 49% -> 51% of each run, Pallas kernels for 0% -> 0%
where the time goes in v4:
time: 771 us; the launch traced here: 761 us
  other arithmetic  288 us (37%)
  local copies, waits for them, and re-layouts  192 us (25%)
  waiting for transfers between devices  155 us (20%)
  matrix products  81.1 us (11%)
  starting transfers between devices  25.5 us (3%)
  between operations  19.1 us (2%)
    another operation x29, other arithmetic, shards(): factor = jnp.linalg.cholesky(symmetric)  166 us
    another operation x4, other arithmetic, shards(): lax.linalg.triangular_solve(factor, eye, left_side=True, lower=True)  79.9 us
    all_to_all x1, waiting for transfers between devices, shards(): lax.all_to_all(send_tiles.reshape(owners, CAP, width, width), ('frow', 'f...  77.4 us
    unnamed x48, local copies, waits for them, and re-layouts  72 us
    all_gather x1, waiting for transfers between devices, shards(): every = lax.all_gather(first, ('frow', 'fcol'), axis=0, tiled=False)  68.7 us
    broadcast_in_dim x1, local copies, waits for them, and re-layouts, shards(): return result[None, :, None, :]  20.5 us
    another operation x27, local copies, waits for them, and re-layouts, shards(): lax.linalg.triangular_solve(factor, eye, left_side=True, lower=True)  19.3 us
    dot_general x1, matrix products, subtract_product(): jnp.dot(row_factor, col_factor.T, precision=lax.Precision.HIGH, preferred...  18 us
  transfers between devices with their start and end apart: 6, of which 3 were waited for; matrix products, arithmetic and copies ran while one was open for 51% of the time, Pallas kernels for 0%

profile of v4, /device:TPU:6, one launch (start us, length us, event | category | flops | bytes accessed | tf_op | source)
XLA Modules:
  0.0 761.3 jit_solution(13863186149921517891)
XLA Ops:
  8.8 1.9 gather_fusion
  11.4 10.5 %all-to-all-start = ((s32[128,1,2]{2,1,0:T(1,128)}), s32[128,1,2]{2,1,0:T(1,128)S(1)}, u32[]{:S(2)}, u32[]{:S(2)}) async-start(s32[128,1,2]{2,1,0:T(1,128)} %bitcast.5), calls=%async_computation | async-start | bytes 131072 | tf_op jit(solution)/shard_map/all_to_all | solution.py:80
  23.1 3.6 fusion.22
  26.7 10.1 %gather_fusion.1 = bf16[256,128,128]{2,1,0:T(8,128)(2,1)} fusion(bf16[64,128,128]{2,1,0:T(8,128)(2,1)} %fusion.22, s32[1024]{0:T(1024)S(1)} %pad_clamp_fusion), kind=kCustom, calls=%fused_computation.1 | custom fusion | bytes 16778240 | tf_op jit(solution)/shard_map/jit(_take)/gather | solution.py:69
  36.8 7.4 select_select_fusion
  44.3 10.2 %all-to-all-start.1 = ((bf16[128,2,128,128]{3,2,1,0:T(8,128)(2,1)}), bf16[128,2,128,128]{3,2,1,0:T(8,128)(2,1)}, u32[]{:S(2)}, u32[]{:S(2)}) async-start(bf16[128,2,128,128]{3,2,1,0:T(8,128)(2,1)} %select_select_fusion), calls=%async_computation.1 | async-start | bytes 16777216 | tf_op jit(solution)/shard_map/all_to_all | solution.py:73
  54.5 20.9 %copy.52 = f32[1,1024,1,2048]{1,3,2,0:T(8,128)} copy(f32[1,1024,1,2048]{3,2,1,0:T(1,128)} %param.20) | data formatting | bytes 16777216 | tf_op args[0]
  76.8 77.4 %all-to-all-done.1 = bf16[128,2,128,128]{3,2,1,0:T(8,128)(2,1)} async-done(((bf16[128,2,128,128]{3,2,1,0:T(8,128)(2,1)}), bf16[128,2,128,128]{3,2,1,0:T(8,128)(2,1)}, u32[]{:S(2)}, u32[]{:S(2)}) %all-to-all-start.1) | async-done | bytes 8388640 | tf_op jit(solution)/shard_map/all_to_all | solution.py:73
  154.2 23.6 %copy.94 = bf16[32,8,128,128]{3,1,2,0:T(8,128)(2,1)} copy(bf16[32,8,128,128]{3,2,1,0:T(8,128)(2,1)} %bitcast.60) | data formatting | bytes 16777216
  177.8 11.9 %copy.54 = bf16[256,16384]{0,1:T(8,128)(2,1)} copy(bf16[256,16384]{1,0:T(8,128)(2,1)} %bitcast.172) | data formatting | bytes 16777216 | tf_op jit(solution)/shard_map/reshape | solution.py:93
  189.6 6.2 fusion.82
  195.8 7.5 copy.93
  203.3 9.3 %copy.55 = f32[1024,2048]{0,1:T(8,128)} copy(f32[1024,2048]{1,0:T(8,128)} %bitcast.173) | data formatting | bytes 16777216 | tf_op jit(solution)/shard_map/reshape | solution.py:98
  212.6 12.1 %bitcast_add_fusion = f32[1024,2048]{0,1:T(8,128)} fusion(f32[1024,2048]{0,1:T(8,128)} %copy.55, f32[1,1024,1,2048]{1,3,2,0:T(8,128)} %copy.52), kind=kLoop, calls=%fused_computation.12 | loop fusion | flops 2097152 | bytes 25165824 | tf_op jit(solution)/shard_map/add | solution.py:100
  229.5 1.8 slice.330
  231.2 68.7 %all-gather.8.cloned.1.call-done = bf16[16384,128]{0,1:T(8,128)(2,1)} async-done(((bf16[128,128]{0,1:T(8,128)(2,1)}), bf16[16384,128]{0,1:T(8,128)(2,1)}) %all-gather.8.cloned.1.call-update) | async-done | bytes 4194320 | tf_op jit(solution)/shard_map/all_gather | solution.py:110
  300.0 5.4 copy.85
  305.5 7.1 copy.58
  312.5 1.7 slice.333
  315.6 2.2 copy_bitcast_fusion.2
  317.8 2.0 copy-done.4
  323.2 11.7 %cholesky.286 = f32[128,128]{1,0:T(8,128)S(1)} custom-call(f32[128,128]{1,0:T(8,128)S(1)} %cholesky.426), custom_call_target="Cholesky" | custom-call | tf_op jit(solution)/shard_map/jit(cholesky)/cholesky | solution.py:142
  335.0 9.8 %custom-call.27 = f32[1,128,128]{1,2,0:T(8,128)S(1)} custom-call(f32[1,128,128]{2,1,0:T(8,128)S(1)} %get-tuple-element.144), custom_call_target="InvertDiagBlocksLowerTriangular" | custom-call | tf_op jit(solution)/shard_map/jit(cholesky)/cholesky | solution.py:142
  347.5 12.1 %cholesky.305 = f32[128,128]{1,0:T(8,128)S(1)} custom-call(f32[128,128]{1,0:T(8,128)S(1)} %cholesky.430), custom_call_target="Cholesky" | custom-call | tf_op jit(solution)/shard_map/jit(cholesky)/cholesky | solution.py:142
  359.6 9.8 %custom-call.28 = f32[1,128,128]{1,2,0:T(8,128)S(1)} custom-call(f32[1,128,128]{2,1,0:T(8,128)S(1)} %get-tuple-element.141), custom_call_target="InvertDiagBlocksLowerTriangular" | custom-call | tf_op jit(solution)/shard_map/jit(cholesky)/cholesky | solution.py:142
  371.0 11.7 %cholesky.326 = f32[128,128]{1,0:T(8,128)S(1)} custom-call(f32[128,128]{1,0:T(8,128)S(1)} %cholesky.435), custom_call_target="Cholesky" | custom-call | tf_op jit(solution)/shard_map/jit(cholesky)/cholesky | solution.py:142
  382.7 9.8 %custom-call.29 = f32[1,128,128]{1,2,0:T(8,128)S(1)} custom-call(f32[1,128,128]{2,1,0:T(8,128)S(1)} %get-tuple-element.138), custom_call_target="InvertDiagBlocksLowerTriangular" | custom-call | tf_op jit(solution)/shard_map/jit(cholesky)/cholesky | solution.py:142
  394.0 11.9 %cholesky.343 = f32[128,128]{1,0:T(8,128)S(1)} custom-call(f32[128,128]{1,0:T(8,128)S(1)} %convolution_subtract_fusion.11), custom_call_target="Cholesky" | custom-call | tf_op jit(solution)/shard_map/jit(cholesky)/cholesky | solution.py:142
  411.8 8.1 %while.10 = (s32[]{:T(128)}, f32[512,512]{1,0:T(8,128)S(1)}, s32[4,2]{0,1:T(2,128)S(1)}, f32[4,128,128]{2,1,0:T(8,128)S(1)}, s32[]{:T(128)}) while((s32[]{:T(128)}, f32[512,512]{1,0:T(8,128)S(1)}, s32[4,2]{0,1:T(2,128)S(1)}, f32[4,128,128]{2,1,0:T(8,128)S(1)}, s32[]{:T(128)}) %tuple.85), condition=%wide.while_cond.6, body=%wide.while_body.6.sunk | while | flops 2 | bytes 131189 | solution.py:143
  419.9 39.3 %custom-call.30 = f32[4,128,128]{1,2,0:T(8,128)S(1)} custom-call(f32[4,128,128]{2,1,0:T(8,128)S(1)} %get-tuple-element.97), custom_call_target="InvertDiagBlocksLowerTriangular" | custom-call | tf_op jit(solution)/shard_map/triangular_solve/custom-call.3 | solution.py:143
  461.6 4.7 collective-permute-start
  467.6 3.7 scatter.14
  471.8 9.3 %collective-permute-done = bf16[128,1024]{0,1:T(8,128)(2,1)S(1)} collective-permute-done((bf16[128,1024]{0,1:T(8,128)(2,1)S(1)}, bf16[128,1024]{0,1:T(8,128)(2,1)S(1)}, u32[]{:S(2)}, u32[]{:S(2)}) %collective-permute-start) | collective-permute-done | bytes 262176 | tf_op jit(solution)/shard_map/ppermute | solution.py:125
  481.8 1.6 convolution_subtract_fusion.5
  483.8 2.9 constant_dynamic-update-slice_fusion.2
  486.7 3.4 broadcast_select_fusion
  491.4 1.8 bitcast_add_fusion.2
  497.0 11.7 %cholesky.358 = f32[128,128]{1,0:T(8,128)S(1)} custom-call(f32[128,128]{1,0:T(8,128)S(1)} %cholesky.439), custom_call_target="Cholesky" | custom-call | tf_op jit(solution)/shard_map/jit(cholesky)/cholesky | solution.py:142
  509.2 9.8 %custom-call.31 = f32[1,128,128]{1,2,0:T(8,128)S(1)} custom-call(f32[1,128,128]{2,1,0:T(8,128)S(1)} %get-tuple-element.134), custom_call_target="InvertDiagBlocksLowerTriangular" | custom-call | tf_op jit(solution)/shard_map/jit(cholesky)/cholesky | solution.py:142
  522.3 12.1 %cholesky.377 = f32[128,128]{1,0:T(8,128)S(1)} custom-call(f32[128,128]{1,0:T(8,128)S(1)} %cholesky.443), custom_call_target="Cholesky" | custom-call | tf_op jit(solution)/shard_map/jit(cholesky)/cholesky | solution.py:142
  535.0 9.8 %custom-call.32 = f32[1,128,128]{1,2,0:T(8,128)S(1)} custom-call(f32[1,128,128]{2,1,0:T(8,128)S(1)} %get-tuple-element.131), custom_call_target="InvertDiagBlocksLowerTriangular" | custom-call | tf_op jit(solution)/shard_map/jit(cholesky)/cholesky | solution.py:142
  547.9 13.2 %cholesky.398 = f32[128,128]{1,0:T(8,128)} custom-call(f32[128,128]{1,0:T(8,128)} %cholesky.448), custom_call_target="Cholesky" | custom-call | tf_op jit(solution)/shard_map/jit(cholesky)/cholesky | solution.py:142
  561.1 2.1 select_reduce_fusion.1
  563.2 11.3 %custom-call.33 = f32[1,128,128]{1,2,0:T(8,128)} custom-call(f32[1,128,128]{2,1,0:T(8,128)} %get-tuple-element.128), custom_call_target="InvertDiagBlocksLowerTriangular" | custom-call | tf_op jit(solution)/shard_map/jit(cholesky)/cholesky | solution.py:142
  576.9 11.7 %cholesky.415 = f32[128,128]{1,0:T(8,128)S(1)} custom-call(f32[128,128]{1,0:T(8,128)S(1)} %convolution_subtract_fusion.10), custom_call_target="Cholesky" | custom-call | tf_op jit(solution)/shard_map/jit(cholesky)/cholesky | solution.py:142
  595.3 1.6 fusion.39
  596.9 8.8 %gather_fusion.2 = f32[1024,1024]{1,0:T(8,128)} fusion(f32[1024,1024]{1,0:T(8,128)} %get-tuple-element.123, s32[1024]{0:T(1024)} %broadcast_clamp_fusion), kind=kCustom, calls=%fused_computation.2 | custom fusion | bytes 8392704 | tf_op jit(solution)/shard_map/jit(_take)/gather | solution.py:165
  607.8 11.4 %while.11 = (s32[]{:T(128)}, f32[512,512]{1,0:T(8,128)}, s32[4,2]{0,1:T(2,128)S(1)}, f32[4,128,128]{2,1,0:T(8,128)S(1)}, s32[]{:T(128)}) while((s32[]{:T(128)}, f32[512,512]{1,0:T(8,128)}, s32[4,2]{0,1:T(2,128)S(1)}, f32[4,128,128]{2,1,0:T(8,128)S(1)}, s32[]{:T(128)}) %tuple.97), condition=%wide.while_cond.6.clone, body=%wide.while_body.6.clone.sunk | while | flops 2 | bytes 131189 | solution.py:143
  608.5 2.2 bitcast_dynamic-update-slice_fusion.5
  611.3 2.2 bitcast_dynamic-update-slice_fusion.5
  614.2 2.2 bitcast_dynamic-update-slice_fusion.5
  617.0 2.1 bitcast_dynamic-update-slice_fusion.5
  619.2 39.3 %custom-call.34 = f32[4,128,128]{1,2,0:T(8,128)S(1)} custom-call(f32[4,128,128]{2,1,0:T(8,128)S(1)} %get-tuple-element.98), custom_call_target="InvertDiagBlocksLowerTriangular" | custom-call | tf_op jit(solution)/shard_map/triangular_solve/custom-call.3 | solution.py:143
  666.0 3.9 copy.57
  670.0 5.7 copy.87
  675.6 7.0 copy.56
  682.7 5.5 fusion.13
  688.2 2.7 copy-done.2
  690.8 11.0 %fusion.148 = f32[3072,512]{1,0:T(8,128)S(1)} fusion(f32[3072,512]{0,1:T(8,128)S(1)} %fusion.13, f32[512,512]{1,0:T(8,128)S(1)} %get-tuple-element.152), kind=kOutput, calls=%fused_computation.272 | convolution fusion | flops 4831838208 | bytes 13631488 | tf_op jit(solution)/shard_map/dot_general | solution.py:158
  701.9 5.3 fusion.2
  707.2 18.0 %fusion.9 = f32[1024,2048]{0,1:T(8,128)} fusion(f32[1024,2048]{0,1:T(8,128)} %bitcast_add_fusion, f32[3072,512]{0,1:T(8,128)S(1)} %fusion.2, f32[3072,512]{0,1:T(8,128)} %copy-done.2), kind=kOutput, calls=%fused_computation.26 | convolution fusion | flops 12890144768 | bytes 29360128 | tf_op jit(solution)/shard_map/dot_general | solution.py:36
  725.2 2.7 fusion.54
  727.9 5.9 select_bitcast_fusion
  733.8 20.5 %copy.68 = f32[1,1024,1,2048]{3,2,1,0:T(1,128)} copy(f32[1,1024,1,2048]{1,3,2,0:T(8,128)} %select_bitcast_fusion) | data formatting | bytes 16777216 | tf_op jit(solution)/shard_map/broadcast_in_dim | solution.py:171
  (164 shorter events, 68.9 us)
Async XLA Ops:
  6.5 16.5 %copy-start = (bf16[64,128,128]{2,1,0:T(8,128)(2,1)S(1)}, bf16[64,128,128]{2,1,0:T(8,128)(2,1)}, u32[]{:S(2)}) copy-start(bf16[64,128,128]{2,1,0:T(8,128)(2,1)} %param.21) | copy-start | bytes 6291460
  11.4 32.8 %all-to-all-start = ((s32[128,1,2]{2,1,0:T(1,128)}), s32[128,1,2]{2,1,0:T(1,128)S(1)}, u32[]{:S(2)}, u32[]{:S(2)}) async-start(s32[128,1,2]{2,1,0:T(1,128)} %bitcast.5), calls=%async_computation | async-start | bytes 131072 | tf_op jit(solution)/shard_map/all_to_all | solution.py:80
  44.3 109.9 %all-to-all-start.1 = ((bf16[128,2,128,128]{3,2,1,0:T(8,128)(2,1)}), bf16[128,2,128,128]{3,2,1,0:T(8,128)(2,1)}, u32[]{:S(2)}, u32[]{:S(2)}) async-start(bf16[128,2,128,128]{3,2,1,0:T(8,128)(2,1)} %select_select_fusion), calls=%async_computation.1 | async-start | bytes 16777216 | tf_op jit(solution)/shard_map/all_to_all | solution.py:73
  54.5 245.5 %all-gather.8.cloned.1.call-start = ((), (), s32[]{:S(2)}) async-start(), calls=%async_computation.3 | async-start | bytes 4227072 | tf_op jit(solution)/shard_map/all_gather | solution.py:110
  226.2 234.3 %all-gather.6.cloned.1.call-start = ((), (), s32[]{:S(2)}) async-start(), calls=%async_computation.2 | async-start | bytes 2359296 | tf_op jit(solution)/shard_map/all_gather | solution.py:114
  305.4 364.5 %all-gather.10.cloned.1.call-start = ((), (), s32[]{:S(2)}) async-start(), calls=%async_computation.4 | async-start | bytes 4456448 | tf_op jit(solution)/shard_map/all_gather | solution.py:126
  317.8 2.0 copy-start.4
  322.2 1.0 copy-start.9
  419.9 39.8 %copy-start.8 = (f32[512,512]{1,0:T(8,128)}, f32[512,512]{1,0:T(8,128)S(1)}, u32[]{:S(2)}) copy-start(f32[512,512]{1,0:T(8,128)S(1)} %get-tuple-element.256) | copy-start | bytes 3145732
  460.5 26.2 %copy-start.6 = (f32[128,512]{1,0:T(8,128)}, f32[128,512]{1,0:T(8,128)S(1)}, u32[]{:S(2)}) copy-start(f32[128,512]{1,0:T(8,128)S(1)} %fusion.94) | copy-start | bytes 786436
  461.6 19.5 %collective-permute-start = (bf16[128,1024]{0,1:T(8,128)(2,1)S(1)}, bf16[128,1024]{0,1:T(8,128)(2,1)S(1)}, u32[]{:S(2)}, u32[]{:S(2)}) collective-permute-start(bf16[128,1024]{0,1:T(8,128)(2,1)S(1)} %constant_dynamic-slice_fusion.2), channel_id=1, source_target_pairs={{0,0},{1,8},{2,16},{3,24},{4,32},{5,40},{6,48},{7,56},{8,1},{9,9},... | collective-permute-start | bytes 786440 | tf_op jit(solution)/shard_map/ppermute | solution.py:125
  471.8 14.9 %copy-start.11 = (f32[128,512]{1,0:T(8,128)}, f32[128,512]{1,0:T(8,128)S(1)}, u32[]{:S(2)}) copy-start(f32[128,512]{1,0:T(8,128)S(1)} %fusion.92) | copy-start | bytes 786436
  481.1 0.7 copy-start.18
  483.8 2.9 copy-start.14
  496.0 1.0 copy-start.10
  521.7 0.7 copy-start.16
  658.5 2.1 copy-start.17
  675.6 7.0 copy-start.7
  675.6 7.0 copy-start.12
  675.6 7.0 copy-start.15
  688.2 2.7 copy-start.2
  690.8 11.0 %copy-start.3 = (bf16[2,8,128,1024]{3,2,0,1:T(8,128)(2,1)S(1)}, bf16[2,8,128,1024]{3,2,0,1:T(8,128)(2,1)}, u32[]{:S(2)}) copy-start(bf16[2,8,128,1024]{3,2,0,1:T(8,128)(2,1)} %copy.56) | copy-start | bytes 12582916
  690.8 11.1 %copy-start.5 = (bf16[1024,1024]{1,0:T(8,128)(2,1)S(1)}, bf16[1024,1024]{1,0:T(8,128)(2,1)}, u32[]{:S(2)}) copy-start(bf16[1024,1024]{1,0:T(8,128)(2,1)} %copy.57) | copy-start | bytes 6291460
  707.2 18.0 %copy-start.13 = (f32[1024,128]{0,1:T(8,128)S(1)}, f32[1024,128]{0,1:T(8,128)}, u32[]{:S(2)}) copy-start(f32[1024,128]{0,1:T(8,128)} %copy.82) | copy-start | bytes 1572868
  707.2 18.0 %copy-start.19 = (pred[1024]{0:T(1024)(128)(4,1)S(1)}, pred[1024]{0:T(1024)(128)(4,1)}, u32[]{:S(2)}) copy-start(pred[1024]{0:T(1024)(128)(4,1)} %get-tuple-element.159) | copy-start | bytes 3076
  707.2 18.0 %copy-start.20 = (pred[1024]{0:T(1024)(128)(4,1)S(1)}, pred[1024]{0:T(1024)(128)(4,1)}, u32[]{:S(2)}) copy-start(pred[1024]{0:T(1024)(128)(4,1)} %get-tuple-element.160) | copy-start | bytes 3076
  727.9 26.4 %copy-start.1 = (bf16[64,128,128]{2,1,0:T(8,128)(2,1)S(1)}, bf16[64,128,128]{2,1,0:T(8,128)(2,1)}, u32[]{:S(2)}) copy-start(bf16[64,128,128]{2,1,0:T(8,128)(2,1)} %param.21) | copy-start | bytes 6291460
Sparse Core Ops, SparseCore 0:
  226.3 73.5 all-gather.7
  305.5 24.0 all-gather.5
  481.9 57.3 all-gather.9

commit v5 on v4

--- a/solution.py
+++ b/solution.py
@@ -105,12 +105,15 @@
     total = NPANEL * PW
     hi = lax.Precision.HIGH
 
-    corner_blocks = total // width
-    first = matrix[:width, :width].astype(jnp.bfloat16)
-    every = lax.all_gather(first, ("frow", "fcol"), axis=0, tiled=False)
-    every, own_column = lax.optimization_barrier((every, matrix[:, :width]))
-    every = every.reshape(row_devs, col_devs, width, width)[:corner_blocks, :corner_blocks]
-    corner = every.transpose(0, 2, 1, 3).reshape(total, total).astype(jnp.float32)
+    first_row = lax.all_gather(
+        matrix[:width, :width].astype(jnp.bfloat16), "fcol", axis=1, tiled=True
+    )[:, :total]
+    split = total // 2
+    left = lax.all_gather(first_row[:, :split], "frow", axis=0, tiled=True)[:total]
+    left, right_src = lax.optimization_barrier((left, first_row[:, split:]))
+    right = lax.all_gather(right_src, "frow", axis=0, tiled=True)[:total]
+    right, own_column = lax.optimization_barrier((right, matrix[:, :width]))
+    corner = jnp.concatenate([left, right], axis=1).astype(jnp.float32)
     row_panel = lax.all_gather(
         own_column.astype(jnp.bfloat16), "fcol", axis=1, tiled=True
     )[:, :total]

time: 771 us -> 773 us (level)
  local copies, waits for them, and re-layouts: 192 us -> 126 us
  waiting for transfers between devices: 155 us -> 196 us
  matrix products: 81.1 us -> 96.1 us
  blocking collectives: 0 us -> 13.7 us
    unnamed x48 -> x41, local copies, waits for them, and re-layouts: 72 us -> 27.9 us
    all_to_all x1, waiting for transfers between devices: 77.4 us -> 97.8 us  [shards(): lax.all_to_all(send_tiles.reshape(owners, CAP, width, width), ('frow', 'f...]
    all_gather x1 -> x2, waiting for transfers between devices: 68.7 us -> 89 us  [the longest x1 48.3 us: shards(): lax.all_gather(first_row[:, :split], 'frow', axis=0, tiled=True)[:total]]
    all_gather x0 -> x1, blocking collectives: none -> 13.7 us  [shards(): lax.all_gather(matrix[:width, :width].astype(jnp.bfloat16), 'fcol', axis=...]
    reshape x1 -> x0, local copies, waits for them, and re-layouts: 9.27 us -> none  [shards(): added = summed.reshape(row_blocks, col_blocks, width, width).transpose(0,...]
    another operation x14, matrix products: 12.4 us -> 21.1 us  [shards(): lax.linalg.triangular_solve(factor, eye, left_side=True, lower=True)]
    broadcast_in_dim x1, local copies, waits for them, and re-layouts: 20.5 us -> 12.5 us  [shards(): return result[None, :, None, :]]
  transfers between devices with their start and end apart: 6 -> 7, of which waited for: 3 -> 4; matrix products, arithmetic and copies ran while one was open for 51% -> 39% of each run, Pallas kernels for 0% -> 0%
where the time goes in v5:
time: 773 us; the launch traced here: 765 us
  other arithmetic  288 us (37%)
  waiting for transfers between devices  196 us (25%)
  local copies, waits for them, and re-layouts  126 us (16%)
  matrix products  96.1 us (12%)
  starting transfers between devices  25.3 us (3%)
  between operations  19.3 us (2%)
  blocking collectives  13.7 us (2%)
    another operation x29, other arithmetic, shards(): factor = jnp.linalg.cholesky(symmetric)  160 us
    all_to_all x1, waiting for transfers between devices, shards(): lax.all_to_all(send_tiles.reshape(owners, CAP, width, width), ('frow', 'f...  97.8 us
    another operation x4, other arithmetic, shards(): lax.linalg.triangular_solve(factor, eye, left_side=True, lower=True)  82.7 us
    all_gather x1, waiting for transfers between devices, shards(): lax.all_gather(first_row[:, :split], 'frow', axis=0, tiled=True)[:total]  48.3 us
    all_gather x1, waiting for transfers between devices, shards(): right = lax.all_gather(right_src, 'frow', axis=0, tiled=True)[:total]  40.7 us
    unnamed x41, local copies, waits for them, and re-layouts  27.9 us
    another operation x14, matrix products, shards(): lax.linalg.triangular_solve(factor, eye, left_side=True, lower=True)  21.1 us
    another operation x27, local copies, waits for them, and re-layouts, shards(): lax.linalg.triangular_solve(factor, eye, left_side=True, lower=True)  20.4 us
  transfers between devices with their start and end apart: 7, of which 4 were waited for; matrix products, arithmetic and copies ran while one was open for 39% of the time, Pallas kernels for 0%

profile of v5, /device:TPU:6, one launch (start us, length us, event | category | flops | bytes accessed | tf_op | source)
XLA Modules:
  0.0 764.8 jit_solution(6197745259395859851)
XLA Ops:
  8.6 1.9 gather_fusion
  11.4 10.5 %all-to-all-start = ((s32[128,1,2]{2,1,0:T(1,128)}), s32[128,1,2]{2,1,0:T(1,128)S(1)}, u32[]{:S(2)}, u32[]{:S(2)}) async-start(s32[128,1,2]{2,1,0:T(1,128)} %bitcast.4), calls=%async_computation | async-start | bytes 131072 | tf_op jit(solution)/shard_map/all_to_all | solution.py:80
  23.0 3.6 fusion.22
  26.7 10.1 %gather_fusion.1 = bf16[256,128,128]{2,1,0:T(8,128)(2,1)} fusion(bf16[64,128,128]{2,1,0:T(8,128)(2,1)} %fusion.22, s32[1024]{0:T(1024)S(1)} %pad_clamp_fusion), kind=kCustom, calls=%fused_computation.1 | custom fusion | bytes 16778240 | tf_op jit(solution)/shard_map/jit(_take)/gather | solution.py:69
  36.8 7.4 select_select_fusion
  44.3 10.2 %all-to-all-start.1 = ((bf16[128,2,128,128]{3,2,1,0:T(8,128)(2,1)}), bf16[128,2,128,128]{3,2,1,0:T(8,128)(2,1)}, u32[]{:S(2)}, u32[]{:S(2)}) async-start(bf16[128,2,128,128]{3,2,1,0:T(8,128)(2,1)} %select_select_fusion), calls=%async_computation.1 | async-start | bytes 16777216 | tf_op jit(solution)/shard_map/all_to_all | solution.py:73
  56.4 97.8 %all-to-all-done.1 = bf16[128,2,128,128]{3,2,1,0:T(8,128)(2,1)} async-done(((bf16[128,2,128,128]{3,2,1,0:T(8,128)(2,1)}), bf16[128,2,128,128]{3,2,1,0:T(8,128)(2,1)}, u32[]{:S(2)}, u32[]{:S(2)}) %all-to-all-start.1) | async-done | bytes 8388640 | tf_op jit(solution)/shard_map/all_to_all | solution.py:73
  154.2 23.3 %copy.70 = bf16[32,8,128,128]{3,1,2,0:T(8,128)(2,1)} copy(bf16[32,8,128,128]{3,2,1,0:T(8,128)(2,1)} %bitcast.58) | data formatting | bytes 16777216
  177.5 11.9 %copy.40 = bf16[256,16384]{0,1:T(8,128)(2,1)} copy(bf16[256,16384]{1,0:T(8,128)(2,1)} %bitcast.154) | data formatting | bytes 16777216 | tf_op jit(solution)/shard_map/reshape | solution.py:93
  189.4 9.6 %fusion.82 = f32[8,16,128,128]{3,1,2,0:T(8,128)} fusion(bf16[128,128,256,1]{2,1,0,3:T(8,128)(2,1)} %bitcast.158, s32[8,16]{1,0:T(8,128)S(1)} %multiply_add_fusion, s32[256]{0:T(256)S(1)} %eq.103), kind=kOutput, calls=%fused_computation.128 | convolution fusion | flops 1073774592 | bytes 16778752 | tf_op jit(solution)/shard_map/dot_general | solution.py:92
  199.0 17.4 %bitcast_add_fusion = f32[1024,2048]{1,0:T(8,128)} fusion(f32[128,8,16,128]{3,2,1,0:T(8,128)} %bitcast.157, f32[1,1024,1,2048]{3,2,1,0:T(1,128)} %param.20), kind=kLoop, calls=%fused_computation.7 | loop fusion | flops 2097152 | bytes 25165824 | tf_op jit(solution)/shard_map/add | solution.py:100
  217.3 13.7 %all_gather.18 = bf16[128,1024]{1,0:T(8,128)(2,1)S(1)} all-gather(bf16[128,128]{1,0:T(8,128)(2,1)S(1)} %slice.421), channel_id=1, replica_groups=mesh['frow'=16,'fcol'=8] {'fcol'}, dimensions={1}, use_global_device_ids=true | all-gather | bytes 294912 | tf_op jit(solution)/shard_map/all_gather | solution.py:108
  231.8 48.3 %all-gather.6.cloned.1.call-done = bf16[2048,512]{1,0:T(8,128)(2,1)} async-done(((bf16[128,512]{1,0:T(8,128)(2,1)}), bf16[2048,512]{1,0:T(8,128)(2,1)}) %all-gather.6.cloned.1.call-update) | async-done | bytes 2097168 | tf_op jit(solution)/shard_map/all_gather | solution.py:112
  283.9 2.1 slice.343
  286.0 40.7 %all-gather.8.cloned.1.call-done = bf16[2048,512]{1,0:T(8,128)(2,1)} async-done(((bf16[128,512]{1,0:T(8,128)(2,1)}), bf16[2048,512]{1,0:T(8,128)(2,1)}) %all-gather.8.cloned.1.call-update) | async-done | bytes 2097168 | tf_op jit(solution)/shard_map/all_gather | solution.py:114
  329.2 2.6 copy.42
  331.8 2.7 bitcast_add_fusion.4
  334.5 2.6 copy.44
  337.1 1.8 fusion.34
  339.9 11.7 %cholesky.286 = f32[128,128]{1,0:T(8,128)S(1)} custom-call(f32[128,128]{1,0:T(8,128)S(1)} %cholesky.426), custom_call_target="Cholesky" | custom-call | tf_op jit(solution)/shard_map/jit(cholesky)/cholesky | solution.py:145
  352.7 9.8 %custom-call.27 = f32[1,128,128]{1,2,0:T(8,128)S(1)} custom-call(f32[1,128,128]{2,1,0:T(8,128)S(1)} %get-tuple-element.148), custom_call_target="InvertDiagBlocksLowerTriangular" | custom-call | tf_op jit(solution)/shard_map/jit(cholesky)/cholesky | solution.py:145
  362.6 1.9 constant_dynamic-update-slice_fusion.1
  365.7 11.7 %cholesky.305 = f32[128,128]{1,0:T(8,128)S(1)} custom-call(f32[128,128]{1,0:T(8,128)S(1)} %cholesky.430), custom_call_target="Cholesky" | custom-call | tf_op jit(solution)/shard_map/jit(cholesky)/cholesky | solution.py:145
  378.1 9.9 %custom-call.28 = f32[1,128,128]{1,2,0:T(8,128)S(1)} custom-call(f32[1,128,128]{2,1,0:T(8,128)S(1)} %get-tuple-element.145), custom_call_target="InvertDiagBlocksLowerTriangular" | custom-call | tf_op jit(solution)/shard_map/jit(cholesky)/cholesky | solution.py:145
  390.5 11.7 %cholesky.326 = f32[128,128]{1,0:T(8,128)S(1)} custom-call(f32[128,128]{1,0:T(8,128)S(1)} %cholesky.435), custom_call_target="Cholesky" | custom-call | tf_op jit(solution)/shard_map/jit(cholesky)/cholesky | solution.py:145
  402.8 9.8 %custom-call.29 = f32[1,128,128]{1,2,0:T(8,128)S(1)} custom-call(f32[1,128,128]{2,1,0:T(8,128)S(1)} %get-tuple-element.142), custom_call_target="InvertDiagBlocksLowerTriangular" | custom-call | tf_op jit(solution)/shard_map/jit(cholesky)/cholesky | solution.py:145
  414.9 11.7 %cholesky.343 = f32[128,128]{1,0:T(8,128)S(1)} custom-call(f32[128,128]{1,0:T(8,128)S(1)} %convolution_subtract_fusion.11), custom_call_target="Cholesky" | custom-call | tf_op jit(solution)/shard_map/jit(cholesky)/cholesky | solution.py:145
  432.1 2.8 fusion.37
  434.9 12.5 %while.10 = (s32[]{:T(128)}, f32[512,512]{1,0:T(8,128)}, s32[4,2]{0,1:T(2,128)S(1)}, f32[4,128,128]{2,1,0:T(8,128)S(1)}, s32[]{:T(128)}) while((s32[]{:T(128)}, f32[512,512]{1,0:T(8,128)}, s32[4,2]{0,1:T(2,128)S(1)}, f32[4,128,128]{2,1,0:T(8,128)S(1)}, s32[]{:T(128)}) %tuple.87), condition=%wide.while_cond.6, body=%wide.while_body.6.sunk | while | flops 2 | bytes 131181 | solution.py:146
  436.0 2.3 bitcast_dynamic-update-slice_fusion.4
  439.0 2.3 bitcast_dynamic-update-slice_fusion.4
  442.1 2.3 bitcast_dynamic-update-slice_fusion.4
  445.1 2.3 bitcast_dynamic-update-slice_fusion.4
  447.4 39.9 %custom-call.30 = f32[4,128,128]{1,2,0:T(8,128)} custom-call(f32[4,128,128]{2,1,0:T(8,128)S(1)} %get-tuple-element.101), custom_call_target="InvertDiagBlocksLowerTriangular" | custom-call | tf_op jit(solution)/shard_map/triangular_solve/custom-call.3 | solution.py:146
  488.6 1.9 convolution_subtract_fusion.3
  491.5 3.9 collective-permute-start
  496.8 3.9 scatter.14
  500.7 2.0 convolution_subtract_fusion.2
  502.7 9.2 %collective-permute-done = bf16[128,1024]{1,0:T(8,128)(2,1)} collective-permute-done((bf16[128,1024]{1,0:T(8,128)(2,1)S(1)}, bf16[128,1024]{1,0:T(8,128)(2,1)}, u32[]{:S(2)}, u32[]{:S(2)}) %collective-permute-start) | collective-permute-done | bytes 262176 | tf_op jit(solution)/shard_map/ppermute | solution.py:128
  513.4 1.8 convolution_subtract_fusion.5
  516.5 2.8 constant_dynamic-update-slice_fusion.2
  519.2 2.5 broadcast_select_fusion
  526.2 11.7 %cholesky.358 = f32[128,128]{1,0:T(8,128)S(1)} custom-call(f32[128,128]{1,0:T(8,128)S(1)} %cholesky.439), custom_call_target="Cholesky" | custom-call | tf_op jit(solution)/shard_map/jit(cholesky)/cholesky | solution.py:145
  538.1 9.8 %custom-call.31 = f32[1,128,128]{1,2,0:T(8,128)S(1)} custom-call(f32[1,128,128]{2,1,0:T(8,128)S(1)} %get-tuple-element.138), custom_call_target="InvertDiagBlocksLowerTriangular" | custom-call | tf_op jit(solution)/shard_map/jit(cholesky)/cholesky | solution.py:145
  550.4 11.9 %cholesky.377 = f32[128,128]{1,0:T(8,128)S(1)} custom-call(f32[128,128]{1,0:T(8,128)S(1)} %cholesky.443), custom_call_target="Cholesky" | custom-call | tf_op jit(solution)/shard_map/jit(cholesky)/cholesky | solution.py:145
  562.3 9.8 %custom-call.32 = f32[1,128,128]{1,2,0:T(8,128)S(1)} custom-call(f32[1,128,128]{2,1,0:T(8,128)S(1)} %get-tuple-element.135), custom_call_target="InvertDiagBlocksLowerTriangular" | custom-call | tf_op jit(solution)/shard_map/jit(cholesky)/cholesky | solution.py:145
  573.7 11.7 %cholesky.398 = f32[128,128]{1,0:T(8,128)S(1)} custom-call(f32[128,128]{1,0:T(8,128)S(1)} %cholesky.448), custom_call_target="Cholesky" | custom-call | tf_op jit(solution)/shard_map/jit(cholesky)/cholesky | solution.py:145
  585.5 10.2 %custom-call.33 = f32[1,128,128]{1,2,0:T(8,128)S(1)} custom-call(f32[1,128,128]{2,1,0:T(8,128)S(1)} %get-tuple-element.132), custom_call_target="InvertDiagBlocksLowerTriangular" | custom-call | tf_op jit(solution)/shard_map/jit(cholesky)/cholesky | solution.py:145
  597.1 11.7 %cholesky.415 = f32[128,128]{1,0:T(8,128)S(1)} custom-call(f32[128,128]{1,0:T(8,128)S(1)} %convolution_subtract_fusion.10), custom_call_target="Cholesky" | custom-call | tf_op jit(solution)/shard_map/jit(cholesky)/cholesky | solution.py:145
  615.5 8.4 %while.11 = (s32[]{:T(128)}, f32[512,512]{1,0:T(8,128)S(1)}, s32[4,2]{0,1:T(2,128)S(1)}, f32[4,128,128]{2,1,0:T(8,128)S(1)}, s32[]{:T(128)}) while((s32[]{:T(128)}, f32[512,512]{1,0:T(8,128)S(1)}, s32[4,2]{0,1:T(2,128)S(1)}, f32[4,128,128]{2,1,0:T(8,128)S(1)}, s32[]{:T(128)}) %tuple.101), condition=%wide.while_cond.6.clone, body=%wide.while_body.6.clone.sunk | while | flops 2 | bytes 131181 | solution.py:146
  624.0 39.9 %custom-call.34 = f32[4,128,128]{1,2,0:T(8,128)} custom-call(f32[4,128,128]{2,1,0:T(8,128)S(1)} %get-tuple-element.102), custom_call_target="InvertDiagBlocksLowerTriangular" | custom-call | tf_op jit(solution)/shard_map/triangular_solve/custom-call.3 | solution.py:146
  663.9 8.7 %gather_fusion.2 = f32[1024,1024]{1,0:T(8,128)} fusion(f32[1024,1024]{1,0:T(8,128)} %get-tuple-element.125, s32[1024]{0:T(1024)S(1)} %broadcast_clamp_fusion), kind=kCustom, calls=%fused_computation.2 | custom fusion | bytes 8392704 | tf_op jit(solution)/shard_map/jit(_take)/gather | solution.py:168
  679.1 1.7 convolution_subtract_fusion.4
  680.7 2.0 fusion.85
  682.7 2.8 copy.41
  685.6 4.7 fusion.13
  690.3 2.6 copy-done.2
  692.9 12.6 %fusion.148 = f32[3072,512]{1,0:T(8,128)} fusion(f32[3072,512]{0,1:T(8,128)S(1)} %fusion.13, f32[512,512]{1,0:T(8,128)S(1)} %get-tuple-element.156), kind=kOutput, calls=%fused_computation.272 | convolution fusion | flops 4831838208 | bytes 13631488 | tf_op jit(solution)/shard_map/dot_general | solution.py:161
  705.6 6.8 copy.48
  712.4 8.1 %fusion.2 = f32[3072,512]{1,0:T(8,128)S(1)} fusion(f32[3072,512]{1,0:T(8,128)} %fusion.148, bf16[2048,1024]{1,0:T(8,128)(2,1)} %bitcast.156, bf16[1024,1024]{1,0:T(8,128)(2,1)S(1)} %copy-done.12, f32[128,512]{1,0:T(8,128)S(1)} %copy-done.19, f32[128,512]{1,0:T(8,128)S(1)} %copy-done.16, f32[128,512]{1,0:T(8,128)S(1)} %fusion.88, f32[128,512]{1,0:T(8,128)S(1)} %fusion.64), kind=kOutput, calls=%fused_computation.16 | convolution fusion | flops 4842061824 | bytes 19922944 | tf_op jit(solution)/shard_map/dot_general | solution.py:148
  720.4 17.8 %fusion.9 = f32[1024,2048]{1,0:T(8,128)} fusion(f32[1024,2048]{1,0:T(8,128)} %bitcast_add_fusion, f32[3072,512]{1,0:T(8,128)S(1)} %fusion.2, f32[3072,512]{1,0:T(8,128)} %copy.48), kind=kOutput, calls=%fused_computation.25 | convolution fusion | flops 12890144768 | bytes 29360128 | tf_op jit(solution)/shard_map/dot_general | solution.py:36
  738.3 3.0 fusion.54
  741.3 4.2 select_bitcast_fusion
  745.5 12.5 %copy.50 = f32[1,1024,1,2048]{3,2,1,0:T(1,128)} copy(f32[1,1024,1,2048]{3,1,2,0:T(8,128)S(1)} %select_bitcast_fusion) | data formatting | bytes 16777216 | tf_op jit(solution)/shard_map/broadcast_in_dim | solution.py:174
  (158 shorter events, 64.0 us)
Async XLA Ops:
  6.5 16.5 %copy-start = (bf16[64,128,128]{2,1,0:T(8,128)(2,1)S(1)}, bf16[64,128,128]{2,1,0:T(8,128)(2,1)}, u32[]{:S(2)}) copy-start(bf16[64,128,128]{2,1,0:T(8,128)(2,1)} %param.21) | copy-start | bytes 6291460
  11.4 32.8 %all-to-all-start = ((s32[128,1,2]{2,1,0:T(1,128)}), s32[128,1,2]{2,1,0:T(1,128)S(1)}, u32[]{:S(2)}, u32[]{:S(2)}) async-start(s32[128,1,2]{2,1,0:T(1,128)} %bitcast.4), calls=%async_computation | async-start | bytes 131072 | tf_op jit(solution)/shard_map/all_to_all | solution.py:80
  44.3 109.9 %all-to-all-start.1 = ((bf16[128,2,128,128]{3,2,1,0:T(8,128)(2,1)}), bf16[128,2,128,128]{3,2,1,0:T(8,128)(2,1)}, u32[]{:S(2)}, u32[]{:S(2)}) async-start(bf16[128,2,128,128]{3,2,1,0:T(8,128)(2,1)} %select_select_fusion), calls=%async_computation.1 | async-start | bytes 16777216 | tf_op jit(solution)/shard_map/all_to_all | solution.py:73
  54.5 225.6 %all-gather.6.cloned.1.call-start = ((), (), s32[]{:S(2)}) async-start(), calls=%async_computation.2 | async-start | bytes 2228224 | tf_op jit(solution)/shard_map/all_gather | solution.py:112
  231.7 95.0 %all-gather.8.cloned.1.call-start = ((), (), s32[]{:S(2)}) async-start(), calls=%async_computation.3 | async-start | bytes 2228224 | tf_op jit(solution)/shard_map/all_gather | solution.py:114
  281.4 209.1 %all-gather.10.cloned.1.call-start = ((), (), s32[]{:S(2)}) async-start(), calls=%async_computation.4 | async-start | bytes 2359296 | tf_op jit(solution)/shard_map/all_gather | solution.py:117
  283.9 229.5 %copy-start.4 = (f32[512,512]{1,0:T(8,128)}, f32[512,512]{1,0:T(8,128)S(1)}, u32[]{:S(2)}) copy-start(f32[512,512]{1,0:T(8,128)S(1)} %fusion.38) | copy-start | bytes 3145732
  338.9 1.0 copy-start.9
  388.1 294.6 %all-gather.12.cloned.1.call-start = ((), (), s32[]{:S(2)}) async-start(), calls=%async_computation.5 | async-start | bytes 4456448 | tf_op jit(solution)/shard_map/all_gather | solution.py:129
  491.5 20.4 %collective-permute-start = (bf16[128,1024]{1,0:T(8,128)(2,1)S(1)}, bf16[128,1024]{1,0:T(8,128)(2,1)}, u32[]{:S(2)}, u32[]{:S(2)}) collective-permute-start(bf16[128,1024]{1,0:T(8,128)(2,1)S(1)} %constant_dynamic-slice_fusion.2), channel_id=1, source_target_pairs={{0,0},{1,8},{2,16},{3,24},{4,32},{5,40},{6,48},{7,56},{8,1},{9,9},... | collective-permute-start | bytes 786440 | tf_op jit(solution)/shard_map/ppermute | solution.py:128
  496.8 3.9 copy-start.6
  511.9 7.3 copy-start.18
  513.4 8.3 %copy-start.13 = (f32[128,512]{1,0:T(8,128)}, f32[128,512]{1,0:T(8,128)S(1)}, u32[]{:S(2)}) copy-start(f32[128,512]{1,0:T(8,128)S(1)} %fusion.92) | copy-start | bytes 786436
  516.5 5.2 copy-start.17
  525.2 1.0 copy-start.10
  624.0 39.9 %copy-start.8 = (f32[512,512]{1,0:T(8,128)}, f32[512,512]{1,0:T(8,128)S(1)}, u32[]{:S(2)}) copy-start(f32[512,512]{1,0:T(8,128)S(1)} %get-tuple-element.261) | copy-start | bytes 3145732
  663.9 8.7 %copy-start.5 = (f32[512,512]{1,0:T(8,128)S(1)}, f32[512,512]{1,0:T(8,128)}, u32[]{:S(2)}) copy-start(f32[512,512]{1,0:T(8,128)} %copy-done.4) | copy-start | bytes 3145732
  675.1 10.4 %copy-start.7 = (f32[128,512]{1,0:T(8,128)S(1)}, f32[128,512]{1,0:T(8,128)}, u32[]{:S(2)}) copy-start(f32[128,512]{1,0:T(8,128)} %copy-done.6) | copy-start | bytes 786436
  675.1 10.4 %copy-start.14 = (f32[128,512]{1,0:T(8,128)S(1)}, f32[128,512]{1,0:T(8,128)}, u32[]{:S(2)}) copy-start(f32[128,512]{1,0:T(8,128)} %copy-done.13) | copy-start | bytes 786436
  679.1 1.7 copy-start.15
  682.7 2.9 copy-start.11
  685.5 4.8 copy-start.3
  690.3 2.6 copy-start.2
  705.5 6.8 copy-start.12
  705.5 6.8 copy-start.16
  705.6 6.8 copy-start.19
  741.3 16.7 %copy-start.1 = (bf16[64,128,128]{2,1,0:T(8,128)(2,1)S(1)}, bf16[64,128,128]{2,1,0:T(8,128)(2,1)}, u32[]{:S(2)}) copy-start(bf16[64,128,128]{2,1,0:T(8,128)(2,1)} %param.21) | copy-start | bytes 6291460
Sparse Core Ops, SparseCore 0:
  231.9 48.1 all-gather.5
  282.2 44.5 all-gather.7
  388.2 26.6 all-gather.9
  512.0 49.9 all-gather.11

commit v6 on v5

--- a/solution.py
+++ b/solution.py
@@ -98,6 +98,12 @@
         .reshape(local.shape)
     )
     matrix = local + added
+    first_ids = jnp.arange(row_blocks, dtype=jnp.int32) * col_blocks
+    first_onehot = (blocks_in.reshape(1, slot_count) == first_ids[:, None]).astype(jnp.bfloat16)
+    first_added = jnp.dot(
+        first_onehot, placed.reshape(slot_count, width * width), preferred_element_type=jnp.float32
+    ).reshape(local.shape[0], width)
+    first_column = local[:, :width] + first_added
     local_rows = jnp.arange(local.shape[0], dtype=jnp.int32)
     local_cols = jnp.arange(local.shape[1], dtype=jnp.int32)
     global_rows = (local_rows // width * row_devs + row_here) * width + local_rows % width
@@ -106,13 +112,13 @@
     hi = lax.Precision.HIGH
 
     first_row = lax.all_gather(
-        matrix[:width, :width].astype(jnp.bfloat16), "fcol", axis=1, tiled=True
+        first_column[:width].astype(jnp.bfloat16), "fcol", axis=1, tiled=True
     )[:, :total]
     split = total // 2
     left = lax.all_gather(first_row[:, :split], "frow", axis=0, tiled=True)[:total]
     left, right_src = lax.optimization_barrier((left, first_row[:, split:]))
     right = lax.all_gather(right_src, "frow", axis=0, tiled=True)[:total]
-    right, own_column = lax.optimization_barrier((right, matrix[:, :width]))
+    right, own_column = lax.optimization_barrier((right, first_column))
     corner = jnp.concatenate([left, right], axis=1).astype(jnp.float32)
     row_panel = lax.all_gather(
         own_column.astype(jnp.bfloat16), "fcol", axis=1, tiled=True

time: 773 us -> 731 us (0.946)
  waiting for transfers between devices: 196 us -> 145 us
  matrix products: 96.1 us -> 116 us
  other arithmetic: 288 us -> 272 us
    all_gather x1, waiting for transfers between devices: 40.7 us -> 0.01 us  [shards(): right = lax.all_gather(right_src, 'frow', axis=0, tiled=True)[:total]]
    add x1, other arithmetic: 17.4 us -> 1.1 us  [shards(): first_column = local[:, :width] + first_added]
    unnamed x41 -> x44, local copies, waits for them, and re-layouts: 27.9 us -> 38.9 us
    all_to_all x1, waiting for transfers between devices: 97.8 us -> 87.1 us  [shards(): lax.all_to_all(send_tiles.reshape(owners, CAP, width, width), ('frow', 'f...]
    dot_general x1, matrix products: 17.8 us -> 26.4 us  [subtract_product(): jnp.dot(row_factor, col_factor.T, precision=lax.Precision.HIGH, preferred...]
    dot_general x0 -> x1, matrix products: none -> 7.84 us  [shards(): jnp.dot(first_onehot, placed.reshape(slot_count, width * width), preferre...]
  transfers between devices with their start and end apart: 7 -> 7, of which waited for: 4 -> 3; matrix products, arithmetic and copies ran while one was open for 39% -> 49% of each run, Pallas kernels for 0% -> 0%
where the time goes in v6:
time: 731 us; the launch traced here: 723 us
  other arithmetic  272 us (37%)
  waiting for transfers between devices  145 us (20%)
  local copies, waits for them, and re-layouts  133 us (18%)
  matrix products  116 us (16%)
  starting transfers between devices  25 us (3%)
  between operations  19.1 us (3%)
  blocking collectives  13.8 us (2%)
    another operation x29, other arithmetic, shards(): factor = jnp.linalg.cholesky(symmetric)  160 us
    all_to_all x1, waiting for transfers between devices, shards(): lax.all_to_all(send_tiles.reshape(owners, CAP, width, width), ('frow', 'f...  87.1 us
    another operation x4, other arithmetic, shards(): lax.linalg.triangular_solve(factor, eye, left_side=True, lower=True)  82.7 us
    all_gather x1, waiting for transfers between devices, shards(): lax.all_gather(first_row[:, :split], 'frow', axis=0, tiled=True)[:total]  48.3 us
    unnamed x44, local copies, waits for them, and re-layouts  38.9 us
    dot_general x1, matrix products, subtract_product(): jnp.dot(row_factor, col_factor.T, precision=lax.Precision.HIGH, preferred...  26.4 us
    another operation x14, matrix products, shards(): lax.linalg.triangular_solve(factor, eye, left_side=True, lower=True)  21.1 us
    another operation x27, local copies, waits for them, and re-layouts, shards(): lax.linalg.triangular_solve(factor, eye, left_side=True, lower=True)  19 us
  transfers between devices with their start and end apart: 7, of which 3 were waited for; matrix products, arithmetic and copies ran while one was open for 49% of the time, Pallas kernels for 0%

profile of v6, /device:TPU:6, one launch (start us, length us, event | category | flops | bytes accessed | tf_op | source)
XLA Modules:
  0.0 723.3 jit_solution(1391171639773767667)
XLA Ops:
  8.6 1.9 gather_fusion
  11.4 10.5 %all-to-all-start = ((s32[128,1,2]{2,1,0:T(1,128)}), s32[128,1,2]{2,1,0:T(1,128)S(1)}, u32[]{:S(2)}, u32[]{:S(2)}) async-start(s32[128,1,2]{2,1,0:T(1,128)} %bitcast.4), calls=%async_computation | async-start | bytes 131072 | tf_op jit(solution)/shard_map/all_to_all | solution.py:80
  23.0 3.6 fusion.22
  26.7 10.1 %gather_fusion.1 = bf16[256,128,128]{2,1,0:T(8,128)(2,1)} fusion(bf16[64,128,128]{2,1,0:T(8,128)(2,1)} %fusion.22, s32[1024]{0:T(1024)S(1)} %pad_clamp_fusion), kind=kCustom, calls=%fused_computation.1 | custom fusion | bytes 16778240 | tf_op jit(solution)/shard_map/jit(_take)/gather | solution.py:69
  36.8 7.4 %select_select_fusion = bf16[128,2,128,128]{3,2,1,0:T(8,128)(2,1)} fusion(bf16[128,2,128,128]{3,2,1,0:T(8,128)(2,1)} %bitcast.159, pred[128,2]{1,0:T(8,128)(4,1)S(1)} %compare_and_fusion, pred[128,2]{1,0:T(8,128)(4,1)S(1)} %broadcast_in_dim.110), kind=kLoop, calls=%fused_computation.15 | loop fusion | flops 8388608 | bytes 16777728 | tf_op jit(solution)/shard_map/jit(_where)/select_n | solution.py:67
  44.3 10.2 %all-to-all-start.1 = ((bf16[128,2,128,128]{3,2,1,0:T(8,128)(2,1)}), bf16[128,2,128,128]{3,2,1,0:T(8,128)(2,1)}, u32[]{:S(2)}, u32[]{:S(2)}) async-start(bf16[128,2,128,128]{3,2,1,0:T(8,128)(2,1)} %select_select_fusion), calls=%async_computation.1 | async-start | bytes 16777216 | tf_op jit(solution)/shard_map/all_to_all | solution.py:73
  54.7 10.7 %copy.74 = f32[1,1024,1,2048]{3,1,2,0:T(8,128)} copy(f32[1,1024,1,2048]{3,2,1,0:T(1,128)} %param.20) | data formatting | bytes 16777216
  67.0 87.1 %all-to-all-done.1 = bf16[128,2,128,128]{3,2,1,0:T(8,128)(2,1)} async-done(((bf16[128,2,128,128]{3,2,1,0:T(8,128)(2,1)}), bf16[128,2,128,128]{3,2,1,0:T(8,128)(2,1)}, u32[]{:S(2)}, u32[]{:S(2)}) %all-to-all-start.1) | async-done | bytes 8388640 | tf_op jit(solution)/shard_map/all_to_all | solution.py:73
  154.2 7.8 %fusion.122 = f32[8,16384]{1,0:T(8,128)S(1)} fusion(s32[256]{0:T(256)S(1)} %eq.116, s32[8]{0:T(128)S(1)} %iota_multiply_fusion.1, bf16[32,8,128,128]{3,2,1,0:T(8,128)(2,1)} %bitcast.58), kind=kOutput, calls=%fused_computation.218 | convolution fusion | flops 67110912 | bytes 8913952 | tf_op jit(solution)/shard_map/dot_general | solution.py:103
  163.2 13.8 %all_gather.18 = bf16[128,1024]{1,0:T(8,128)(2,1)S(1)} all-gather(bf16[128,128]{1,0:T(8,128)(2,1)S(1)} %slice.422), channel_id=1, replica_groups=mesh['frow'=16,'fcol'=8] {'fcol'}, dimensions={1}, use_global_device_ids=true | all-gather | bytes 294912 | tf_op jit(solution)/shard_map/all_gather | solution.py:114
  177.8 48.3 %all-gather.6.cloned.1.call-done = bf16[2048,512]{1,0:T(8,128)(2,1)} async-done(((bf16[128,512]{1,0:T(8,128)(2,1)}), bf16[2048,512]{1,0:T(8,128)(2,1)}) %all-gather.6.cloned.1.call-update) | async-done | bytes 2097168 | tf_op jit(solution)/shard_map/all_gather | solution.py:118
  230.0 23.7 %copy.73 = bf16[32,8,128,128]{3,1,2,0:T(8,128)(2,1)} copy(bf16[32,8,128,128]{3,2,1,0:T(8,128)(2,1)} %bitcast.58) | data formatting | bytes 16777216
  253.6 11.9 %copy.40 = bf16[256,16384]{0,1:T(8,128)(2,1)} copy(bf16[256,16384]{1,0:T(8,128)(2,1)} %bitcast.160) | data formatting | bytes 16777216 | tf_op jit(solution)/shard_map/reshape | solution.py:93
  265.6 9.7 %fusion.82 = f32[8,16,128,128]{3,1,2,0:T(8,128)} fusion(bf16[128,128,256,1]{2,1,0,3:T(8,128)(2,1)} %bitcast.165, s32[8,16]{1,0:T(8,128)S(1)} %multiply_add_fusion, s32[256]{0:T(256)S(1)} %eq.116), kind=kOutput, calls=%fused_computation.130 | convolution fusion | flops 1073774592 | bytes 16778752 | tf_op jit(solution)/shard_map/dot_general | solution.py:92
  277.7 2.5 copy.42
  280.3 2.8 bitcast_add_fusion.4
  283.0 2.5 copy.44
  285.6 1.8 fusion.34
  288.3 11.7 %cholesky.286 = f32[128,128]{1,0:T(8,128)S(1)} custom-call(f32[128,128]{1,0:T(8,128)S(1)} %cholesky.426), custom_call_target="Cholesky" | custom-call | tf_op jit(solution)/shard_map/jit(cholesky)/cholesky | solution.py:151
  301.2 9.8 %custom-call.27 = f32[1,128,128]{1,2,0:T(8,128)S(1)} custom-call(f32[1,128,128]{2,1,0:T(8,128)S(1)} %get-tuple-element.148), custom_call_target="InvertDiagBlocksLowerTriangular" | custom-call | tf_op jit(solution)/shard_map/jit(cholesky)/cholesky | solution.py:151
  311.0 1.9 constant_dynamic-update-slice_fusion.1
  314.2 12.1 %cholesky.305 = f32[128,128]{1,0:T(8,128)S(1)} custom-call(f32[128,128]{1,0:T(8,128)S(1)} %cholesky.430), custom_call_target="Cholesky" | custom-call | tf_op jit(solution)/shard_map/jit(cholesky)/cholesky | solution.py:151
  327.0 9.8 %custom-call.28 = f32[1,128,128]{1,2,0:T(8,128)S(1)} custom-call(f32[1,128,128]{2,1,0:T(8,128)S(1)} %get-tuple-element.145), custom_call_target="InvertDiagBlocksLowerTriangular" | custom-call | tf_op jit(solution)/shard_map/jit(cholesky)/cholesky | solution.py:151
  339.2 11.7 %cholesky.326 = f32[128,128]{1,0:T(8,128)S(1)} custom-call(f32[128,128]{1,0:T(8,128)S(1)} %cholesky.435), custom_call_target="Cholesky" | custom-call | tf_op jit(solution)/shard_map/jit(cholesky)/cholesky | solution.py:151
  351.6 9.8 %custom-call.29 = f32[1,128,128]{1,2,0:T(8,128)S(1)} custom-call(f32[1,128,128]{2,1,0:T(8,128)S(1)} %get-tuple-element.142), custom_call_target="InvertDiagBlocksLowerTriangular" | custom-call | tf_op jit(solution)/shard_map/jit(cholesky)/cholesky | solution.py:151
  363.7 11.7 %cholesky.343 = f32[128,128]{1,0:T(8,128)S(1)} custom-call(f32[128,128]{1,0:T(8,128)S(1)} %convolution_subtract_fusion.11), custom_call_target="Cholesky" | custom-call | tf_op jit(solution)/shard_map/jit(cholesky)/cholesky | solution.py:151
  380.2 2.8 fusion.37
  383.0 11.2 %while.10 = (s32[]{:T(128)}, f32[512,512]{1,0:T(8,128)}, s32[4,2]{0,1:T(2,128)S(1)}, f32[4,128,128]{2,1,0:T(8,128)S(1)}, s32[]{:T(128)}) while((s32[]{:T(128)}, f32[512,512]{1,0:T(8,128)}, s32[4,2]{0,1:T(2,128)S(1)}, f32[4,128,128]{2,1,0:T(8,128)S(1)}, s32[]{:T(128)}) %tuple.87), condition=%wide.while_cond.6, body=%wide.while_body.6.sunk | while | flops 2 | bytes 131181 | solution.py:152
  383.8 2.2 bitcast_dynamic-update-slice_fusion.4
  386.6 2.2 bitcast_dynamic-update-slice_fusion.4
  389.4 2.2 bitcast_dynamic-update-slice_fusion.4
  392.1 2.1 bitcast_dynamic-update-slice_fusion.4
  394.3 39.9 %custom-call.30 = f32[4,128,128]{1,2,0:T(8,128)} custom-call(f32[4,128,128]{2,1,0:T(8,128)S(1)} %get-tuple-element.101), custom_call_target="InvertDiagBlocksLowerTriangular" | custom-call | tf_op jit(solution)/shard_map/triangular_solve/custom-call.3 | solution.py:152
  435.5 1.9 convolution_subtract_fusion.3
  438.3 4.0 collective-permute-start
  443.7 3.8 scatter.14
  447.6 2.0 convolution_subtract_fusion.2
  449.6 9.1 %collective-permute-done = bf16[128,1024]{1,0:T(8,128)(2,1)} collective-permute-done((bf16[128,1024]{1,0:T(8,128)(2,1)S(1)}, bf16[128,1024]{1,0:T(8,128)(2,1)}, u32[]{:S(2)}, u32[]{:S(2)}) %collective-permute-start) | collective-permute-done | bytes 262176 | tf_op jit(solution)/shard_map/ppermute | solution.py:134
  460.3 1.8 convolution_subtract_fusion.5
  463.3 2.8 constant_dynamic-update-slice_fusion.2
  466.2 2.5 broadcast_select_fusion
  468.6 1.6 copy.46
  473.1 11.7 %cholesky.358 = f32[128,128]{1,0:T(8,128)S(1)} custom-call(f32[128,128]{1,0:T(8,128)S(1)} %cholesky.439), custom_call_target="Cholesky" | custom-call | tf_op jit(solution)/shard_map/jit(cholesky)/cholesky | solution.py:151
  485.0 9.8 %custom-call.31 = f32[1,128,128]{1,2,0:T(8,128)S(1)} custom-call(f32[1,128,128]{2,1,0:T(8,128)S(1)} %get-tuple-element.138), custom_call_target="InvertDiagBlocksLowerTriangular" | custom-call | tf_op jit(solution)/shard_map/jit(cholesky)/cholesky | solution.py:151
  497.3 12.1 %cholesky.377 = f32[128,128]{1,0:T(8,128)S(1)} custom-call(f32[128,128]{1,0:T(8,128)S(1)} %cholesky.443), custom_call_target="Cholesky" | custom-call | tf_op jit(solution)/shard_map/jit(cholesky)/cholesky | solution.py:151
  509.5 9.8 %custom-call.32 = f32[1,128,128]{1,2,0:T(8,128)S(1)} custom-call(f32[1,128,128]{2,1,0:T(8,128)S(1)} %get-tuple-element.135), custom_call_target="InvertDiagBlocksLowerTriangular" | custom-call | tf_op jit(solution)/shard_map/jit(cholesky)/cholesky | solution.py:151
  520.9 11.7 %cholesky.398 = f32[128,128]{1,0:T(8,128)S(1)} custom-call(f32[128,128]{1,0:T(8,128)S(1)} %cholesky.448), custom_call_target="Cholesky" | custom-call | tf_op jit(solution)/shard_map/jit(cholesky)/cholesky | solution.py:151
  532.6 9.9 %custom-call.33 = f32[1,128,128]{1,2,0:T(8,128)S(1)} custom-call(f32[1,128,128]{2,1,0:T(8,128)S(1)} %get-tuple-element.132), custom_call_target="InvertDiagBlocksLowerTriangular" | custom-call | tf_op jit(solution)/shard_map/jit(cholesky)/cholesky | solution.py:151
  544.0 11.7 %cholesky.415 = f32[128,128]{1,0:T(8,128)S(1)} custom-call(f32[128,128]{1,0:T(8,128)S(1)} %convolution_subtract_fusion.10), custom_call_target="Cholesky" | custom-call | tf_op jit(solution)/shard_map/jit(cholesky)/cholesky | solution.py:151
  562.3 8.1 %while.11 = (s32[]{:T(128)}, f32[512,512]{1,0:T(8,128)S(1)}, s32[4,2]{0,1:T(2,128)S(1)}, f32[4,128,128]{2,1,0:T(8,128)S(1)}, s32[]{:T(128)}) while((s32[]{:T(128)}, f32[512,512]{1,0:T(8,128)S(1)}, s32[4,2]{0,1:T(2,128)S(1)}, f32[4,128,128]{2,1,0:T(8,128)S(1)}, s32[]{:T(128)}) %tuple.101), condition=%wide.while_cond.6.clone, body=%wide.while_body.6.clone.sunk | while | flops 2 | bytes 131181 | solution.py:152
  570.4 39.9 %custom-call.34 = f32[4,128,128]{1,2,0:T(8,128)} custom-call(f32[4,128,128]{2,1,0:T(8,128)S(1)} %get-tuple-element.102), custom_call_target="InvertDiagBlocksLowerTriangular" | custom-call | tf_op jit(solution)/shard_map/triangular_solve/custom-call.3 | solution.py:152
  610.3 8.7 %gather_fusion.2 = f32[1024,1024]{1,0:T(8,128)} fusion(f32[1024,1024]{1,0:T(8,128)} %get-tuple-element.125, s32[1024]{0:T(1024)S(1)} %broadcast_clamp_fusion), kind=kCustom, calls=%fused_computation.2 | custom fusion | bytes 8392704 | tf_op jit(solution)/shard_map/jit(_take)/gather | solution.py:174
  625.4 1.7 convolution_subtract_fusion.4
  627.1 2.0 fusion.85
  629.1 2.8 copy.41
  631.9 4.7 fusion.13
  636.7 2.6 copy-done.2
  639.3 12.7 %fusion.152 = f32[3072,512]{1,0:T(8,128)} fusion(f32[3072,512]{0,1:T(8,128)S(1)} %fusion.13, f32[512,512]{1,0:T(8,128)S(1)} %get-tuple-element.156), kind=kOutput, calls=%fused_computation.279 | convolution fusion | flops 4831838208 | bytes 13631488 | tf_op jit(solution)/shard_map/dot_general | solution.py:167
  652.0 6.8 copy.48
  658.8 11.2 %fusion.3 = f32[3072,512]{1,0:T(8,128)} fusion(f32[3072,512]{1,0:T(8,128)} %fusion.152, bf16[2048,1024]{1,0:T(8,128)(2,1)} %bitcast.163, bf16[1024,1024]{1,0:T(8,128)(2,1)S(1)} %copy-done.12, f32[128,512]{1,0:T(8,128)S(1)} %copy-done.20, f32[128,512]{1,0:T(8,128)S(1)} %copy-done.16, f32[128,512]{1,0:T(8,128)S(1)} %fusion.88, f32[128,512]{1,0:T(8,128)S(1)} %fusion.64), kind=kOutput, calls=%fused_computation.18 | convolution fusion | flops 4842061824 | bytes 19922944 | tf_op jit(solution)/shard_map/dot_general | solution.py:154
  670.0 26.4 %fusion = f32[1024,2048]{1,0:T(8,128)} fusion(f32[128,8,16,128]{3,2,1,0:T(8,128)} %bitcast.161, f32[3072,512]{1,0:T(8,128)} %fusion.3, f32[3072,512]{1,0:T(8,128)} %copy.48, f32[1,1024,1,2048]{3,2,1,0:T(1,128)} %param.20), kind=kOutput, calls=%fused_computation.8 | convolution fusion | flops 12892241920 | bytes 37748736 | tf_op jit(solution)/shard_map/dot_general | solution.py:36
  696.4 3.3 fusion.54
  699.6 4.2 select_bitcast_fusion
  703.8 12.5 %copy.50 = f32[1,1024,1,2048]{3,2,1,0:T(1,128)} copy(f32[1,1024,1,2048]{3,1,2,0:T(8,128)S(1)} %select_bitcast_fusion) | data formatting | bytes 16777216 | tf_op jit(solution)/shard_map/broadcast_in_dim | solution.py:180
  (163 shorter events, 61.9 us)
Async XLA Ops:
  6.5 16.5 %copy-start = (bf16[64,128,128]{2,1,0:T(8,128)(2,1)S(1)}, bf16[64,128,128]{2,1,0:T(8,128)(2,1)}, u32[]{:S(2)}) copy-start(bf16[64,128,128]{2,1,0:T(8,128)(2,1)} %param.21) | copy-start | bytes 6291460
  11.4 32.8 %all-to-all-start = ((s32[128,1,2]{2,1,0:T(1,128)}), s32[128,1,2]{2,1,0:T(1,128)S(1)}, u32[]{:S(2)}, u32[]{:S(2)}) async-start(s32[128,1,2]{2,1,0:T(1,128)} %bitcast.4), calls=%async_computation | async-start | bytes 131072 | tf_op jit(solution)/shard_map/all_to_all | solution.py:80
  44.3 109.9 %all-to-all-start.1 = ((bf16[128,2,128,128]{3,2,1,0:T(8,128)(2,1)}), bf16[128,2,128,128]{3,2,1,0:T(8,128)(2,1)}, u32[]{:S(2)}, u32[]{:S(2)}) async-start(bf16[128,2,128,128]{3,2,1,0:T(8,128)(2,1)} %select_select_fusion), calls=%async_computation.1 | async-start | bytes 16777216 | tf_op jit(solution)/shard_map/all_to_all | solution.py:73
  54.5 171.6 %all-gather.6.cloned.1.call-start = ((), (), s32[]{:S(2)}) async-start(), calls=%async_computation.2 | async-start | bytes 2228224 | tf_op jit(solution)/shard_map/all_gather | solution.py:118
  163.2 90.5 %copy-start.17 = (bf16[1024,128]{1,0:T(8,128)(2,1)}, bf16[1024,128]{1,0:T(8,128)(2,1)S(1)}, u32[]{:S(2)}) copy-start(bf16[1024,128]{1,0:T(8,128)(2,1)S(1)} %slice_add_fusion) | copy-start | bytes 786436
  177.7 97.5 %all-gather.8.cloned.1.call-start = ((), (), s32[]{:S(2)}) async-start(), calls=%async_computation.3 | async-start | bytes 2228224 | tf_op jit(solution)/shard_map/all_gather | solution.py:120
  227.4 210.0 %all-gather.10.cloned.1.call-start = ((), (), s32[]{:S(2)}) async-start(), calls=%async_computation.4 | async-start | bytes 2359296 | tf_op jit(solution)/shard_map/all_gather | solution.py:123
  229.9 230.3 %copy-start.4 = (f32[512,512]{1,0:T(8,128)}, f32[512,512]{1,0:T(8,128)S(1)}, u32[]{:S(2)}) copy-start(f32[512,512]{1,0:T(8,128)S(1)} %fusion.38) | copy-start | bytes 3145732
  287.4 1.0 copy-start.9
  336.8 292.3 %all-gather.12.cloned.1.call-start = ((), (), s32[]{:S(2)}) async-start(), calls=%async_computation.5 | async-start | bytes 4456448 | tf_op jit(solution)/shard_map/all_gather | solution.py:135
  438.3 20.4 %collective-permute-start = (bf16[128,1024]{1,0:T(8,128)(2,1)S(1)}, bf16[128,1024]{1,0:T(8,128)(2,1)}, u32[]{:S(2)}, u32[]{:S(2)}) collective-permute-start(bf16[128,1024]{1,0:T(8,128)(2,1)S(1)} %constant_dynamic-slice_fusion.2), channel_id=1, source_target_pairs={{0,0},{1,8},{2,16},{3,24},{4,32},{5,40},{6,48},{7,56},{8,1},{9,9},... | collective-permute-start | bytes 786440 | tf_op jit(solution)/shard_map/ppermute | solution.py:134
  443.7 3.9 copy-start.6
  458.8 7.4 %copy-start.19 = (pred[512,512]{1,0:T(32,128)(4,1)S(1)}, pred[512,512]{1,0:T(32,128)(4,1)}, u32[]{:S(2)}) copy-start(pred[512,512]{1,0:T(32,128)(4,1)} %copy.45) | copy-start | bytes 786436
  460.3 8.3 %copy-start.13 = (f32[128,512]{1,0:T(8,128)}, f32[128,512]{1,0:T(8,128)S(1)}, u32[]{:S(2)}) copy-start(f32[128,512]{1,0:T(8,128)S(1)} %fusion.92) | copy-start | bytes 786436
  463.3 5.3 copy-start.18
  472.1 1.0 copy-start.10
  570.4 39.9 %copy-start.8 = (f32[512,512]{1,0:T(8,128)}, f32[512,512]{1,0:T(8,128)S(1)}, u32[]{:S(2)}) copy-start(f32[512,512]{1,0:T(8,128)S(1)} %get-tuple-element.261) | copy-start | bytes 3145732
  610.3 8.7 %copy-start.5 = (f32[512,512]{1,0:T(8,128)S(1)}, f32[512,512]{1,0:T(8,128)}, u32[]{:S(2)}) copy-start(f32[512,512]{1,0:T(8,128)} %copy-done.4) | copy-start | bytes 3145732
  621.5 10.4 %copy-start.7 = (f32[128,512]{1,0:T(8,128)S(1)}, f32[128,512]{1,0:T(8,128)}, u32[]{:S(2)}) copy-start(f32[128,512]{1,0:T(8,128)} %copy-done.6) | copy-start | bytes 786436
  621.5 10.4 %copy-start.14 = (f32[128,512]{1,0:T(8,128)S(1)}, f32[128,512]{1,0:T(8,128)}, u32[]{:S(2)}) copy-start(f32[128,512]{1,0:T(8,128)} %copy-done.13) | copy-start | bytes 786436
  625.4 1.7 copy-start.15
  629.1 2.9 copy-start.11
  631.9 4.8 copy-start.3
  636.7 2.6 copy-start.2
  652.0 6.8 copy-start.12
  652.0 6.8 copy-start.16
  652.0 6.8 copy-start.20
  699.6 16.7 %copy-start.1 = (bf16[64,128,128]{2,1,0:T(8,128)(2,1)S(1)}, bf16[64,128,128]{2,1,0:T(8,128)(2,1)}, u32[]{:S(2)}) copy-start(bf16[64,128,128]{2,1,0:T(8,128)(2,1)} %param.21) | copy-start | bytes 6291460
Sparse Core Ops, SparseCore 0:
  177.8 48.1 all-gather.5
  228.2 44.5 all-gather.7
  336.9 26.5 all-gather.9
  458.9 50.0 all-gather.11

commit v7 on v6

--- a/solution.py
+++ b/solution.py
@@ -140,33 +140,51 @@
     )
     rows_all = jnp.concatenate([row_panel, col_panel], axis=0).astype(jnp.float32)
     n_own = local.shape[0]
+    full = lax.Precision.HIGHEST
+    corner_blocks = total // width
     factor_full = jnp.zeros((total, total), jnp.float32)
-    pieces = []
-    eye = jnp.eye(PW, dtype=jnp.float32)
-    for panel_idx in range(NPANEL):
-        start = panel_idx * PW
-        stop = start + PW
+    eye = jnp.eye(width, dtype=jnp.float32)
+    inverses = []
+    for blk in range(corner_blocks):
+        start = blk * width
+        stop = start + width
         diag_block = corner[start:stop, start:stop]
         symmetric = jnp.tril(diag_block) + jnp.tril(diag_block, -1).T
         factor = jnp.linalg.cholesky(symmetric)
         inverse = lax.linalg.triangular_solve(factor, eye, left_side=True, lower=True)
+        inverses.append(inverse)
         factor_full = factor_full.at[start:stop, start:stop].set(factor)
-        solved_rows = jnp.dot(
-            rows_all[:, start:stop], inverse.T, precision=hi, preferred_element_type=jnp.float32
-        )
-        pieces.append(solved_rows)
         if stop < total:
             below = jnp.dot(
-                corner[stop:, start:stop], inverse.T, precision=hi, preferred_element_type=jnp.float32
+                corner[stop:, start:stop], inverse.T, precision=full, preferred_element_type=jnp.float32
             )
             factor_full = factor_full.at[stop:, start:stop].set(below)
             corner = corner.at[stop:, stop:].add(
-                -jnp.dot(below, below.T, precision=hi, preferred_element_type=jnp.float32)
+                -jnp.dot(below, below.T, precision=full, preferred_element_type=jnp.float32)
             )
-            rows_all = rows_all.at[:, stop:].add(
-                -jnp.dot(solved_rows, below.T, precision=hi, preferred_element_type=jnp.float32)
-            )
-    solved = jnp.concatenate(pieces, axis=1)
+    inv_blocks = jnp.stack(inverses)
+    size = width
+    while size < total:
+        pairs_n = total // (2 * size)
+        grid = factor_full.reshape(pairs_n, 2 * size, pairs_n, 2 * size)
+        idx = jnp.arange(pairs_n)
+        diag_pairs = grid[idx, :, idx, :]
+        lower_left = diag_pairs[:, size:, :size]
+        upper_inv = inv_blocks[0::2]
+        lower_inv = inv_blocks[1::2]
+        mixed = -jnp.einsum(
+            "nab,nbc->nac",
+            lower_inv,
+            jnp.einsum("nab,nbc->nac", lower_left, upper_inv, precision=full),
+            precision=full,
+        )
+        zeros = jnp.zeros_like(mixed)
+        top = jnp.concatenate([upper_inv, zeros], axis=2)
+        bottom = jnp.concatenate([mixed, lower_inv], axis=2)
+        inv_blocks = jnp.concatenate([top, bottom], axis=1)
+        size *= 2
+    factor_inverse = inv_blocks[0]
+    solved = jnp.dot(rows_all, factor_inverse.T, precision=hi, preferred_element_type=jnp.float32)
     row_factor = solved[:n_own]
     col_factor = solved[n_own:]
     matrix = subtract_product(matrix, row_factor, col_factor)

time: 731 us -> 691 us (0.945)
  other arithmetic: 272 us -> 212 us
  local copies, waits for them, and re-layouts: 133 us -> 181 us
  matrix products: 116 us -> 102 us
  waiting for transfers between devices: 145 us -> 133 us
    another operation x29 -> x24, other arithmetic: 160 us -> 100 us  [shards(): factor = jnp.linalg.cholesky(symmetric)]
    reshape x0 -> x5, local copies, waits for them, and re-layouts: none -> 29.2 us  [the longest x4 20 us: shards(): grid = factor_full.reshape(pairs_n, 2 * size, pairs_n, 2 * size)]
    unnamed x44 -> x28, local copies, waits for them, and re-layouts: 38.9 us -> 66.1 us
    dot_general x5 -> x21, matrix products: 33.9 us -> 56.5 us  [the longest x1 23.1 us: shards(): jnp.dot(rows_all, factor_inverse.T, precision=hi, preferred_element_type=...]
    another operation x35 -> x2, local copies, waits for them, and re-layouts: 20.3 us -> 1.51 us  [the longest x27 19 us: shards(): lax.linalg.triangular_solve(factor, eye, left_side=True, lower=True)]
    another operation x14 -> x8, matrix products: 21.1 us -> 2.9 us  [shards(): lax.linalg.triangular_solve(factor, eye, left_side=True, lower=True)]
    another operation x12 -> x0, matrix products: 13.3 us -> none  [shards(): factor = jnp.linalg.cholesky(symmetric)]
    all_to_all x1, waiting for transfers between devices: 87.1 us -> 77.4 us  [shards(): lax.all_to_all(send_tiles.reshape(owners, CAP, width, width), ('frow', 'f...]
  transfers between devices with their start and end apart: 7 -> 7, of which waited for: 3 -> 3; matrix products, arithmetic and copies ran while one was open for 49% -> 55% of each run, Pallas kernels for 0% -> 0%
where the time goes in v7:
time: 691 us; the launch traced here: 683 us
  other arithmetic  212 us (31%)
  local copies, waits for them, and re-layouts  181 us (26%)
  waiting for transfers between devices  133 us (19%)
  matrix products  102 us (15%)
  starting transfers between devices  25.2 us (4%)
  blocking collectives  15.3 us (2%)
  between operations  14.3 us (2%)
    another operation x24, other arithmetic, shards(): factor = jnp.linalg.cholesky(symmetric)  100 us
    another operation x9, other arithmetic, shards(): lax.linalg.triangular_solve(factor, eye, left_side=True, lower=True)  79.5 us
    all_to_all x1, waiting for transfers between devices, shards(): lax.all_to_all(send_tiles.reshape(owners, CAP, width, width), ('frow', 'f...  77.4 us
    unnamed x28, local copies, waits for them, and re-layouts  66.1 us
    all_gather x1, waiting for transfers between devices, shards(): lax.all_gather(first_row[:, :split], 'frow', axis=0, tiled=True)[:total]  50.8 us
    dot_general x1, matrix products, subtract_product(): jnp.dot(row_factor, col_factor.T, precision=lax.Precision.HIGH, preferred...  25 us
    dot_general x1, matrix products, shards(): jnp.dot(rows_all, factor_inverse.T, precision=hi, preferred_element_type=...  23.1 us
    broadcast_in_dim x1, local copies, waits for them, and re-layouts, shards(): return result[None, :, None, :]  20.6 us
  transfers between devices with their start and end apart: 7, of which 3 were waited for; matrix products, arithmetic and copies ran while one was open for 55% of the time, Pallas kernels for 0%

profile of v7, /device:TPU:6, one launch (start us, length us, event | category | flops | bytes accessed | tf_op | source)
XLA Modules:
  0.0 682.8 jit_solution(2270206713225068291)
XLA Ops:
  8.8 1.9 gather_fusion
  11.5 10.5 %all-to-all-start = ((s32[128,1,2]{2,1,0:T(1,128)}), s32[128,1,2]{2,1,0:T(1,128)S(1)}, u32[]{:S(2)}, u32[]{:S(2)}) async-start(s32[128,1,2]{2,1,0:T(1,128)} %bitcast.5), calls=%async_computation | async-start | bytes 131072 | tf_op jit(solution)/shard_map/all_to_all | solution.py:80
  23.1 3.6 fusion.22
  26.7 10.1 %gather_fusion.1 = bf16[256,128,128]{2,1,0:T(8,128)(2,1)} fusion(bf16[64,128,128]{2,1,0:T(8,128)(2,1)} %fusion.22, s32[1024]{0:T(1024)S(1)} %get-tuple-element.349), kind=kCustom, calls=%fused_computation.1 | custom fusion | bytes 16778240 | tf_op jit(solution)/shard_map/jit(_take)/gather | solution.py:69
  36.8 7.4 %select_select_fusion = bf16[128,2,128,128]{3,2,1,0:T(8,128)(2,1)} fusion(bf16[128,2,128,128]{3,2,1,0:T(8,128)(2,1)} %bitcast.218, pred[128,2]{1,0:T(8,128)(4,1)S(1)} %compare_and_fusion, pred[128,2]{1,0:T(8,128)(4,1)S(1)} %broadcast_in_dim.129), kind=kLoop, calls=%fused_computation.11 | loop fusion | flops 8388608 | bytes 16777728 | tf_op jit(solution)/shard_map/jit(_where)/select_n | solution.py:67
  44.3 10.2 %all-to-all-start.1 = ((bf16[128,2,128,128]{3,2,1,0:T(8,128)(2,1)}), bf16[128,2,128,128]{3,2,1,0:T(8,128)(2,1)}, u32[]{:S(2)}, u32[]{:S(2)}) async-start(bf16[128,2,128,128]{3,2,1,0:T(8,128)(2,1)} %select_select_fusion), calls=%async_computation.1 | async-start | bytes 16777216 | tf_op jit(solution)/shard_map/all_to_all | solution.py:73
  54.7 20.7 %copy.161 = f32[1,1024,1,2048]{1,3,2,0:T(8,128)} copy(f32[1,1024,1,2048]{3,2,1,0:T(1,128)} %param.54) | data formatting | bytes 16777216 | tf_op args[0]
  76.8 77.4 %all-to-all-done.1 = bf16[128,2,128,128]{3,2,1,0:T(8,128)(2,1)} async-done(((bf16[128,2,128,128]{3,2,1,0:T(8,128)(2,1)}), bf16[128,2,128,128]{3,2,1,0:T(8,128)(2,1)}, u32[]{:S(2)}, u32[]{:S(2)}) %all-to-all-start.1) | async-done | bytes 8388640 | tf_op jit(solution)/shard_map/all_to_all | solution.py:73
  154.2 7.8 %fusion.114 = f32[8,16384]{1,0:T(8,128)S(1)} fusion(s32[256]{0:T(256)S(1)} %eq.128, s32[8]{0:T(128)S(1)} %iota_multiply_fusion, bf16[32,8,128,128]{3,2,1,0:T(8,128)(2,1)} %bitcast.75), kind=kOutput, calls=%fused_computation.219 | convolution fusion | flops 67110912 | bytes 8913952 | tf_op jit(solution)/shard_map/dot_general | solution.py:103
  163.5 15.3 %all_gather.18 = bf16[128,1024]{0,1:T(8,128)(2,1)S(1)} all-gather(bf16[128,128]{0,1:T(8,128)(2,1)S(1)} %slice.793), channel_id=1, replica_groups=mesh['frow'=16,'fcol'=8] {'fcol'}, dimensions={1}, use_global_device_ids=true | all-gather | bytes 294912 | tf_op jit(solution)/shard_map/all_gather | solution.py:114
  179.6 50.8 %all-gather.6.cloned.1.call-done = bf16[2048,512]{0,1:T(8,128)(2,1)} async-done(((bf16[128,512]{0,1:T(8,128)(2,1)}), bf16[2048,512]{0,1:T(8,128)(2,1)}) %all-gather.6.cloned.1.call-update) | async-done | bytes 2097168 | tf_op jit(solution)/shard_map/all_gather | solution.py:118
  233.0 23.6 %copy.249 = bf16[32,8,128,128]{3,1,2,0:T(8,128)(2,1)} copy(bf16[32,8,128,128]{3,2,1,0:T(8,128)(2,1)} %bitcast.75) | data formatting | bytes 16777216
  256.6 11.9 %copy.163 = bf16[256,16384]{0,1:T(8,128)(2,1)} copy(bf16[256,16384]{1,0:T(8,128)(2,1)} %bitcast.219) | data formatting | bytes 16777216 | tf_op jit(solution)/shard_map/reshape | solution.py:93
  268.6 6.4 fusion.66
  275.0 7.5 %copy.248 = f32[128,8,16,128]{3,1,2,0:T(8,128)} copy(f32[128,8,16,128]{3,2,1,0:T(8,128)S(1)} %bitcast.224) | data formatting | bytes 16777216
  282.5 9.2 %copy.226 = f32[1024,2048]{0,1:T(8,128)} copy(f32[1024,2048]{1,0:T(8,128)} %bitcast.220) | data formatting | bytes 16777216 | tf_op jit(solution)/shard_map/reshape | solution.py:98
  293.6 11.7 %cholesky.134 = f32[128,128]{1,0:T(8,128)S(1)} custom-call(f32[128,128]{1,0:T(8,128)S(1)} %copy.173), custom_call_target="Cholesky" | custom-call | tf_op jit(solution)/shard_map/jit(cholesky)/cholesky | solution.py:153
  306.7 9.8 %custom-call.16 = f32[1,128,128]{1,2,0:T(8,128)S(1)} custom-call(f32[1,128,128]{2,1,0:T(8,128)S(1)} %get-tuple-element.291), custom_call_target="InvertDiagBlocksLowerTriangular" | custom-call | tf_op jit(solution)/shard_map/triangular_solve/custom-call.0 | solution.py:154
  316.8 2.5 scatter.54
  320.5 3.0 negate_add_fusion
  323.5 1.7 copy-done.3
  326.3 11.9 %cholesky.145 = f32[128,128]{1,0:T(8,128)S(1)} custom-call(f32[128,128]{1,0:T(8,128)S(1)} %copy.180), custom_call_target="Cholesky" | custom-call | tf_op jit(solution)/shard_map/jit(cholesky)/cholesky | solution.py:153
  340.1 9.8 %custom-call.17 = f32[1,128,128]{1,2,0:T(8,128)S(1)} custom-call(f32[1,128,128]{2,1,0:T(8,128)S(1)} %get-tuple-element.314), custom_call_target="InvertDiagBlocksLowerTriangular" | custom-call | tf_op jit(solution)/shard_map/triangular_solve/custom-call.0 | solution.py:154
  350.2 2.5 constant_dynamic-update-slice_fusion.6
  352.8 3.7 slice_add_fusion
  356.5 1.4 copy-done.4
  359.1 11.7 %cholesky.156 = f32[128,128]{1,0:T(8,128)S(1)} custom-call(f32[128,128]{1,0:T(8,128)S(1)} %copy.187), custom_call_target="Cholesky" | custom-call | tf_op jit(solution)/shard_map/jit(cholesky)/cholesky | solution.py:153
  372.7 10.2 %custom-call.18 = f32[1,128,128]{1,2,0:T(8,128)S(1)} custom-call(f32[1,128,128]{2,1,0:T(8,128)S(1)} %get-tuple-element.312), custom_call_target="InvertDiagBlocksLowerTriangular" | custom-call | tf_op jit(solution)/shard_map/triangular_solve/custom-call.0 | solution.py:154
  383.2 2.6 constant_dynamic-update-slice_fusion.5
  385.8 2.9 slice_add_fusion.1
  389.2 11.7 %cholesky.167 = f32[128,128]{1,0:T(8,128)S(1)} custom-call(f32[128,128]{1,0:T(8,128)S(1)} %fusion.80), custom_call_target="Cholesky" | custom-call | tf_op jit(solution)/shard_map/jit(cholesky)/cholesky | solution.py:153
  402.8 9.8 %custom-call.19 = f32[1,128,128]{1,2,0:T(8,128)S(1)} custom-call(f32[1,128,128]{2,1,0:T(8,128)S(1)} %get-tuple-element.310), custom_call_target="InvertDiagBlocksLowerTriangular" | custom-call | tf_op jit(solution)/shard_map/triangular_solve/custom-call.0 | solution.py:154
  412.6 1.4 copy.192
  416.2 2.2 fusion.26
  418.8 11.9 %cholesky.178 = f32[128,128]{1,0:T(8,128)S(1)} custom-call(f32[128,128]{1,0:T(8,128)S(1)} %fusion.78), custom_call_target="Cholesky" | custom-call | tf_op jit(solution)/shard_map/jit(cholesky)/cholesky | solution.py:153
  431.7 4.0 collective-permute-start
  437.5 9.8 %custom-call.20 = f32[1,128,128]{1,2,0:T(8,128)S(1)} custom-call(f32[1,128,128]{2,1,0:T(8,128)S(1)} %get-tuple-element.308), custom_call_target="InvertDiagBlocksLowerTriangular" | custom-call | tf_op jit(solution)/shard_map/triangular_solve/custom-call.0 | solution.py:154
  447.3 4.3 collective-permute-done
  454.6 11.7 %cholesky.189 = f32[128,128]{1,0:T(8,128)S(1)} custom-call(f32[128,128]{1,0:T(8,128)S(1)} %fusion.76), custom_call_target="Cholesky" | custom-call | tf_op jit(solution)/shard_map/jit(cholesky)/cholesky | solution.py:153
  468.4 9.8 %custom-call.21 = f32[1,128,128]{1,2,0:T(8,128)S(1)} custom-call(f32[1,128,128]{2,1,0:T(8,128)S(1)} %get-tuple-element.306), custom_call_target="InvertDiagBlocksLowerTriangular" | custom-call | tf_op jit(solution)/shard_map/triangular_solve/custom-call.0 | solution.py:154
  480.1 12.1 %cholesky.200 = f32[128,128]{1,0:T(8,128)S(1)} custom-call(f32[128,128]{1,0:T(8,128)S(1)} %fusion.74), custom_call_target="Cholesky" | custom-call | tf_op jit(solution)/shard_map/jit(cholesky)/cholesky | solution.py:153
  494.3 9.8 %custom-call.22 = f32[1,128,128]{1,2,0:T(8,128)S(1)} custom-call(f32[1,128,128]{2,1,0:T(8,128)S(1)} %get-tuple-element.304), custom_call_target="InvertDiagBlocksLowerTriangular" | custom-call | tf_op jit(solution)/shard_map/triangular_solve/custom-call.0 | solution.py:154
  505.9 11.7 %cholesky.211 = f32[128,128]{1,0:T(8,128)S(1)} custom-call(f32[128,128]{1,0:T(8,128)S(1)} %fusion.72), custom_call_target="Cholesky" | custom-call | tf_op jit(solution)/shard_map/jit(cholesky)/cholesky | solution.py:153
  519.6 6.6 reshape.950
  526.2 5.6 reshape.949
  531.8 9.8 %custom-call.23 = f32[1,128,128]{1,2,0:T(8,128)S(1)} custom-call(f32[1,128,128]{2,1,0:T(8,128)S(1)} %get-tuple-element.302), custom_call_target="InvertDiagBlocksLowerTriangular" | custom-call | tf_op jit(solution)/shard_map/triangular_solve/custom-call.0 | solution.py:154
  541.6 8.8 %gather_fusion.4 = f32[1024,1024]{1,0:T(8,128)} fusion(f32[1024,1024]{1,0:T(8,128)} %get-tuple-element.301, s32[1024]{0:T(1024)S(1)} %get-tuple-element.350), kind=kCustom, calls=%fused_computation.4 | custom fusion | bytes 8392704 | tf_op jit(solution)/shard_map/jit(_take)/gather | solution.py:192
  551.7 5.1 copy.208
  556.8 2.7 copy.205
  559.5 4.3 gather_fusion.3
  563.8 2.8 gather_fusion.2
  568.3 2.1 fusion.35
  571.4 3.1 fusion.31
  574.5 2.8 fusion.25
  577.3 1.5 fusion.142
  578.8 2.9 copy.167
  581.7 5.6 copy.244
  587.3 6.7 copy.166
  594.0 23.1 %fusion.2 = f32[3072,1024]{1,0:T(8,128)S(1)} fusion(bf16[2048,1024]{1,0:T(8,128)(2,1)} %bitcast.226, bf16[1024,1024]{1,0:T(8,128)(2,1)S(1)} %copy.167, f32[1,512,512]{2,1,0:T(8,128)} %get-tuple-element.294, f32[1,512,512]{2,1,0:T(8,128)} %get-tuple-element.293, f32[1,512,512]{2,1,0:T(8,128)} %fusion.25), kind=kOutput, calls=%fused_computation.12 | convolution fusion | flops 19344130048 | bytes 22020096 | tf_op jit(solution)/shard_map/dot_general | solution.py:187
  617.1 4.6 copy-done.5
  621.7 25.0 %add_subtract_fusion = f32[1024,2048]{0,1:T(8,128)} fusion(f32[1024,2048]{0,1:T(8,128)} %copy.226, f32[3072,1024]{1,0:T(8,128)} %copy-done.5, f32[1,1024,1,2048]{1,3,2,0:T(8,128)} %copy.161), kind=kOutput, calls=%fused_computation.10 | convolution fusion | flops 12889096192 | bytes 37748736 | tf_op jit(solution)/shard_map/dot_general | solution.py:36
  647.0 2.6 fusion.34
  649.6 5.8 select_bitcast_fusion
  655.4 20.6 %copy.215 = f32[1,1024,1,2048]{3,2,1,0:T(1,128)} copy(f32[1,1024,1,2048]{1,3,2,0:T(8,128)} %select_bitcast_fusion) | data formatting | bytes 16777216 | tf_op jit(solution)/shard_map/broadcast_in_dim | solution.py:198
  (166 shorter events, 46.4 us)
Async XLA Ops:
  6.5 16.5 %copy-start = (bf16[64,128,128]{2,1,0:T(8,128)(2,1)S(1)}, bf16[64,128,128]{2,1,0:T(8,128)(2,1)}, u32[]{:S(2)}) copy-start(bf16[64,128,128]{2,1,0:T(8,128)(2,1)} %param.55) | copy-start | bytes 6291460
  11.5 32.8 %all-to-all-start = ((s32[128,1,2]{2,1,0:T(1,128)}), s32[128,1,2]{2,1,0:T(1,128)S(1)}, u32[]{:S(2)}, u32[]{:S(2)}) async-start(s32[128,1,2]{2,1,0:T(1,128)} %bitcast.5), calls=%async_computation | async-start | bytes 131072 | tf_op jit(solution)/shard_map/all_to_all | solution.py:80
  44.3 109.9 %all-to-all-start.1 = ((bf16[128,2,128,128]{3,2,1,0:T(8,128)(2,1)}), bf16[128,2,128,128]{3,2,1,0:T(8,128)(2,1)}, u32[]{:S(2)}, u32[]{:S(2)}) async-start(bf16[128,2,128,128]{3,2,1,0:T(8,128)(2,1)} %select_select_fusion), calls=%async_computation.1 | async-start | bytes 16777216 | tf_op jit(solution)/shard_map/all_to_all | solution.py:73
  54.5 175.8 %all-gather.6.cloned.1.call-start = ((), (), s32[]{:S(2)}) async-start(), calls=%async_computation.2 | async-start | bytes 2228224 | tf_op jit(solution)/shard_map/all_gather | solution.py:118
  163.4 93.2 %copy-start.8 = (bf16[1024,128]{0,1:T(8,128)(2,1)}, bf16[1024,128]{0,1:T(8,128)(2,1)S(1)}, u32[]{:S(2)}) copy-start(bf16[1024,128]{0,1:T(8,128)(2,1)S(1)} %slice_add_fusion.2) | copy-start | bytes 786436
  179.5 112.2 %all-gather.8.cloned.1.call-start = ((), (), s32[]{:S(2)}) async-start(), calls=%async_computation.3 | async-start | bytes 2228224 | tf_op jit(solution)/shard_map/all_gather | solution.py:120
  231.7 199.0 %all-gather.10.cloned.1.call-start = ((), (), s32[]{:S(2)}) async-start(), calls=%async_computation.4 | async-start | bytes 2359296 | tf_op jit(solution)/shard_map/all_gather | solution.py:123
  293.0 288.7 %all-gather.12.cloned.1.call-start = ((), (), s32[]{:S(2)}) async-start(), calls=%async_computation.5 | async-start | bytes 4456448 | tf_op jit(solution)/shard_map/all_gather | solution.py:135
  323.5 1.7 copy-start.3
  356.5 1.4 copy-start.4
  383.2 5.5 copy-start.6
  414.9 37.4 %copy-start.7 = (f32[8,128,128]{2,1,0:T(8,128)S(1)}, f32[8,128,128]{2,1,0:T(8,128)}, u32[]{:S(2)}) copy-start(f32[8,128,128]{2,1,0:T(8,128)} %get-tuple-element.331) | copy-start | bytes 1572868
  431.7 20.0 %collective-permute-start = (bf16[128,1024]{0,1:T(8,128)(2,1)S(1)}, bf16[128,1024]{0,1:T(8,128)(2,1)S(1)}, u32[]{:S(2)}, u32[]{:S(2)}) collective-permute-start(bf16[128,1024]{0,1:T(8,128)(2,1)S(1)} %constant_dynamic-slice_fusion.1), channel_id=1, source_target_pairs={{0,0},{1,8},{2,16},{3,24},{4,32},{5,40},{6,48},{7,56},{8,1},{9,9},... | collective-permute-start | bytes 786440 | tf_op jit(solution)/shard_map/ppermute | solution.py:134
  451.6 0.7 copy-start.9
  551.7 5.1 copy-start.2
  617.1 4.6 copy-start.5
  621.7 25.0 %slice-start = ((f32[3072,1024]{1,0:T(8,128)}), f32[1024,1024]{1,0:T(8,128)S(1)}, s32[]{:S(2)}) async-start(f32[3072,1024]{1,0:T(8,128)} %copy-done.5), calls=%async_computation.6 | async-start | bytes 8388608
  655.4 20.7 %copy-start.1 = (bf16[64,128,128]{2,1,0:T(8,128)(2,1)S(1)}, bf16[64,128,128]{2,1,0:T(8,128)(2,1)}, u32[]{:S(2)}) copy-start(bf16[64,128,128]{2,1,0:T(8,128)(2,1)} %param.55) | copy-start | bytes 6291460
Sparse Core Ops, SparseCore 0:
  179.6 50.6 all-gather.5
  232.5 47.0 all-gather.7
  293.2 23.6 all-gather.9
  452.5 57.3 all-gather.11

commit v8 on v7

--- a/solution.py
+++ b/solution.py
@@ -166,10 +166,12 @@
     size = width
     while size < total:
         pairs_n = total // (2 * size)
-        grid = factor_full.reshape(pairs_n, 2 * size, pairs_n, 2 * size)
-        idx = jnp.arange(pairs_n)
-        diag_pairs = grid[idx, :, idx, :]
-        lower_left = diag_pairs[:, size:, :size]
+        lower_left = jnp.stack(
+            [
+                factor_full[(2 * k + 1) * size : (2 * k + 2) * size, 2 * k * size : (2 * k + 1) * size]
+                for k in range(pairs_n)
+            ]
+        )
         upper_inv = inv_blocks[0::2]
         lower_inv = inv_blocks[1::2]
         mixed = -jnp.einsum(
@@ -188,9 +190,11 @@
     row_factor = solved[:n_own]
     col_factor = solved[n_own:]
     matrix = subtract_product(matrix, row_factor, col_factor)
-    in_corner = (global_rows < total)[:, None]
-    corner_rows = jnp.take(factor_full, jnp.clip(global_rows, 0, total - 1), axis=0)
-    panel_vals = jnp.where(in_corner, corner_rows, row_factor)
+    corner_rows = lax.dynamic_slice_in_dim(
+        factor_full, jnp.minimum(row_here, total // width - 1) * width, width, axis=0
+    )
+    head = jnp.where(row_here * width < total, corner_rows, row_factor[:width])
+    panel_vals = jnp.concatenate([head, row_factor[width:]], axis=0)
     own_part = lax.dynamic_slice_in_dim(panel_vals, col_here * width, width, axis=1)
     matrix = matrix.at[:, :width].set(own_part)
     lower_part = global_rows[:, None] >= global_cols[None, :]

time: 691 us -> 673 us (0.974)
  local copies, waits for them, and re-layouts: 181 us -> 161 us
  matrix products: 102 us -> 89.2 us
  waiting for transfers between devices: 133 us -> 143 us
    reshape x4 -> x0, local copies, waits for them, and re-layouts: 20 us -> none  [shards(): grid = factor_full.reshape(pairs_n, 2 * size, pairs_n, 2 * size)]
    gather x3 -> x0, local copies, waits for them, and re-layouts: 15.8 us -> none  [the longest x1 8.76 us: shards(): jnp.take(factor_full, jnp.clip(global_rows, 0, total - 1), axis=0)]
    ppermute x1, waiting for transfers between devices: 4.3 us -> 14.9 us  [shards(): piece = lax.ppermute(piece, ('frow', 'fcol'), pairs)]
    unnamed x28 -> x34, local copies, waits for them, and re-layouts: 66.1 us -> 69.8 us
    another operation x9 -> x11, other arithmetic: 79.5 us -> 80.6 us  [shards(): lax.linalg.triangular_solve(factor, eye, left_side=True, lower=True)]
  transfers between devices with their start and end apart: 7 -> 7, of which waited for: 3 -> 3; matrix products, arithmetic and copies ran while one was open for 55% -> 43% of each run, Pallas kernels for 0% -> 0%
where the time goes in v8:
time: 673 us; the launch traced here: 664 us
  other arithmetic  216 us (32%)
  local copies, waits for them, and re-layouts  161 us (24%)
  waiting for transfers between devices  143 us (21%)
  matrix products  89.2 us (13%)
  starting transfers between devices  25.7 us (4%)
  blocking collectives  15.3 us (2%)
  between operations  14.8 us (2%)
    another operation x24, other arithmetic, shards(): factor = jnp.linalg.cholesky(symmetric)  100 us
    another operation x11, other arithmetic, shards(): lax.linalg.triangular_solve(factor, eye, left_side=True, lower=True)  80.6 us
    all_to_all x1, waiting for transfers between devices, shards(): lax.all_to_all(send_tiles.reshape(owners, CAP, width, width), ('frow', 'f...  77.4 us
    unnamed x34, local copies, waits for them, and re-layouts  69.8 us
    all_gather x1, waiting for transfers between devices, shards(): lax.all_gather(first_row[:, :split], 'frow', axis=0, tiled=True)[:total]  50.8 us
    dot_general x1, matrix products, subtract_product(): jnp.dot(row_factor, col_factor.T, precision=lax.Precision.HIGH, preferred...  25 us
    broadcast_in_dim x1, local copies, waits for them, and re-layouts, shards(): return result[None, :, None, :]  20.6 us
    dot_general x1, matrix products, shards(): jnp.dot(rows_all, factor_inverse.T, precision=hi, preferred_element_type=...  16.6 us
  transfers between devices with their start and end apart: 7, of which 3 were waited for; matrix products, arithmetic and copies ran while one was open for 43% of the time, Pallas kernels for 0%

profile of v8, /device:TPU:6, one launch (start us, length us, event | category | flops | bytes accessed | tf_op | source)
XLA Modules:
  0.0 664.4 jit_solution(9629916240180808150)
XLA Ops:
  8.8 1.9 gather_fusion
  11.4 10.5 %all-to-all-start = ((s32[128,1,2]{2,1,0:T(1,128)}), s32[128,1,2]{2,1,0:T(1,128)S(1)}, u32[]{:S(2)}, u32[]{:S(2)}) async-start(s32[128,1,2]{2,1,0:T(1,128)} %bitcast.5), calls=%async_computation | async-start | bytes 131072 | tf_op jit(solution)/shard_map/all_to_all | solution.py:80
  23.0 3.6 fusion.25
  26.7 10.1 %gather_fusion.1 = bf16[256,128,128]{2,1,0:T(8,128)(2,1)} fusion(bf16[64,128,128]{2,1,0:T(8,128)(2,1)} %fusion.25, s32[1024]{0:T(1024)S(1)} %pad_clamp_fusion), kind=kCustom, calls=%fused_computation.1 | custom fusion | bytes 16778240 | tf_op jit(solution)/shard_map/jit(_take)/gather | solution.py:69
  36.8 7.4 %select_select_fusion = bf16[128,2,128,128]{3,2,1,0:T(8,128)(2,1)} fusion(bf16[128,2,128,128]{3,2,1,0:T(8,128)(2,1)} %bitcast.221, pred[128,2]{1,0:T(8,128)(4,1)S(1)} %compare_and_fusion, pred[128,2]{1,0:T(8,128)(4,1)S(1)} %broadcast_in_dim.106), kind=kLoop, calls=%fused_computation.8 | loop fusion | flops 8388608 | bytes 16777728 | tf_op jit(solution)/shard_map/jit(_where)/select_n | solution.py:67
  44.3 10.2 %all-to-all-start.1 = ((bf16[128,2,128,128]{3,2,1,0:T(8,128)(2,1)}), bf16[128,2,128,128]{3,2,1,0:T(8,128)(2,1)}, u32[]{:S(2)}, u32[]{:S(2)}) async-start(bf16[128,2,128,128]{3,2,1,0:T(8,128)(2,1)} %select_select_fusion), calls=%async_computation.1 | async-start | bytes 16777216 | tf_op jit(solution)/shard_map/all_to_all | solution.py:73
  54.7 20.7 %copy.246 = f32[1,1024,1,2048]{1,3,2,0:T(8,128)} copy(f32[1,1024,1,2048]{3,2,1,0:T(1,128)} %param.54) | data formatting | bytes 16777216 | tf_op args[0]
  76.8 77.4 %all-to-all-done.1 = bf16[128,2,128,128]{3,2,1,0:T(8,128)(2,1)} async-done(((bf16[128,2,128,128]{3,2,1,0:T(8,128)(2,1)}), bf16[128,2,128,128]{3,2,1,0:T(8,128)(2,1)}, u32[]{:S(2)}, u32[]{:S(2)}) %all-to-all-start.1) | async-done | bytes 8388640 | tf_op jit(solution)/shard_map/all_to_all | solution.py:73
  154.2 7.8 %fusion.132 = f32[8,16384]{1,0:T(8,128)S(1)} fusion(s32[256]{0:T(256)S(1)} %eq.128, s32[8]{0:T(128)S(1)} %iota_multiply_fusion, bf16[32,8,128,128]{3,2,1,0:T(8,128)(2,1)} %bitcast.76), kind=kOutput, calls=%fused_computation.232 | convolution fusion | flops 67110912 | bytes 8913952 | tf_op jit(solution)/shard_map/dot_general | solution.py:103
  163.4 15.3 %all_gather.18 = bf16[128,1024]{0,1:T(8,128)(2,1)S(1)} all-gather(bf16[128,128]{0,1:T(8,128)(2,1)S(1)} %slice.821), channel_id=1, replica_groups=mesh['frow'=16,'fcol'=8] {'fcol'}, dimensions={1}, use_global_device_ids=true | all-gather | bytes 294912 | tf_op jit(solution)/shard_map/all_gather | solution.py:114
  179.6 50.8 %all-gather.6.cloned.1.call-done = bf16[2048,512]{0,1:T(8,128)(2,1)} async-done(((bf16[128,512]{0,1:T(8,128)(2,1)}), bf16[2048,512]{0,1:T(8,128)(2,1)}) %all-gather.6.cloned.1.call-update) | async-done | bytes 2097168 | tf_op jit(solution)/shard_map/all_gather | solution.py:118
  230.3 1.3 slice.720
  234.8 23.3 %copy.364 = bf16[32,8,128,128]{3,1,2,0:T(8,128)(2,1)} copy(bf16[32,8,128,128]{3,2,1,0:T(8,128)(2,1)} %bitcast.76) | data formatting | bytes 16777216
  258.1 11.9 %copy.248 = bf16[256,16384]{0,1:T(8,128)(2,1)} copy(bf16[256,16384]{1,0:T(8,128)(2,1)} %bitcast.222) | data formatting | bytes 16777216 | tf_op jit(solution)/shard_map/reshape | solution.py:93
  270.0 6.2 fusion.80
  276.2 7.5 %copy.363 = f32[128,8,16,128]{3,1,2,0:T(8,128)} copy(f32[128,8,16,128]{3,2,1,0:T(8,128)S(1)} %bitcast.227) | data formatting | bytes 16777216
  283.7 9.4 %copy.342 = f32[1024,2048]{0,1:T(8,128)} copy(f32[1024,2048]{1,0:T(8,128)} %bitcast.223) | data formatting | bytes 16777216 | tf_op jit(solution)/shard_map/reshape | solution.py:98
  293.2 1.3 slice.722
  294.8 11.7 %cholesky.134 = f32[128,128]{1,0:T(8,128)S(1)} custom-call(f32[128,128]{1,0:T(8,128)S(1)} %copy.258), custom_call_target="Cholesky" | custom-call | tf_op jit(solution)/shard_map/jit(cholesky)/cholesky | solution.py:153
  307.4 1.3 select_bitcast_fusion.8
  308.8 9.8 %custom-call.12 = f32[1,128,128]{1,2,0:T(8,128)S(1)} custom-call(f32[1,128,128]{2,1,0:T(8,128)S(1)} %copy.261), custom_call_target="InvertDiagBlocksLowerTriangular" | custom-call | tf_op jit(solution)/shard_map/triangular_solve/custom-call.0 | solution.py:154
  319.5 3.0 negate_add_fusion
  322.5 1.7 copy-done.2
  325.4 12.1 %cholesky.145 = f32[128,128]{1,0:T(8,128)S(1)} custom-call(f32[128,128]{1,0:T(8,128)S(1)} %copy.268), custom_call_target="Cholesky" | custom-call | tf_op jit(solution)/shard_map/jit(cholesky)/cholesky | solution.py:153
  338.3 3.3 scatter.54
  342.5 1.2 fusion.110
  343.8 9.8 %custom-call.13 = f32[1,128,128]{1,2,0:T(8,128)S(1)} custom-call(f32[1,128,128]{2,1,0:T(8,128)S(1)} %copy.271), custom_call_target="InvertDiagBlocksLowerTriangular" | custom-call | tf_op jit(solution)/shard_map/triangular_solve/custom-call.0 | solution.py:154
  353.9 1.8 fusion.45
  355.8 5.1 slice_add_fusion
  363.2 11.7 %cholesky.156 = f32[128,128]{1,0:T(8,128)S(1)} custom-call(f32[128,128]{1,0:T(8,128)S(1)} %copy.278), custom_call_target="Cholesky" | custom-call | tf_op jit(solution)/shard_map/jit(cholesky)/cholesky | solution.py:153
  376.6 1.3 fusion.111
  378.0 9.8 %custom-call.14 = f32[1,128,128]{1,2,0:T(8,128)S(1)} custom-call(f32[1,128,128]{2,1,0:T(8,128)S(1)} %copy.281), custom_call_target="InvertDiagBlocksLowerTriangular" | custom-call | tf_op jit(solution)/shard_map/triangular_solve/custom-call.0 | solution.py:154
  388.2 1.9 fusion.47
  390.2 2.9 slice_add_fusion.1
  394.2 11.9 %cholesky.167 = f32[128,128]{1,0:T(8,128)S(1)} custom-call(f32[128,128]{1,0:T(8,128)S(1)} %fusion.94), custom_call_target="Cholesky" | custom-call | tf_op jit(solution)/shard_map/jit(cholesky)/cholesky | solution.py:153
  407.7 1.3 fusion.112
  409.1 9.8 %custom-call.15 = f32[1,128,128]{1,2,0:T(8,128)S(1)} custom-call(f32[1,128,128]{2,1,0:T(8,128)S(1)} %copy.288), custom_call_target="InvertDiagBlocksLowerTriangular" | custom-call | tf_op jit(solution)/shard_map/triangular_solve/custom-call.0 | solution.py:154
  422.3 11.7 %cholesky.178 = f32[128,128]{1,0:T(8,128)S(1)} custom-call(f32[128,128]{1,0:T(8,128)S(1)} %fusion.92), custom_call_target="Cholesky" | custom-call | tf_op jit(solution)/shard_map/jit(cholesky)/cholesky | solution.py:153
  435.6 1.3 fusion.113
  437.0 9.8 %custom-call.16 = f32[1,128,128]{1,2,0:T(8,128)S(1)} custom-call(f32[1,128,128]{2,1,0:T(8,128)S(1)} %copy.295), custom_call_target="InvertDiagBlocksLowerTriangular" | custom-call | tf_op jit(solution)/shard_map/triangular_solve/custom-call.0 | solution.py:154
  448.6 4.4 collective-permute-start
  453.8 14.9 %collective-permute-done = bf16[128,1024]{0,1:T(8,128)(2,1)S(1)} collective-permute-done((bf16[128,1024]{0,1:T(8,128)(2,1)S(1)}, bf16[128,1024]{0,1:T(8,128)(2,1)S(1)}, u32[]{:S(2)}, u32[]{:S(2)}) %collective-permute-start) | collective-permute-done | bytes 262176 | tf_op jit(solution)/shard_map/ppermute | solution.py:134
  469.7 11.7 %cholesky.189 = f32[128,128]{1,0:T(8,128)S(1)} custom-call(f32[128,128]{1,0:T(8,128)S(1)} %fusion.90), custom_call_target="Cholesky" | custom-call | tf_op jit(solution)/shard_map/jit(cholesky)/cholesky | solution.py:153
  483.0 1.3 fusion.114
  484.4 9.8 %custom-call.17 = f32[1,128,128]{1,2,0:T(8,128)S(1)} custom-call(f32[1,128,128]{2,1,0:T(8,128)S(1)} %copy.301), custom_call_target="InvertDiagBlocksLowerTriangular" | custom-call | tf_op jit(solution)/shard_map/triangular_solve/custom-call.0 | solution.py:154
  495.6 11.7 %cholesky.200 = f32[128,128]{1,0:T(8,128)S(1)} custom-call(f32[128,128]{1,0:T(8,128)S(1)} %fusion.88), custom_call_target="Cholesky" | custom-call | tf_op jit(solution)/shard_map/jit(cholesky)/cholesky | solution.py:153
  508.9 1.3 fusion.115
  510.3 9.9 %custom-call.18 = f32[1,128,128]{1,2,0:T(8,128)S(1)} custom-call(f32[1,128,128]{2,1,0:T(8,128)S(1)} %copy.307), custom_call_target="InvertDiagBlocksLowerTriangular" | custom-call | tf_op jit(solution)/shard_map/triangular_solve/custom-call.0 | solution.py:154
  521.5 11.7 %cholesky.211 = f32[128,128]{1,0:T(8,128)S(1)} custom-call(f32[128,128]{1,0:T(8,128)S(1)} %fusion.86), custom_call_target="Cholesky" | custom-call | tf_op jit(solution)/shard_map/jit(cholesky)/cholesky | solution.py:153
  534.7 9.8 %custom-call.19 = f32[1,128,128]{1,2,0:T(8,128)S(1)} custom-call(f32[1,128,128]{2,1,0:T(8,128)S(1)} %get-tuple-element.291), custom_call_target="InvertDiagBlocksLowerTriangular" | custom-call | tf_op jit(solution)/shard_map/triangular_solve/custom-call.0 | solution.py:154
  551.7 3.3 fusion.34
  555.0 1.8 fusion.28
  556.9 1.5 fusion.157
  558.4 2.9 copy.252
  561.3 5.6 copy.359
  566.9 6.7 %copy.251 = bf16[2,8,128,1024]{3,2,0,1:T(8,128)(2,1)} copy(bf16[2,8,128,1024]{2,1,0,3:T(8,128)(2,1)} %bitcast.224) | data formatting | bytes 8388608 | tf_op jit(solution)/shard_map/reshape | solution.py:137
  573.6 16.6 %fusion.2 = f32[3072,1024]{1,0:T(8,128)S(1)} fusion(bf16[2048,1024]{1,0:T(8,128)(2,1)} %bitcast.229, bf16[1024,1024]{1,0:T(8,128)(2,1)S(1)} %copy.252, f32[1,512,512]{2,1,0:T(8,128)} %get-tuple-element.302, f32[1,512,512]{2,1,0:T(8,128)} %get-tuple-element.301, f32[1,512,512]{2,1,0:T(8,128)S(1)} %fusion.28), kind=kOutput, calls=%fused_computation.9 | convolution fusion | flops 19344130048 | bytes 22020096 | tf_op jit(solution)/shard_map/dot_general | solution.py:189
  590.2 4.6 copy-done.5
  594.8 2.3 slice.753
  597.0 25.0 %add_subtract_fusion = f32[1024,2048]{0,1:T(8,128)} fusion(f32[1024,2048]{0,1:T(8,128)} %copy.342, f32[3072,1024]{1,0:T(8,128)} %copy-done.5, f32[1,1024,1,2048]{1,3,2,0:T(8,128)} %copy.246), kind=kOutput, calls=%fused_computation.7 | convolution fusion | flops 12889096192 | bytes 37748736 | tf_op jit(solution)/shard_map/dot_general | solution.py:36
  622.2 5.0 copy.344
  628.4 2.6 fusion.40
  631.0 5.8 select_bitcast_fusion
  636.8 20.6 %copy.329 = f32[1,1024,1,2048]{3,2,1,0:T(1,128)} copy(f32[1,1024,1,2048]{1,3,2,0:T(8,128)} %select_bitcast_fusion) | data formatting | bytes 16777216 | tf_op jit(solution)/shard_map/broadcast_in_dim | solution.py:202
  (195 shorter events, 47.8 us)
Async XLA Ops:
  6.5 16.5 %copy-start = (bf16[64,128,128]{2,1,0:T(8,128)(2,1)S(1)}, bf16[64,128,128]{2,1,0:T(8,128)(2,1)}, u32[]{:S(2)}) copy-start(bf16[64,128,128]{2,1,0:T(8,128)(2,1)} %param.55) | copy-start | bytes 6291460
  11.4 32.8 %all-to-all-start = ((s32[128,1,2]{2,1,0:T(1,128)}), s32[128,1,2]{2,1,0:T(1,128)S(1)}, u32[]{:S(2)}, u32[]{:S(2)}) async-start(s32[128,1,2]{2,1,0:T(1,128)} %bitcast.5), calls=%async_computation | async-start | bytes 131072 | tf_op jit(solution)/shard_map/all_to_all | solution.py:80
  44.3 109.9 %all-to-all-start.1 = ((bf16[128,2,128,128]{3,2,1,0:T(8,128)(2,1)}), bf16[128,2,128,128]{3,2,1,0:T(8,128)(2,1)}, u32[]{:S(2)}, u32[]{:S(2)}) async-start(bf16[128,2,128,128]{3,2,1,0:T(8,128)(2,1)} %select_select_fusion), calls=%async_computation.1 | async-start | bytes 16777216 | tf_op jit(solution)/shard_map/all_to_all | solution.py:73
  54.5 175.8 %all-gather.6.cloned.1.call-start = ((), (), s32[]{:S(2)}) async-start(), calls=%async_computation.2 | async-start | bytes 2228224 | tf_op jit(solution)/shard_map/all_gather | solution.py:118
  163.4 16.1 %copy-start.6 = (bf16[1024,128]{0,1:T(8,128)(2,1)}, bf16[1024,128]{0,1:T(8,128)(2,1)S(1)}, u32[]{:S(2)}) copy-start(bf16[1024,128]{0,1:T(8,128)(2,1)S(1)} %slice_add_fusion.2) | copy-start | bytes 786436
  179.5 113.7 %all-gather.8.cloned.1.call-start = ((), (), s32[]{:S(2)}) async-start(), calls=%async_computation.3 | async-start | bytes 2228224 | tf_op jit(solution)/shard_map/all_gather | solution.py:120
  231.6 216.0 %all-gather.10.cloned.1.call-start = ((), (), s32[]{:S(2)}) async-start(), calls=%async_computation.4 | async-start | bytes 2359296 | tf_op jit(solution)/shard_map/all_gather | solution.py:123
  231.7 0.5 copy-start.11
  232.4 62.2 %copy-start.7 = (pred[128,128]{0,1:T(8,128)(4,1)}, pred[128,128]{0,1:T(8,128)(4,1)S(1)}, u32[]{:S(2)}) copy-start(pred[128,128]{0,1:T(8,128)(4,1)S(1)} %copy.255) | copy-start | bytes 49156
  322.5 1.7 copy-start.2
  342.5 19.7 %copy-start.8 = (pred[128,128]{0,1:T(8,128)(4,1)S(1)}, pred[128,128]{0,1:T(8,128)(4,1)}, u32[]{:S(2)}) copy-start(pred[128,128]{0,1:T(8,128)(4,1)} %copy-done.7) | copy-start | bytes 49156
  361.0 200.3 %all-gather.12.cloned.1.call-start = ((), (), s32[]{:S(2)}) async-start(), calls=%async_computation.5 | async-start | bytes 4456448 | tf_op jit(solution)/shard_map/all_gather | solution.py:135
  388.1 4.9 copy-start.3
  393.2 28.8 %copy-start.12 = (s32[128]{0:T(128)S(1)}, s32[128]{0:T(128)}, u32[]{:S(2)}) copy-start(s32[128]{0:T(128)} %copy-done.11) | copy-start | bytes 1540
  420.4 26.4 %copy-start.4 = (f32[8,128,128]{2,1,0:T(8,128)S(1)}, f32[8,128,128]{2,1,0:T(8,128)}, u32[]{:S(2)}) copy-start(f32[8,128,128]{2,1,0:T(8,128)} %get-tuple-element.331) | copy-start | bytes 1572868
  448.6 20.1 %collective-permute-start = (bf16[128,1024]{0,1:T(8,128)(2,1)S(1)}, bf16[128,1024]{0,1:T(8,128)(2,1)S(1)}, u32[]{:S(2)}, u32[]{:S(2)}) collective-permute-start(bf16[128,1024]{0,1:T(8,128)(2,1)S(1)} %constant_dynamic-slice_fusion), channel_id=1, source_target_pairs={{0,0},{1,8},{2,16},{3,24},{4,32},{5,40},{6,48},{7,56},{8,1},{9,9},... | collective-permute-start | bytes 786440 | tf_op jit(solution)/shard_map/ppermute | solution.py:134
  468.7 0.7 copy-start.9
  590.2 4.6 copy-start.5
  597.0 25.0 %slice-start = ((f32[3072,1024]{1,0:T(8,128)}), f32[128,1024]{1,0:T(8,128)S(1)}, s32[]{:S(2)}) async-start(f32[3072,1024]{1,0:T(8,128)} %copy-done.5), calls=%async_computation.6 | async-start | bytes 1048576 | tf_op jit(solution)/shard_map/slice | solution.py:196
  627.3 3.7 copy-start.10
  627.3 3.7 copy-start.13
  636.8 20.7 %copy-start.1 = (bf16[64,128,128]{2,1,0:T(8,128)(2,1)S(1)}, bf16[64,128,128]{2,1,0:T(8,128)(2,1)}, u32[]{:S(2)}) copy-start(bf16[64,128,128]{2,1,0:T(8,128)(2,1)} %param.55) | copy-start | bytes 6291460
Sparse Core Ops, SparseCore 0:
  179.6 50.6 all-gather.5
  232.4 47.0 all-gather.7
  361.1 23.4 all-gather.9
  469.6 57.0 all-gather.11

commit v9 on v8

--- a/solution.py
+++ b/solution.py
@@ -116,7 +116,7 @@
     )[:, :total]
     split = total // 2
     left = lax.all_gather(first_row[:, :split], "frow", axis=0, tiled=True)[:total]
-    left, right_src = lax.optimization_barrier((left, first_row[:, split:]))
+    left, right_src, matrix = lax.optimization_barrier((left, first_row[:, split:], matrix))
     right = lax.all_gather(right_src, "frow", axis=0, tiled=True)[:total]
     right, own_column = lax.optimization_barrier((right, first_column))
     corner = jnp.concatenate([left, right], axis=1).astype(jnp.float32)

time: 673 us -> 680 us (1.010)
  other arithmetic: 216 us -> 227 us
  matrix products: 89.2 us -> 82 us
    all_gather x1, waiting for transfers between devices: 50.8 us -> 0.01 us  [shards(): lax.all_gather(first_row[:, :split], 'frow', axis=0, tiled=True)[:total]]
    all_gather x1, waiting for transfers between devices: 0.02 us -> 47.7 us  [shards(): right = lax.all_gather(right_src, 'frow', axis=0, tiled=True)[:total]]
    add x0 -> x1, other arithmetic: none -> 12.1 us  [shards(): matrix = local + added]
    dot_general x1, matrix products: 25 us -> 17.7 us  [subtract_product(): jnp.dot(row_factor, col_factor.T, precision=lax.Precision.HIGH, preferred...]
    unnamed x34 -> x32, local copies, waits for them, and re-layouts: 69.8 us -> 75.2 us
  transfers between devices with their start and end apart: 7 -> 7, of which waited for: 3 -> 3; matrix products, arithmetic and copies ran while one was open for 43% -> 45% of each run, Pallas kernels for 0% -> 0%
where the time goes in v9:
time: 680 us; the launch traced here: 672 us
  other arithmetic  227 us (33%)
  local copies, waits for them, and re-layouts  166 us (24%)
  waiting for transfers between devices  140 us (21%)
  matrix products  82 us (12%)
  starting transfers between devices  26 us (4%)
  blocking collectives  15.3 us (2%)
  between operations  14.7 us (2%)
    another operation x24, other arithmetic, shards(): factor = jnp.linalg.cholesky(symmetric)  100 us
    another operation x11, other arithmetic, shards(): lax.linalg.triangular_solve(factor, eye, left_side=True, lower=True)  80.6 us
    all_to_all x1, waiting for transfers between devices, shards(): lax.all_to_all(send_tiles.reshape(owners, CAP, width, width), ('frow', 'f...  77.4 us
    unnamed x32, local copies, waits for them, and re-layouts  75.2 us
    all_gather x1, waiting for transfers between devices, shards(): right = lax.all_gather(right_src, 'frow', axis=0, tiled=True)[:total]  47.7 us
    broadcast_in_dim x1, local copies, waits for them, and re-layouts, shards(): return result[None, :, None, :]  20.6 us
    dot_general x1, matrix products, subtract_product(): jnp.dot(row_factor, col_factor.T, precision=lax.Precision.HIGH, preferred...  17.7 us
    dot_general x1, matrix products, shards(): jnp.dot(rows_all, factor_inverse.T, precision=hi, preferred_element_type=...  16.6 us
  transfers between devices with their start and end apart: 7, of which 3 were waited for; matrix products, arithmetic and copies ran while one was open for 45% of the time, Pallas kernels for 0%

profile of v9, /device:TPU:6, one launch (start us, length us, event | category | flops | bytes accessed | tf_op | source)
XLA Modules:
  0.0 671.6 jit_solution(4850545478601370905)
XLA Ops:
  8.8 1.9 gather_fusion
  11.4 10.5 %all-to-all-start = ((s32[128,1,2]{2,1,0:T(1,128)}), s32[128,1,2]{2,1,0:T(1,128)S(1)}, u32[]{:S(2)}, u32[]{:S(2)}) async-start(s32[128,1,2]{2,1,0:T(1,128)} %bitcast.5), calls=%async_computation | async-start | bytes 131072 | tf_op jit(solution)/shard_map/all_to_all | solution.py:80
  23.0 3.6 fusion.26
  26.7 10.1 %gather_fusion.1 = bf16[256,128,128]{2,1,0:T(8,128)(2,1)} fusion(bf16[64,128,128]{2,1,0:T(8,128)(2,1)} %fusion.26, s32[1024]{0:T(1024)S(1)} %pad_clamp_fusion), kind=kCustom, calls=%fused_computation.1 | custom fusion | bytes 16778240 | tf_op jit(solution)/shard_map/jit(_take)/gather | solution.py:69
  36.8 7.4 %select_select_fusion = bf16[128,2,128,128]{3,2,1,0:T(8,128)(2,1)} fusion(bf16[128,2,128,128]{3,2,1,0:T(8,128)(2,1)} %bitcast.222, pred[128,2]{1,0:T(8,128)(4,1)S(1)} %compare_and_fusion, pred[128,2]{1,0:T(8,128)(4,1)S(1)} %broadcast_in_dim.106), kind=kLoop, calls=%fused_computation.7 | loop fusion | flops 8388608 | bytes 16777728 | tf_op jit(solution)/shard_map/jit(_where)/select_n | solution.py:67
  44.3 10.2 %all-to-all-start.1 = ((bf16[128,2,128,128]{3,2,1,0:T(8,128)(2,1)}), bf16[128,2,128,128]{3,2,1,0:T(8,128)(2,1)}, u32[]{:S(2)}, u32[]{:S(2)}) async-start(bf16[128,2,128,128]{3,2,1,0:T(8,128)(2,1)} %select_select_fusion), calls=%async_computation.1 | async-start | bytes 16777216 | tf_op jit(solution)/shard_map/all_to_all | solution.py:73
  54.8 20.7 %copy.246 = f32[1,1024,1,2048]{1,3,2,0:T(8,128)} copy(f32[1,1024,1,2048]{3,2,1,0:T(1,128)} %param.54) | data formatting | bytes 16777216 | tf_op args[0]
  76.8 77.4 %all-to-all-done.1 = bf16[128,2,128,128]{3,2,1,0:T(8,128)(2,1)} async-done(((bf16[128,2,128,128]{3,2,1,0:T(8,128)(2,1)}), bf16[128,2,128,128]{3,2,1,0:T(8,128)(2,1)}, u32[]{:S(2)}, u32[]{:S(2)}) %all-to-all-start.1) | async-done | bytes 8388640 | tf_op jit(solution)/shard_map/all_to_all | solution.py:73
  154.2 7.8 %fusion.133 = f32[8,16384]{1,0:T(8,128)S(1)} fusion(s32[256]{0:T(256)S(1)} %eq.128, s32[8]{0:T(128)S(1)} %iota_multiply_fusion, bf16[32,8,128,128]{3,2,1,0:T(8,128)(2,1)} %bitcast.76), kind=kOutput, calls=%fused_computation.232 | convolution fusion | flops 67110912 | bytes 8913952 | tf_op jit(solution)/shard_map/dot_general | solution.py:103
  163.4 15.3 %all_gather.18 = bf16[128,1024]{0,1:T(8,128)(2,1)S(1)} all-gather(bf16[128,128]{0,1:T(8,128)(2,1)S(1)} %slice.821), channel_id=1, replica_groups=mesh['frow'=16,'fcol'=8] {'fcol'}, dimensions={1}, use_global_device_ids=true | all-gather | bytes 294912 | tf_op jit(solution)/shard_map/all_gather | solution.py:114
  179.9 33.4 %copy.364 = bf16[32,8,128,128]{3,1,2,0:T(8,128)(2,1)} copy(bf16[32,8,128,128]{3,2,1,0:T(8,128)(2,1)} %bitcast.76) | data formatting | bytes 16777216
  213.3 11.9 %copy.249 = bf16[256,16384]{0,1:T(8,128)(2,1)} copy(bf16[256,16384]{1,0:T(8,128)(2,1)} %bitcast.223) | data formatting | bytes 16777216 | tf_op jit(solution)/shard_map/reshape | solution.py:104
  225.3 6.3 fusion.81
  231.6 7.5 %copy.363 = f32[128,8,16,128]{3,1,2,0:T(8,128)} copy(f32[128,8,16,128]{3,2,1,0:T(8,128)S(1)} %bitcast.227) | data formatting | bytes 16777216
  239.1 9.3 %copy.342 = f32[1024,2048]{0,1:T(8,128)} copy(f32[1024,2048]{1,0:T(8,128)} %bitcast.224) | data formatting | bytes 16777216 | tf_op jit(solution)/shard_map/reshape | solution.py:98
  248.4 12.1 %bitcast_add_fusion.16 = f32[1024,2048]{0,1:T(8,128)} fusion(f32[1024,2048]{0,1:T(8,128)} %copy.342, f32[1,1024,1,2048]{1,3,2,0:T(8,128)} %copy.246), kind=kLoop, calls=%fused_computation.275 | loop fusion | flops 2097152 | bytes 25165824 | tf_op jit(solution)/shard_map/add | solution.py:100
  260.5 1.3 slice.720
  264.8 47.7 %all-gather.8.cloned.1.call-done = bf16[2048,512]{0,1:T(8,128)(2,1)} async-done(((bf16[128,512]{0,1:T(8,128)(2,1)}), bf16[2048,512]{0,1:T(8,128)(2,1)}) %all-gather.8.cloned.1.call-update) | async-done | bytes 2097168 | tf_op jit(solution)/shard_map/all_gather | solution.py:120
  312.5 1.3 slice.722
  314.1 11.7 %cholesky.134 = f32[128,128]{1,0:T(8,128)S(1)} custom-call(f32[128,128]{1,0:T(8,128)S(1)} %copy.258), custom_call_target="Cholesky" | custom-call | tf_op jit(solution)/shard_map/jit(cholesky)/cholesky | solution.py:153
  326.7 1.3 select_bitcast_fusion.8
  328.1 9.8 %custom-call.12 = f32[1,128,128]{1,2,0:T(8,128)S(1)} custom-call(f32[1,128,128]{2,1,0:T(8,128)S(1)} %copy.261), custom_call_target="InvertDiagBlocksLowerTriangular" | custom-call | tf_op jit(solution)/shard_map/triangular_solve/custom-call.0 | solution.py:154
  338.8 3.0 negate_add_fusion
  341.8 1.7 copy-done.2
  344.7 12.1 %cholesky.145 = f32[128,128]{1,0:T(8,128)S(1)} custom-call(f32[128,128]{1,0:T(8,128)S(1)} %copy.268), custom_call_target="Cholesky" | custom-call | tf_op jit(solution)/shard_map/jit(cholesky)/cholesky | solution.py:153
  357.6 3.3 scatter.54
  361.8 1.2 fusion.111
  363.1 9.8 %custom-call.13 = f32[1,128,128]{1,2,0:T(8,128)S(1)} custom-call(f32[1,128,128]{2,1,0:T(8,128)S(1)} %copy.271), custom_call_target="InvertDiagBlocksLowerTriangular" | custom-call | tf_op jit(solution)/shard_map/triangular_solve/custom-call.0 | solution.py:154
  373.2 1.8 fusion.46
  375.2 5.2 slice_add_fusion
  382.6 11.7 %cholesky.156 = f32[128,128]{1,0:T(8,128)S(1)} custom-call(f32[128,128]{1,0:T(8,128)S(1)} %copy.278), custom_call_target="Cholesky" | custom-call | tf_op jit(solution)/shard_map/jit(cholesky)/cholesky | solution.py:153
  396.0 1.2 fusion.112
  397.2 9.8 %custom-call.14 = f32[1,128,128]{1,2,0:T(8,128)S(1)} custom-call(f32[1,128,128]{2,1,0:T(8,128)S(1)} %copy.281), custom_call_target="InvertDiagBlocksLowerTriangular" | custom-call | tf_op jit(solution)/shard_map/triangular_solve/custom-call.0 | solution.py:154
  407.4 1.9 fusion.48
  409.4 2.9 slice_add_fusion.1
  413.4 11.9 %cholesky.167 = f32[128,128]{1,0:T(8,128)S(1)} custom-call(f32[128,128]{1,0:T(8,128)S(1)} %fusion.95), custom_call_target="Cholesky" | custom-call | tf_op jit(solution)/shard_map/jit(cholesky)/cholesky | solution.py:153
  426.9 1.2 fusion.113
  428.1 9.8 %custom-call.15 = f32[1,128,128]{1,2,0:T(8,128)S(1)} custom-call(f32[1,128,128]{2,1,0:T(8,128)S(1)} %copy.288), custom_call_target="InvertDiagBlocksLowerTriangular" | custom-call | tf_op jit(solution)/shard_map/triangular_solve/custom-call.0 | solution.py:154
  441.3 11.7 %cholesky.178 = f32[128,128]{1,0:T(8,128)S(1)} custom-call(f32[128,128]{1,0:T(8,128)S(1)} %fusion.93), custom_call_target="Cholesky" | custom-call | tf_op jit(solution)/shard_map/jit(cholesky)/cholesky | solution.py:153
  454.6 1.3 fusion.114
  456.0 9.8 %custom-call.16 = f32[1,128,128]{1,2,0:T(8,128)S(1)} custom-call(f32[1,128,128]{2,1,0:T(8,128)S(1)} %copy.295), custom_call_target="InvertDiagBlocksLowerTriangular" | custom-call | tf_op jit(solution)/shard_map/triangular_solve/custom-call.0 | solution.py:154
  467.6 4.4 collective-permute-start
  472.8 14.8 %collective-permute-done = bf16[128,1024]{0,1:T(8,128)(2,1)S(1)} collective-permute-done((bf16[128,1024]{0,1:T(8,128)(2,1)S(1)}, bf16[128,1024]{0,1:T(8,128)(2,1)S(1)}, u32[]{:S(2)}, u32[]{:S(2)}) %collective-permute-start) | collective-permute-done | bytes 262176 | tf_op jit(solution)/shard_map/ppermute | solution.py:134
  488.5 11.7 %cholesky.189 = f32[128,128]{1,0:T(8,128)S(1)} custom-call(f32[128,128]{1,0:T(8,128)S(1)} %fusion.91), custom_call_target="Cholesky" | custom-call | tf_op jit(solution)/shard_map/jit(cholesky)/cholesky | solution.py:153
  501.9 1.3 fusion.115
  503.3 9.8 %custom-call.17 = f32[1,128,128]{1,2,0:T(8,128)S(1)} custom-call(f32[1,128,128]{2,1,0:T(8,128)S(1)} %copy.301), custom_call_target="InvertDiagBlocksLowerTriangular" | custom-call | tf_op jit(solution)/shard_map/triangular_solve/custom-call.0 | solution.py:154
  514.5 11.7 %cholesky.200 = f32[128,128]{1,0:T(8,128)S(1)} custom-call(f32[128,128]{1,0:T(8,128)S(1)} %fusion.89), custom_call_target="Cholesky" | custom-call | tf_op jit(solution)/shard_map/jit(cholesky)/cholesky | solution.py:153
  527.9 1.3 fusion.116
  529.3 9.9 %custom-call.18 = f32[1,128,128]{1,2,0:T(8,128)S(1)} custom-call(f32[1,128,128]{2,1,0:T(8,128)S(1)} %copy.307), custom_call_target="InvertDiagBlocksLowerTriangular" | custom-call | tf_op jit(solution)/shard_map/triangular_solve/custom-call.0 | solution.py:154
  540.4 11.7 %cholesky.211 = f32[128,128]{1,0:T(8,128)S(1)} custom-call(f32[128,128]{1,0:T(8,128)S(1)} %fusion.87), custom_call_target="Cholesky" | custom-call | tf_op jit(solution)/shard_map/jit(cholesky)/cholesky | solution.py:153
  553.6 9.8 %custom-call.19 = f32[1,128,128]{1,2,0:T(8,128)S(1)} custom-call(f32[1,128,128]{2,1,0:T(8,128)S(1)} %get-tuple-element.293), custom_call_target="InvertDiagBlocksLowerTriangular" | custom-call | tf_op jit(solution)/shard_map/triangular_solve/custom-call.0 | solution.py:154
  570.6 3.3 fusion.35
  573.9 1.8 fusion.29
  575.8 1.5 fusion.158
  577.3 2.9 copy.252
  580.2 5.6 copy.359
  585.8 6.7 copy.251
  592.5 16.6 %fusion.2 = f32[3072,1024]{1,0:T(8,128)S(1)} fusion(bf16[2048,1024]{1,0:T(8,128)(2,1)} %bitcast.229, bf16[1024,1024]{1,0:T(8,128)(2,1)S(1)} %copy.252, f32[1,512,512]{2,1,0:T(8,128)} %get-tuple-element.304, f32[1,512,512]{2,1,0:T(8,128)} %get-tuple-element.303, f32[1,512,512]{2,1,0:T(8,128)S(1)} %fusion.29), kind=kOutput, calls=%fused_computation.8 | convolution fusion | flops 19344130048 | bytes 22020096 | tf_op jit(solution)/shard_map/dot_general | solution.py:189
  609.1 2.3 slice.753
  611.4 17.7 %fusion.15 = f32[1024,2048]{0,1:T(8,128)} fusion(f32[1024,2048]{0,1:T(8,128)} %bitcast_add_fusion.16, f32[3072,1024]{1,0:T(8,128)S(1)} %fusion.2), kind=kOutput, calls=%fused_computation.26 | convolution fusion | flops 12886999040 | bytes 29360128 | tf_op jit(solution)/shard_map/dot_general | solution.py:36
  629.4 5.0 copy.344
  635.5 2.7 fusion.41
  638.2 5.8 select_bitcast_fusion
  644.0 20.6 %copy.329 = f32[1,1024,1,2048]{3,2,1,0:T(1,128)} copy(f32[1,1024,1,2048]{1,3,2,0:T(8,128)} %select_bitcast_fusion) | data formatting | bytes 16777216 | tf_op jit(solution)/shard_map/broadcast_in_dim | solution.py:202
  (193 shorter events, 47.8 us)
Async XLA Ops:
  6.5 16.5 %copy-start = (bf16[64,128,128]{2,1,0:T(8,128)(2,1)S(1)}, bf16[64,128,128]{2,1,0:T(8,128)(2,1)}, u32[]{:S(2)}) copy-start(bf16[64,128,128]{2,1,0:T(8,128)(2,1)} %param.55) | copy-start | bytes 6291460
  11.4 32.8 %all-to-all-start = ((s32[128,1,2]{2,1,0:T(1,128)}), s32[128,1,2]{2,1,0:T(1,128)S(1)}, u32[]{:S(2)}, u32[]{:S(2)}) async-start(s32[128,1,2]{2,1,0:T(1,128)} %bitcast.5), calls=%async_computation | async-start | bytes 131072 | tf_op jit(solution)/shard_map/all_to_all | solution.py:80
  44.3 109.9 %all-to-all-start.1 = ((bf16[128,2,128,128]{3,2,1,0:T(8,128)(2,1)}), bf16[128,2,128,128]{3,2,1,0:T(8,128)(2,1)}, u32[]{:S(2)}, u32[]{:S(2)}) async-start(bf16[128,2,128,128]{3,2,1,0:T(8,128)(2,1)} %select_select_fusion), calls=%async_computation.1 | async-start | bytes 16777216 | tf_op jit(solution)/shard_map/all_to_all | solution.py:73
  54.5 206.0 %all-gather.6.cloned.1.call-start = ((), (), s32[]{:S(2)}) async-start(), calls=%async_computation.2 | async-start | bytes 2228224 | tf_op jit(solution)/shard_map/all_gather | solution.py:118
  163.4 49.9 %copy-start.5 = (bf16[1024,128]{0,1:T(8,128)(2,1)}, bf16[1024,128]{0,1:T(8,128)(2,1)S(1)}, u32[]{:S(2)}) copy-start(bf16[1024,128]{0,1:T(8,128)(2,1)S(1)} %slice_add_fusion.2) | copy-start | bytes 786436
  179.5 133.0 %all-gather.8.cloned.1.call-start = ((), (), s32[]{:S(2)}) async-start(), calls=%async_computation.3 | async-start | bytes 2228224 | tf_op jit(solution)/shard_map/all_gather | solution.py:120
  261.8 204.8 %all-gather.10.cloned.1.call-start = ((), (), s32[]{:S(2)}) async-start(), calls=%async_computation.4 | async-start | bytes 2359296 | tf_op jit(solution)/shard_map/all_gather | solution.py:123
  261.9 0.5 copy-start.10
  262.5 75.6 %copy-start.6 = (pred[128,128]{0,1:T(8,128)(4,1)}, pred[128,128]{0,1:T(8,128)(4,1)S(1)}, u32[]{:S(2)}) copy-start(pred[128,128]{0,1:T(8,128)(4,1)S(1)} %copy.255) | copy-start | bytes 49156
  341.8 1.7 copy-start.2
  361.8 19.7 %copy-start.7 = (pred[128,128]{0,1:T(8,128)(4,1)S(1)}, pred[128,128]{0,1:T(8,128)(4,1)}, u32[]{:S(2)}) copy-start(pred[128,128]{0,1:T(8,128)(4,1)} %copy-done.6) | copy-start | bytes 49156
  380.3 199.9 %all-gather.12.cloned.1.call-start = ((), (), s32[]{:S(2)}) async-start(), calls=%async_computation.5 | async-start | bytes 4456448 | tf_op jit(solution)/shard_map/all_gather | solution.py:135
  407.4 4.9 copy-start.3
  412.5 28.6 %copy-start.11 = (s32[128]{0:T(128)S(1)}, s32[128]{0:T(128)}, u32[]{:S(2)}) copy-start(s32[128]{0:T(128)} %copy-done.10) | copy-start | bytes 1540
  439.5 26.4 %copy-start.4 = (f32[8,128,128]{2,1,0:T(8,128)S(1)}, f32[8,128,128]{2,1,0:T(8,128)}, u32[]{:S(2)}) copy-start(f32[8,128,128]{2,1,0:T(8,128)} %get-tuple-element.333) | copy-start | bytes 1572868
  467.6 20.0 %collective-permute-start = (bf16[128,1024]{0,1:T(8,128)(2,1)S(1)}, bf16[128,1024]{0,1:T(8,128)(2,1)S(1)}, u32[]{:S(2)}, u32[]{:S(2)}) collective-permute-start(bf16[128,1024]{0,1:T(8,128)(2,1)S(1)} %constant_dynamic-slice_fusion), channel_id=1, source_target_pairs={{0,0},{1,8},{2,16},{3,24},{4,32},{5,40},{6,48},{7,56},{8,1},{9,9},... | collective-permute-start | bytes 786440 | tf_op jit(solution)/shard_map/ppermute | solution.py:134
  487.6 0.7 copy-start.8
  634.4 3.8 copy-start.9
  634.4 3.8 copy-start.12
  644.0 20.7 %copy-start.1 = (bf16[64,128,128]{2,1,0:T(8,128)(2,1)S(1)}, bf16[64,128,128]{2,1,0:T(8,128)(2,1)}, u32[]{:S(2)}) copy-start(bf16[64,128,128]{2,1,0:T(8,128)(2,1)} %param.55) | copy-start | bytes 6291460
Sparse Core Ops, SparseCore 0:
  179.6 50.6 all-gather.5
  262.0 50.4 all-gather.7
  380.5 23.3 all-gather.9
  488.4 57.0 all-gather.11

commit v10 on v9

--- a/solution.py
+++ b/solution.py
@@ -119,7 +119,7 @@
     left, right_src, matrix = lax.optimization_barrier((left, first_row[:, split:], matrix))
     right = lax.all_gather(right_src, "frow", axis=0, tiled=True)[:total]
     right, own_column = lax.optimization_barrier((right, first_column))
-    corner = jnp.concatenate([left, right], axis=1).astype(jnp.float32)
+    halves = [left.astype(jnp.float32), right.astype(jnp.float32)]
     row_panel = lax.all_gather(
         own_column.astype(jnp.bfloat16), "fcol", axis=1, tiled=True
     )[:, :total]
@@ -145,23 +145,39 @@
     factor_full = jnp.zeros((total, total), jnp.float32)
     eye = jnp.eye(width, dtype=jnp.float32)
     inverses = []
-    for blk in range(corner_blocks):
-        start = blk * width
-        stop = start + width
-        diag_block = corner[start:stop, start:stop]
-        symmetric = jnp.tril(diag_block) + jnp.tril(diag_block, -1).T
-        factor = jnp.linalg.cholesky(symmetric)
-        inverse = lax.linalg.triangular_solve(factor, eye, left_side=True, lower=True)
-        inverses.append(inverse)
-        factor_full = factor_full.at[start:stop, start:stop].set(factor)
-        if stop < total:
-            below = jnp.dot(
-                corner[stop:, start:stop], inverse.T, precision=full, preferred_element_type=jnp.float32
+    for h, cur in enumerate(halves):
+        if h > 0:
+            done_cols = factor_full[:, : h * split]
+            cur = cur - jnp.dot(
+                done_cols,
+                done_cols[h * split : (h + 1) * split].T,
+                precision=full,
+                preferred_element_type=jnp.float32,
             )
-            factor_full = factor_full.at[stop:, start:stop].set(below)
-            corner = corner.at[stop:, stop:].add(
-                -jnp.dot(below, below.T, precision=full, preferred_element_type=jnp.float32)
-            )
+        for b in range(split // width):
+            start = h * split + b * width
+            stop = start + width
+            lb = b * width
+            diag_block = cur[start:stop, lb : lb + width]
+            symmetric = jnp.tril(diag_block) + jnp.tril(diag_block, -1).T
+            factor = jnp.linalg.cholesky(symmetric)
+            inverse = lax.linalg.triangular_solve(factor, eye, left_side=True, lower=True)
+            inverses.append(inverse)
+            factor_full = factor_full.at[start:stop, start:stop].set(factor)
+            if stop < total:
+                below = jnp.dot(
+                    cur[stop:, lb : lb + width], inverse.T, precision=full, preferred_element_type=jnp.float32
+                )
+                factor_full = factor_full.at[stop:, start:stop].set(below)
+                if lb + width < split:
+                    cur = cur.at[stop:, lb + width :].add(
+                        -jnp.dot(
+                            below,
+                            below[: split - lb - width].T,
+                            precision=full,
+                            preferred_element_type=jnp.float32,
+                        )
+                    )
     inv_blocks = jnp.stack(inverses)
     size = width
     while size < total:

time: 680 us -> 620 us (0.912)
  waiting for transfers between devices: 140 us -> 92.9 us
  local copies, waits for them, and re-layouts: 166 us -> 154 us
    all_gather x1, waiting for transfers between devices: 47.7 us -> 0.01 us  [shards(): right = lax.all_gather(right_src, 'frow', axis=0, tiled=True)[:total]]
    unnamed x32, local copies, waits for them, and re-layouts: 75.2 us -> 64.4 us
  transfers between devices with their start and end apart: 7 -> 7, of which waited for: 3 -> 2; matrix products, arithmetic and copies ran while one was open for 45% -> 59% of each run, Pallas kernels for 0% -> 0%
where the time goes in v10:
time: 620 us; the launch traced here: 610 us
  other arithmetic  227 us (37%)
  local copies, waits for them, and re-layouts  154 us (25%)
  waiting for transfers between devices  92.9 us (15%)
  matrix products  82 us (13%)
  starting transfers between devices  25.2 us (4%)
  blocking collectives  15.3 us (2%)
  between operations  14.4 us (2%)
    another operation x24, other arithmetic, shards(): factor = jnp.linalg.cholesky(symmetric)  100 us
    another operation x11, other arithmetic, shards(): lax.linalg.triangular_solve(factor, eye, left_side=True, lower=True)  80 us
    all_to_all x1, waiting for transfers between devices, shards(): lax.all_to_all(send_tiles.reshape(owners, CAP, width, width), ('frow', 'f...  77.3 us
    unnamed x32, local copies, waits for them, and re-layouts  64.4 us
    broadcast_in_dim x1, local copies, waits for them, and re-layouts, shards(): return result[None, :, None, :]  20.5 us
    dot_general x1, matrix products, subtract_product(): jnp.dot(row_factor, col_factor.T, precision=lax.Precision.HIGH, preferred...  17.7 us
    dot_general x1, matrix products, shards(): jnp.dot(rows_all, factor_inverse.T, precision=hi, preferred_element_type=...  16.6 us
    ppermute x1, waiting for transfers between devices, shards(): piece = lax.ppermute(piece, ('frow', 'fcol'), pairs)  15.5 us
  transfers between devices with their start and end apart: 7, of which 2 were waited for; matrix products, arithmetic and copies ran while one was open for 59% of the time, Pallas kernels for 0%

profile of v10, /device:TPU:6, one launch (start us, length us, event | category | flops | bytes accessed | tf_op | source)
XLA Modules:
  0.0 610.2 jit_solution(1710537951863947196)
XLA Ops:
  8.8 1.9 gather_fusion
  11.4 10.5 %all-to-all-start = ((s32[128,1,2]{2,1,0:T(1,128)}), s32[128,1,2]{2,1,0:T(1,128)S(1)}, u32[]{:S(2)}, u32[]{:S(2)}) async-start(s32[128,1,2]{2,1,0:T(1,128)} %bitcast.5), calls=%async_computation | async-start | bytes 131072 | tf_op jit(solution)/shard_map/all_to_all | solution.py:80
  23.0 3.6 fusion.28
  26.7 10.1 %gather_fusion.1 = bf16[256,128,128]{2,1,0:T(8,128)(2,1)} fusion(bf16[64,128,128]{2,1,0:T(8,128)(2,1)} %fusion.28, s32[1024]{0:T(1024)S(1)} %pad_clamp_fusion), kind=kCustom, calls=%fused_computation.1 | custom fusion | bytes 16778240 | tf_op jit(solution)/shard_map/jit(_take)/gather | solution.py:69
  36.8 7.4 %select_select_fusion = bf16[128,2,128,128]{3,2,1,0:T(8,128)(2,1)} fusion(bf16[128,2,128,128]{3,2,1,0:T(8,128)(2,1)} %bitcast.217, pred[128,2]{1,0:T(8,128)(4,1)S(1)} %compare_and_fusion, pred[128,2]{1,0:T(8,128)(4,1)S(1)} %broadcast_in_dim.106), kind=kLoop, calls=%fused_computation.7 | loop fusion | flops 8388608 | bytes 16777728 | tf_op jit(solution)/shard_map/jit(_where)/select_n | solution.py:67
  44.3 10.2 %all-to-all-start.1 = ((bf16[128,2,128,128]{3,2,1,0:T(8,128)(2,1)}), bf16[128,2,128,128]{3,2,1,0:T(8,128)(2,1)}, u32[]{:S(2)}, u32[]{:S(2)}) async-start(bf16[128,2,128,128]{3,2,1,0:T(8,128)(2,1)} %select_select_fusion), calls=%async_computation.1 | async-start | bytes 16777216 | tf_op jit(solution)/shard_map/all_to_all | solution.py:73
  54.8 20.7 %copy.246 = f32[1,1024,1,2048]{1,3,2,0:T(8,128)} copy(f32[1,1024,1,2048]{3,2,1,0:T(1,128)} %param.52) | data formatting | bytes 16777216 | tf_op args[0]
  76.9 77.3 %all-to-all-done.1 = bf16[128,2,128,128]{3,2,1,0:T(8,128)(2,1)} async-done(((bf16[128,2,128,128]{3,2,1,0:T(8,128)(2,1)}), bf16[128,2,128,128]{3,2,1,0:T(8,128)(2,1)}, u32[]{:S(2)}, u32[]{:S(2)}) %all-to-all-start.1) | async-done | bytes 8388640 | tf_op jit(solution)/shard_map/all_to_all | solution.py:73
  154.2 7.8 %fusion.143 = f32[8,16384]{1,0:T(8,128)S(1)} fusion(s32[256]{0:T(256)S(1)} %eq.128, s32[8]{0:T(128)S(1)} %iota_multiply_fusion, bf16[32,8,128,128]{3,2,1,0:T(8,128)(2,1)} %bitcast.76), kind=kOutput, calls=%fused_computation.238 | convolution fusion | flops 67110912 | bytes 8913952 | tf_op jit(solution)/shard_map/dot_general | solution.py:103
  163.4 15.3 %all_gather.18 = bf16[128,1024]{0,1:T(8,128)(2,1)S(1)} all-gather(bf16[128,128]{0,1:T(8,128)(2,1)S(1)} %slice.839), channel_id=1, replica_groups=mesh['frow'=16,'fcol'=8] {'fcol'}, dimensions={1}, use_global_device_ids=true | all-gather | bytes 294912 | tf_op jit(solution)/shard_map/all_gather | solution.py:114
  180.0 1.2 compare_reduce_fusion.8
  182.3 23.3 %copy.365 = bf16[32,8,128,128]{3,1,2,0:T(8,128)(2,1)} copy(bf16[32,8,128,128]{3,2,1,0:T(8,128)(2,1)} %bitcast.76) | data formatting | bytes 16777216
  205.6 11.9 %copy.249 = bf16[256,16384]{0,1:T(8,128)(2,1)} copy(bf16[256,16384]{1,0:T(8,128)(2,1)} %bitcast.218) | data formatting | bytes 16777216 | tf_op jit(solution)/shard_map/reshape | solution.py:104
  217.6 6.3 %fusion.90 = f32[8,16,128,128]{3,1,2,0:T(8,128)S(1)} fusion(bf16[128,128,256,1]{2,1,0,3:T(8,128)(2,1)} %bitcast.221, s32[8,16]{1,0:T(8,128)S(1)} %multiply_add_fusion, s32[256]{0:T(256)S(1)} %eq.128), kind=kOutput, calls=%fused_computation.113 | convolution fusion | flops 1073774592 | bytes 16778752 | tf_op jit(solution)/shard_map/dot_general | solution.py:92
  223.8 7.5 %copy.364 = f32[128,8,16,128]{3,1,2,0:T(8,128)} copy(f32[128,8,16,128]{3,2,1,0:T(8,128)S(1)} %bitcast.222) | data formatting | bytes 16777216
  231.4 9.3 %copy.343 = f32[1024,2048]{0,1:T(8,128)} copy(f32[1024,2048]{1,0:T(8,128)} %bitcast.219) | data formatting | bytes 16777216 | tf_op jit(solution)/shard_map/reshape | solution.py:98
  240.6 12.1 %bitcast_add_fusion.16 = f32[1024,2048]{0,1:T(8,128)} fusion(f32[1024,2048]{0,1:T(8,128)} %copy.343, f32[1,1024,1,2048]{1,3,2,0:T(8,128)} %copy.246), kind=kLoop, calls=%fused_computation.280 | loop fusion | flops 2097152 | bytes 25165824 | tf_op jit(solution)/shard_map/add | solution.py:100
  252.8 1.3 slice.718
  255.2 11.7 %cholesky.134 = f32[128,128]{1,0:T(8,128)S(1)} custom-call(f32[128,128]{1,0:T(8,128)S(1)} %copy.258), custom_call_target="Cholesky" | custom-call | tf_op jit(solution)/shard_map/jit(cholesky)/cholesky | solution.py:163
  268.6 9.8 %custom-call.12 = f32[1,128,128]{1,2,0:T(8,128)S(1)} custom-call(f32[1,128,128]{2,1,0:T(8,128)S(1)} %copy.261), custom_call_target="InvertDiagBlocksLowerTriangular" | custom-call | tf_op jit(solution)/shard_map/triangular_solve/custom-call.0 | solution.py:164
  279.4 1.2 fusion.82
  280.5 2.0 copy.289
  282.5 2.3 fusion.34
  285.9 11.9 %cholesky.145 = f32[128,128]{1,0:T(8,128)S(1)} custom-call(f32[128,128]{1,0:T(8,128)S(1)} %copy.268), custom_call_target="Cholesky" | custom-call | tf_op jit(solution)/shard_map/jit(cholesky)/cholesky | solution.py:163
  297.9 2.5 scatter.54
  302.1 1.3 fusion.121
  303.5 9.8 %custom-call.13 = f32[1,128,128]{1,2,0:T(8,128)S(1)} custom-call(f32[1,128,128]{2,1,0:T(8,128)S(1)} %copy.271), custom_call_target="InvertDiagBlocksLowerTriangular" | custom-call | tf_op jit(solution)/shard_map/triangular_solve/custom-call.0 | solution.py:164
  316.4 11.7 %cholesky.156 = f32[128,128]{1,0:T(8,128)S(1)} custom-call(f32[128,128]{1,0:T(8,128)S(1)} %copy.278), custom_call_target="Cholesky" | custom-call | tf_op jit(solution)/shard_map/jit(cholesky)/cholesky | solution.py:163
  329.9 1.3 fusion.122
  331.3 9.8 %custom-call.14 = f32[1,128,128]{1,2,0:T(8,128)S(1)} custom-call(f32[1,128,128]{2,1,0:T(8,128)S(1)} %copy.281), custom_call_target="InvertDiagBlocksLowerTriangular" | custom-call | tf_op jit(solution)/shard_map/triangular_solve/custom-call.0 | solution.py:164
  343.9 11.7 %cholesky.167 = f32[128,128]{1,0:T(8,128)S(1)} custom-call(f32[128,128]{1,0:T(8,128)S(1)} %fusion.105), custom_call_target="Cholesky" | custom-call | tf_op jit(solution)/shard_map/jit(cholesky)/cholesky | solution.py:163
  357.3 1.3 fusion.123
  358.7 9.8 %custom-call.15 = f32[1,128,128]{1,2,0:T(8,128)S(1)} custom-call(f32[1,128,128]{2,1,0:T(8,128)S(1)} %copy.288), custom_call_target="InvertDiagBlocksLowerTriangular" | custom-call | tf_op jit(solution)/shard_map/triangular_solve/custom-call.0 | solution.py:164
  371.5 5.4 fusion.31
  376.9 1.3 copy-done.2
  379.4 11.7 %cholesky.178 = f32[128,128]{1,0:T(8,128)S(1)} custom-call(f32[128,128]{1,0:T(8,128)S(1)} %fusion.103), custom_call_target="Cholesky" | custom-call | tf_op jit(solution)/shard_map/jit(cholesky)/cholesky | solution.py:163
  392.0 1.3 fusion.124
  393.4 9.8 %custom-call.16 = f32[1,128,128]{1,2,0:T(8,128)S(1)} custom-call(f32[1,128,128]{2,1,0:T(8,128)S(1)} %copy.299), custom_call_target="InvertDiagBlocksLowerTriangular" | custom-call | tf_op jit(solution)/shard_map/triangular_solve/custom-call.0 | solution.py:164
  403.5 1.3 fusion.84
  405.9 3.4 collective-permute-start
  409.3 1.7 fusion.37
  411.1 15.5 %collective-permute-done = bf16[128,1024]{0,1:T(8,128)(2,1)S(1)} collective-permute-done((bf16[128,1024]{0,1:T(8,128)(2,1)S(1)}, bf16[128,1024]{0,1:T(8,128)(2,1)S(1)}, u32[]{:S(2)}, u32[]{:S(2)}) %collective-permute-start) | collective-permute-done | bytes 262176 | tf_op jit(solution)/shard_map/ppermute | solution.py:134
  427.5 11.7 %cholesky.189 = f32[128,128]{1,0:T(8,128)S(1)} custom-call(f32[128,128]{1,0:T(8,128)S(1)} %fusion.101), custom_call_target="Cholesky" | custom-call | tf_op jit(solution)/shard_map/jit(cholesky)/cholesky | solution.py:163
  440.9 1.3 fusion.125
  442.2 9.8 %custom-call.17 = f32[1,128,128]{1,2,0:T(8,128)S(1)} custom-call(f32[1,128,128]{2,1,0:T(8,128)S(1)} %copy.305), custom_call_target="InvertDiagBlocksLowerTriangular" | custom-call | tf_op jit(solution)/shard_map/triangular_solve/custom-call.0 | solution.py:164
  453.4 11.7 %cholesky.200 = f32[128,128]{1,0:T(8,128)S(1)} custom-call(f32[128,128]{1,0:T(8,128)S(1)} %fusion.99), custom_call_target="Cholesky" | custom-call | tf_op jit(solution)/shard_map/jit(cholesky)/cholesky | solution.py:163
  466.7 1.3 fusion.126
  468.1 10.0 %custom-call.18 = f32[1,128,128]{1,2,0:T(8,128)S(1)} custom-call(f32[1,128,128]{2,1,0:T(8,128)S(1)} %copy.311), custom_call_target="InvertDiagBlocksLowerTriangular" | custom-call | tf_op jit(solution)/shard_map/triangular_solve/custom-call.0 | solution.py:164
  479.3 11.7 %cholesky.211 = f32[128,128]{1,0:T(8,128)S(1)} custom-call(f32[128,128]{1,0:T(8,128)S(1)} %fusion.97), custom_call_target="Cholesky" | custom-call | tf_op jit(solution)/shard_map/jit(cholesky)/cholesky | solution.py:163
  492.4 9.8 %custom-call.19 = f32[1,128,128]{1,2,0:T(8,128)S(1)} custom-call(f32[1,128,128]{2,1,0:T(8,128)S(1)} %get-tuple-element.281), custom_call_target="InvertDiagBlocksLowerTriangular" | custom-call | tf_op jit(solution)/shard_map/triangular_solve/custom-call.0 | solution.py:164
  509.4 3.5 fusion.42
  512.9 1.9 fusion.35
  514.8 1.5 fusion.168
  516.3 2.9 copy.252
  519.2 5.6 copy.360
  524.8 6.7 %copy.251 = bf16[2,8,128,1024]{3,2,0,1:T(8,128)(2,1)} copy(bf16[2,8,128,1024]{2,1,0,3:T(8,128)(2,1)} %bitcast.220) | data formatting | bytes 8388608 | tf_op jit(solution)/shard_map/reshape | solution.py:137
  531.4 16.6 %fusion.2 = f32[3072,1024]{1,0:T(8,128)S(1)} fusion(bf16[2048,1024]{1,0:T(8,128)(2,1)} %bitcast.224, bf16[1024,1024]{1,0:T(8,128)(2,1)S(1)} %copy.252, f32[1,512,512]{2,1,0:T(8,128)} %get-tuple-element.292, f32[1,512,512]{2,1,0:T(8,128)} %get-tuple-element.291, f32[1,512,512]{2,1,0:T(8,128)S(1)} %fusion.35), kind=kOutput, calls=%fused_computation.8 | convolution fusion | flops 19344130048 | bytes 22020096 | tf_op jit(solution)/shard_map/dot_general | solution.py:205
  548.1 2.3 slice.757
  550.4 17.7 %fusion.15 = f32[1024,2048]{0,1:T(8,128)} fusion(f32[1024,2048]{0,1:T(8,128)} %bitcast_add_fusion.16, f32[3072,1024]{1,0:T(8,128)S(1)} %fusion.2), kind=kOutput, calls=%fused_computation.26 | convolution fusion | flops 12886999040 | bytes 29360128 | tf_op jit(solution)/shard_map/dot_general | solution.py:36
  568.3 5.0 copy.345
  573.3 1.1 dynamic-slice_select_fusion
  574.5 2.6 fusion.49
  577.1 5.9 select_bitcast_fusion
  583.0 20.5 %copy.329 = f32[1,1024,1,2048]{3,2,1,0:T(1,128)} copy(f32[1,1024,1,2048]{1,3,2,0:T(8,128)} %select_bitcast_fusion) | data formatting | bytes 16777216 | tf_op jit(solution)/shard_map/broadcast_in_dim | solution.py:218
  (192 shorter events, 47.3 us)
Async XLA Ops:
  6.5 16.5 %copy-start = (bf16[64,128,128]{2,1,0:T(8,128)(2,1)S(1)}, bf16[64,128,128]{2,1,0:T(8,128)(2,1)}, u32[]{:S(2)}) copy-start(bf16[64,128,128]{2,1,0:T(8,128)(2,1)} %param.53) | copy-start | bytes 6291460
  11.4 32.8 %all-to-all-start = ((s32[128,1,2]{2,1,0:T(1,128)}), s32[128,1,2]{2,1,0:T(1,128)S(1)}, u32[]{:S(2)}, u32[]{:S(2)}) async-start(s32[128,1,2]{2,1,0:T(1,128)} %bitcast.5), calls=%async_computation | async-start | bytes 131072 | tf_op jit(solution)/shard_map/all_to_all | solution.py:80
  44.3 109.9 %all-to-all-start.1 = ((bf16[128,2,128,128]{3,2,1,0:T(8,128)(2,1)}), bf16[128,2,128,128]{3,2,1,0:T(8,128)(2,1)}, u32[]{:S(2)}, u32[]{:S(2)}) async-start(bf16[128,2,128,128]{3,2,1,0:T(8,128)(2,1)} %select_select_fusion), calls=%async_computation.1 | async-start | bytes 16777216 | tf_op jit(solution)/shard_map/all_to_all | solution.py:73
  54.5 198.3 %all-gather.6.cloned.1.call-start = ((), (), s32[]{:S(2)}) async-start(), calls=%async_computation.2 | async-start | bytes 2228224 | tf_op jit(solution)/shard_map/all_gather | solution.py:118
  163.4 42.2 %copy-start.5 = (bf16[1024,128]{0,1:T(8,128)(2,1)}, bf16[1024,128]{0,1:T(8,128)(2,1)S(1)}, u32[]{:S(2)}) copy-start(bf16[1024,128]{0,1:T(8,128)(2,1)S(1)} %slice_add_fusion) | copy-start | bytes 786436
  179.5 162.5 %all-gather.8.cloned.1.call-start = ((), (), s32[]{:S(2)}) async-start(), calls=%async_computation.3 | async-start | bytes 2228224 | tf_op jit(solution)/shard_map/all_gather | solution.py:120
  179.6 26.0 %copy-start.10 = (s32[128]{0:T(128)}, s32[128]{0:T(128)S(1)}, u32[]{:S(2)}) copy-start(s32[128]{0:T(128)S(1)} %iota_add_fusion) | copy-start | bytes 1540
  179.8 75.1 %copy-start.6 = (pred[128,128]{0,1:T(8,128)(4,1)}, pred[128,128]{0,1:T(8,128)(4,1)S(1)}, u32[]{:S(2)}) copy-start(pred[128,128]{0,1:T(8,128)(4,1)S(1)} %copy.255) | copy-start | bytes 49156
  254.4 150.5 %all-gather.10.cloned.1.call-start = ((), (), s32[]{:S(2)}) async-start(), calls=%async_computation.4 | async-start | bytes 2359296 | tf_op jit(solution)/shard_map/all_gather | solution.py:123
  284.8 16.4 %copy-start.4 = (f32[896,128]{0,1:T(8,128)S(1)}, f32[896,128]{0,1:T(8,128)}, u32[]{:S(2)}) copy-start(f32[896,128]{0,1:T(8,128)} %copy.289) | copy-start | bytes 1376260
  297.9 18.2 %copy-start.7 = (pred[128,128]{0,1:T(8,128)(4,1)S(1)}, pred[128,128]{0,1:T(8,128)(4,1)}, u32[]{:S(2)}) copy-start(pred[128,128]{0,1:T(8,128)(4,1)} %copy-done.6) | copy-start | bytes 49156
  316.0 27.7 %copy-start.11 = (s32[128]{0:T(128)S(1)}, s32[128]{0:T(128)}, u32[]{:S(2)}) copy-start(s32[128]{0:T(128)} %copy-done.10) | copy-start | bytes 1540
  342.0 28.5 %slice-start = ((bf16[2048,512]{0,1:T(8,128)(2,1)}), bf16[1024,512]{0,1:T(8,128)(2,1)S(1)}, s32[]{:S(2)}) async-start(bf16[2048,512]{0,1:T(8,128)(2,1)} %all-gather.8.cloned.1.call-done), calls=%async_computation.6 | async-start | bytes 2097152 | tf_op jit(solution)/shard_map/slice | solution.py:120
  342.0 177.2 %all-gather.12.cloned.1.call-start = ((), (), s32[]{:S(2)}) async-start(), calls=%async_computation.5 | async-start | bytes 4456448 | tf_op jit(solution)/shard_map/all_gather | solution.py:135
  371.4 31.7 %copy-start.3 = (f32[8,128,128]{2,1,0:T(8,128)S(1)}, f32[8,128,128]{2,1,0:T(8,128)}, u32[]{:S(2)}) copy-start(f32[8,128,128]{2,1,0:T(8,128)} %get-tuple-element.321) | copy-start | bytes 1572868
  376.9 1.4 copy-start.2
  405.9 20.7 %collective-permute-start = (bf16[128,1024]{0,1:T(8,128)(2,1)S(1)}, bf16[128,1024]{0,1:T(8,128)(2,1)S(1)}, u32[]{:S(2)}, u32[]{:S(2)}) collective-permute-start(bf16[128,1024]{0,1:T(8,128)(2,1)S(1)} %constant_dynamic-slice_fusion), channel_id=1, source_target_pairs={{0,0},{1,8},{2,16},{3,24},{4,32},{5,40},{6,48},{7,56},{8,1},{9,9},... | collective-permute-start | bytes 786440 | tf_op jit(solution)/shard_map/ppermute | solution.py:134
  426.6 0.7 copy-start.8
  573.3 3.7 copy-start.9
  573.3 3.7 copy-start.12
  577.1 26.4 %copy-start.1 = (bf16[64,128,128]{2,1,0:T(8,128)(2,1)S(1)}, bf16[64,128,128]{2,1,0:T(8,128)(2,1)}, u32[]{:S(2)}) copy-start(bf16[64,128,128]{2,1,0:T(8,128)(2,1)} %param.53) | copy-start | bytes 6291460
Sparse Core Ops, SparseCore 0:
  179.6 50.6 all-gather.5
  254.5 50.8 all-gather.7
  342.1 26.9 all-gather.9
  427.4 57.7 all-gather.11

commit v11 on v10

--- a/solution.py
+++ b/solution.py
@@ -69,7 +69,6 @@
         jnp.take(placed_here, source_tile, axis=0),
         jnp.zeros((), jnp.bfloat16),
     )
-    send_blocks = jnp.where(filled, jnp.take(block_of, source_tile, axis=0), -1)
     placed = lax.all_to_all(
         send_tiles.reshape(owners, CAP, width, width),
         ("frow", "fcol"),
@@ -77,12 +76,15 @@
         concat_axis=0,
         tiled=True,
     )
-    blocks_in = lax.all_to_all(
-        send_blocks.reshape(owners, CAP),
-        ("frow", "fcol"),
-        split_axis=0,
-        concat_axis=0,
-        tiled=True,
+    targets_all = lax.all_gather(tile_target, ("frow", "fcol"), axis=0, tiled=True)
+    me = row_here * col_devs + col_here
+    mine_all = targets_all[:, 0].reshape(owners, held) == me
+    rank_all = jnp.cumsum(mine_all.astype(jnp.int32), axis=1) - 1
+    block_all = targets_all[:, 1].reshape(owners, held)
+    slot_rank = jnp.arange(CAP, dtype=jnp.int32)
+    hit = mine_all[:, None, :] & (rank_all[:, None, :] == slot_rank[None, :, None])
+    blocks_in = jnp.where(
+        jnp.any(hit, axis=2), jnp.sum(jnp.where(hit, block_all[:, None, :], 0), axis=2), -1
     )
     local = front_orig[0, :, 0, :]
     row_blocks = local.shape[0] // width

time: 620 us -> 651 us (1.050)
  blocking collectives: 15.3 us -> 140 us
  waiting for transfers between devices: 92.9 us -> 13.4 us
  starting transfers between devices: 25.2 us -> 16.6 us
    all_gather x0 -> x1, blocking collectives: none -> 127 us  [shards(): lax.all_gather(tile_target, ('frow', 'fcol'), axis=0, tiled=True)]
    all_to_all x1, waiting for transfers between devices: 77.3 us -> 0.01 us  [shards(): lax.all_to_all(send_tiles.reshape(owners, CAP, width, width), ('frow', 'f...]
    all_to_all x1 -> x0, starting transfers between devices: 10.5 us -> none  [shards(): lax.all_to_all(send_blocks.reshape(owners, CAP), ('frow', 'fcol'), split_...]
    unnamed x32 -> x35, local copies, waits for them, and re-layouts: 64.4 us -> 64.5 us
  transfers between devices with their start and end apart: 7 -> 6, of which waited for: 2 -> 1; matrix products, arithmetic and copies ran while one was open for 59% -> 52% of each run, Pallas kernels for 0% -> 0%
where the time goes in v11:
time: 651 us; the launch traced here: 644 us
  other arithmetic  226 us (35%)
  local copies, waits for them, and re-layouts  152 us (23%)
  blocking collectives  140 us (22%)
  matrix products  82 us (13%)
  starting transfers between devices  16.6 us (3%)
  between operations  14.5 us (2%)
  waiting for transfers between devices  13.4 us (2%)
    all_gather x1, blocking collectives, shards(): lax.all_gather(tile_target, ('frow', 'fcol'), axis=0, tiled=True)  127 us
    another operation x24, other arithmetic, shards(): factor = jnp.linalg.cholesky(symmetric)  100 us
    another operation x11, other arithmetic, shards(): lax.linalg.triangular_solve(factor, eye, left_side=True, lower=True)  80 us
    unnamed x35, local copies, waits for them, and re-layouts  64.5 us
    broadcast_in_dim x1, local copies, waits for them, and re-layouts, shards(): return result[None, :, None, :]  20.6 us
    dot_general x1, matrix products, subtract_product(): jnp.dot(row_factor, col_factor.T, precision=lax.Precision.HIGH, preferred...  17.7 us
    dot_general x1, matrix products, shards(): jnp.dot(rows_all, factor_inverse.T, precision=hi, preferred_element_type=...  16.6 us
    ppermute x1, waiting for transfers between devices, shards(): piece = lax.ppermute(piece, ('frow', 'fcol'), pairs)  13.2 us
  transfers between devices with their start and end apart: 6, of which 1 were waited for; matrix products, arithmetic and copies ran while one was open for 52% of the time, Pallas kernels for 0%

profile of v11, /device:TPU:6, one launch (start us, length us, event | category | flops | bytes accessed | tf_op | source)
XLA Modules:
  0.0 643.8 jit_solution(11749480308008025956)
XLA Ops:
  9.6 3.6 fusion.28
  13.2 10.1 %gather_fusion = bf16[256,128,128]{2,1,0:T(8,128)(2,1)} fusion(bf16[64,128,128]{2,1,0:T(8,128)(2,1)} %fusion.28, s32[1024]{0:T(1024)S(1)} %pad_clamp_fusion), kind=kCustom, calls=%fused_computation | custom fusion | bytes 16778240 | tf_op jit(solution)/shard_map/jit(_take)/gather | solution.py:69
  23.4 7.4 %select_select_fusion = bf16[128,2,128,128]{3,2,1,0:T(8,128)(2,1)} fusion(bf16[128,2,128,128]{3,2,1,0:T(8,128)(2,1)} %bitcast.217, pred[128,2]{1,0:T(8,128)(4,1)S(1)} %compare_and_fusion, pred[128,2]{1,0:T(8,128)(4,1)S(1)} %broadcast_in_dim.117), kind=kLoop, calls=%fused_computation.6 | loop fusion | flops 8388608 | bytes 16777728 | tf_op jit(solution)/shard_map/jit(_where)/select_n | solution.py:67
  30.8 10.9 %all-to-all-start = ((bf16[128,2,128,128]{3,2,1,0:T(8,128)(2,1)}), bf16[128,2,128,128]{3,2,1,0:T(8,128)(2,1)}, u32[]{:S(2)}, u32[]{:S(2)}) async-start(bf16[128,2,128,128]{3,2,1,0:T(8,128)(2,1)} %select_select_fusion), calls=%async_computation | async-start | bytes 16777216 | tf_op jit(solution)/shard_map/all_to_all | solution.py:72
  41.8 127.3 %all-gather.1 = s32[128,64,2]{1,2,0:T(2,128)S(1)} all-gather(s32[1,64,2]{1,2,0:T(2,128)S(1)} %bitcast.229), channel_id=1, replica_groups=mesh['frow'=16,'fcol'=8] {'frow','fcol'}, dimensions={0}, use_global_device_ids=true | all-gather | bytes 66048 | tf_op jit(solution)/shard_map/all_gather | solution.py:79
  170.3 20.7 %copy.253 = f32[1,1024,1,2048]{1,3,2,0:T(8,128)} copy(f32[1,1024,1,2048]{3,2,1,0:T(1,128)} %param.52) | data formatting | bytes 16777216 | tf_op args[0]
  191.0 7.8 %fusion.145 = f32[8,16384]{1,0:T(8,128)S(1)} fusion(s32[256]{0:T(256)S(1)} %select_n.167, s32[8]{0:T(128)S(1)} %iota_multiply_fusion, bf16[32,8,128,128]{3,2,1,0:T(8,128)(2,1)} %bitcast.76), kind=kOutput, calls=%fused_computation.242 | convolution fusion | flops 67110912 | bytes 8913952 | tf_op jit(solution)/shard_map/dot_general | solution.py:105
  199.1 1.1 slice_add_fusion
  200.2 12.8 %all_gather.22 = bf16[128,1024]{0,1:T(8,128)(2,1)S(1)} all-gather(bf16[128,128]{0,1:T(8,128)(2,1)S(1)} %slice.844), channel_id=1, replica_groups=mesh['frow'=16,'fcol'=8] {'fcol'}, dimensions={1}, use_global_device_ids=true | all-gather | bytes 294912 | tf_op jit(solution)/shard_map/all_gather | solution.py:116
  214.2 1.2 compare_reduce_fusion.9
  216.6 23.3 %copy.376 = bf16[32,8,128,128]{3,1,2,0:T(8,128)(2,1)} copy(bf16[32,8,128,128]{3,2,1,0:T(8,128)(2,1)} %bitcast.76) | data formatting | bytes 16777216
  239.9 11.9 %copy.260 = bf16[256,16384]{0,1:T(8,128)(2,1)} copy(bf16[256,16384]{1,0:T(8,128)(2,1)} %bitcast.218) | data formatting | bytes 16777216 | tf_op jit(solution)/shard_map/reshape | solution.py:106
  251.8 6.3 fusion.90
  258.1 7.5 %copy.375 = f32[128,8,16,128]{3,1,2,0:T(8,128)} copy(f32[128,8,16,128]{3,2,1,0:T(8,128)S(1)} %bitcast.222) | data formatting | bytes 16777216
  265.6 9.3 %copy.354 = f32[1024,2048]{0,1:T(8,128)} copy(f32[1024,2048]{1,0:T(8,128)} %bitcast.219) | data formatting | bytes 16777216 | tf_op jit(solution)/shard_map/reshape | solution.py:100
  274.9 12.1 %bitcast_add_fusion.16 = f32[1024,2048]{0,1:T(8,128)} fusion(f32[1024,2048]{0,1:T(8,128)} %copy.354, f32[1,1024,1,2048]{1,3,2,0:T(8,128)} %copy.253), kind=kLoop, calls=%fused_computation.284 | loop fusion | flops 2097152 | bytes 25165824 | tf_op jit(solution)/shard_map/add | solution.py:102
  287.0 1.3 slice.722
  289.4 11.7 %cholesky.134 = f32[128,128]{1,0:T(8,128)S(1)} custom-call(f32[128,128]{1,0:T(8,128)S(1)} %copy.269), custom_call_target="Cholesky" | custom-call | tf_op jit(solution)/shard_map/jit(cholesky)/cholesky | solution.py:165
  302.9 9.8 %custom-call.12 = f32[1,128,128]{1,2,0:T(8,128)S(1)} custom-call(f32[1,128,128]{2,1,0:T(8,128)S(1)} %copy.272), custom_call_target="InvertDiagBlocksLowerTriangular" | custom-call | tf_op jit(solution)/shard_map/triangular_solve/custom-call.0 | solution.py:166
  313.6 1.2 fusion.82
  314.8 2.0 copy.300
  316.8 2.3 fusion.34
  320.2 11.9 %cholesky.145 = f32[128,128]{1,0:T(8,128)S(1)} custom-call(f32[128,128]{1,0:T(8,128)S(1)} %copy.279), custom_call_target="Cholesky" | custom-call | tf_op jit(solution)/shard_map/jit(cholesky)/cholesky | solution.py:165
  332.2 2.5 scatter.54
  336.3 1.3 fusion.123
  337.8 9.8 %custom-call.13 = f32[1,128,128]{1,2,0:T(8,128)S(1)} custom-call(f32[1,128,128]{2,1,0:T(8,128)S(1)} %copy.282), custom_call_target="InvertDiagBlocksLowerTriangular" | custom-call | tf_op jit(solution)/shard_map/triangular_solve/custom-call.0 | solution.py:166
  350.6 11.7 %cholesky.156 = f32[128,128]{1,0:T(8,128)S(1)} custom-call(f32[128,128]{1,0:T(8,128)S(1)} %copy.289), custom_call_target="Cholesky" | custom-call | tf_op jit(solution)/shard_map/jit(cholesky)/cholesky | solution.py:165
  364.1 1.3 fusion.124
  365.5 9.8 %custom-call.14 = f32[1,128,128]{1,2,0:T(8,128)S(1)} custom-call(f32[1,128,128]{2,1,0:T(8,128)S(1)} %copy.292), custom_call_target="InvertDiagBlocksLowerTriangular" | custom-call | tf_op jit(solution)/shard_map/triangular_solve/custom-call.0 | solution.py:166
  378.2 11.7 %cholesky.167 = f32[128,128]{1,0:T(8,128)S(1)} custom-call(f32[128,128]{1,0:T(8,128)S(1)} %fusion.105), custom_call_target="Cholesky" | custom-call | tf_op jit(solution)/shard_map/jit(cholesky)/cholesky | solution.py:165
  391.6 1.3 fusion.125
  392.9 9.8 %custom-call.15 = f32[1,128,128]{1,2,0:T(8,128)S(1)} custom-call(f32[1,128,128]{2,1,0:T(8,128)S(1)} %copy.299), custom_call_target="InvertDiagBlocksLowerTriangular" | custom-call | tf_op jit(solution)/shard_map/triangular_solve/custom-call.0 | solution.py:166
  403.7 1.1 convolution_dynamic-update-slice_fusion
  405.7 5.4 fusion.31
  411.2 1.3 copy-done.2
  413.7 11.7 %cholesky.178 = f32[128,128]{1,0:T(8,128)S(1)} custom-call(f32[128,128]{1,0:T(8,128)S(1)} %fusion.103), custom_call_target="Cholesky" | custom-call | tf_op jit(solution)/shard_map/jit(cholesky)/cholesky | solution.py:165
  426.3 1.3 fusion.126
  427.6 9.8 %custom-call.16 = f32[1,128,128]{1,2,0:T(8,128)S(1)} custom-call(f32[1,128,128]{2,1,0:T(8,128)S(1)} %copy.310), custom_call_target="InvertDiagBlocksLowerTriangular" | custom-call | tf_op jit(solution)/shard_map/triangular_solve/custom-call.0 | solution.py:166
  437.7 1.3 fusion.84
  440.1 4.9 collective-permute-start
  445.1 1.7 fusion.37
  446.9 13.2 %collective-permute-done = bf16[128,1024]{0,1:T(8,128)(2,1)S(1)} collective-permute-done((bf16[128,1024]{0,1:T(8,128)(2,1)S(1)}, bf16[128,1024]{0,1:T(8,128)(2,1)S(1)}, u32[]{:S(2)}, u32[]{:S(2)}) %collective-permute-start) | collective-permute-done | bytes 262176 | tf_op jit(solution)/shard_map/ppermute | solution.py:136
  461.1 11.7 %cholesky.189 = f32[128,128]{1,0:T(8,128)S(1)} custom-call(f32[128,128]{1,0:T(8,128)S(1)} %fusion.101), custom_call_target="Cholesky" | custom-call | tf_op jit(solution)/shard_map/jit(cholesky)/cholesky | solution.py:165
  474.4 1.3 fusion.127
  475.8 9.8 %custom-call.17 = f32[1,128,128]{1,2,0:T(8,128)S(1)} custom-call(f32[1,128,128]{2,1,0:T(8,128)S(1)} %copy.316), custom_call_target="InvertDiagBlocksLowerTriangular" | custom-call | tf_op jit(solution)/shard_map/triangular_solve/custom-call.0 | solution.py:166
  487.0 11.7 %cholesky.200 = f32[128,128]{1,0:T(8,128)S(1)} custom-call(f32[128,128]{1,0:T(8,128)S(1)} %fusion.99), custom_call_target="Cholesky" | custom-call | tf_op jit(solution)/shard_map/jit(cholesky)/cholesky | solution.py:165
  500.3 1.3 fusion.128
  501.6 10.0 %custom-call.18 = f32[1,128,128]{1,2,0:T(8,128)S(1)} custom-call(f32[1,128,128]{2,1,0:T(8,128)S(1)} %copy.322), custom_call_target="InvertDiagBlocksLowerTriangular" | custom-call | tf_op jit(solution)/shard_map/triangular_solve/custom-call.0 | solution.py:166
  512.9 11.7 %cholesky.211 = f32[128,128]{1,0:T(8,128)S(1)} custom-call(f32[128,128]{1,0:T(8,128)S(1)} %fusion.97), custom_call_target="Cholesky" | custom-call | tf_op jit(solution)/shard_map/jit(cholesky)/cholesky | solution.py:165
  525.9 9.8 %custom-call.19 = f32[1,128,128]{1,2,0:T(8,128)S(1)} custom-call(f32[1,128,128]{2,1,0:T(8,128)S(1)} %get-tuple-element.281), custom_call_target="InvertDiagBlocksLowerTriangular" | custom-call | tf_op jit(solution)/shard_map/triangular_solve/custom-call.0 | solution.py:166
  542.9 3.5 fusion.42
  546.5 1.8 fusion.35
  548.3 1.5 fusion.170
  549.9 2.9 copy.263
  552.7 5.6 copy.371
  558.3 6.7 %copy.262 = bf16[2,8,128,1024]{3,2,0,1:T(8,128)(2,1)} copy(bf16[2,8,128,1024]{2,1,0,3:T(8,128)(2,1)} %bitcast.220) | data formatting | bytes 8388608 | tf_op jit(solution)/shard_map/reshape | solution.py:139
  565.0 16.6 %fusion.2 = f32[3072,1024]{1,0:T(8,128)S(1)} fusion(bf16[2048,1024]{1,0:T(8,128)(2,1)} %bitcast.224, bf16[1024,1024]{1,0:T(8,128)(2,1)S(1)} %copy.263, f32[1,512,512]{2,1,0:T(8,128)} %get-tuple-element.292, f32[1,512,512]{2,1,0:T(8,128)} %get-tuple-element.291, f32[1,512,512]{2,1,0:T(8,128)S(1)} %fusion.35), kind=kOutput, calls=%fused_computation.7 | convolution fusion | flops 19344130048 | bytes 22020096 | tf_op jit(solution)/shard_map/dot_general | solution.py:207
  581.7 2.3 slice.761
  584.0 17.7 %fusion.15 = f32[1024,2048]{0,1:T(8,128)} fusion(f32[1024,2048]{0,1:T(8,128)} %bitcast_add_fusion.16, f32[3072,1024]{1,0:T(8,128)S(1)} %fusion.2), kind=kOutput, calls=%fused_computation.25 | convolution fusion | flops 12886999040 | bytes 29360128 | tf_op jit(solution)/shard_map/dot_general | solution.py:36
  601.8 5.0 copy.356
  606.9 1.1 dynamic-slice_select_fusion
  608.0 2.6 fusion.49
  610.6 5.8 select_bitcast_fusion
  616.4 20.6 %copy.340 = f32[1,1024,1,2048]{3,2,1,0:T(1,128)} copy(f32[1,1024,1,2048]{1,3,2,0:T(8,128)} %select_bitcast_fusion) | data formatting | bytes 16777216 | tf_op jit(solution)/shard_map/broadcast_in_dim | solution.py:220
  (202 shorter events, 43.5 us)
Async XLA Ops:
  6.5 3.0 copy-start
  30.8 11.0 %copy-start.13 = (s32[64,2]{0,1:T(2,128)S(1)}, s32[64,2]{0,1:T(2,128)}, u32[]{:S(2)}) copy-start(s32[64,2]{0,1:T(2,128)} %param.54) | copy-start | bytes 1540
  30.8 160.2 %all-to-all-start = ((bf16[128,2,128,128]{3,2,1,0:T(8,128)(2,1)}), bf16[128,2,128,128]{3,2,1,0:T(8,128)(2,1)}, u32[]{:S(2)}, u32[]{:S(2)}) async-start(bf16[128,2,128,128]{3,2,1,0:T(8,128)(2,1)} %select_select_fusion), calls=%async_computation | async-start | bytes 16777216 | tf_op jit(solution)/shard_map/all_to_all | solution.py:72
  41.7 245.3 %all-gather.7.cloned.1.call-start = ((), (), s32[]{:S(2)}) async-start(), calls=%async_computation.1 | async-start | bytes 2228224 | tf_op jit(solution)/shard_map/all_gather | solution.py:120
  200.2 39.7 %copy-start.5 = (bf16[1024,128]{0,1:T(8,128)(2,1)}, bf16[1024,128]{0,1:T(8,128)(2,1)S(1)}, u32[]{:S(2)}) copy-start(bf16[1024,128]{0,1:T(8,128)(2,1)S(1)} %slice_add_fusion) | copy-start | bytes 786436
  213.8 162.5 %all-gather.9.cloned.1.call-start = ((), (), s32[]{:S(2)}) async-start(), calls=%async_computation.2 | async-start | bytes 2228224 | tf_op jit(solution)/shard_map/all_gather | solution.py:122
  213.9 26.0 %copy-start.10 = (s32[128]{0:T(128)}, s32[128]{0:T(128)S(1)}, u32[]{:S(2)}) copy-start(s32[128]{0:T(128)S(1)} %iota_add_fusion) | copy-start | bytes 1540
  214.1 75.1 %copy-start.6 = (pred[128,128]{0,1:T(8,128)(4,1)}, pred[128,128]{0,1:T(8,128)(4,1)S(1)}, u32[]{:S(2)}) copy-start(pred[128,128]{0,1:T(8,128)(4,1)S(1)} %copy.266) | copy-start | bytes 49156
  288.6 150.5 %all-gather.11.cloned.1.call-start = ((), (), s32[]{:S(2)}) async-start(), calls=%async_computation.3 | async-start | bytes 2359296 | tf_op jit(solution)/shard_map/all_gather | solution.py:125
  319.1 16.4 %copy-start.4 = (f32[896,128]{0,1:T(8,128)S(1)}, f32[896,128]{0,1:T(8,128)}, u32[]{:S(2)}) copy-start(f32[896,128]{0,1:T(8,128)} %copy.300) | copy-start | bytes 1376260
  332.2 18.2 %copy-start.7 = (pred[128,128]{0,1:T(8,128)(4,1)S(1)}, pred[128,128]{0,1:T(8,128)(4,1)}, u32[]{:S(2)}) copy-start(pred[128,128]{0,1:T(8,128)(4,1)} %copy-done.6) | copy-start | bytes 49156
  350.3 27.7 %copy-start.11 = (s32[128]{0:T(128)S(1)}, s32[128]{0:T(128)}, u32[]{:S(2)}) copy-start(s32[128]{0:T(128)} %copy-done.10) | copy-start | bytes 1540
  376.3 28.5 %slice-start = ((bf16[2048,512]{0,1:T(8,128)(2,1)}), bf16[1024,512]{0,1:T(8,128)(2,1)S(1)}, s32[]{:S(2)}) async-start(bf16[2048,512]{0,1:T(8,128)(2,1)} %all-gather.9.cloned.1.call-done), calls=%async_computation.5 | async-start | bytes 2097152 | tf_op jit(solution)/shard_map/slice | solution.py:122
  376.3 176.4 %all-gather.13.cloned.1.call-start = ((), (), s32[]{:S(2)}) async-start(), calls=%async_computation.4 | async-start | bytes 4456448 | tf_op jit(solution)/shard_map/all_gather | solution.py:137
  405.7 31.7 %copy-start.3 = (f32[8,128,128]{2,1,0:T(8,128)S(1)}, f32[8,128,128]{2,1,0:T(8,128)}, u32[]{:S(2)}) copy-start(f32[8,128,128]{2,1,0:T(8,128)} %get-tuple-element.319) | copy-start | bytes 1572868
  411.2 1.4 copy-start.2
  440.1 20.0 %collective-permute-start = (bf16[128,1024]{0,1:T(8,128)(2,1)S(1)}, bf16[128,1024]{0,1:T(8,128)(2,1)S(1)}, u32[]{:S(2)}, u32[]{:S(2)}) collective-permute-start(bf16[128,1024]{0,1:T(8,128)(2,1)S(1)} %constant_dynamic-slice_fusion), channel_id=1, source_target_pairs={{0,0},{1,8},{2,16},{3,24},{4,32},{5,40},{6,48},{7,56},{8,1},{9,9},... | collective-permute-start | bytes 786440 | tf_op jit(solution)/shard_map/ppermute | solution.py:136
  460.1 0.7 copy-start.8
  606.9 3.7 copy-start.9
  606.9 3.7 copy-start.12
  616.4 20.7 %copy-start.1 = (bf16[64,128,128]{2,1,0:T(8,128)(2,1)S(1)}, bf16[64,128,128]{2,1,0:T(8,128)(2,1)}, u32[]{:S(2)}) copy-start(bf16[64,128,128]{2,1,0:T(8,128)(2,1)} %param.53) | copy-start | bytes 6291460
Sparse Core Ops, SparseCore 0:
  213.9 47.9 all-gather.6
  288.7 48.2 all-gather.8
  376.4 24.1 all-gather.10
  461.0 56.9 all-gather.12

commit v12 on v10

--- a/solution.py
+++ b/solution.py
@@ -2,6 +2,7 @@
 import jax.numpy as jnp
 from jax import lax
 from jax.sharding import PartitionSpec as P
+from jax.experimental import pallas as pl
 
 PW = 512
 NPANEL = 2
@@ -40,6 +41,41 @@
         preferred_element_type=jnp.float32,
     )
     return matrix - product
+
+
+def _update_kernel(rows_ref, cols_ref, m_ref, r_ref, c_ref, o_ref):
+    r = r_ref[...]
+    c = c_ref[...]
+    r_hi = r.astype(jnp.bfloat16)
+    r_lo = (r - r_hi.astype(jnp.float32)).astype(jnp.bfloat16)
+    c_hi = c.astype(jnp.bfloat16)
+    c_lo = (c - c_hi.astype(jnp.float32)).astype(jnp.bfloat16)
+    dims = (((1,), (1,)), ((), ()))
+    acc = lax.dot_general(r_hi, c_hi, dims, preferred_element_type=jnp.float32)
+    acc = acc + lax.dot_general(r_hi, c_lo, dims, preferred_element_type=jnp.float32)
+    acc = acc + lax.dot_general(r_lo, c_hi, dims, preferred_element_type=jnp.float32)
+    keep = rows_ref[...] >= cols_ref[...]
+    o_ref[...] = jnp.where(keep, m_ref[...] - acc, 0.0)
+
+
+def lower_update(matrix, row_factor, col_factor, global_rows, global_cols):
+    n_rows, n_cols = matrix.shape
+    depth = row_factor.shape[1]
+    tm = 256
+    tn = 512
+    return pl.pallas_call(
+        _update_kernel,
+        grid=(n_rows // tm, n_cols // tn),
+        in_specs=[
+            pl.BlockSpec((tm, 1), lambda i, j: (i, 0)),
+            pl.BlockSpec((1, tn), lambda i, j: (0, j)),
+            pl.BlockSpec((tm, tn), lambda i, j: (i, j)),
+            pl.BlockSpec((tm, depth), lambda i, j: (i, 0)),
+            pl.BlockSpec((tn, depth), lambda i, j: (j, 0)),
+        ],
+        out_specs=pl.BlockSpec((tm, tn), lambda i, j: (i, j)),
+        out_shape=jax.ShapeDtypeStruct(matrix.shape, jnp.float32),
+    )(global_rows[:, None], global_cols[None, :], matrix, row_factor, col_factor)
 
 
 def shards(front_orig, child_tiles, tile_target, tile_rows, tile_cols):
@@ -205,16 +241,14 @@
     solved = jnp.dot(rows_all, factor_inverse.T, precision=hi, preferred_element_type=jnp.float32)
     row_factor = solved[:n_own]
     col_factor = solved[n_own:]
-    matrix = subtract_product(matrix, row_factor, col_factor)
+    matrix = lower_update(matrix, row_factor, col_factor, global_rows, global_cols)
     corner_rows = lax.dynamic_slice_in_dim(
         factor_full, jnp.minimum(row_here, total // width - 1) * width, width, axis=0
     )
     head = jnp.where(row_here * width < total, corner_rows, row_factor[:width])
     panel_vals = jnp.concatenate([head, row_factor[width:]], axis=0)
     own_part = lax.dynamic_slice_in_dim(panel_vals, col_here * width, width, axis=1)
-    matrix = matrix.at[:, :width].set(own_part)
-    lower_part = global_rows[:, None] >= global_cols[None, :]
-    result = jnp.where(lower_part, matrix, 0.0)
+    result = matrix.at[:, :width].set(own_part)
     return result[None, :, None, :]
 
 

time: 620 us -> 578 us (0.932)
  local copies, waits for them, and re-layouts: 154 us -> 103 us
  Pallas kernels: 0 us -> 27.8 us
  matrix products: 82 us -> 69.8 us
    pallas_call x0 -> x1, Pallas kernels: none -> 27.8 us  [lower_update(): pl.pallas_call(_update_kernel, grid=(n_rows // tm, n_cols // tn), in_spec...]
    unnamed x32 -> x20, local copies, waits for them, and re-layouts: 64.4 us -> 42.3 us
    broadcast_in_dim x1 -> x0, local copies, waits for them, and re-layouts: 20.5 us -> none  [shards(): return result[None, :, None, :]]
    dot_general x1 -> x0, matrix products: 17.7 us -> none  [subtract_product(): jnp.dot(row_factor, col_factor.T, precision=lax.Precision.HIGH, preferred...]
    ppermute x1, waiting for transfers between devices: 15.5 us -> 4.12 us  [shards(): piece = lax.ppermute(piece, ('frow', 'fcol'), pairs)]
    all_to_all x1, waiting for transfers between devices: 77.3 us -> 87.4 us  [shards(): lax.all_to_all(send_tiles.reshape(owners, CAP, width, width), ('frow', 'f...]
    reshape x1 -> x0, local copies, waits for them, and re-layouts: 9.27 us -> none  [shards(): added = summed.reshape(row_blocks, col_blocks, width, width).transpose(0,...]
    scatter x6 -> x1, local copies, waits for them, and re-layouts: 4.47 us -> 12.5 us  [shards(): result = matrix.at[:, :width].set(own_part)]
  transfers between devices with their start and end apart: 7 -> 7, of which waited for: 2 -> 2; matrix products, arithmetic and copies ran while one was open for 59% -> 58% of each run, Pallas kernels for 0% -> 0%
where the time goes in v12:
time: 578 us; the launch traced here: 569 us
  other arithmetic  223 us (39%)
  local copies, waits for them, and re-layouts  103 us (18%)
  waiting for transfers between devices  91.6 us (16%)
  matrix products  69.8 us (12%)
  Pallas kernels  27.8 us (5%)
  starting transfers between devices  26.2 us (5%)
  between operations  14.1 us (2%)
  blocking collectives  13.8 us (2%)
    another operation x24, other arithmetic, shards(): factor = jnp.linalg.cholesky(symmetric)  99.6 us
    all_to_all x1, waiting for transfers between devices, shards(): lax.all_to_all(send_tiles.reshape(owners, CAP, width, width), ('frow', 'f...  87.4 us
    another operation x10, other arithmetic, shards(): lax.linalg.triangular_solve(factor, eye, left_side=True, lower=True)  79.5 us
    unnamed x20, local copies, waits for them, and re-layouts  42.3 us
    pallas_call x1, Pallas kernels, lower_update(): pl.pallas_call(_update_kernel, grid=(n_rows // tm, n_cols // tn), in_spec...  27.8 us
    add x1, other arithmetic, shards(): matrix = local + added  17.4 us
    dot_general x1, matrix products, shards(): jnp.dot(rows_all, factor_inverse.T, precision=hi, preferred_element_type=...  14.4 us
    all_gather x1, blocking collectives, shards(): lax.all_gather(first_column[:width].astype(jnp.bfloat16), 'fcol', axis=1,...  13.8 us
  transfers between devices with their start and end apart: 7, of which 2 were waited for; matrix products, arithmetic and copies ran while one was open for 58% of the time, Pallas kernels for 0%

profile of v12, /device:TPU:6, one launch (start us, length us, event | category | flops | bytes accessed | tf_op | source)
XLA Modules:
  0.0 569.5 jit_solution(7611932788611495554)
XLA Ops:
  8.8 1.9 gather_fusion
  11.4 10.5 %all-to-all-start = ((s32[128,1,2]{2,1,0:T(1,128)}), s32[128,1,2]{2,1,0:T(1,128)S(1)}, u32[]{:S(2)}, u32[]{:S(2)}) async-start(s32[128,1,2]{2,1,0:T(1,128)} %bitcast.4), calls=%async_computation | async-start | bytes 131072 | tf_op jit(solution)/shard_map/all_to_all | solution.py:116
  23.1 3.6 fusion.20
  26.7 10.1 %gather_fusion.1 = bf16[256,128,128]{2,1,0:T(8,128)(2,1)} fusion(bf16[64,128,128]{2,1,0:T(8,128)(2,1)} %fusion.20, s32[1024]{0:T(1024)S(1)} %pad_clamp_fusion), kind=kCustom, calls=%fused_computation.1 | custom fusion | bytes 16778240 | tf_op jit(solution)/shard_map/jit(_take)/gather | solution.py:105
  36.8 7.4 %select_select_fusion = bf16[128,2,128,128]{3,2,1,0:T(8,128)(2,1)} fusion(bf16[128,2,128,128]{3,2,1,0:T(8,128)(2,1)} %bitcast.218, pred[128,2]{1,0:T(8,128)(4,1)S(1)} %compare_and_fusion, pred[128,2]{1,0:T(8,128)(4,1)S(1)} %broadcast_in_dim.104), kind=kLoop, calls=%fused_computation.5 | loop fusion | flops 8388608 | bytes 16777728 | tf_op jit(solution)/shard_map/jit(_where)/select_n | solution.py:103
  44.3 10.2 %all-to-all-start.1 = ((bf16[128,2,128,128]{3,2,1,0:T(8,128)(2,1)}), bf16[128,2,128,128]{3,2,1,0:T(8,128)(2,1)}, u32[]{:S(2)}, u32[]{:S(2)}) async-start(bf16[128,2,128,128]{3,2,1,0:T(8,128)(2,1)} %select_select_fusion), calls=%async_computation.1 | async-start | bytes 16777216 | tf_op jit(solution)/shard_map/all_to_all | solution.py:109
  54.7 10.7 %copy.259 = f32[1,1024,1,2048]{3,1,2,0:T(8,128)} copy(f32[1,1024,1,2048]{3,2,1,0:T(1,128)} %param.52) | data formatting | bytes 16777216
  66.8 87.4 %all-to-all-done.1 = bf16[128,2,128,128]{3,2,1,0:T(8,128)(2,1)} async-done(((bf16[128,2,128,128]{3,2,1,0:T(8,128)(2,1)}), bf16[128,2,128,128]{3,2,1,0:T(8,128)(2,1)}, u32[]{:S(2)}, u32[]{:S(2)}) %all-to-all-start.1) | async-done | bytes 8388640 | tf_op jit(solution)/shard_map/all_to_all | solution.py:109
  154.2 7.8 %fusion.135 = f32[8,16384]{1,0:T(8,128)S(1)} fusion(s32[256]{0:T(256)S(1)} %eq.128, s32[8]{0:T(128)S(1)} %iota_multiply_fusion, bf16[32,8,128,128]{3,2,1,0:T(8,128)(2,1)} %bitcast.78), kind=kOutput, calls=%fused_computation.235 | convolution fusion | flops 67110912 | bytes 8913952 | tf_op jit(solution)/shard_map/dot_general | solution.py:139
  162.1 1.1 slice_add_fusion
  163.2 13.8 %all_gather.18 = bf16[128,1024]{1,0:T(8,128)(2,1)S(1)} all-gather(bf16[128,128]{1,0:T(8,128)(2,1)S(1)} %slice.832), channel_id=1, replica_groups=mesh['frow'=16,'fcol'=8] {'fcol'}, dimensions={1}, use_global_device_ids=true | all-gather | bytes 294912 | tf_op jit(solution)/shard_map/all_gather | solution.py:150
  179.2 23.3 %copy.258 = bf16[32,8,128,128]{3,1,2,0:T(8,128)(2,1)} copy(bf16[32,8,128,128]{3,2,1,0:T(8,128)(2,1)} %bitcast.78) | data formatting | bytes 16777216
  202.5 11.9 %copy.185 = bf16[256,16384]{0,1:T(8,128)(2,1)} copy(bf16[256,16384]{1,0:T(8,128)(2,1)} %bitcast.219) | data formatting | bytes 16777216 | tf_op jit(solution)/shard_map/reshape | solution.py:140
  214.4 9.7 %fusion.93 = f32[8,16,128,128]{3,1,2,0:T(8,128)} fusion(bf16[128,128,256,1]{2,1,0,3:T(8,128)(2,1)} %bitcast.222, s32[8,16]{1,0:T(8,128)S(1)} %multiply_add_fusion, s32[256]{0:T(256)S(1)} %eq.128), kind=kOutput, calls=%fused_computation.125 | convolution fusion | flops 1073774592 | bytes 16778752 | tf_op jit(solution)/shard_map/dot_general | solution.py:128
  224.1 17.4 %bitcast_add_fusion.m_ref = f32[1024,2048]{1,0:T(8,128)} fusion(f32[128,8,16,128]{3,2,1,0:T(8,128)} %bitcast.221, f32[1,1024,1,2048]{3,2,1,0:T(1,128)} %param.52), kind=kLoop, calls=%fused_computation.2 | loop fusion | flops 2097152 | bytes 25165824 | tf_op jit(solution)/shard_map/add | solution.py:136
  241.5 1.3 slice.718
  245.3 11.7 %cholesky.134 = f32[128,128]{1,0:T(8,128)S(1)} custom-call(f32[128,128]{1,0:T(8,128)S(1)} %fusion.114), custom_call_target="Cholesky" | custom-call | tf_op jit(solution)/shard_map/jit(cholesky)/cholesky | solution.py:199
  258.4 9.8 %custom-call.12 = f32[1,128,128]{1,2,0:T(8,128)S(1)} custom-call(f32[1,128,128]{2,1,0:T(8,128)S(1)} %get-tuple-element.281), custom_call_target="InvertDiagBlocksLowerTriangular" | custom-call | tf_op jit(solution)/shard_map/triangular_solve/custom-call.0 | solution.py:200
  268.2 2.6 scatter.54
  271.7 1.2 constant_dynamic-update-slice_fusion
  272.9 1.3 fusion.25
  274.4 11.9 %cholesky.145 = f32[128,128]{1,0:T(8,128)S(1)} custom-call(f32[128,128]{1,0:T(8,128)S(1)} %fusion.112), custom_call_target="Cholesky" | custom-call | tf_op jit(solution)/shard_map/jit(cholesky)/cholesky | solution.py:199
  286.9 1.2 fusion.123
  288.1 9.8 %custom-call.13 = f32[1,128,128]{1,2,0:T(8,128)S(1)} custom-call(f32[1,128,128]{2,1,0:T(8,128)S(1)} %get-tuple-element.310), custom_call_target="InvertDiagBlocksLowerTriangular" | custom-call | tf_op jit(solution)/shard_map/triangular_solve/custom-call.0 | solution.py:200
  298.9 1.3 constant_dynamic-update-slice_fusion.5
  301.3 11.7 %cholesky.156 = f32[128,128]{1,0:T(8,128)S(1)} custom-call(f32[128,128]{1,0:T(8,128)S(1)} %fusion.110), custom_call_target="Cholesky" | custom-call | tf_op jit(solution)/shard_map/jit(cholesky)/cholesky | solution.py:199
  313.7 1.3 fusion.124
  315.0 9.8 %custom-call.14 = f32[1,128,128]{1,2,0:T(8,128)S(1)} custom-call(f32[1,128,128]{2,1,0:T(8,128)S(1)} %get-tuple-element.308), custom_call_target="InvertDiagBlocksLowerTriangular" | custom-call | tf_op jit(solution)/shard_map/triangular_solve/custom-call.0 | solution.py:200
  325.7 1.2 constant_dynamic-update-slice_fusion.4
  327.7 11.7 %cholesky.167 = f32[128,128]{1,0:T(8,128)S(1)} custom-call(f32[128,128]{1,0:T(8,128)S(1)} %copy.205), custom_call_target="Cholesky" | custom-call | tf_op jit(solution)/shard_map/jit(cholesky)/cholesky | solution.py:199
  340.1 1.3 fusion.125
  341.4 10.2 %custom-call.15 = f32[1,128,128]{1,2,0:T(8,128)S(1)} custom-call(f32[1,128,128]{2,1,0:T(8,128)S(1)} %get-tuple-element.306), custom_call_target="InvertDiagBlocksLowerTriangular" | custom-call | tf_op jit(solution)/shard_map/triangular_solve/custom-call.0 | solution.py:200
  352.5 1.1 convolution_dynamic-update-slice_fusion
  353.6 5.3 convert_subtract_fusion
  359.3 11.7 %cholesky.178 = f32[128,128]{1,0:T(8,128)S(1)} custom-call(f32[128,128]{1,0:T(8,128)S(1)} %copy.209), custom_call_target="Cholesky" | custom-call | tf_op jit(solution)/shard_map/jit(cholesky)/cholesky | solution.py:199
  372.7 4.7 collective-permute-start
  377.4 1.3 fusion.126
  378.7 9.8 %custom-call.16 = f32[1,128,128]{1,2,0:T(8,128)S(1)} custom-call(f32[1,128,128]{2,1,0:T(8,128)S(1)} %get-tuple-element.304), custom_call_target="InvertDiagBlocksLowerTriangular" | custom-call | tf_op jit(solution)/shard_map/triangular_solve/custom-call.0 | solution.py:200
  389.5 4.1 collective-permute-done
  396.4 11.7 %cholesky.189 = f32[128,128]{1,0:T(8,128)S(1)} custom-call(f32[128,128]{1,0:T(8,128)S(1)} %copy.214), custom_call_target="Cholesky" | custom-call | tf_op jit(solution)/shard_map/jit(cholesky)/cholesky | solution.py:199
  408.8 1.2 fusion.127
  410.0 9.8 %custom-call.17 = f32[1,128,128]{1,2,0:T(8,128)S(1)} custom-call(f32[1,128,128]{2,1,0:T(8,128)S(1)} %get-tuple-element.302), custom_call_target="InvertDiagBlocksLowerTriangular" | custom-call | tf_op jit(solution)/shard_map/triangular_solve/custom-call.0 | solution.py:200
  422.4 11.9 %cholesky.200 = f32[128,128]{1,0:T(8,128)S(1)} custom-call(f32[128,128]{1,0:T(8,128)S(1)} %copy.218), custom_call_target="Cholesky" | custom-call | tf_op jit(solution)/shard_map/jit(cholesky)/cholesky | solution.py:199
  435.0 1.2 fusion.128
  436.2 9.8 %custom-call.18 = f32[1,128,128]{1,2,0:T(8,128)S(1)} custom-call(f32[1,128,128]{2,1,0:T(8,128)S(1)} %get-tuple-element.300), custom_call_target="InvertDiagBlocksLowerTriangular" | custom-call | tf_op jit(solution)/shard_map/triangular_solve/custom-call.0 | solution.py:200
  448.3 11.7 %cholesky.211 = f32[128,128]{1,0:T(8,128)S(1)} custom-call(f32[128,128]{1,0:T(8,128)S(1)} %fusion.100), custom_call_target="Cholesky" | custom-call | tf_op jit(solution)/shard_map/jit(cholesky)/cholesky | solution.py:199
  460.7 1.2 fusion.129
  462.0 9.8 %custom-call.19 = f32[1,128,128]{1,2,0:T(8,128)S(1)} custom-call(f32[1,128,128]{2,1,0:T(8,128)S(1)} %get-tuple-element.298), custom_call_target="InvertDiagBlocksLowerTriangular" | custom-call | tf_op jit(solution)/shard_map/triangular_solve/custom-call.0 | solution.py:200
  473.6 1.5 fusion.62
  475.2 1.1 fusion.154
  476.3 2.0 convolution_negate_fusion.6
  481.5 3.1 fusion.33
  484.6 1.8 fusion.26
  486.4 1.5 fusion.152
  488.0 2.8 copy.186
  491.5 14.4 %fusion = f32[3072,1024]{1,0:T(8,128)S(1)} fusion(bf16[2048,1024]{1,0:T(8,128)(2,1)S(1)} %bitcast.224, bf16[1024,1024]{1,0:T(8,128)(2,1)S(1)} %copy-done.7, f32[1,512,512]{2,1,0:T(8,128)S(1)} %copy-done.5, f32[1,512,512]{2,1,0:T(8,128)S(1)} %copy-done.4, f32[1,512,512]{2,1,0:T(8,128)S(1)} %fusion.26), kind=kOutput, calls=%fused_computation.6 | convolution fusion | flops 19344130048 | bytes 22020096 | tf_op jit(solution)/shard_map/dot_general | solution.py:241
  505.8 2.5 slice.754.r_ref
  508.3 3.3 copy-done.2
  511.7 4.2 slice.755.c_ref
  515.9 27.8 %shard_map.55 = f32[1024,2048]{1,0:T(8,128)} custom-call(s32[1024,1]{1,0:T(8,128)} %fusion.47.rows_ref, s32[1,2048]{1,0:T(1,128)} %fusion.131.cols_ref, f32[1024,2048]{1,0:T(8,128)} %bitcast_add_fusion.m_ref, f32[1024,1024]{1,0:T(8,128)} %slice.754.r_ref, f32[2048,1024]{1,0:T(8,128)} %slice.755.c_ref), custom_call_target="tpu_custom_call" | custom-call | tf_op jit(solution)/shard_map/pallas_call | solution.py:66
  543.7 3.5 copy.281
  547.2 1.3 slice_select_fusion
  548.5 1.7 fusion.52
  550.2 12.5 %copy.229 = f32[1,1024,1,2048]{3,2,1,0:T(1,128)} copy(f32[1,1024,1,2048]{3,1,2,0:T(8,128)S(1)} %fusion.52) | data formatting | bytes 16777216 | tf_op jit(solution)/shard_map/scatter | solution.py:251
  (149 shorter events, 37.7 us)
Async XLA Ops:
  6.5 16.5 %copy-start = (bf16[64,128,128]{2,1,0:T(8,128)(2,1)S(1)}, bf16[64,128,128]{2,1,0:T(8,128)(2,1)}, u32[]{:S(2)}) copy-start(bf16[64,128,128]{2,1,0:T(8,128)(2,1)} %param.53) | copy-start | bytes 6291460
  11.4 32.8 %all-to-all-start = ((s32[128,1,2]{2,1,0:T(1,128)}), s32[128,1,2]{2,1,0:T(1,128)S(1)}, u32[]{:S(2)}, u32[]{:S(2)}) async-start(s32[128,1,2]{2,1,0:T(1,128)} %bitcast.4), calls=%async_computation | async-start | bytes 131072 | tf_op jit(solution)/shard_map/all_to_all | solution.py:116
  44.3 109.9 %all-to-all-start.1 = ((bf16[128,2,128,128]{3,2,1,0:T(8,128)(2,1)}), bf16[128,2,128,128]{3,2,1,0:T(8,128)(2,1)}, u32[]{:S(2)}, u32[]{:S(2)}) async-start(bf16[128,2,128,128]{3,2,1,0:T(8,128)(2,1)} %select_select_fusion), calls=%async_computation.1 | async-start | bytes 16777216 | tf_op jit(solution)/shard_map/all_to_all | solution.py:109
  54.5 187.0 %all-gather.6.cloned.1.call-start = ((), (), s32[]{:S(2)}) async-start(), calls=%async_computation.2 | async-start | bytes 2228224 | tf_op jit(solution)/shard_map/all_gather | solution.py:154
  163.2 39.3 %copy-start.3 = (bf16[1024,128]{1,0:T(8,128)(2,1)}, bf16[1024,128]{1,0:T(8,128)(2,1)S(1)}, u32[]{:S(2)}) copy-start(bf16[1024,128]{1,0:T(8,128)(2,1)S(1)} %slice_add_fusion) | copy-start | bytes 786436
  177.8 123.4 %all-gather.8.cloned.1.call-start = ((), (), s32[]{:S(2)}) async-start(), calls=%async_computation.3 | async-start | bytes 2228224 | tf_op jit(solution)/shard_map/all_gather | solution.py:156
  242.8 128.9 %all-gather.10.cloned.1.call-start = ((), (), s32[]{:S(2)}) async-start(), calls=%async_computation.4 | async-start | bytes 2359296 | tf_op jit(solution)/shard_map/all_gather | solution.py:159
  301.2 52.4 %slice-start.1 = ((bf16[2048,512]{1,0:T(8,128)(2,1)}), bf16[1024,512]{1,0:T(8,128)(2,1)S(1)}, s32[]{:S(2)}) async-start(bf16[2048,512]{1,0:T(8,128)(2,1)} %all-gather.8.cloned.1.call-done), calls=%async_computation.7 | async-start | bytes 2097152 | tf_op jit(solution)/shard_map/slice | solution.py:156
  301.2 186.8 %all-gather.12.cloned.1.call-start = ((), (), s32[]{:S(2)}) async-start(), calls=%async_computation.5 | async-start | bytes 4456448 | tf_op jit(solution)/shard_map/all_gather | solution.py:171
  372.7 20.9 %collective-permute-start = (bf16[128,1024]{1,0:T(8,128)(2,1)S(1)}, bf16[128,1024]{1,0:T(8,128)(2,1)S(1)}, u32[]{:S(2)}, u32[]{:S(2)}) collective-permute-start(bf16[128,1024]{1,0:T(8,128)(2,1)S(1)} %constant_dynamic-slice_fusion), channel_id=1, source_target_pairs={{0,0},{1,8},{2,16},{3,24},{4,32},{5,40},{6,48},{7,56},{8,1},{9,9},... | collective-permute-start | bytes 786440 | tf_op jit(solution)/shard_map/ppermute | solution.py:170
  393.6 0.7 copy-start.6
  488.0 2.9 copy-start.4
  488.0 2.9 copy-start.5
  488.0 3.5 copy-start.7
  505.8 5.8 %copy-start.2 = (f32[3072,1024]{1,0:T(8,128)}, f32[3072,1024]{1,0:T(8,128)S(1)}, u32[]{:S(2)}) copy-start(f32[3072,1024]{1,0:T(8,128)S(1)} %fusion) | copy-start | bytes 37748740
  543.7 4.8 slice-start
  550.2 12.5 %copy-start.1 = (bf16[64,128,128]{2,1,0:T(8,128)(2,1)S(1)}, bf16[64,128,128]{2,1,0:T(8,128)(2,1)}, u32[]{:S(2)}) copy-start(bf16[64,128,128]{2,1,0:T(8,128)(2,1)} %param.53) | copy-start | bytes 6291460
Sparse Core Ops, SparseCore 0:
  177.9 48.1 all-gather.5
  242.9 48.2 all-gather.7
  301.3 29.6 all-gather.9
  394.4 51.8 all-gather.11

commit v13 on v12

--- a/solution.py
+++ b/solution.py
@@ -43,26 +43,31 @@
     return matrix - product
 
 
-def _update_kernel(rows_ref, cols_ref, m_ref, r_ref, c_ref, o_ref):
-    r = r_ref[...]
-    c = c_ref[...]
-    r_hi = r.astype(jnp.bfloat16)
-    r_lo = (r - r_hi.astype(jnp.float32)).astype(jnp.bfloat16)
-    c_hi = c.astype(jnp.bfloat16)
-    c_lo = (c - c_hi.astype(jnp.float32)).astype(jnp.bfloat16)
+def _update_kernel(rows_ref, cols_ref, m_ref, rh_ref, rl_ref, ch_ref, cl_ref, o_ref):
     dims = (((1,), (1,)), ((), ()))
+    r_hi = rh_ref[...]
+    c_hi = ch_ref[...]
     acc = lax.dot_general(r_hi, c_hi, dims, preferred_element_type=jnp.float32)
-    acc = acc + lax.dot_general(r_hi, c_lo, dims, preferred_element_type=jnp.float32)
-    acc = acc + lax.dot_general(r_lo, c_hi, dims, preferred_element_type=jnp.float32)
+    acc = acc + lax.dot_general(r_hi, cl_ref[...], dims, preferred_element_type=jnp.float32)
+    acc = acc + lax.dot_general(rl_ref[...], c_hi, dims, preferred_element_type=jnp.float32)
     keep = rows_ref[...] >= cols_ref[...]
     o_ref[...] = jnp.where(keep, m_ref[...] - acc, 0.0)
+
+
+def split_bf16(x):
+    hi = x.astype(jnp.bfloat16)
+    return hi, (x - hi.astype(jnp.float32)).astype(jnp.bfloat16)
 
 
 def lower_update(matrix, row_factor, col_factor, global_rows, global_cols):
     n_rows, n_cols = matrix.shape
     depth = row_factor.shape[1]
-    tm = 256
+    tm = 512
     tn = 512
+    r_hi, r_lo = split_bf16(row_factor)
+    c_hi, c_lo = split_bf16(col_factor)
+    row_spec = pl.BlockSpec((tm, depth), lambda i, j: (i, 0))
+    col_spec = pl.BlockSpec((tn, depth), lambda i, j: (j, 0))
     return pl.pallas_call(
         _update_kernel,
         grid=(n_rows // tm, n_cols // tn),
@@ -70,12 +75,14 @@
             pl.BlockSpec((tm, 1), lambda i, j: (i, 0)),
             pl.BlockSpec((1, tn), lambda i, j: (0, j)),
             pl.BlockSpec((tm, tn), lambda i, j: (i, j)),
-            pl.BlockSpec((tm, depth), lambda i, j: (i, 0)),
-            pl.BlockSpec((tn, depth), lambda i, j: (j, 0)),
+            row_spec,
+            row_spec,
+            col_spec,
+            col_spec,
         ],
         out_specs=pl.BlockSpec((tm, tn), lambda i, j: (i, j)),
         out_shape=jax.ShapeDtypeStruct(matrix.shape, jnp.float32),
-    )(global_rows[:, None], global_cols[None, :], matrix, row_factor, col_factor)
+    )(global_rows[:, None], global_cols[None, :], matrix, r_hi, r_lo, c_hi, c_lo)
 
 
 def shards(front_orig, child_tiles, tile_target, tile_rows, tile_cols):

time: 578 us -> 574 us (level)
  other arithmetic: 223 us -> 232 us
  Pallas kernels: 27.8 us -> 20.5 us
    convert_element_type x0 -> x2, other arithmetic: none -> 7.73 us  [split_bf16(): return (hi, (x - hi.astype(jnp.float32)).astype(jnp.bfloat16))]
    pallas_call x1, Pallas kernels: 27.8 us -> 20.5 us  [lower_update(): pl.pallas_call(_update_kernel, grid=(n_rows // tm, n_cols // tn), in_spec...]
    slice x2 -> x0, local copies, waits for them, and re-layouts: 6.72 us -> none  [the longest x1 4.24 us: shards(): col_factor = solved[n_own:]]
    unnamed x20 -> x18, local copies, waits for them, and re-layouts: 42.3 us -> 47.3 us
where the time goes in v13:
time: 574 us; the launch traced here: 566 us
  other arithmetic  232 us (40%)
  local copies, waits for them, and re-layouts  98.1 us (17%)
  waiting for transfers between devices  91.6 us (16%)
  matrix products  69.7 us (12%)
  starting transfers between devices  26.2 us (5%)
  Pallas kernels  20.5 us (4%)
  between operations  14.2 us (2%)
  blocking collectives  13.8 us (2%)
    another operation x24, other arithmetic, shards(): factor = jnp.linalg.cholesky(symmetric)  99.8 us
    all_to_all x1, waiting for transfers between devices, shards(): lax.all_to_all(send_tiles.reshape(owners, CAP, width, width), ('frow', 'f...  87.4 us
    another operation x10, other arithmetic, shards(): lax.linalg.triangular_solve(factor, eye, left_side=True, lower=True)  79.5 us
    unnamed x18, local copies, waits for them, and re-layouts  47.3 us
    pallas_call x1, Pallas kernels, lower_update(): pl.pallas_call(_update_kernel, grid=(n_rows // tm, n_cols // tn), in_spec...  20.5 us
    add x1, other arithmetic, shards(): matrix = local + added  17.4 us
    dot_general x1, matrix products, shards(): jnp.dot(rows_all, factor_inverse.T, precision=hi, preferred_element_type=...  14.4 us
    all_gather x1, blocking collectives, shards(): lax.all_gather(first_column[:width].astype(jnp.bfloat16), 'fcol', axis=1,...  13.8 us
  transfers between devices with their start and end apart: 7, of which 2 were waited for; matrix products, arithmetic and copies ran while one was open for 58% of the time, Pallas kernels for 0%

profile of v13, /device:TPU:6, one launch (start us, length us, event | category | flops | bytes accessed | tf_op | source)
XLA Modules:
  0.0 566.3 jit_solution(13541433390574427058)
XLA Ops:
  8.8 1.9 gather_fusion
  11.4 10.5 %all-to-all-start = ((s32[128,1,2]{2,1,0:T(1,128)}), s32[128,1,2]{2,1,0:T(1,128)S(1)}, u32[]{:S(2)}, u32[]{:S(2)}) async-start(s32[128,1,2]{2,1,0:T(1,128)} %bitcast.4), calls=%async_computation | async-start | bytes 131072 | tf_op jit(solution)/shard_map/all_to_all | solution.py:123
  23.1 3.6 fusion.20
  26.7 10.1 %gather_fusion.1 = bf16[256,128,128]{2,1,0:T(8,128)(2,1)} fusion(bf16[64,128,128]{2,1,0:T(8,128)(2,1)} %fusion.20, s32[1024]{0:T(1024)S(1)} %pad_clamp_fusion), kind=kCustom, calls=%fused_computation.1 | custom fusion | bytes 16778240 | tf_op jit(solution)/shard_map/jit(_take)/gather | solution.py:112
  36.8 7.4 %select_select_fusion = bf16[128,2,128,128]{3,2,1,0:T(8,128)(2,1)} fusion(bf16[128,2,128,128]{3,2,1,0:T(8,128)(2,1)} %bitcast.218, pred[128,2]{1,0:T(8,128)(4,1)S(1)} %compare_and_fusion, pred[128,2]{1,0:T(8,128)(4,1)S(1)} %broadcast_in_dim.104), kind=kLoop, calls=%fused_computation.6 | loop fusion | flops 8388608 | bytes 16777728 | tf_op jit(solution)/shard_map/jit(_where)/select_n | solution.py:110
  44.3 10.2 %all-to-all-start.1 = ((bf16[128,2,128,128]{3,2,1,0:T(8,128)(2,1)}), bf16[128,2,128,128]{3,2,1,0:T(8,128)(2,1)}, u32[]{:S(2)}, u32[]{:S(2)}) async-start(bf16[128,2,128,128]{3,2,1,0:T(8,128)(2,1)} %select_select_fusion), calls=%async_computation.1 | async-start | bytes 16777216 | tf_op jit(solution)/shard_map/all_to_all | solution.py:116
  54.7 10.7 %copy.259 = f32[1,1024,1,2048]{3,1,2,0:T(8,128)} copy(f32[1,1024,1,2048]{3,2,1,0:T(1,128)} %param.52) | data formatting | bytes 16777216
  66.8 87.4 %all-to-all-done.1 = bf16[128,2,128,128]{3,2,1,0:T(8,128)(2,1)} async-done(((bf16[128,2,128,128]{3,2,1,0:T(8,128)(2,1)}), bf16[128,2,128,128]{3,2,1,0:T(8,128)(2,1)}, u32[]{:S(2)}, u32[]{:S(2)}) %all-to-all-start.1) | async-done | bytes 8388640 | tf_op jit(solution)/shard_map/all_to_all | solution.py:116
  154.2 7.8 %fusion.135 = f32[8,16384]{1,0:T(8,128)S(1)} fusion(s32[256]{0:T(256)S(1)} %eq.128, s32[8]{0:T(128)S(1)} %iota_multiply_fusion, bf16[32,8,128,128]{3,2,1,0:T(8,128)(2,1)} %bitcast.78), kind=kOutput, calls=%fused_computation.239 | convolution fusion | flops 67110912 | bytes 8913952 | tf_op jit(solution)/shard_map/dot_general | solution.py:146
  162.1 1.1 slice_add_fusion
  163.2 13.8 %all_gather.18 = bf16[128,1024]{1,0:T(8,128)(2,1)S(1)} all-gather(bf16[128,128]{1,0:T(8,128)(2,1)S(1)} %slice.838), channel_id=1, replica_groups=mesh['frow'=16,'fcol'=8] {'fcol'}, dimensions={1}, use_global_device_ids=true | all-gather | bytes 294912 | tf_op jit(solution)/shard_map/all_gather | solution.py:157
  179.2 23.3 %copy.258 = bf16[32,8,128,128]{3,1,2,0:T(8,128)(2,1)} copy(bf16[32,8,128,128]{3,2,1,0:T(8,128)(2,1)} %bitcast.78) | data formatting | bytes 16777216
  202.5 11.9 %copy.185 = bf16[256,16384]{0,1:T(8,128)(2,1)} copy(bf16[256,16384]{1,0:T(8,128)(2,1)} %bitcast.219) | data formatting | bytes 16777216 | tf_op jit(solution)/shard_map/reshape | solution.py:147
  214.4 9.7 %fusion.93 = f32[8,16,128,128]{3,1,2,0:T(8,128)} fusion(bf16[128,128,256,1]{2,1,0,3:T(8,128)(2,1)} %bitcast.222, s32[8,16]{1,0:T(8,128)S(1)} %multiply_add_fusion, s32[256]{0:T(256)S(1)} %eq.128), kind=kOutput, calls=%fused_computation.129 | convolution fusion | flops 1073774592 | bytes 16778752 | tf_op jit(solution)/shard_map/dot_general | solution.py:135
  224.1 17.4 %bitcast_add_fusion.m_ref = f32[1024,2048]{1,0:T(8,128)} fusion(f32[128,8,16,128]{3,2,1,0:T(8,128)} %bitcast.221, f32[1,1024,1,2048]{3,2,1,0:T(1,128)} %param.52), kind=kLoop, calls=%fused_computation.2 | loop fusion | flops 2097152 | bytes 25165824 | tf_op jit(solution)/shard_map/add | solution.py:143
  241.5 1.3 slice.718
  245.4 11.7 %cholesky.134 = f32[128,128]{1,0:T(8,128)S(1)} custom-call(f32[128,128]{1,0:T(8,128)S(1)} %fusion.114), custom_call_target="Cholesky" | custom-call | tf_op jit(solution)/shard_map/jit(cholesky)/cholesky | solution.py:206
  258.4 9.8 %custom-call.12 = f32[1,128,128]{1,2,0:T(8,128)S(1)} custom-call(f32[1,128,128]{2,1,0:T(8,128)S(1)} %get-tuple-element.285), custom_call_target="InvertDiagBlocksLowerTriangular" | custom-call | tf_op jit(solution)/shard_map/triangular_solve/custom-call.0 | solution.py:207
  268.2 2.5 scatter.54
  271.6 1.2 constant_dynamic-update-slice_fusion
  272.8 1.3 fusion.25
  274.3 11.9 %cholesky.145 = f32[128,128]{1,0:T(8,128)S(1)} custom-call(f32[128,128]{1,0:T(8,128)S(1)} %fusion.112), custom_call_target="Cholesky" | custom-call | tf_op jit(solution)/shard_map/jit(cholesky)/cholesky | solution.py:206
  286.8 1.2 fusion.123
  288.0 9.8 %custom-call.13 = f32[1,128,128]{1,2,0:T(8,128)S(1)} custom-call(f32[1,128,128]{2,1,0:T(8,128)S(1)} %get-tuple-element.314), custom_call_target="InvertDiagBlocksLowerTriangular" | custom-call | tf_op jit(solution)/shard_map/triangular_solve/custom-call.0 | solution.py:207
  298.8 1.3 constant_dynamic-update-slice_fusion.5
  301.2 11.7 %cholesky.156 = f32[128,128]{1,0:T(8,128)S(1)} custom-call(f32[128,128]{1,0:T(8,128)S(1)} %fusion.110), custom_call_target="Cholesky" | custom-call | tf_op jit(solution)/shard_map/jit(cholesky)/cholesky | solution.py:206
  313.6 1.3 fusion.124
  314.9 9.8 %custom-call.14 = f32[1,128,128]{1,2,0:T(8,128)S(1)} custom-call(f32[1,128,128]{2,1,0:T(8,128)S(1)} %get-tuple-element.312), custom_call_target="InvertDiagBlocksLowerTriangular" | custom-call | tf_op jit(solution)/shard_map/triangular_solve/custom-call.0 | solution.py:207
  325.6 1.2 constant_dynamic-update-slice_fusion.4
  327.6 11.7 %cholesky.167 = f32[128,128]{1,0:T(8,128)S(1)} custom-call(f32[128,128]{1,0:T(8,128)S(1)} %copy.205), custom_call_target="Cholesky" | custom-call | tf_op jit(solution)/shard_map/jit(cholesky)/cholesky | solution.py:206
  340.0 1.3 fusion.125
  341.3 10.2 %custom-call.15 = f32[1,128,128]{1,2,0:T(8,128)S(1)} custom-call(f32[1,128,128]{2,1,0:T(8,128)S(1)} %get-tuple-element.310), custom_call_target="InvertDiagBlocksLowerTriangular" | custom-call | tf_op jit(solution)/shard_map/triangular_solve/custom-call.0 | solution.py:207
  352.4 1.1 convolution_dynamic-update-slice_fusion
  353.5 5.3 convert_subtract_fusion
  359.2 11.7 %cholesky.178 = f32[128,128]{1,0:T(8,128)S(1)} custom-call(f32[128,128]{1,0:T(8,128)S(1)} %copy.209), custom_call_target="Cholesky" | custom-call | tf_op jit(solution)/shard_map/jit(cholesky)/cholesky | solution.py:206
  372.6 4.7 collective-permute-start
  377.3 1.3 fusion.126
  378.6 9.8 %custom-call.16 = f32[1,128,128]{1,2,0:T(8,128)S(1)} custom-call(f32[1,128,128]{2,1,0:T(8,128)S(1)} %get-tuple-element.308), custom_call_target="InvertDiagBlocksLowerTriangular" | custom-call | tf_op jit(solution)/shard_map/triangular_solve/custom-call.0 | solution.py:207
  389.4 4.1 collective-permute-done
  396.2 11.7 %cholesky.189 = f32[128,128]{1,0:T(8,128)S(1)} custom-call(f32[128,128]{1,0:T(8,128)S(1)} %copy.214), custom_call_target="Cholesky" | custom-call | tf_op jit(solution)/shard_map/jit(cholesky)/cholesky | solution.py:206
  408.7 1.3 fusion.127
  410.0 9.8 %custom-call.17 = f32[1,128,128]{1,2,0:T(8,128)S(1)} custom-call(f32[1,128,128]{2,1,0:T(8,128)S(1)} %get-tuple-element.306), custom_call_target="InvertDiagBlocksLowerTriangular" | custom-call | tf_op jit(solution)/shard_map/triangular_solve/custom-call.0 | solution.py:207
  422.4 11.9 %cholesky.200 = f32[128,128]{1,0:T(8,128)S(1)} custom-call(f32[128,128]{1,0:T(8,128)S(1)} %copy.218), custom_call_target="Cholesky" | custom-call | tf_op jit(solution)/shard_map/jit(cholesky)/cholesky | solution.py:206
  435.0 1.3 fusion.128
  436.3 9.8 %custom-call.18 = f32[1,128,128]{1,2,0:T(8,128)S(1)} custom-call(f32[1,128,128]{2,1,0:T(8,128)S(1)} %get-tuple-element.304), custom_call_target="InvertDiagBlocksLowerTriangular" | custom-call | tf_op jit(solution)/shard_map/triangular_solve/custom-call.0 | solution.py:207
  448.4 11.7 %cholesky.211 = f32[128,128]{1,0:T(8,128)S(1)} custom-call(f32[128,128]{1,0:T(8,128)S(1)} %fusion.100), custom_call_target="Cholesky" | custom-call | tf_op jit(solution)/shard_map/jit(cholesky)/cholesky | solution.py:206
  460.9 1.3 fusion.129
  462.2 9.8 %custom-call.19 = f32[1,128,128]{1,2,0:T(8,128)S(1)} custom-call(f32[1,128,128]{2,1,0:T(8,128)S(1)} %get-tuple-element.302), custom_call_target="InvertDiagBlocksLowerTriangular" | custom-call | tf_op jit(solution)/shard_map/triangular_solve/custom-call.0 | solution.py:207
  473.9 1.6 fusion.62
  475.4 1.1 fusion.154
  476.5 2.0 convolution_negate_fusion.6
  481.8 3.1 fusion.33
  484.8 1.9 fusion.26
  486.9 2.8 copy.186
  489.8 14.4 %fusion = f32[3072,1024]{1,0:T(8,128)S(1)} fusion(bf16[2048,1024]{1,0:T(8,128)(2,1)S(1)} %bitcast.224, bf16[1024,1024]{1,0:T(8,128)(2,1)S(1)} %copy-done.6, f32[1,512,512]{2,1,0:T(8,128)S(1)} %get-tuple-element.294, f32[1,512,512]{2,1,0:T(8,128)S(1)} %get-tuple-element.293, f32[1,512,512]{2,1,0:T(8,128)S(1)} %fusion.26), kind=kOutput, calls=%fused_computation.8 | convolution fusion | flops 19344130048 | bytes 22020096 | tf_op jit(solution)/shard_map/dot_general | solution.py:248
  504.1 3.4 subtract_convert_fusion.1
  507.5 2.5 copy-done.2
  509.9 4.4 subtract_convert_fusion
  514.3 20.5 %shard_map.55 = f32[1024,2048]{1,0:T(8,128)} custom-call(s32[1024,1]{1,0:T(8,128)} %fusion.47.rows_ref, s32[1,2048]{1,0:T(1,128)} %fusion.131.cols_ref, f32[1024,2048]{1,0:T(8,128)} %bitcast_add_fusion.m_ref, bf16[1024,1024]{1,0:T(8,128)(2,1)} %get-tuple-element.284.rh_ref, bf16[1024,1024]{1,0:T(8,128)(2,1)} %get-tuple-element.283.rl_ref, ...), custom_call_target="tpu_custom_call" | custom-call | tf_op jit(solution)/shard_map/pallas_call | solution.py:71
  534.8 8.9 %copy.281 = f32[1,1024,1,2048]{3,1,2,0:T(8,128)} copy(f32[1,1024,1,2048]{3,1,2,0:T(8,128)} %bitcast.217) | data formatting | bytes 16777216
  543.7 1.1 copy-done.3
  544.8 1.2 slice_select_fusion
  545.9 2.6 fusion.52
  548.5 11.0 %copy.229 = f32[1,1024,1,2048]{3,2,1,0:T(1,128)} copy(f32[1,1024,1,2048]{3,1,2,0:T(8,128)} %fusion.52) | data formatting | bytes 16777216 | tf_op jit(solution)/shard_map/scatter | solution.py:258
  (147 shorter events, 37.5 us)
Async XLA Ops:
  6.5 16.5 %copy-start = (bf16[64,128,128]{2,1,0:T(8,128)(2,1)S(1)}, bf16[64,128,128]{2,1,0:T(8,128)(2,1)}, u32[]{:S(2)}) copy-start(bf16[64,128,128]{2,1,0:T(8,128)(2,1)} %param.53) | copy-start | bytes 6291460
  11.4 32.8 %all-to-all-start = ((s32[128,1,2]{2,1,0:T(1,128)}), s32[128,1,2]{2,1,0:T(1,128)S(1)}, u32[]{:S(2)}, u32[]{:S(2)}) async-start(s32[128,1,2]{2,1,0:T(1,128)} %bitcast.4), calls=%async_computation | async-start | bytes 131072 | tf_op jit(solution)/shard_map/all_to_all | solution.py:123
  44.3 109.9 %all-to-all-start.1 = ((bf16[128,2,128,128]{3,2,1,0:T(8,128)(2,1)}), bf16[128,2,128,128]{3,2,1,0:T(8,128)(2,1)}, u32[]{:S(2)}, u32[]{:S(2)}) async-start(bf16[128,2,128,128]{3,2,1,0:T(8,128)(2,1)} %select_select_fusion), calls=%async_computation.1 | async-start | bytes 16777216 | tf_op jit(solution)/shard_map/all_to_all | solution.py:116
  54.5 187.0 %all-gather.6.cloned.1.call-start = ((), (), s32[]{:S(2)}) async-start(), calls=%async_computation.2 | async-start | bytes 2228224 | tf_op jit(solution)/shard_map/all_gather | solution.py:161
  163.2 39.3 %copy-start.4 = (bf16[1024,128]{1,0:T(8,128)(2,1)}, bf16[1024,128]{1,0:T(8,128)(2,1)S(1)}, u32[]{:S(2)}) copy-start(bf16[1024,128]{1,0:T(8,128)(2,1)S(1)} %slice_add_fusion) | copy-start | bytes 786436
  177.8 123.3 %all-gather.8.cloned.1.call-start = ((), (), s32[]{:S(2)}) async-start(), calls=%async_computation.3 | async-start | bytes 2228224 | tf_op jit(solution)/shard_map/all_gather | solution.py:163
  242.8 128.8 %all-gather.10.cloned.1.call-start = ((), (), s32[]{:S(2)}) async-start(), calls=%async_computation.4 | async-start | bytes 2359296 | tf_op jit(solution)/shard_map/all_gather | solution.py:166
  301.1 52.4 %slice-start.1 = ((bf16[2048,512]{1,0:T(8,128)(2,1)}), bf16[1024,512]{1,0:T(8,128)(2,1)S(1)}, s32[]{:S(2)}) async-start(bf16[2048,512]{1,0:T(8,128)(2,1)} %all-gather.8.cloned.1.call-done), calls=%async_computation.7 | async-start | bytes 2097152 | tf_op jit(solution)/shard_map/slice | solution.py:163
  301.1 185.8 %all-gather.12.cloned.1.call-start = ((), (), s32[]{:S(2)}) async-start(), calls=%async_computation.5 | async-start | bytes 4456448 | tf_op jit(solution)/shard_map/all_gather | solution.py:178
  372.6 20.9 %collective-permute-start = (bf16[128,1024]{1,0:T(8,128)(2,1)S(1)}, bf16[128,1024]{1,0:T(8,128)(2,1)S(1)}, u32[]{:S(2)}, u32[]{:S(2)}) collective-permute-start(bf16[128,1024]{1,0:T(8,128)(2,1)S(1)} %constant_dynamic-slice_fusion), channel_id=1, source_target_pairs={{0,0},{1,8},{2,16},{3,24},{4,32},{5,40},{6,48},{7,56},{8,1},{9,9},... | collective-permute-start | bytes 786440 | tf_op jit(solution)/shard_map/ppermute | solution.py:177
  393.5 0.7 copy-start.5
  486.9 2.9 copy-start.6
  504.1 5.8 %copy-start.2 = (f32[3072,1024]{1,0:T(8,128)}, f32[3072,1024]{1,0:T(8,128)S(1)}, u32[]{:S(2)}) copy-start(f32[3072,1024]{1,0:T(8,128)S(1)} %fusion) | copy-start | bytes 37748740
  534.8 10.0 %copy-start.3 = (f32[3072,1024]{1,0:T(8,128)S(1)}, f32[3072,1024]{1,0:T(8,128)}, u32[]{:S(2)}) copy-start(f32[3072,1024]{1,0:T(8,128)} %copy-done.2) | copy-start | bytes 37748740
  534.8 11.2 %slice-start = ((f32[3072,1024]{1,0:T(8,128)}), f32[896,1024]{1,0:T(8,128)S(1)}, s32[]{:S(2)}) async-start(f32[3072,1024]{1,0:T(8,128)} %copy-done.2), calls=%async_computation.6 | async-start | bytes 7340032 | tf_op jit(solution)/shard_map/slice | solution.py:256
  548.5 11.0 %copy-start.1 = (bf16[64,128,128]{2,1,0:T(8,128)(2,1)S(1)}, bf16[64,128,128]{2,1,0:T(8,128)(2,1)}, u32[]{:S(2)}) copy-start(bf16[64,128,128]{2,1,0:T(8,128)(2,1)} %param.53) | copy-start | bytes 6291460
Sparse Core Ops, SparseCore 0:
  177.9 48.1 all-gather.5
  242.9 48.4 all-gather.7
  301.3 29.6 all-gather.9
  394.3 51.7 all-gather.11

commit v14 on v13

--- a/solution.py
+++ b/solution.py
@@ -43,7 +43,7 @@
     return matrix - product
 
 
-def _update_kernel(rows_ref, cols_ref, m_ref, rh_ref, rl_ref, ch_ref, cl_ref, o_ref):
+def _update_kernel(rows_ref, cols_ref, m_ref, rh_ref, rl_ref, ch_ref, cl_ref, panel_ref, o_ref):
     dims = (((1,), (1,)), ((), ()))
     r_hi = rh_ref[...]
     c_hi = ch_ref[...]
@@ -53,13 +53,17 @@
     keep = rows_ref[...] >= cols_ref[...]
     o_ref[...] = jnp.where(keep, m_ref[...] - acc, 0.0)
 
+    @pl.when(pl.program_id(1) == 0)
+    def _():
+        o_ref[:, : panel_ref.shape[1]] = panel_ref[...]
+
 
 def split_bf16(x):
     hi = x.astype(jnp.bfloat16)
     return hi, (x - hi.astype(jnp.float32)).astype(jnp.bfloat16)
 
 
-def lower_update(matrix, row_factor, col_factor, global_rows, global_cols):
+def lower_update(matrix, row_factor, col_factor, global_rows, global_cols, panel):
     n_rows, n_cols = matrix.shape
     depth = row_factor.shape[1]
     tm = 512
@@ -79,10 +83,11 @@
             row_spec,
             col_spec,
             col_spec,
+            pl.BlockSpec((tm, panel.shape[1]), lambda i, j: (i, 0)),
         ],
         out_specs=pl.BlockSpec((tm, tn), lambda i, j: (i, j)),
         out_shape=jax.ShapeDtypeStruct(matrix.shape, jnp.float32),
-    )(global_rows[:, None], global_cols[None, :], matrix, r_hi, r_lo, c_hi, c_lo)
+    )(global_rows[:, None], global_cols[None, :], matrix, r_hi, r_lo, c_hi, c_lo, panel)
 
 
 def shards(front_orig, child_tiles, tile_target, tile_rows, tile_cols):
@@ -248,14 +253,13 @@
     solved = jnp.dot(rows_all, factor_inverse.T, precision=hi, preferred_element_type=jnp.float32)
     row_factor = solved[:n_own]
     col_factor = solved[n_own:]
-    matrix = lower_update(matrix, row_factor, col_factor, global_rows, global_cols)
     corner_rows = lax.dynamic_slice_in_dim(
         factor_full, jnp.minimum(row_here, total // width - 1) * width, width, axis=0
     )
     head = jnp.where(row_here * width < total, corner_rows, row_factor[:width])
     panel_vals = jnp.concatenate([head, row_factor[width:]], axis=0)
     own_part = lax.dynamic_slice_in_dim(panel_vals, col_here * width, width, axis=1)
-    result = matrix.at[:, :width].set(own_part)
+    result = lower_update(matrix, row_factor, col_factor, global_rows, global_cols, own_part)
     return result[None, :, None, :]
 
 

time: 574 us -> 561 us (0.977)
  local copies, waits for them, and re-layouts: 98.1 us -> 88.1 us
    unnamed x18 -> x17, local copies, waits for them, and re-layouts: 47.3 us -> 35.4 us
    broadcast_in_dim x0 -> x1, local copies, waits for them, and re-layouts: none -> 11 us  [shards(): return result[None, :, None, :]]
    scatter x1 -> x0, local copies, waits for them, and re-layouts: 11 us -> none  [shards(): result = matrix.at[:, :width].set(own_part)]
  transfers between devices with their start and end apart: 7 -> 7, of which waited for: 2 -> 2; matrix products, arithmetic and copies ran while one was open for 58% -> 60% of each run, Pallas kernels for 0% -> 0%
where the time goes in v14:
time: 561 us; the launch traced here: 553 us
  other arithmetic  229 us (41%)
  waiting for transfers between devices  91.6 us (16%)
  local copies, waits for them, and re-layouts  88.1 us (16%)
  matrix products  69.4 us (12%)
  starting transfers between devices  26.6 us (5%)
  Pallas kernels  20.8 us (4%)
  between operations  14.1 us (3%)
  blocking collectives  13.8 us (2%)
    another operation x24, other arithmetic, shards(): factor = jnp.linalg.cholesky(symmetric)  99.8 us
    all_to_all x1, waiting for transfers between devices, shards(): lax.all_to_all(send_tiles.reshape(owners, CAP, width, width), ('frow', 'f...  87.4 us
    another operation x10, other arithmetic, shards(): lax.linalg.triangular_solve(factor, eye, left_side=True, lower=True)  79.5 us
    unnamed x17, local copies, waits for them, and re-layouts  35.4 us
    pallas_call x1, Pallas kernels, lower_update(): pl.pallas_call(_update_kernel, grid=(n_rows // tm, n_cols // tn), in_spec...  20.8 us
    add x1, other arithmetic, shards(): matrix = local + added  17.4 us
    dot_general x1, matrix products, shards(): jnp.dot(rows_all, factor_inverse.T, precision=hi, preferred_element_type=...  14.4 us
    all_gather x1, blocking collectives, shards(): lax.all_gather(first_column[:width].astype(jnp.bfloat16), 'fcol', axis=1,...  13.8 us
  transfers between devices with their start and end apart: 7, of which 2 were waited for; matrix products, arithmetic and copies ran while one was open for 60% of the time, Pallas kernels for 0%

profile of v14, /device:TPU:6, one launch (start us, length us, event | category | flops | bytes accessed | tf_op | source)
XLA Modules:
  0.0 553.2 jit_solution(324046510356559711)
XLA Ops:
  8.6 1.9 gather_fusion
  11.4 10.5 %all-to-all-start = ((s32[128,1,2]{2,1,0:T(1,128)}), s32[128,1,2]{2,1,0:T(1,128)S(1)}, u32[]{:S(2)}, u32[]{:S(2)}) async-start(s32[128,1,2]{2,1,0:T(1,128)} %bitcast.4), calls=%async_computation | async-start | bytes 131072 | tf_op jit(solution)/shard_map/all_to_all | solution.py:128
  23.0 3.6 fusion.20
  26.7 10.1 %gather_fusion.1 = bf16[256,128,128]{2,1,0:T(8,128)(2,1)} fusion(bf16[64,128,128]{2,1,0:T(8,128)(2,1)} %fusion.20, s32[1024]{0:T(1024)S(1)} %pad_clamp_fusion), kind=kCustom, calls=%fused_computation.1 | custom fusion | bytes 16778240 | tf_op jit(solution)/shard_map/jit(_take)/gather | solution.py:117
  36.8 7.4 %select_select_fusion = bf16[128,2,128,128]{3,2,1,0:T(8,128)(2,1)} fusion(bf16[128,2,128,128]{3,2,1,0:T(8,128)(2,1)} %bitcast.213, pred[128,2]{1,0:T(8,128)(4,1)S(1)} %compare_and_fusion, pred[128,2]{1,0:T(8,128)(4,1)S(1)} %broadcast_in_dim.102), kind=kLoop, calls=%fused_computation.6 | loop fusion | flops 8388608 | bytes 16777728 | tf_op jit(solution)/shard_map/jit(_where)/select_n | solution.py:115
  44.3 10.2 %all-to-all-start.1 = ((bf16[128,2,128,128]{3,2,1,0:T(8,128)(2,1)}), bf16[128,2,128,128]{3,2,1,0:T(8,128)(2,1)}, u32[]{:S(2)}, u32[]{:S(2)}) async-start(bf16[128,2,128,128]{3,2,1,0:T(8,128)(2,1)} %select_select_fusion), calls=%async_computation.1 | async-start | bytes 16777216 | tf_op jit(solution)/shard_map/all_to_all | solution.py:121
  54.7 10.7 %copy.259 = f32[1,1024,1,2048]{3,1,2,0:T(8,128)} copy(f32[1,1024,1,2048]{3,2,1,0:T(1,128)} %param.50) | data formatting | bytes 16777216
  66.8 87.4 %all-to-all-done.1 = bf16[128,2,128,128]{3,2,1,0:T(8,128)(2,1)} async-done(((bf16[128,2,128,128]{3,2,1,0:T(8,128)(2,1)}), bf16[128,2,128,128]{3,2,1,0:T(8,128)(2,1)}, u32[]{:S(2)}, u32[]{:S(2)}) %all-to-all-start.1) | async-done | bytes 8388640 | tf_op jit(solution)/shard_map/all_to_all | solution.py:121
  154.2 7.8 %fusion.132 = f32[8,16384]{1,0:T(8,128)S(1)} fusion(s32[256]{0:T(256)S(1)} %eq.128, s32[8]{0:T(128)S(1)} %iota_multiply_fusion, bf16[32,8,128,128]{3,2,1,0:T(8,128)(2,1)} %bitcast.77), kind=kOutput, calls=%fused_computation.236 | convolution fusion | flops 67110912 | bytes 8913952 | tf_op jit(solution)/shard_map/dot_general | solution.py:151
  162.1 1.1 slice_add_fusion
  163.2 13.8 %all_gather.18 = bf16[128,1024]{1,0:T(8,128)(2,1)S(1)} all-gather(bf16[128,128]{1,0:T(8,128)(2,1)S(1)} %slice.816), channel_id=1, replica_groups=mesh['frow'=16,'fcol'=8] {'fcol'}, dimensions={1}, use_global_device_ids=true | all-gather | bytes 294912 | tf_op jit(solution)/shard_map/all_gather | solution.py:162
  178.5 23.3 %copy.258 = bf16[32,8,128,128]{3,1,2,0:T(8,128)(2,1)} copy(bf16[32,8,128,128]{3,2,1,0:T(8,128)(2,1)} %bitcast.77) | data formatting | bytes 16777216
  201.9 11.9 %copy.185 = bf16[256,16384]{0,1:T(8,128)(2,1)} copy(bf16[256,16384]{1,0:T(8,128)(2,1)} %bitcast.214) | data formatting | bytes 16777216 | tf_op jit(solution)/shard_map/reshape | solution.py:152
  213.7 9.7 %fusion.90 = f32[8,16,128,128]{3,1,2,0:T(8,128)} fusion(bf16[128,128,256,1]{2,1,0,3:T(8,128)(2,1)} %bitcast.218, s32[8,16]{1,0:T(8,128)S(1)} %multiply_add_fusion, s32[256]{0:T(256)S(1)} %eq.128), kind=kOutput, calls=%fused_computation.126 | convolution fusion | flops 1073774592 | bytes 16778752 | tf_op jit(solution)/shard_map/dot_general | solution.py:140
  223.4 17.4 %bitcast_add_fusion.m_ref = f32[1024,2048]{1,0:T(8,128)} fusion(f32[128,8,16,128]{3,2,1,0:T(8,128)} %bitcast.217, f32[1,1024,1,2048]{3,2,1,0:T(1,128)} %param.50), kind=kLoop, calls=%fused_computation.2 | loop fusion | flops 2097152 | bytes 25165824 | tf_op jit(solution)/shard_map/add | solution.py:148
  240.8 1.3 slice.698
  244.6 11.7 %cholesky.134 = f32[128,128]{1,0:T(8,128)S(1)} custom-call(f32[128,128]{1,0:T(8,128)S(1)} %fusion.111), custom_call_target="Cholesky" | custom-call | tf_op jit(solution)/shard_map/jit(cholesky)/cholesky | solution.py:211
  257.7 9.8 %custom-call.12 = f32[1,128,128]{1,2,0:T(8,128)S(1)} custom-call(f32[1,128,128]{2,1,0:T(8,128)S(1)} %get-tuple-element.273), custom_call_target="InvertDiagBlocksLowerTriangular" | custom-call | tf_op jit(solution)/shard_map/triangular_solve/custom-call.0 | solution.py:212
  267.5 2.5 scatter.50
  271.0 1.1 constant_dynamic-update-slice_fusion
  272.1 1.3 fusion.25
  273.6 11.9 %cholesky.145 = f32[128,128]{1,0:T(8,128)S(1)} custom-call(f32[128,128]{1,0:T(8,128)S(1)} %fusion.109), custom_call_target="Cholesky" | custom-call | tf_op jit(solution)/shard_map/jit(cholesky)/cholesky | solution.py:211
  286.1 1.2 fusion.120
  287.3 9.8 %custom-call.13 = f32[1,128,128]{1,2,0:T(8,128)S(1)} custom-call(f32[1,128,128]{2,1,0:T(8,128)S(1)} %get-tuple-element.302), custom_call_target="InvertDiagBlocksLowerTriangular" | custom-call | tf_op jit(solution)/shard_map/triangular_solve/custom-call.0 | solution.py:212
  298.1 1.2 constant_dynamic-update-slice_fusion.5
  300.4 11.7 %cholesky.156 = f32[128,128]{1,0:T(8,128)S(1)} custom-call(f32[128,128]{1,0:T(8,128)S(1)} %fusion.107), custom_call_target="Cholesky" | custom-call | tf_op jit(solution)/shard_map/jit(cholesky)/cholesky | solution.py:211
  312.9 1.3 fusion.121
  314.1 9.8 %custom-call.14 = f32[1,128,128]{1,2,0:T(8,128)S(1)} custom-call(f32[1,128,128]{2,1,0:T(8,128)S(1)} %get-tuple-element.300), custom_call_target="InvertDiagBlocksLowerTriangular" | custom-call | tf_op jit(solution)/shard_map/triangular_solve/custom-call.0 | solution.py:212
  324.9 1.2 constant_dynamic-update-slice_fusion.4
  326.8 11.7 %cholesky.167 = f32[128,128]{1,0:T(8,128)S(1)} custom-call(f32[128,128]{1,0:T(8,128)S(1)} %copy.205), custom_call_target="Cholesky" | custom-call | tf_op jit(solution)/shard_map/jit(cholesky)/cholesky | solution.py:211
  339.2 1.3 fusion.122
  340.5 10.2 %custom-call.15 = f32[1,128,128]{1,2,0:T(8,128)S(1)} custom-call(f32[1,128,128]{2,1,0:T(8,128)S(1)} %get-tuple-element.298), custom_call_target="InvertDiagBlocksLowerTriangular" | custom-call | tf_op jit(solution)/shard_map/triangular_solve/custom-call.0 | solution.py:212
  351.6 1.1 convolution_dynamic-update-slice_fusion
  352.7 5.3 convert_subtract_fusion
  358.4 11.7 %cholesky.178 = f32[128,128]{1,0:T(8,128)S(1)} custom-call(f32[128,128]{1,0:T(8,128)S(1)} %copy.209), custom_call_target="Cholesky" | custom-call | tf_op jit(solution)/shard_map/jit(cholesky)/cholesky | solution.py:211
  371.8 4.8 collective-permute-start
  376.6 1.3 fusion.123
  377.9 9.8 %custom-call.16 = f32[1,128,128]{1,2,0:T(8,128)S(1)} custom-call(f32[1,128,128]{2,1,0:T(8,128)S(1)} %get-tuple-element.296), custom_call_target="InvertDiagBlocksLowerTriangular" | custom-call | tf_op jit(solution)/shard_map/triangular_solve/custom-call.0 | solution.py:212
  388.6 4.1 collective-permute-done
  393.4 1.0 constant_dynamic-update-slice_fusion.3
  395.4 11.7 %cholesky.189 = f32[128,128]{1,0:T(8,128)S(1)} custom-call(f32[128,128]{1,0:T(8,128)S(1)} %copy.214), custom_call_target="Cholesky" | custom-call | tf_op jit(solution)/shard_map/jit(cholesky)/cholesky | solution.py:211
  407.9 1.3 fusion.124
  409.2 9.8 %custom-call.17 = f32[1,128,128]{1,2,0:T(8,128)S(1)} custom-call(f32[1,128,128]{2,1,0:T(8,128)S(1)} %get-tuple-element.294), custom_call_target="InvertDiagBlocksLowerTriangular" | custom-call | tf_op jit(solution)/shard_map/triangular_solve/custom-call.0 | solution.py:212
  421.6 11.9 %cholesky.200 = f32[128,128]{1,0:T(8,128)S(1)} custom-call(f32[128,128]{1,0:T(8,128)S(1)} %copy.218), custom_call_target="Cholesky" | custom-call | tf_op jit(solution)/shard_map/jit(cholesky)/cholesky | solution.py:211
  434.2 1.3 fusion.125
  435.5 9.8 %custom-call.18 = f32[1,128,128]{1,2,0:T(8,128)S(1)} custom-call(f32[1,128,128]{2,1,0:T(8,128)S(1)} %get-tuple-element.292), custom_call_target="InvertDiagBlocksLowerTriangular" | custom-call | tf_op jit(solution)/shard_map/triangular_solve/custom-call.0 | solution.py:212
  447.6 11.7 %cholesky.211 = f32[128,128]{1,0:T(8,128)S(1)} custom-call(f32[128,128]{1,0:T(8,128)S(1)} %fusion.97), custom_call_target="Cholesky" | custom-call | tf_op jit(solution)/shard_map/jit(cholesky)/cholesky | solution.py:211
  460.0 1.3 fusion.126
  461.3 9.8 %custom-call.19 = f32[1,128,128]{1,2,0:T(8,128)S(1)} custom-call(f32[1,128,128]{2,1,0:T(8,128)S(1)} %get-tuple-element.290), custom_call_target="InvertDiagBlocksLowerTriangular" | custom-call | tf_op jit(solution)/shard_map/triangular_solve/custom-call.0 | solution.py:212
  473.0 1.5 fusion.59
  474.5 1.1 fusion.151
  475.6 2.0 convolution_negate_fusion.6
  477.7 1.1 slice_bitcast_fusion.1
  478.8 1.0 fusion.50
  480.9 3.1 fusion.33
  483.9 1.8 fusion.26
  485.8 1.5 fusion.149
  487.3 2.8 copy.186
  490.8 14.4 %fusion = f32[3072,1024]{1,0:T(8,128)S(1)} fusion(bf16[2048,1024]{1,0:T(8,128)(2,1)S(1)} %bitcast.220, bf16[1024,1024]{1,0:T(8,128)(2,1)S(1)} %copy-done.6, f32[1,512,512]{2,1,0:T(8,128)S(1)} %copy-done.4, f32[1,512,512]{2,1,0:T(8,128)S(1)} %copy-done.3, f32[1,512,512]{2,1,0:T(8,128)S(1)} %fusion.26), kind=kOutput, calls=%fused_computation.8 | convolution fusion | flops 19344130048 | bytes 22020096 | tf_op jit(solution)/shard_map/dot_general | solution.py:253
  505.7 4.1 subtract_convert_fusion
  509.7 2.9 subtract_convert_fusion.1
  512.7 1.1 slice_select_fusion
  514.7 20.8 %shard_map.55 = f32[1024,2048]{1,0:T(8,128)} custom-call(s32[1024,1]{1,0:T(8,128)} %fusion.47.rows_ref, s32[1,2048]{1,0:T(1,128)} %fusion.128.cols_ref, f32[1024,2048]{1,0:T(8,128)} %bitcast_add_fusion.m_ref, bf16[1024,1024]{1,0:T(8,128)(2,1)} %get-tuple-element.272.rh_ref, bf16[1024,1024]{1,0:T(8,128)(2,1)} %get-tuple-element.271.rl_ref, ...), custom_call_target="tpu_custom_call" | custom-call | tf_op jit(solution)/shard_map/pallas_call | solution.py:75
  535.5 11.0 %copy.229 = f32[1,1024,1,2048]{3,2,1,0:T(1,128)} copy(f32[1,1024,1,2048]{3,1,2,0:T(8,128)} %bitcast.215) | data formatting | bytes 16777216 | tf_op jit(solution)/shard_map/broadcast_in_dim | solution.py:263
  (144 shorter events, 35.4 us)
Async XLA Ops:
  6.5 16.5 %copy-start = (bf16[64,128,128]{2,1,0:T(8,128)(2,1)S(1)}, bf16[64,128,128]{2,1,0:T(8,128)(2,1)}, u32[]{:S(2)}) copy-start(bf16[64,128,128]{2,1,0:T(8,128)(2,1)} %param.51) | copy-start | bytes 6291460
  11.4 32.8 %all-to-all-start = ((s32[128,1,2]{2,1,0:T(1,128)}), s32[128,1,2]{2,1,0:T(1,128)S(1)}, u32[]{:S(2)}, u32[]{:S(2)}) async-start(s32[128,1,2]{2,1,0:T(1,128)} %bitcast.4), calls=%async_computation | async-start | bytes 131072 | tf_op jit(solution)/shard_map/all_to_all | solution.py:128
  44.3 109.9 %all-to-all-start.1 = ((bf16[128,2,128,128]{3,2,1,0:T(8,128)(2,1)}), bf16[128,2,128,128]{3,2,1,0:T(8,128)(2,1)}, u32[]{:S(2)}, u32[]{:S(2)}) async-start(bf16[128,2,128,128]{3,2,1,0:T(8,128)(2,1)} %select_select_fusion), calls=%async_computation.1 | async-start | bytes 16777216 | tf_op jit(solution)/shard_map/all_to_all | solution.py:121
  54.5 186.3 %all-gather.6.cloned.1.call-start = ((), (), s32[]{:S(2)}) async-start(), calls=%async_computation.2 | async-start | bytes 2228224 | tf_op jit(solution)/shard_map/all_gather | solution.py:166
  163.2 38.6 %copy-start.2 = (bf16[1024,128]{1,0:T(8,128)(2,1)}, bf16[1024,128]{1,0:T(8,128)(2,1)S(1)}, u32[]{:S(2)}) copy-start(bf16[1024,128]{1,0:T(8,128)(2,1)S(1)} %slice_add_fusion) | copy-start | bytes 786436
  177.8 122.6 %all-gather.8.cloned.1.call-start = ((), (), s32[]{:S(2)}) async-start(), calls=%async_computation.3 | async-start | bytes 2228224 | tf_op jit(solution)/shard_map/all_gather | solution.py:168
  242.1 128.7 %all-gather.10.cloned.1.call-start = ((), (), s32[]{:S(2)}) async-start(), calls=%async_computation.4 | async-start | bytes 2359296 | tf_op jit(solution)/shard_map/all_gather | solution.py:171
  300.3 52.4 %slice-start = ((bf16[2048,512]{1,0:T(8,128)(2,1)}), bf16[1024,512]{1,0:T(8,128)(2,1)S(1)}, s32[]{:S(2)}) async-start(bf16[2048,512]{1,0:T(8,128)(2,1)} %all-gather.8.cloned.1.call-done), calls=%async_computation.6 | async-start | bytes 2097152 | tf_op jit(solution)/shard_map/slice | solution.py:168
  300.4 186.9 %all-gather.12.cloned.1.call-start = ((), (), s32[]{:S(2)}) async-start(), calls=%async_computation.5 | async-start | bytes 4456448 | tf_op jit(solution)/shard_map/all_gather | solution.py:183
  371.8 20.9 %collective-permute-start = (bf16[128,1024]{1,0:T(8,128)(2,1)S(1)}, bf16[128,1024]{1,0:T(8,128)(2,1)S(1)}, u32[]{:S(2)}, u32[]{:S(2)}) collective-permute-start(bf16[128,1024]{1,0:T(8,128)(2,1)S(1)} %constant_dynamic-slice_fusion), channel_id=1, source_target_pairs={{0,0},{1,8},{2,16},{3,24},{4,32},{5,40},{6,48},{7,56},{8,1},{9,9},... | collective-permute-start | bytes 786440 | tf_op jit(solution)/shard_map/ppermute | solution.py:182
  392.7 0.7 copy-start.5
  487.3 2.8 copy-start.3
  487.3 2.9 copy-start.4
  487.3 3.5 copy-start.6
  535.5 11.0 %copy-start.1 = (bf16[64,128,128]{2,1,0:T(8,128)(2,1)S(1)}, bf16[64,128,128]{2,1,0:T(8,128)(2,1)}, u32[]{:S(2)}) copy-start(bf16[64,128,128]{2,1,0:T(8,128)(2,1)} %param.51) | copy-start | bytes 6291460
Sparse Core Ops, SparseCore 0:
  177.9 48.1 all-gather.5
  242.2 48.2 all-gather.7
  300.5 29.8 all-gather.9
  393.5 51.8 all-gather.11

commit v15 on v14

--- a/solution.py
+++ b/solution.py
@@ -67,7 +67,7 @@
     n_rows, n_cols = matrix.shape
     depth = row_factor.shape[1]
     tm = 512
-    tn = 512
+    tn = 1024
     r_hi, r_lo = split_bf16(row_factor)
     c_hi, c_lo = split_bf16(col_factor)
     row_spec = pl.BlockSpec((tm, depth), lambda i, j: (i, 0))

time: 561 us -> 560 us (level)
  no operation moved by 1% of the time
where the time goes in v15:
time: 560 us; the launch traced here: 552 us
  other arithmetic  229 us (41%)
  waiting for transfers between devices  91.6 us (16%)
  local copies, waits for them, and re-layouts  88.1 us (16%)
  matrix products  69.4 us (12%)
  starting transfers between devices  26.6 us (5%)
  Pallas kernels  19.6 us (4%)
  between operations  14.2 us (3%)
  blocking collectives  13.8 us (2%)
    another operation x24, other arithmetic, shards(): factor = jnp.linalg.cholesky(symmetric)  99.8 us
    all_to_all x1, waiting for transfers between devices, shards(): lax.all_to_all(send_tiles.reshape(owners, CAP, width, width), ('frow', 'f...  87.4 us
    another operation x10, other arithmetic, shards(): lax.linalg.triangular_solve(factor, eye, left_side=True, lower=True)  79.5 us
    unnamed x17, local copies, waits for them, and re-layouts  35.4 us
    pallas_call x1, Pallas kernels, lower_update(): pl.pallas_call(_update_kernel, grid=(n_rows // tm, n_cols // tn), in_spec...  19.6 us
    add x1, other arithmetic, shards(): matrix = local + added  17.4 us
    dot_general x1, matrix products, shards(): jnp.dot(rows_all, factor_inverse.T, precision=hi, preferred_element_type=...  14.4 us
    all_gather x1, blocking collectives, shards(): lax.all_gather(first_column[:width].astype(jnp.bfloat16), 'fcol', axis=1,...  13.8 us
  transfers between devices with their start and end apart: 7, of which 2 were waited for; matrix products, arithmetic and copies ran while one was open for 60% of the time, Pallas kernels for 0%

profile of v15, /device:TPU:6, one launch (start us, length us, event | category | flops | bytes accessed | tf_op | source)
XLA Modules:
  0.0 552.3 jit_solution(14378132241020277148)
XLA Ops:
  8.6 1.9 gather_fusion
  11.4 10.5 %all-to-all-start = ((s32[128,1,2]{2,1,0:T(1,128)}), s32[128,1,2]{2,1,0:T(1,128)S(1)}, u32[]{:S(2)}, u32[]{:S(2)}) async-start(s32[128,1,2]{2,1,0:T(1,128)} %bitcast.4), calls=%async_computation | async-start | bytes 131072 | tf_op jit(solution)/shard_map/all_to_all | solution.py:128
  23.0 3.6 fusion.20
  26.7 10.1 %gather_fusion.1 = bf16[256,128,128]{2,1,0:T(8,128)(2,1)} fusion(bf16[64,128,128]{2,1,0:T(8,128)(2,1)} %fusion.20, s32[1024]{0:T(1024)S(1)} %pad_clamp_fusion), kind=kCustom, calls=%fused_computation.1 | custom fusion | bytes 16778240 | tf_op jit(solution)/shard_map/jit(_take)/gather | solution.py:117
  36.8 7.4 %select_select_fusion = bf16[128,2,128,128]{3,2,1,0:T(8,128)(2,1)} fusion(bf16[128,2,128,128]{3,2,1,0:T(8,128)(2,1)} %bitcast.213, pred[128,2]{1,0:T(8,128)(4,1)S(1)} %compare_and_fusion, pred[128,2]{1,0:T(8,128)(4,1)S(1)} %broadcast_in_dim.102), kind=kLoop, calls=%fused_computation.6 | loop fusion | flops 8388608 | bytes 16777728 | tf_op jit(solution)/shard_map/jit(_where)/select_n | solution.py:115
  44.3 10.2 %all-to-all-start.1 = ((bf16[128,2,128,128]{3,2,1,0:T(8,128)(2,1)}), bf16[128,2,128,128]{3,2,1,0:T(8,128)(2,1)}, u32[]{:S(2)}, u32[]{:S(2)}) async-start(bf16[128,2,128,128]{3,2,1,0:T(8,128)(2,1)} %select_select_fusion), calls=%async_computation.1 | async-start | bytes 16777216 | tf_op jit(solution)/shard_map/all_to_all | solution.py:121
  54.7 10.7 %copy.259 = f32[1,1024,1,2048]{3,1,2,0:T(8,128)} copy(f32[1,1024,1,2048]{3,2,1,0:T(1,128)} %param.50) | data formatting | bytes 16777216
  66.8 87.4 %all-to-all-done.1 = bf16[128,2,128,128]{3,2,1,0:T(8,128)(2,1)} async-done(((bf16[128,2,128,128]{3,2,1,0:T(8,128)(2,1)}), bf16[128,2,128,128]{3,2,1,0:T(8,128)(2,1)}, u32[]{:S(2)}, u32[]{:S(2)}) %all-to-all-start.1) | async-done | bytes 8388640 | tf_op jit(solution)/shard_map/all_to_all | solution.py:121
  154.2 7.8 %fusion.132 = f32[8,16384]{1,0:T(8,128)S(1)} fusion(s32[256]{0:T(256)S(1)} %eq.128, s32[8]{0:T(128)S(1)} %iota_multiply_fusion, bf16[32,8,128,128]{3,2,1,0:T(8,128)(2,1)} %bitcast.77), kind=kOutput, calls=%fused_computation.236 | convolution fusion | flops 67110912 | bytes 8913952 | tf_op jit(solution)/shard_map/dot_general | solution.py:151
  162.1 1.1 slice_add_fusion
  163.2 13.8 %all_gather.18 = bf16[128,1024]{1,0:T(8,128)(2,1)S(1)} all-gather(bf16[128,128]{1,0:T(8,128)(2,1)S(1)} %slice.816), channel_id=1, replica_groups=mesh['frow'=16,'fcol'=8] {'fcol'}, dimensions={1}, use_global_device_ids=true | all-gather | bytes 294912 | tf_op jit(solution)/shard_map/all_gather | solution.py:162
  178.5 23.3 %copy.258 = bf16[32,8,128,128]{3,1,2,0:T(8,128)(2,1)} copy(bf16[32,8,128,128]{3,2,1,0:T(8,128)(2,1)} %bitcast.77) | data formatting | bytes 16777216
  201.8 11.9 %copy.185 = bf16[256,16384]{0,1:T(8,128)(2,1)} copy(bf16[256,16384]{1,0:T(8,128)(2,1)} %bitcast.214) | data formatting | bytes 16777216 | tf_op jit(solution)/shard_map/reshape | solution.py:152
  213.7 9.7 %fusion.90 = f32[8,16,128,128]{3,1,2,0:T(8,128)} fusion(bf16[128,128,256,1]{2,1,0,3:T(8,128)(2,1)} %bitcast.218, s32[8,16]{1,0:T(8,128)S(1)} %multiply_add_fusion, s32[256]{0:T(256)S(1)} %eq.128), kind=kOutput, calls=%fused_computation.126 | convolution fusion | flops 1073774592 | bytes 16778752 | tf_op jit(solution)/shard_map/dot_general | solution.py:140
  223.4 17.4 %bitcast_add_fusion.m_ref = f32[1024,2048]{1,0:T(8,128)} fusion(f32[128,8,16,128]{3,2,1,0:T(8,128)} %bitcast.217, f32[1,1024,1,2048]{3,2,1,0:T(1,128)} %param.50), kind=kLoop, calls=%fused_computation.2 | loop fusion | flops 2097152 | bytes 25165824 | tf_op jit(solution)/shard_map/add | solution.py:148
  240.7 1.3 slice.698
  244.6 11.7 %cholesky.134 = f32[128,128]{1,0:T(8,128)S(1)} custom-call(f32[128,128]{1,0:T(8,128)S(1)} %fusion.111), custom_call_target="Cholesky" | custom-call | tf_op jit(solution)/shard_map/jit(cholesky)/cholesky | solution.py:211
  257.7 9.8 %custom-call.12 = f32[1,128,128]{1,2,0:T(8,128)S(1)} custom-call(f32[1,128,128]{2,1,0:T(8,128)S(1)} %get-tuple-element.273), custom_call_target="InvertDiagBlocksLowerTriangular" | custom-call | tf_op jit(solution)/shard_map/triangular_solve/custom-call.0 | solution.py:212
  267.5 2.5 scatter.50
  270.9 1.1 constant_dynamic-update-slice_fusion
  272.1 1.3 fusion.25
  273.6 11.9 %cholesky.145 = f32[128,128]{1,0:T(8,128)S(1)} custom-call(f32[128,128]{1,0:T(8,128)S(1)} %fusion.109), custom_call_target="Cholesky" | custom-call | tf_op jit(solution)/shard_map/jit(cholesky)/cholesky | solution.py:211
  286.1 1.2 fusion.120
  287.3 9.8 %custom-call.13 = f32[1,128,128]{1,2,0:T(8,128)S(1)} custom-call(f32[1,128,128]{2,1,0:T(8,128)S(1)} %get-tuple-element.302), custom_call_target="InvertDiagBlocksLowerTriangular" | custom-call | tf_op jit(solution)/shard_map/triangular_solve/custom-call.0 | solution.py:212
  298.0 1.2 constant_dynamic-update-slice_fusion.5
  300.4 11.7 %cholesky.156 = f32[128,128]{1,0:T(8,128)S(1)} custom-call(f32[128,128]{1,0:T(8,128)S(1)} %fusion.107), custom_call_target="Cholesky" | custom-call | tf_op jit(solution)/shard_map/jit(cholesky)/cholesky | solution.py:211
  312.9 1.3 fusion.121
  314.1 9.8 %custom-call.14 = f32[1,128,128]{1,2,0:T(8,128)S(1)} custom-call(f32[1,128,128]{2,1,0:T(8,128)S(1)} %get-tuple-element.300), custom_call_target="InvertDiagBlocksLowerTriangular" | custom-call | tf_op jit(solution)/shard_map/triangular_solve/custom-call.0 | solution.py:212
  324.9 1.2 constant_dynamic-update-slice_fusion.4
  326.8 11.7 %cholesky.167 = f32[128,128]{1,0:T(8,128)S(1)} custom-call(f32[128,128]{1,0:T(8,128)S(1)} %copy.205), custom_call_target="Cholesky" | custom-call | tf_op jit(solution)/shard_map/jit(cholesky)/cholesky | solution.py:211
  339.2 1.3 fusion.122
  340.5 10.2 %custom-call.15 = f32[1,128,128]{1,2,0:T(8,128)S(1)} custom-call(f32[1,128,128]{2,1,0:T(8,128)S(1)} %get-tuple-element.298), custom_call_target="InvertDiagBlocksLowerTriangular" | custom-call | tf_op jit(solution)/shard_map/triangular_solve/custom-call.0 | solution.py:212
  351.6 1.1 convolution_dynamic-update-slice_fusion
  352.7 5.3 convert_subtract_fusion
  358.4 11.7 %cholesky.178 = f32[128,128]{1,0:T(8,128)S(1)} custom-call(f32[128,128]{1,0:T(8,128)S(1)} %copy.209), custom_call_target="Cholesky" | custom-call | tf_op jit(solution)/shard_map/jit(cholesky)/cholesky | solution.py:211
  371.8 4.8 collective-permute-start
  376.6 1.3 fusion.123
  377.8 9.8 %custom-call.16 = f32[1,128,128]{1,2,0:T(8,128)S(1)} custom-call(f32[1,128,128]{2,1,0:T(8,128)S(1)} %get-tuple-element.296), custom_call_target="InvertDiagBlocksLowerTriangular" | custom-call | tf_op jit(solution)/shard_map/triangular_solve/custom-call.0 | solution.py:212
  388.6 4.1 collective-permute-done
  393.4 1.0 constant_dynamic-update-slice_fusion.3
  395.4 11.7 %cholesky.189 = f32[128,128]{1,0:T(8,128)S(1)} custom-call(f32[128,128]{1,0:T(8,128)S(1)} %copy.214), custom_call_target="Cholesky" | custom-call | tf_op jit(solution)/shard_map/jit(cholesky)/cholesky | solution.py:211
  407.9 1.3 fusion.124
  409.2 9.8 %custom-call.17 = f32[1,128,128]{1,2,0:T(8,128)S(1)} custom-call(f32[1,128,128]{2,1,0:T(8,128)S(1)} %get-tuple-element.294), custom_call_target="InvertDiagBlocksLowerTriangular" | custom-call | tf_op jit(solution)/shard_map/triangular_solve/custom-call.0 | solution.py:212
  421.5 11.9 %cholesky.200 = f32[128,128]{1,0:T(8,128)S(1)} custom-call(f32[128,128]{1,0:T(8,128)S(1)} %copy.218), custom_call_target="Cholesky" | custom-call | tf_op jit(solution)/shard_map/jit(cholesky)/cholesky | solution.py:211
  434.2 1.3 fusion.125
  435.4 9.8 %custom-call.18 = f32[1,128,128]{1,2,0:T(8,128)S(1)} custom-call(f32[1,128,128]{2,1,0:T(8,128)S(1)} %get-tuple-element.292), custom_call_target="InvertDiagBlocksLowerTriangular" | custom-call | tf_op jit(solution)/shard_map/triangular_solve/custom-call.0 | solution.py:212
  447.6 11.7 %cholesky.211 = f32[128,128]{1,0:T(8,128)S(1)} custom-call(f32[128,128]{1,0:T(8,128)S(1)} %fusion.97), custom_call_target="Cholesky" | custom-call | tf_op jit(solution)/shard_map/jit(cholesky)/cholesky | solution.py:211
  460.0 1.3 fusion.126
  461.3 9.8 %custom-call.19 = f32[1,128,128]{1,2,0:T(8,128)S(1)} custom-call(f32[1,128,128]{2,1,0:T(8,128)S(1)} %get-tuple-element.290), custom_call_target="InvertDiagBlocksLowerTriangular" | custom-call | tf_op jit(solution)/shard_map/triangular_solve/custom-call.0 | solution.py:212
  473.0 1.5 fusion.59
  474.5 1.1 fusion.151
  475.6 2.0 convolution_negate_fusion.6
  477.7 1.1 slice_bitcast_fusion.1
  478.8 1.0 fusion.50
  480.9 3.1 fusion.33
  483.9 1.8 fusion.26
  485.8 1.5 fusion.149
  487.3 2.8 copy.186
  490.8 14.4 %fusion = f32[3072,1024]{1,0:T(8,128)S(1)} fusion(bf16[2048,1024]{1,0:T(8,128)(2,1)S(1)} %bitcast.220, bf16[1024,1024]{1,0:T(8,128)(2,1)S(1)} %copy-done.6, f32[1,512,512]{2,1,0:T(8,128)S(1)} %copy-done.4, f32[1,512,512]{2,1,0:T(8,128)S(1)} %copy-done.3, f32[1,512,512]{2,1,0:T(8,128)S(1)} %fusion.26), kind=kOutput, calls=%fused_computation.8 | convolution fusion | flops 19344130048 | bytes 22020096 | tf_op jit(solution)/shard_map/dot_general | solution.py:253
  505.6 4.3 subtract_convert_fusion
  510.0 2.9 subtract_convert_fusion.1
  512.9 1.1 slice_select_fusion
  514.9 19.6 %shard_map.55 = f32[1024,2048]{1,0:T(8,128)} custom-call(s32[1024,1]{1,0:T(8,128)} %fusion.47.rows_ref, s32[1,2048]{1,0:T(1,128)} %fusion.128.cols_ref, f32[1024,2048]{1,0:T(8,128)} %bitcast_add_fusion.m_ref, bf16[1024,1024]{1,0:T(8,128)(2,1)} %get-tuple-element.272.rh_ref, bf16[1024,1024]{1,0:T(8,128)(2,1)} %get-tuple-element.271.rl_ref, ...), custom_call_target="tpu_custom_call" | custom-call | tf_op jit(solution)/shard_map/pallas_call | solution.py:75
  534.5 11.0 %copy.229 = f32[1,1024,1,2048]{3,2,1,0:T(1,128)} copy(f32[1,1024,1,2048]{3,1,2,0:T(8,128)} %bitcast.215) | data formatting | bytes 16777216 | tf_op jit(solution)/shard_map/broadcast_in_dim | solution.py:263
  (144 shorter events, 35.4 us)
Async XLA Ops:
  6.5 16.5 %copy-start = (bf16[64,128,128]{2,1,0:T(8,128)(2,1)S(1)}, bf16[64,128,128]{2,1,0:T(8,128)(2,1)}, u32[]{:S(2)}) copy-start(bf16[64,128,128]{2,1,0:T(8,128)(2,1)} %param.51) | copy-start | bytes 6291460
  11.4 32.8 %all-to-all-start = ((s32[128,1,2]{2,1,0:T(1,128)}), s32[128,1,2]{2,1,0:T(1,128)S(1)}, u32[]{:S(2)}, u32[]{:S(2)}) async-start(s32[128,1,2]{2,1,0:T(1,128)} %bitcast.4), calls=%async_computation | async-start | bytes 131072 | tf_op jit(solution)/shard_map/all_to_all | solution.py:128
  44.3 109.9 %all-to-all-start.1 = ((bf16[128,2,128,128]{3,2,1,0:T(8,128)(2,1)}), bf16[128,2,128,128]{3,2,1,0:T(8,128)(2,1)}, u32[]{:S(2)}, u32[]{:S(2)}) async-start(bf16[128,2,128,128]{3,2,1,0:T(8,128)(2,1)} %select_select_fusion), calls=%async_computation.1 | async-start | bytes 16777216 | tf_op jit(solution)/shard_map/all_to_all | solution.py:121
  54.5 186.3 %all-gather.6.cloned.1.call-start = ((), (), s32[]{:S(2)}) async-start(), calls=%async_computation.2 | async-start | bytes 2228224 | tf_op jit(solution)/shard_map/all_gather | solution.py:166
  163.2 38.6 %copy-start.2 = (bf16[1024,128]{1,0:T(8,128)(2,1)}, bf16[1024,128]{1,0:T(8,128)(2,1)S(1)}, u32[]{:S(2)}) copy-start(bf16[1024,128]{1,0:T(8,128)(2,1)S(1)} %slice_add_fusion) | copy-start | bytes 786436
  177.7 122.6 %all-gather.8.cloned.1.call-start = ((), (), s32[]{:S(2)}) async-start(), calls=%async_computation.3 | async-start | bytes 2228224 | tf_op jit(solution)/shard_map/all_gather | solution.py:168
  242.1 128.7 %all-gather.10.cloned.1.call-start = ((), (), s32[]{:S(2)}) async-start(), calls=%async_computation.4 | async-start | bytes 2359296 | tf_op jit(solution)/shard_map/all_gather | solution.py:171
  300.3 52.4 %slice-start = ((bf16[2048,512]{1,0:T(8,128)(2,1)}), bf16[1024,512]{1,0:T(8,128)(2,1)S(1)}, s32[]{:S(2)}) async-start(bf16[2048,512]{1,0:T(8,128)(2,1)} %all-gather.8.cloned.1.call-done), calls=%async_computation.6 | async-start | bytes 2097152 | tf_op jit(solution)/shard_map/slice | solution.py:168
  300.4 186.9 %all-gather.12.cloned.1.call-start = ((), (), s32[]{:S(2)}) async-start(), calls=%async_computation.5 | async-start | bytes 4456448 | tf_op jit(solution)/shard_map/all_gather | solution.py:183
  371.8 20.9 %collective-permute-start = (bf16[128,1024]{1,0:T(8,128)(2,1)S(1)}, bf16[128,1024]{1,0:T(8,128)(2,1)S(1)}, u32[]{:S(2)}, u32[]{:S(2)}) collective-permute-start(bf16[128,1024]{1,0:T(8,128)(2,1)S(1)} %constant_dynamic-slice_fusion), channel_id=1, source_target_pairs={{0,0},{1,8},{2,16},{3,24},{4,32},{5,40},{6,48},{7,56},{8,1},{9,9},... | collective-permute-start | bytes 786440 | tf_op jit(solution)/shard_map/ppermute | solution.py:182
  392.7 0.7 copy-start.5
  487.3 2.8 copy-start.3
  487.3 2.9 copy-start.4
  487.3 3.5 copy-start.6
  534.5 11.0 %copy-start.1 = (bf16[64,128,128]{2,1,0:T(8,128)(2,1)S(1)}, bf16[64,128,128]{2,1,0:T(8,128)(2,1)}, u32[]{:S(2)}) copy-start(bf16[64,128,128]{2,1,0:T(8,128)(2,1)} %param.51) | copy-start | bytes 6291460
Sparse Core Ops, SparseCore 0:
  177.9 48.1 all-gather.5
  242.2 48.3 all-gather.7
  300.5 29.8 all-gather.9
  393.5 51.8 all-gather.11
